TPU v7x, 32 devices: a whole 2x2x4 slice. The times are simulated.
32 devices in a mesh: ctx: 4 (over z), fsdp: 2 (over y), rep: 4 (over x, core).
Axes of the slice: x: 2, y: 2, z: 4, core: 2. Of those that a mesh axis runs over, the one named last changes fastest.
Arguments:
- frames_in: bfloat16 [8, 512, 1024], P('rep', 'ctx', 'fsdp'), parts along dimension 0, may hold values from -6 to 6
- lengths: int32 [8], P('rep'), parts along dimension 0, may hold values from 128 to 512, as said below
- conv_weight: bfloat16 [16, 128, 64, 64], P('fsdp'), may hold values from -0.0625 to 0.0625
- conv_bias: bfloat16 [1024], P('fsdp'), may hold values from -3 to 3
- norm_gain: float32 [1024], replicated, may hold values from 0.1 to 1.9
- norm_shift: float32 [1024], replicated, may hold values from -3 to 3
- w_query: bfloat16 [1024, 512], replicated
- w_key: bfloat16 [1024, 512], replicated
- w_value: bfloat16 [1024, 512], replicated, may hold values from -0.1875 to 0.1875
Outputs:
- hidden: bfloat16 [8, 512, 1024], P('rep', 'ctx', 'fsdp'), parts along dimension 0
- context: bfloat16 [8, 512, 512], P(('rep', 'fsdp'), 'ctx'), parts along dimension 0
There are 4 independent parts, one for each index of `rep`. A program takes and returns all parts, laid end to end along the dimension named above; an argument that names none is the same for every part. Nothing has to cross between parts.
Inputs may be any that keep to these rules, and one draw needn't show every extreme that they name: `lengths`: one recording in every draw has all 512 frames live.
All inputs are finite; a program needn't handle non-finite values.
Results may differ from a plain program's by a relative error of at most 0.012.
Values may be sent and summed in bfloat16 or wider, within the bound.
No kernel may reach another device: no remote copies, remote signals or barrier semaphores. Data moves between devices by JAX's collectives and lax.ppermute only.
A program may use at most 128 MiB of HBM per device.

v0:
```python
import math

import jax
import jax.numpy as jnp
from jax import lax
from jax.sharding import PartitionSpec as P
from jax.experimental import pallas as pl
from jax.experimental.pallas import tpu as pltpu

HD = 64


def padded_2(x, sides, width):
    for axis, dim in sides:
        size, length = (lax.axis_size(axis), x.shape[dim])
        up = [(i, (i + 1) % size) for i in range(size - 1)]
        down = [(j, i) for i, j in up]
        last = lax.slice_in_dim(x, length - width, length, axis=dim)
        first = lax.slice_in_dim(x, 0, width, axis=dim)
        before = lax.ppermute(last, axis, up)
        after = lax.ppermute(first, axis, down)
        x = jnp.concatenate([before, x, after], axis=dim)
    return x


def conv_body(x_ref, w_ref, out_ref):
    recs, chans, lanes = x_ref.shape[1], x_ref.shape[2], x_ref.shape[3]
    taps = w_ref.shape[3]
    rows = out_ref.shape[2]
    outs = w_ref.shape[2]

    def octet_step(q, acc):
        base = pl.multiple_of(q * 8, 8)
        hankels = []
        for r in range(recs):
            block = x_ref[0, r, pl.ds(base, 8), :]
            per_chan = []
            for c in range(8):
                row = jnp.broadcast_to(block[c : c + 1, :], (rows, lanes))
                rolled = pltpu.roll(row, 0, 1, stride=1, stride_axis=0)
                per_chan.append(rolled[:, :taps].astype(jnp.bfloat16))
            hankels.append(per_chan)
        for pair in range(4):
            lhs = jnp.concatenate(
                [jnp.concatenate(hankels[r][2 * pair : 2 * pair + 2], axis=1) for r in range(recs)],
                axis=0,
            )
            rhs = jnp.concatenate(
                [w_ref[0, base + 2 * pair], w_ref[0, base + 2 * pair + 1]], axis=1
            )
            acc = acc + lax.dot_general(
                lhs, rhs, (((1,), (1,)), ((), ())), preferred_element_type=jnp.float32
            )
        return acc

    acc = lax.fori_loop(0, chans // 8, octet_step, jnp.zeros((recs * rows, outs), jnp.float32))
    out_ref[0] = acc.reshape(recs, rows, outs)


def hankel_conv(xt, wv, rows):
    groups, recs, chans, lanes = xt.shape
    taps, outs = wv.shape[3], wv.shape[2]
    return pl.pallas_call(
        conv_body,
        grid=(groups,),
        in_specs=[pl.BlockSpec((1, recs, chans, lanes), lambda g: (g, 0, 0, 0)),
                  pl.BlockSpec((1, chans, outs, taps), lambda g: (g, 0, 0, 0))],
        out_specs=pl.BlockSpec((1, recs, rows, outs), lambda g: (g, 0, 0, 0)),
        out_shape=jax.ShapeDtypeStruct((groups, recs, rows, outs), jnp.float32),
        cost_estimate=pl.CostEstimate(
            flops=2 * groups * recs * rows * taps * chans * outs,
            bytes_accessed=xt.size * 4 + wv.size * 2 + groups * recs * rows * outs * 4,
            transcendentals=0,
        ),
    )(xt, wv)


def grouped_conv(padded, conv_weight, frame_rows):
    recs, span = padded.shape[0], padded.shape[1]
    groups_here, taps, group_in, group_out = conv_weight.shape
    lanes = -(-(frame_rows + taps - 1) // 128) * 128
    grouped = jnp.pad(padded, ((0, 0), (0, lanes - span), (0, 0)))
    grouped = jnp.roll(grouped, 1 - frame_rows, axis=1)
    grouped = grouped.reshape(recs, lanes, groups_here, group_in).transpose(2, 0, 3, 1)
    out = hankel_conv(grouped.astype(jnp.float32), jnp.transpose(conv_weight, (0, 2, 3, 1)), frame_rows)
    out = jnp.flip(out, axis=2)
    return out.transpose(1, 2, 0, 3).reshape(recs, frame_rows, groups_here * group_out)


def gather_ring(x, axis, rows):
    size = lax.axis_size(axis)
    place = lax.axis_index(axis)
    pieces, starts = [x], [place * rows]
    for shift in range(1, size):
        pairs = [(i, (i + shift) % size) for i in range(size)]
        pieces.append(lax.ppermute(x, axis, pairs))
        starts.append(((place - shift) % size) * rows)
    return pieces, starts


def attend(carry, piece, start, queries, own_length):
    best, total, accum = carry
    keys_part, vals_part = piece
    count = keys_part.shape[0]
    head_count = queries.shape[1]
    keys_part = keys_part.reshape(count, head_count, HD)
    vals_part = vals_part.reshape(count, head_count, HD)
    scores = jnp.einsum(
        "fhd,nhd->fhn", queries, keys_part, preferred_element_type=jnp.float32
    ) / math.sqrt(HD)
    valid = (start + jnp.arange(count, dtype=jnp.int32) < own_length)[None, None, :]
    scores = jnp.where(valid, scores, -1e30)
    fresh = jnp.maximum(best, jnp.max(scores, axis=2))
    weights = jnp.where(valid, jnp.exp(scores - fresh[:, :, None]), 0.0)
    factor = jnp.exp(best - fresh)
    total = total * factor + jnp.sum(weights, axis=2)
    accum = accum * factor[:, :, None] + jnp.einsum(
        "fhn,nhd->fhd", weights.astype(jnp.bfloat16), vals_part, preferred_element_type=jnp.float32
    )
    return (fresh, total, accum)


def start_state(rows, heads_here):
    return (
        jnp.full((rows, heads_here), -1e30, jnp.float32),
        jnp.zeros((rows, heads_here), jnp.float32),
        jnp.zeros((rows, heads_here, HD), jnp.float32),
    )


def blockwise(carry, all_keys, all_vals, queries, own_length, block_rows):
    block_count = all_keys.shape[0] // block_rows

    def block_step(state, index):
        begin = index * block_rows
        piece = (
            lax.dynamic_slice_in_dim(all_keys, begin, block_rows, 0),
            lax.dynamic_slice_in_dim(all_vals, begin, block_rows, 0),
        )
        return (attend(state, piece, begin, queries, own_length), None)

    final, unused = lax.scan(block_step, carry, jnp.arange(block_count, dtype=jnp.int32))
    return final


def finish(final, query_pos, own_length):
    best, total, accum = final
    result = accum / total[:, :, None]
    query_live = (query_pos < own_length)[:, None, None]
    result = jnp.where(query_live, result, 0.0)
    return result.reshape(result.shape[0], result.shape[1] * HD).astype(jnp.bfloat16)


def per_device(
    frames_in, lengths, conv_weight, conv_bias, norm_gain, norm_shift, w_query, w_key, w_value
):
    record_count, frame_rows, channels = frames_in.shape
    ctx_place = lax.axis_index("ctx")
    positions = ctx_place * frame_rows + jnp.arange(frame_rows, dtype=jnp.int32)
    live = positions[None, :] < lengths[:, None]
    masked = jnp.where(live[:, :, None], frames_in, jnp.zeros((), frames_in.dtype))
    groups_here, kernel_width, group_in, group_out = conv_weight.shape
    half_width = kernel_width // 2
    padded = padded_2(masked, (("ctx", 1),), half_width)
    conv_out = grouped_conv(padded, conv_weight, frame_rows)
    hidden = (
        masked.astype(jnp.float32)
        + jax.nn.gelu(conv_out + conv_bias.astype(jnp.float32), approximate=False)
    ).astype(jnp.bfloat16)
    record = lax.all_to_all(hidden, "fsdp", split_axis=0, concat_axis=2, tiled=True)
    own_length = lax.dynamic_index_in_dim(lengths, lax.axis_index("fsdp"), 0, keepdims=False)
    flat = record[0].astype(jnp.float32)
    centre = jnp.mean(flat, axis=1, keepdims=True)
    spread = jnp.mean((flat - centre) ** 2, axis=1, keepdims=True)
    normed = ((flat - centre) / jnp.sqrt(spread + 1e-05) * norm_gain + norm_shift).astype(
        jnp.bfloat16
    )
    query_flat = jnp.dot(normed, w_query, preferred_element_type=jnp.float32).astype(jnp.bfloat16)
    key_flat = jnp.dot(normed, w_key, preferred_element_type=jnp.float32).astype(jnp.bfloat16)
    val_flat = jnp.dot(normed, w_value, preferred_element_type=jnp.float32).astype(jnp.bfloat16)
    head_count = query_flat.shape[1] // HD
    width = key_flat.shape[1]
    both = jnp.concatenate([key_flat, val_flat], axis=1)
    pieces, starts = gather_ring(both, "ctx", frame_rows)
    whole = jnp.concatenate(pieces, axis=0)
    key_pos = jnp.concatenate(
        [start + jnp.arange(frame_rows, dtype=jnp.int32) for start in starts]
    )
    queries = query_flat.reshape(frame_rows, head_count, HD)
    keys = whole[:, :width].reshape(-1, head_count, HD)
    vals = whole[:, width:].reshape(-1, head_count, HD)
    scores = jnp.einsum(
        "fhd,nhd->hfn", queries, keys, preferred_element_type=jnp.float32
    ) / math.sqrt(HD)
    valid = (key_pos < own_length)[None, None, :]
    scores = jnp.where(valid, scores, -1e30)
    rowmax = jnp.max(scores, axis=2, keepdims=True)
    weights = jnp.where(valid, jnp.exp(scores - rowmax), 0.0)
    total = jnp.sum(weights, axis=2, keepdims=True)
    summed = jnp.einsum(
        "hfn,nhd->hfd", weights.astype(jnp.bfloat16), vals, preferred_element_type=jnp.float32
    )
    out = summed / total
    query_live = (positions < own_length)[None, :, None]
    out = jnp.where(query_live, out, 0.0).transpose(1, 0, 2)
    result = out.reshape(1, frame_rows, head_count * HD).astype(jnp.bfloat16)
    return (hidden, result)


def solution(mesh):
    in_specs = (
        P("rep", "ctx", "fsdp"),
        P("rep"),
        P("fsdp", None, None, None),
        P("fsdp"),
        P(),
        P(),
        P(),
        P(),
        P(),
    )
    out_specs = (P("rep", "ctx", "fsdp"), P(("rep", "fsdp"), "ctx", None))
    return jax.shard_map(
        per_device, mesh=mesh, in_specs=in_specs, out_specs=out_specs, check_vma=False
    )
```

profile of v0, /device:TPU:0, one launch (start us, length us, event | category | flops | bytes accessed | tf_op | source)
XLA Modules:
  0.0 104.6 jit_solution(6552143613489772347)
XLA Ops:
  0.6 0.0 copy-start
  0.6 0.0 copy-start.5
  0.7 0.0 copy-start.4
  0.7 1.2 %copy.15 = bf16[2,128,512]{1,2,0:T(8,128)(2,1)S(1)} copy(bf16[2,128,512]{2,1,0:T(8,128)(2,1)} %param.9) | data formatting | bytes 524288 | tf_op args[0]
  1.9 0.7 broadcast_compare_fusion
  2.7 0.1 fusion.38
  2.8 1.3 %collective-permute-start = (bf16[2,64,512]{1,2,0:T(8,128)(2,1)S(1)}, bf16[2,64,512]{1,2,0:T(8,128)(2,1)S(1)}, u32[]{:S(2)}, u32[]{:S(2)}) collective-permute-start(bf16[2,64,512]{1,2,0:T(8,128)(2,1)S(1)} %get-tuple-element.8), channel_id=1, source_target_pairs={{8,0},{16,8},{24,16},{9,1},{17,9},{25,17},{10,2},{18,10},{26,18},{... | collective-permute-start | bytes 393224 | tf_op jit(solution)/shard_map/ppermute | solution.py:21
  4.1 5.6 %collective-permute-start.1 = (bf16[2,64,512]{1,2,0:T(8,128)(2,1)S(1)}, bf16[2,64,512]{1,2,0:T(8,128)(2,1)S(1)}, u32[]{:S(2)}, u32[]{:S(2)}) collective-permute-start(bf16[2,64,512]{1,2,0:T(8,128)(2,1)S(1)} %get-tuple-element.9), channel_id=1, source_target_pairs={{0,8},{8,16},{16,24},{1,9},{9,17},{17,25},{2,10},{10,18},{18,26},{... | collective-permute-start | bytes 393224 | tf_op jit(solution)/shard_map/ppermute | solution.py:20
  9.7 0.0 copy-done.5
  9.7 0.6 dynamic_slice.4
  10.3 0.0 copy-done.4
  10.3 3.7 %collective-permute-done = bf16[2,64,512]{1,2,0:T(8,128)(2,1)S(1)} collective-permute-done((bf16[2,64,512]{1,2,0:T(8,128)(2,1)S(1)}, bf16[2,64,512]{1,2,0:T(8,128)(2,1)S(1)}, u32[]{:S(2)}, u32[]{:S(2)}) %collective-permute-start) | collective-permute-done | bytes 131104 | tf_op jit(solution)/shard_map/ppermute | solution.py:21
  14.0 1.2 %collective-permute-done.1 = bf16[2,64,512]{1,2,0:T(8,128)(2,1)S(1)} collective-permute-done((bf16[2,64,512]{1,2,0:T(8,128)(2,1)S(1)}, bf16[2,64,512]{1,2,0:T(8,128)(2,1)S(1)}, u32[]{:S(2)}, u32[]{:S(2)}) %collective-permute-start.1) | collective-permute-done | bytes 131104 | tf_op jit(solution)/shard_map/ppermute | solution.py:20
  15.2 0.4 fusion.13
  15.7 1.1 %copy_bitcast_fusion.x_ref = f32[8,2,64,256]{3,2,1,0:T(8,128)} fusion(bf16[2,256,8,64]{1,3,2,0:T(8,128)(2,1)S(1)} %bitcast.56), kind=kLoop, calls=%fused_computation.12 | loop fusion | flops 262144 | bytes 1572864 | tf_op jit(solution)/shard_map/convert_element_type | solution.py:85
  16.7 33.4 %shard_map.104 = f32[8,2,128,64]{3,2,1,0:T(8,128)} custom-call(f32[8,2,64,256]{3,2,1,0:T(8,128)} %copy_bitcast_fusion.x_ref, bf16[8,64,64,128]{3,2,1,0:T(8,128)(2,1)} %bitcast.54), custom_call_target="tpu_custom_call" | custom-call | flops 2147483648 | bytes 9961472 | tf_op jit(solution)/shard_map/pallas_call | solution.py:63
  50.1 6.8 %rev.4 = f32[8,2,128,64]{3,2,1,0:T(8,128)S(1)} reverse(f32[8,2,128,64]{3,2,1,0:T(8,128)} %shard_map.104), dimensions={2} | reverse | bytes 1048576 | tf_op jit(solution)/shard_map/jit(_flip)/rev | solution.py:86
  57.0 0.0 copy-start.2
  57.0 0.0 copy-start.3
  57.0 0.3 copy.17
  57.3 2.0 %fusion.12 = bf16[2,128,512]{1,2,0:T(8,128)(2,1)} fusion(f32[2,128,8,64]{1,3,2,0:T(8,128)S(1)} %copy.17, f32[512]{0:T(512)S(1)} %convert_element_type.69, bf16[2,128,512]{1,2,0:T(8,128)(2,1)S(1)} %copy.15, pred[2,128]{1,0:T(4,128)(4,1)S(1)} %broadcast_compare_fusion), kind=kLoop, calls=%fused_computation.21 | loop fusion | flops 9043968 | bytes 1050880 | tf_op jit(solution)/shard_map/convert_element_type | solution.py:169
  59.3 3.6 %all-to-all-start = ((bf16[2,128,512]{1,2,0:T(8,128)(2,1)}), bf16[2,128,512]{1,2,0:T(8,128)(2,1)S(1)}, u32[]{:S(2)}, u32[]{:S(2)}) async-start(bf16[2,128,512]{1,2,0:T(8,128)(2,1)} %fusion.12), calls=%async_computation | async-start | bytes 524288 | tf_op jit(solution)/shard_map/all_to_all | solution.py:170
  62.8 0.7 broadcast_compare_fusion.1
  63.5 4.5 %all-to-all-done = bf16[2,128,512]{1,2,0:T(8,128)(2,1)S(1)} async-done(((bf16[2,128,512]{1,2,0:T(8,128)(2,1)}), bf16[2,128,512]{1,2,0:T(8,128)(2,1)S(1)}, u32[]{:S(2)}, u32[]{:S(2)}) %all-to-all-start) | async-done | bytes 262176 | tf_op jit(solution)/shard_map/all_to_all | solution.py:170
  68.0 0.2 convert_reduce_fusion
  68.2 0.2 fusion.18
  68.3 0.3 fusion.25
  68.7 0.0 copy-done
  68.7 0.3 convolution_convert_fusion
  69.0 0.3 convolution_convert_fusion.1
  69.4 4.7 %collective-permute-start.4 = (bf16[128,1024]{1,0:T(8,128)(2,1)S(1)}, bf16[128,1024]{1,0:T(8,128)(2,1)S(1)}, u32[]{:S(2)}, u32[]{:S(2)}) collective-permute-start(bf16[128,1024]{1,0:T(8,128)(2,1)S(1)} %pad_maximum_fusion.3), channel_id=1, source_target_pairs={{0,24},{8,0},{16,8},{24,16},{1,25},{9,1},{17,9},{25,17},{2,26},{10... | collective-permute-start | bytes 786440 | tf_op jit(solution)/shard_map/ppermute | solution.py:96
  74.2 0.0 collective-permute-start.3
  74.2 1.0 collective-permute-start.2
  75.1 0.7 add_compare_fusion
  75.8 1.8 %copy.21 = bf16[2,128,512]{2,1,0:T(8,128)(2,1)} copy(bf16[2,128,512]{1,2,0:T(8,128)(2,1)} %fusion.12) | data formatting | bytes 524288
  77.6 1.6 %convolution_convert_fusion.2 = bf16[128,512]{1,0:T(8,128)(2,1)S(1)} fusion(bf16[128,1024]{0,1:T(8,128)(2,1)S(1)} %fusion.25, bf16[1024,512]{1,0:T(8,128)(2,1)} %param.15), kind=kOutput, calls=%fused_computation.10 | convolution fusion | flops 134283264 | bytes 1441792 | tf_op jit(solution)/shard_map/dot_general | solution.py:178
  79.2 0.1 copy.18
  79.3 1.6 %collective-permute-done.4 = bf16[128,1024]{1,0:T(8,128)(2,1)S(1)} collective-permute-done((bf16[128,1024]{1,0:T(8,128)(2,1)S(1)}, bf16[128,1024]{1,0:T(8,128)(2,1)S(1)}, u32[]{:S(2)}, u32[]{:S(2)}) %collective-permute-start.4) | collective-permute-done | bytes 262176 | tf_op jit(solution)/shard_map/ppermute | solution.py:96
  80.9 13.6 %collective-permute-done.3 = bf16[128,1024]{1,0:T(8,128)(2,1)S(1)} collective-permute-done((bf16[128,1024]{1,0:T(8,128)(2,1)S(1)}, bf16[128,1024]{1,0:T(8,128)(2,1)S(1)}, u32[]{:S(2)}, u32[]{:S(2)}) %collective-permute-start.3) | collective-permute-done | bytes 262176 | tf_op jit(solution)/shard_map/ppermute | solution.py:96
  94.5 0.0 collective-permute-done.2
  94.5 0.1 pad_maximum_fusion
  94.6 0.9 fusion.37
  95.5 1.0 copy.19
  96.5 1.5 %fusion.40 = f32[8,128,512]{2,1,0:T(8,128)S(1)} fusion(bf16[128,8,64]{0,2,1:T(8,128)(2,1)S(1)} %bitcast.60, bf16[512,8,64]{0,2,1:T(8,128)(2,1)} %bitcast.57), kind=kOutput, calls=%fused_computation.71 | convolution fusion | flops 67108864 | bytes 2752512 | tf_op jit(solution)/shard_map/fhd,nhd->hfn/dot_general | solution.py:192
  98.0 2.0 %fusion.39 = f32[8,128]{1,0:T(8,128)S(1)} fusion(pred[512]{0:T(512)(128)(4,1)S(1)} %add_compare_fusion, bf16[128,8,64]{0,2,1:T(8,128)(2,1)S(1)} %bitcast.61, bf16[512,8,64]{0,2,1:T(8,128)(2,1)} %bitcast.58), kind=kOutput, calls=%fused_computation.70 | convolution fusion | flops 69730816 | bytes 659968 | tf_op jit(solution)/shard_map/sub | solution.py:198
  100.0 2.1 %copy.20 = bf16[512,512]{0,1:T(8,128)(2,1)} copy(bf16[512,512]{1,0:T(8,128)(2,1)} %get-tuple-element.7) | data formatting | bytes 1048576 | tf_op jit(solution)/shard_map/slice | solution.py:191
  102.0 1.8 %fusion.4 = bf16[128,8,64]{0,2,1:T(8,128)(2,1)S(1)} fusion(bf16[512,8,64]{0,2,1:T(8,128)(2,1)} %bitcast.59, f32[8,128,512]{2,1,0:T(8,128)S(1)} %fusion.40, pred[512]{0:T(512)(128)(4,1)S(1)} %add_compare_fusion, f32[128,8]{0,1:T(8,128)S(1)} %bitcast.63, pred[128]{0:T(512)(128)(4,1)S(1)} %broadcast_compare_fusion.1), kind=kOutput, calls=%fused_computation.7 | convolution fusion | flops 69928448 | bytes 2757248 | tf_op jit(solution)/shard_map/hfn,nhd->hfd/dot_general | solution.py:200
  103.8 0.8 copy.22
  (11 shorter events, 0.1 us)
Async XLA Ops:
  0.6 68.1 %copy-start = (bf16[1024,512]{1,0:T(8,128)(2,1)S(1)}, bf16[1024,512]{1,0:T(8,128)(2,1)}, u32[]{:S(2)}) copy-start(bf16[1024,512]{1,0:T(8,128)(2,1)} %param.17) | copy-start | bytes 3145732
  0.6 9.0 %copy-start.5 = (s32[2]{0:T(128)S(1)}, s32[2]{0:T(128)}, u32[]{:S(2)}) copy-start(s32[2]{0:T(128)} %param.10) | copy-start | bytes 28
  0.7 9.6 %copy-start.4 = (bf16[512]{0:T(512)(128)(2,1)S(1)}, bf16[512]{0:T(512)(128)(2,1)}, u32[]{:S(2)}) copy-start(bf16[512]{0:T(512)(128)(2,1)} %param.12) | copy-start | bytes 3076
  2.8 11.2 %collective-permute-start = (bf16[2,64,512]{1,2,0:T(8,128)(2,1)S(1)}, bf16[2,64,512]{1,2,0:T(8,128)(2,1)S(1)}, u32[]{:S(2)}, u32[]{:S(2)}) collective-permute-start(bf16[2,64,512]{1,2,0:T(8,128)(2,1)S(1)} %get-tuple-element.8), channel_id=1, source_target_pairs={{8,0},{16,8},{24,16},{9,1},{17,9},{25,17},{10,2},{18,10},{26,18},{... | collective-permute-start | bytes 393224 | tf_op jit(solution)/shard_map/ppermute | solution.py:21
  4.1 11.1 %collective-permute-start.1 = (bf16[2,64,512]{1,2,0:T(8,128)(2,1)S(1)}, bf16[2,64,512]{1,2,0:T(8,128)(2,1)S(1)}, u32[]{:S(2)}, u32[]{:S(2)}) collective-permute-start(bf16[2,64,512]{1,2,0:T(8,128)(2,1)S(1)} %get-tuple-element.9), channel_id=1, source_target_pairs={{0,8},{8,16},{16,24},{1,9},{9,17},{17,25},{2,10},{10,18},{18,26},{... | collective-permute-start | bytes 393224 | tf_op jit(solution)/shard_map/ppermute | solution.py:20
  57.0 11.4 %copy-start.2 = (f32[1024]{0:T(1024)S(1)}, f32[1024]{0:T(1024)}, u32[]{:S(2)}) copy-start(f32[1024]{0:T(1024)} %param.14) | copy-start | bytes 12292
  57.0 11.4 %copy-start.3 = (f32[1024]{0:T(1024)S(1)}, f32[1024]{0:T(1024)}, u32[]{:S(2)}) copy-start(f32[1024]{0:T(1024)} %param.13) | copy-start | bytes 12292
  59.3 9.8 %copy-start.1 = (bf16[1024,512]{1,0:T(8,128)(2,1)S(1)}, bf16[1024,512]{1,0:T(8,128)(2,1)}, u32[]{:S(2)}) copy-start(bf16[1024,512]{1,0:T(8,128)(2,1)} %param.16) | copy-start | bytes 3145732
  59.3 8.7 %all-to-all-start = ((bf16[2,128,512]{1,2,0:T(8,128)(2,1)}), bf16[2,128,512]{1,2,0:T(8,128)(2,1)S(1)}, u32[]{:S(2)}, u32[]{:S(2)}) async-start(bf16[2,128,512]{1,2,0:T(8,128)(2,1)} %fusion.12), calls=%async_computation | async-start | bytes 524288 | tf_op jit(solution)/shard_map/all_to_all | solution.py:170
  69.4 11.5 %collective-permute-start.4 = (bf16[128,1024]{1,0:T(8,128)(2,1)S(1)}, bf16[128,1024]{1,0:T(8,128)(2,1)S(1)}, u32[]{:S(2)}, u32[]{:S(2)}) collective-permute-start(bf16[128,1024]{1,0:T(8,128)(2,1)S(1)} %pad_maximum_fusion.3), channel_id=1, source_target_pairs={{0,24},{8,0},{16,8},{24,16},{1,25},{9,1},{17,9},{25,17},{2,26},{10... | collective-permute-start | bytes 786440 | tf_op jit(solution)/shard_map/ppermute | solution.py:96
  74.2 20.3 %collective-permute-start.3 = (bf16[128,1024]{1,0:T(8,128)(2,1)S(1)}, bf16[128,1024]{1,0:T(8,128)(2,1)S(1)}, u32[]{:S(2)}, u32[]{:S(2)}) collective-permute-start(bf16[128,1024]{1,0:T(8,128)(2,1)S(1)} %pad_maximum_fusion.3), channel_id=1, source_target_pairs={{0,16},{8,24},{16,0},{24,8},{1,17},{9,25},{17,1},{25,9},{2,18},{10... | collective-permute-start | bytes 786440 | tf_op jit(solution)/shard_map/ppermute | solution.py:96
  74.2 20.3 %collective-permute-start.2 = (bf16[128,1024]{1,0:T(8,128)(2,1)S(1)}, bf16[128,1024]{1,0:T(8,128)(2,1)S(1)}, u32[]{:S(2)}, u32[]{:S(2)}) collective-permute-start(bf16[128,1024]{1,0:T(8,128)(2,1)S(1)} %pad_maximum_fusion.3), channel_id=1, source_target_pairs={{0,8},{8,16},{16,24},{24,0},{1,9},{9,17},{17,25},{25,1},{2,10},{10... | collective-permute-start | bytes 786440 | tf_op jit(solution)/shard_map/ppermute | solution.py:96
where the time goes:
time: 105 us
  Pallas kernels  33.4 us (32%)
  waiting for transfers between devices  24.6 us (23%)
  starting transfers between devices  16.2 us (15%)
  local copies, waits for them, and re-layouts  15.7 us (15%)
  matrix products  7.48 us (7%)
  other arithmetic  6.31 us (6%)
    pallas_call x1, Pallas kernels, hankel_conv(): pl.pallas_call(conv_body, grid=(groups,), in_specs=[pl.BlockSpec((1, recs...  33.4 us
    ppermute x3, waiting for transfers between devices, gather_ring(): pieces.append(lax.ppermute(x, axis, pairs))  15.2 us
    rev x1, local copies, waits for them, and re-layouts, grouped_conv(): out = jnp.flip(out, axis=2)  6.83 us
    ppermute x3, starting transfers between devices, gather_ring(): pieces.append(lax.ppermute(x, axis, pairs))  5.73 us
    ppermute x1, starting transfers between devices, padded_2(): before = lax.ppermute(last, axis, up)  5.57 us
    all_to_all x1, waiting for transfers between devices, per_device(): lax.all_to_all(hidden, 'fsdp', split_axis=0, concat_axis=2, tiled=True)  4.45 us
    unnamed x15, local copies, waits for them, and re-layouts  3.8 us
    ppermute x1, waiting for transfers between devices, padded_2(): after = lax.ppermute(first, axis, down)  3.74 us
  transfers between devices with their start and end apart: 6, of which 5 were waited for; matrix products, arithmetic and copies ran while one was open for 5% of the time, Pallas kernels for 0%

commit v1 on v0

--- a/solution.py
+++ b/solution.py
@@ -54,7 +54,19 @@
         return acc
 
     acc = lax.fori_loop(0, chans // 8, octet_step, jnp.zeros((recs * rows, outs), jnp.float32))
-    out_ref[0] = acc.reshape(recs, rows, outs)
+    across = lax.broadcasted_iota(jnp.int32, (rows, rows), 0) + lax.broadcasted_iota(
+        jnp.int32, (rows, rows), 1
+    )
+    flip = jnp.where(across == rows - 1, 1.0, 0.0).astype(jnp.bfloat16)
+    for r in range(recs):
+        part = acc[r * rows : (r + 1) * rows]
+        high = part.astype(jnp.bfloat16)
+        rest = part - high.astype(jnp.float32)
+        middle = rest.astype(jnp.bfloat16)
+        low = (rest - middle.astype(jnp.float32)).astype(jnp.bfloat16)
+        total = jnp.dot(flip, high, preferred_element_type=jnp.float32)
+        total = total + jnp.dot(flip, middle, preferred_element_type=jnp.float32)
+        out_ref[0, r] = total + jnp.dot(flip, low, preferred_element_type=jnp.float32)
 
 
 def hankel_conv(xt, wv, rows):
@@ -83,18 +95,23 @@
     grouped = jnp.roll(grouped, 1 - frame_rows, axis=1)
     grouped = grouped.reshape(recs, lanes, groups_here, group_in).transpose(2, 0, 3, 1)
     out = hankel_conv(grouped.astype(jnp.float32), jnp.transpose(conv_weight, (0, 2, 3, 1)), frame_rows)
-    out = jnp.flip(out, axis=2)
     return out.transpose(1, 2, 0, 3).reshape(recs, frame_rows, groups_here * group_out)
 
 
 def gather_ring(x, axis, rows):
     size = lax.axis_size(axis)
     place = lax.axis_index(axis)
+    ups = [(i, i + 1) for i in range(size - 1)]
+    downs = [(i + 1, i) for i in range(size - 1)]
+    from_below, from_above = [x], [x]
+    for step in range(1, size):
+        from_below.append(lax.ppermute(from_below[-1], axis, ups))
+        from_above.append(lax.ppermute(from_above[-1], axis, downs))
     pieces, starts = [x], [place * rows]
-    for shift in range(1, size):
-        pairs = [(i, (i + shift) % size) for i in range(size)]
-        pieces.append(lax.ppermute(x, axis, pairs))
-        starts.append(((place - shift) % size) * rows)
+    for offset in range(1, size):
+        above = place + offset < size
+        pieces.append(jnp.where(above, from_above[offset], from_below[size - offset]))
+        starts.append(((place + offset) % size) * rows)
     return pieces, starts
 
 

time: 105 us -> 106 us (level)
  waiting for transfers between devices: 24.6 us -> 13.4 us
  starting transfers between devices: 16.2 us -> 25.5 us
  blocking collectives: 0 us -> 7.92 us
  local copies, waits for them, and re-layouts: 15.7 us -> 9.21 us
  Pallas kernels: 33.4 us -> 35 us
  matrix products: 7.48 us -> 6.26 us
    ppermute x3 -> x6, starting transfers between devices: 5.73 us -> 18.6 us  [the longest x3 14.7 us: gather_ring(): from_below.append(lax.ppermute(from_below[-1], axis, ups))]
    all_to_all x0 -> x1, blocking collectives: none -> 7.92 us  [per_device(): lax.all_to_all(hidden, 'fsdp', split_axis=0, concat_axis=2, tiled=True)]
    ppermute x3 -> x6, waiting for transfers between devices: 15.2 us -> 7.89 us  [the longest x3 4.27 us: gather_ring(): from_above.append(lax.ppermute(from_above[-1], axis, downs))]
    rev x1 -> x0, local copies, waits for them, and re-layouts: 6.83 us -> none  [grouped_conv(): out = jnp.flip(out, axis=2)]
    all_to_all x1 -> x0, waiting for transfers between devices: 4.45 us -> none  [per_device(): lax.all_to_all(hidden, 'fsdp', split_axis=0, concat_axis=2, tiled=True)]
    all_to_all x1 -> x0, starting transfers between devices: 3.57 us -> none  [per_device(): lax.all_to_all(hidden, 'fsdp', split_axis=0, concat_axis=2, tiled=True)]
    pallas_call x1, Pallas kernels: 33.4 us -> 35 us  [hankel_conv(): pl.pallas_call(conv_body, grid=(groups,), in_specs=[pl.BlockSpec((1, recs...]
    transpose x1, local copies, waits for them, and re-layouts: 0.31 us -> 1.56 us  [grouped_conv(): out.transpose(1, 2, 0, 3).reshape(recs, frame_rows, groups_here * group_out)]
  transfers between devices with their start and end apart: 6 -> 8, of which waited for: 5 -> 5; matrix products, arithmetic and copies ran while one was open for 5% -> 4% of each run, Pallas kernels for 0% -> 0%
where the time goes in v1:
time: 106 us; the launch traced here: 105 us
  Pallas kernels  35 us (33%)
  starting transfers between devices  25.5 us (24%)
  waiting for transfers between devices  13.4 us (13%)
  local copies, waits for them, and re-layouts  9.21 us (9%)
  blocking collectives  7.92 us (7%)
  other arithmetic  6.67 us (6%)
  matrix products  6.26 us (6%)
    pallas_call x1, Pallas kernels, hankel_conv(): pl.pallas_call(conv_body, grid=(groups,), in_specs=[pl.BlockSpec((1, recs...  35 us
    ppermute x3, starting transfers between devices, gather_ring(): from_below.append(lax.ppermute(from_below[-1], axis, ups))  14.7 us
    all_to_all x1, blocking collectives, per_device(): lax.all_to_all(hidden, 'fsdp', split_axis=0, concat_axis=2, tiled=True)  7.92 us
    ppermute x1, starting transfers between devices, padded_2(): before = lax.ppermute(last, axis, up)  5.57 us
    ppermute x1, waiting for transfers between devices, padded_2(): after = lax.ppermute(first, axis, down)  4.33 us
    ppermute x3, waiting for transfers between devices, gather_ring(): from_above.append(lax.ppermute(from_above[-1], axis, downs))  4.27 us
    ppermute x3, starting transfers between devices, gather_ring(): from_above.append(lax.ppermute(from_above[-1], axis, downs))  3.88 us
    ppermute x3, waiting for transfers between devices, gather_ring(): from_below.append(lax.ppermute(from_below[-1], axis, ups))  3.62 us
  transfers between devices with their start and end apart: 8, of which 5 were waited for; matrix products, arithmetic and copies ran while one was open for 4% of the time, Pallas kernels for 0%

profile of v1, /device:TPU:0, one launch (start us, length us, event | category | flops | bytes accessed | tf_op | source)
XLA Modules:
  0.0 104.9 jit_solution(10628345529980929442)
XLA Ops:
  0.6 0.0 copy-start
  0.7 1.2 %copy.15 = bf16[2,128,512]{1,2,0:T(8,128)(2,1)S(1)} copy(bf16[2,128,512]{2,1,0:T(8,128)(2,1)} %param.9) | data formatting | bytes 524288 | tf_op args[0]
  1.9 0.7 broadcast_compare_fusion
  2.6 0.1 fusion.38
  2.8 1.3 %collective-permute-start = (bf16[2,64,512]{1,2,0:T(8,128)(2,1)S(1)}, bf16[2,64,512]{1,2,0:T(8,128)(2,1)S(1)}, u32[]{:S(2)}, u32[]{:S(2)}) collective-permute-start(bf16[2,64,512]{1,2,0:T(8,128)(2,1)S(1)} %get-tuple-element.8), channel_id=1, source_target_pairs={{8,0},{16,8},{24,16},{9,1},{17,9},{25,17},{10,2},{18,10},{26,18},{... | collective-permute-start | bytes 393224 | tf_op jit(solution)/shard_map/ppermute | solution.py:21
  4.1 5.6 %collective-permute-start.1 = (bf16[2,64,512]{1,2,0:T(8,128)(2,1)S(1)}, bf16[2,64,512]{1,2,0:T(8,128)(2,1)S(1)}, u32[]{:S(2)}, u32[]{:S(2)}) collective-permute-start(bf16[2,64,512]{1,2,0:T(8,128)(2,1)S(1)} %get-tuple-element.9), channel_id=1, source_target_pairs={{0,8},{8,16},{16,24},{1,9},{9,17},{17,25},{2,10},{10,18},{18,26},{... | collective-permute-start | bytes 393224 | tf_op jit(solution)/shard_map/ppermute | solution.py:20
  9.7 4.3 %collective-permute-done = bf16[2,64,512]{1,2,0:T(8,128)(2,1)S(1)} collective-permute-done((bf16[2,64,512]{1,2,0:T(8,128)(2,1)S(1)}, bf16[2,64,512]{1,2,0:T(8,128)(2,1)S(1)}, u32[]{:S(2)}, u32[]{:S(2)}) %collective-permute-start) | collective-permute-done | bytes 131104 | tf_op jit(solution)/shard_map/ppermute | solution.py:21
  14.0 1.2 %collective-permute-done.1 = bf16[2,64,512]{1,2,0:T(8,128)(2,1)S(1)} collective-permute-done((bf16[2,64,512]{1,2,0:T(8,128)(2,1)S(1)}, bf16[2,64,512]{1,2,0:T(8,128)(2,1)S(1)}, u32[]{:S(2)}, u32[]{:S(2)}) %collective-permute-start.1) | collective-permute-done | bytes 131104 | tf_op jit(solution)/shard_map/ppermute | solution.py:20
  15.2 0.4 fusion.13
  15.6 1.1 %copy_bitcast_fusion.x_ref = f32[8,2,64,256]{3,2,1,0:T(8,128)} fusion(bf16[2,256,8,64]{1,3,2,0:T(8,128)(2,1)S(1)} %bitcast.56), kind=kLoop, calls=%fused_computation.12 | loop fusion | flops 262144 | bytes 1572864 | tf_op jit(solution)/shard_map/convert_element_type | solution.py:97
  16.7 35.0 %shard_map.104 = f32[8,2,128,64]{3,2,1,0:T(8,128)} custom-call(f32[8,2,64,256]{3,2,1,0:T(8,128)} %copy_bitcast_fusion.x_ref, bf16[8,64,64,128]{3,2,1,0:T(8,128)(2,1)} %bitcast.54), custom_call_target="tpu_custom_call" | custom-call | flops 2147483648 | bytes 9961472 | tf_op jit(solution)/shard_map/pallas_call | solution.py:75
  51.8 1.6 %copy.17 = f32[2,128,8,64]{1,3,2,0:T(8,128)S(1)} copy(f32[2,128,8,64]{3,1,0,2:T(8,128)} %bitcast.55) | data formatting | bytes 1048576 | tf_op jit(solution)/shard_map/transpose | solution.py:98
  53.3 0.0 copy-start.1
  53.3 1.3 %fusion.12 = bf16[2,128,512]{1,2,0:T(8,128)(2,1)S(1)} fusion(f32[2,128,8,64]{1,3,2,0:T(8,128)S(1)} %copy.17, f32[512]{0:T(512)S(1)} %convert_element_type.69, bf16[2,128,512]{1,2,0:T(8,128)(2,1)S(1)} %copy.15, pred[2,128]{1,0:T(4,128)(4,1)S(1)} %broadcast_compare_fusion), kind=kLoop, calls=%fused_computation.21 | loop fusion | flops 9043968 | bytes 1050880 | tf_op jit(solution)/shard_map/convert_element_type | solution.py:186
  54.6 7.9 %all_to_all.4 = bf16[2,128,512]{1,2,0:T(8,128)(2,1)S(1)} all-to-all(bf16[2,128,512]{1,2,0:T(8,128)(2,1)S(1)} %fusion.12), channel_id=1, replica_groups=mesh['ctx'=4,'fsdp'=2,'rep'=4] {'fsdp'}, dimensions={0} | all-to-all | bytes 524288 | tf_op jit(solution)/shard_map/all_to_all | solution.py:187
  62.5 0.2 convert_reduce_fusion
  62.7 0.2 fusion.18
  62.9 0.3 fusion.25
  63.2 0.0 copy-start.2
  63.2 0.3 convolution_convert_fusion
  63.6 0.3 convolution_convert_fusion.1
  64.0 4.4 %collective-permute-start.3 = (bf16[128,1024]{1,0:T(8,128)(2,1)S(1)}, bf16[128,1024]{1,0:T(8,128)(2,1)S(1)}, u32[]{:S(2)}, u32[]{:S(2)}) collective-permute-start(bf16[128,1024]{1,0:T(8,128)(2,1)S(1)} %pad_maximum_fusion.3), channel_id=1, source_target_pairs={{0,8},{8,16},{16,24},{1,9},{9,17},{17,25},{2,10},{10,18},{18,26},{... | collective-permute-start | bytes 786440 | tf_op jit(solution)/shard_map/ppermute | solution.py:108
  68.4 1.3 %collective-permute-start.2 = (bf16[128,1024]{1,0:T(8,128)(2,1)S(1)}, bf16[128,1024]{1,0:T(8,128)(2,1)}, u32[]{:S(2)}, u32[]{:S(2)}) collective-permute-start(bf16[128,1024]{1,0:T(8,128)(2,1)S(1)} %pad_maximum_fusion.3), channel_id=1, source_target_pairs={{8,0},{16,8},{24,16},{9,1},{17,9},{25,17},{10,2},{18,10},{26,18},{... | collective-permute-start | bytes 786440 | tf_op jit(solution)/shard_map/ppermute | solution.py:109
  69.7 0.6 dynamic_slice.4
  70.3 2.0 %collective-permute-done.3 = bf16[128,1024]{1,0:T(8,128)(2,1)S(1)} collective-permute-done((bf16[128,1024]{1,0:T(8,128)(2,1)S(1)}, bf16[128,1024]{1,0:T(8,128)(2,1)S(1)}, u32[]{:S(2)}, u32[]{:S(2)}) %collective-permute-start.3) | collective-permute-done | bytes 262176 | tf_op jit(solution)/shard_map/ppermute | solution.py:108
  72.2 5.1 %collective-permute-start.4 = (bf16[128,1024]{1,0:T(8,128)(2,1)S(1)}, bf16[128,1024]{1,0:T(8,128)(2,1)}, u32[]{:S(2)}, u32[]{:S(2)}) collective-permute-start(bf16[128,1024]{1,0:T(8,128)(2,1)S(1)} %collective-permute-done.3), channel_id=1, source_target_pairs={{0,8},{8,16},{16,24},{1,9},{9,17},{17,25},{2,10},{10,18},{18,26},{... | collective-permute-start | bytes 786440 | tf_op jit(solution)/shard_map/ppermute | solution.py:108
  77.3 0.7 broadcast_compare_fusion.1
  78.0 0.0 collective-permute-done.2
  78.0 1.3 %collective-permute-start.6 = (bf16[128,1024]{1,0:T(8,128)(2,1)}, bf16[128,1024]{1,0:T(8,128)(2,1)S(1)}, u32[]{:S(2)}, u32[]{:S(2)}) collective-permute-start(bf16[128,1024]{1,0:T(8,128)(2,1)} %collective-permute-done.2), channel_id=1, source_target_pairs={{8,0},{16,8},{24,16},{9,1},{17,9},{25,17},{10,2},{18,10},{26,18},{... | collective-permute-start | bytes 786440 | tf_op jit(solution)/shard_map/ppermute | solution.py:109
  79.3 0.7 add_compare_fusion
  80.0 0.9 copy.21
  80.8 0.0 collective-permute-done.4
  80.8 5.2 %collective-permute-start.5 = (bf16[128,1024]{1,0:T(8,128)(2,1)}, bf16[128,1024]{1,0:T(8,128)(2,1)}, u32[]{:S(2)}, u32[]{:S(2)}) collective-permute-start(bf16[128,1024]{1,0:T(8,128)(2,1)} %collective-permute-done.4), channel_id=1, source_target_pairs={{0,8},{8,16},{16,24},{1,9},{9,17},{17,25},{2,10},{10,18},{18,26},{... | collective-permute-start | bytes 786440 | tf_op jit(solution)/shard_map/ppermute | solution.py:108
  86.1 0.3 convolution_convert_fusion.2
  86.4 0.1 copy.18
  86.5 0.0 collective-permute-done.6
  86.5 1.3 %collective-permute-start.7 = (bf16[128,1024]{1,0:T(8,128)(2,1)S(1)}, bf16[128,1024]{1,0:T(8,128)(2,1)S(1)}, u32[]{:S(2)}, u32[]{:S(2)}) collective-permute-start(bf16[128,1024]{1,0:T(8,128)(2,1)S(1)} %collective-permute-done.6), channel_id=1, source_target_pairs={{8,0},{16,8},{24,16},{9,1},{17,9},{25,17},{10,2},{18,10},{26,18},{... | collective-permute-start | bytes 786440 | tf_op jit(solution)/shard_map/ppermute | solution.py:109
  87.9 1.7 %collective-permute-done.5 = bf16[128,1024]{1,0:T(8,128)(2,1)} collective-permute-done((bf16[128,1024]{1,0:T(8,128)(2,1)}, bf16[128,1024]{1,0:T(8,128)(2,1)}, u32[]{:S(2)}, u32[]{:S(2)}) %collective-permute-start.5) | collective-permute-done | bytes 262176 | tf_op jit(solution)/shard_map/ppermute | solution.py:108
  89.6 1.0 broadcast_select_fusion.2
  90.5 4.3 %collective-permute-done.7 = bf16[128,1024]{1,0:T(8,128)(2,1)S(1)} collective-permute-done((bf16[128,1024]{1,0:T(8,128)(2,1)S(1)}, bf16[128,1024]{1,0:T(8,128)(2,1)S(1)}, u32[]{:S(2)}, u32[]{:S(2)}) %collective-permute-start.7) | collective-permute-done | bytes 262176 | tf_op jit(solution)/shard_map/ppermute | solution.py:109
  94.8 0.1 pad_maximum_fusion
  94.9 0.9 fusion.37
  95.8 1.0 copy.19
  96.8 1.5 %fusion.40 = f32[8,128,512]{2,1,0:T(8,128)S(1)} fusion(bf16[128,8,64]{0,2,1:T(8,128)(2,1)S(1)} %bitcast.60, bf16[512,8,64]{0,2,1:T(8,128)(2,1)} %bitcast.57), kind=kOutput, calls=%fused_computation.74 | convolution fusion | flops 67108864 | bytes 2752512 | tf_op jit(solution)/shard_map/fhd,nhd->hfn/dot_general | solution.py:209
  98.3 2.0 %fusion.39 = f32[8,128]{1,0:T(8,128)S(1)} fusion(pred[512]{0:T(512)(128)(4,1)S(1)} %add_compare_fusion, bf16[128,8,64]{0,2,1:T(8,128)(2,1)S(1)} %bitcast.61, bf16[512,8,64]{0,2,1:T(8,128)(2,1)} %bitcast.58), kind=kOutput, calls=%fused_computation.73 | convolution fusion | flops 69730816 | bytes 659968 | tf_op jit(solution)/shard_map/sub | solution.py:215
  100.3 2.1 %copy.20 = bf16[512,512]{0,1:T(8,128)(2,1)} copy(bf16[512,512]{1,0:T(8,128)(2,1)} %get-tuple-element.7) | data formatting | bytes 1048576 | tf_op jit(solution)/shard_map/slice | solution.py:208
  102.4 1.8 %fusion.4 = bf16[128,8,64]{0,2,1:T(8,128)(2,1)S(1)} fusion(bf16[512,8,64]{0,2,1:T(8,128)(2,1)} %bitcast.59, f32[8,128,512]{2,1,0:T(8,128)S(1)} %fusion.40, pred[512]{0:T(512)(128)(4,1)S(1)} %add_compare_fusion, f32[128,8]{0,1:T(8,128)S(1)} %bitcast.63, pred[128]{0:T(512)(128)(4,1)S(1)} %broadcast_compare_fusion.1), kind=kOutput, calls=%fused_computation.7 | convolution fusion | flops 69928448 | bytes 2757248 | tf_op jit(solution)/shard_map/hfn,nhd->hfd/dot_general | solution.py:217
  104.1 0.8 copy.22
  (20 shorter events, 0.2 us)
Async XLA Ops:
  0.6 62.6 %copy-start = (bf16[1024,512]{1,0:T(8,128)(2,1)S(1)}, bf16[1024,512]{1,0:T(8,128)(2,1)}, u32[]{:S(2)}) copy-start(bf16[1024,512]{1,0:T(8,128)(2,1)} %param.17) | copy-start | bytes 3145732
  0.6 9.0 %copy-start.5 = (bf16[512]{0:T(512)(128)(2,1)S(1)}, bf16[512]{0:T(512)(128)(2,1)}, u32[]{:S(2)}) copy-start(bf16[512]{0:T(512)(128)(2,1)} %param.12) | copy-start | bytes 3076
  2.8 11.2 %collective-permute-start = (bf16[2,64,512]{1,2,0:T(8,128)(2,1)S(1)}, bf16[2,64,512]{1,2,0:T(8,128)(2,1)S(1)}, u32[]{:S(2)}, u32[]{:S(2)}) collective-permute-start(bf16[2,64,512]{1,2,0:T(8,128)(2,1)S(1)} %get-tuple-element.8), channel_id=1, source_target_pairs={{8,0},{16,8},{24,16},{9,1},{17,9},{25,17},{10,2},{18,10},{26,18},{... | collective-permute-start | bytes 393224 | tf_op jit(solution)/shard_map/ppermute | solution.py:21
  4.1 11.1 %collective-permute-start.1 = (bf16[2,64,512]{1,2,0:T(8,128)(2,1)S(1)}, bf16[2,64,512]{1,2,0:T(8,128)(2,1)S(1)}, u32[]{:S(2)}, u32[]{:S(2)}) collective-permute-start(bf16[2,64,512]{1,2,0:T(8,128)(2,1)S(1)} %get-tuple-element.9), channel_id=1, source_target_pairs={{0,8},{8,16},{16,24},{1,9},{9,17},{17,25},{2,10},{10,18},{18,26},{... | collective-permute-start | bytes 393224 | tf_op jit(solution)/shard_map/ppermute | solution.py:20
  51.7 11.1 %copy-start.3 = (f32[1024]{0:T(1024)S(1)}, f32[1024]{0:T(1024)}, u32[]{:S(2)}) copy-start(f32[1024]{0:T(1024)} %param.14) | copy-start | bytes 12292
  51.7 11.1 %copy-start.4 = (f32[1024]{0:T(1024)S(1)}, f32[1024]{0:T(1024)}, u32[]{:S(2)}) copy-start(f32[1024]{0:T(1024)} %param.13) | copy-start | bytes 12292
  53.3 10.2 %copy-start.1 = (bf16[1024,512]{1,0:T(8,128)(2,1)S(1)}, bf16[1024,512]{1,0:T(8,128)(2,1)}, u32[]{:S(2)}) copy-start(bf16[1024,512]{1,0:T(8,128)(2,1)} %param.16) | copy-start | bytes 3145732
  62.7 7.0 %copy-start.6 = (s32[2]{0:T(128)S(1)}, s32[2]{0:T(128)}, u32[]{:S(2)}) copy-start(s32[2]{0:T(128)} %param.10) | copy-start | bytes 28
  63.2 22.9 %copy-start.2 = (bf16[1024,512]{1,0:T(8,128)(2,1)S(1)}, bf16[1024,512]{1,0:T(8,128)(2,1)}, u32[]{:S(2)}) copy-start(bf16[1024,512]{1,0:T(8,128)(2,1)} %param.15) | copy-start | bytes 3145732
  64.0 8.3 %collective-permute-start.3 = (bf16[128,1024]{1,0:T(8,128)(2,1)S(1)}, bf16[128,1024]{1,0:T(8,128)(2,1)S(1)}, u32[]{:S(2)}, u32[]{:S(2)}) collective-permute-start(bf16[128,1024]{1,0:T(8,128)(2,1)S(1)} %pad_maximum_fusion.3), channel_id=1, source_target_pairs={{0,8},{8,16},{16,24},{1,9},{9,17},{17,25},{2,10},{10,18},{18,26},{... | collective-permute-start | bytes 786440 | tf_op jit(solution)/shard_map/ppermute | solution.py:108
  68.4 9.6 %collective-permute-start.2 = (bf16[128,1024]{1,0:T(8,128)(2,1)S(1)}, bf16[128,1024]{1,0:T(8,128)(2,1)}, u32[]{:S(2)}, u32[]{:S(2)}) collective-permute-start(bf16[128,1024]{1,0:T(8,128)(2,1)S(1)} %pad_maximum_fusion.3), channel_id=1, source_target_pairs={{8,0},{16,8},{24,16},{9,1},{17,9},{25,17},{10,2},{18,10},{26,18},{... | collective-permute-start | bytes 786440 | tf_op jit(solution)/shard_map/ppermute | solution.py:109
  72.2 8.6 %collective-permute-start.4 = (bf16[128,1024]{1,0:T(8,128)(2,1)S(1)}, bf16[128,1024]{1,0:T(8,128)(2,1)}, u32[]{:S(2)}, u32[]{:S(2)}) collective-permute-start(bf16[128,1024]{1,0:T(8,128)(2,1)S(1)} %collective-permute-done.3), channel_id=1, source_target_pairs={{0,8},{8,16},{16,24},{1,9},{9,17},{17,25},{2,10},{10,18},{18,26},{... | collective-permute-start | bytes 786440 | tf_op jit(solution)/shard_map/ppermute | solution.py:108
  78.0 8.5 %collective-permute-start.6 = (bf16[128,1024]{1,0:T(8,128)(2,1)}, bf16[128,1024]{1,0:T(8,128)(2,1)S(1)}, u32[]{:S(2)}, u32[]{:S(2)}) collective-permute-start(bf16[128,1024]{1,0:T(8,128)(2,1)} %collective-permute-done.2), channel_id=1, source_target_pairs={{8,0},{16,8},{24,16},{9,1},{17,9},{25,17},{10,2},{18,10},{26,18},{... | collective-permute-start | bytes 786440 | tf_op jit(solution)/shard_map/ppermute | solution.py:109
  80.8 8.7 %collective-permute-start.5 = (bf16[128,1024]{1,0:T(8,128)(2,1)}, bf16[128,1024]{1,0:T(8,128)(2,1)}, u32[]{:S(2)}, u32[]{:S(2)}) collective-permute-start(bf16[128,1024]{1,0:T(8,128)(2,1)} %collective-permute-done.4), channel_id=1, source_target_pairs={{0,8},{8,16},{16,24},{1,9},{9,17},{17,25},{2,10},{10,18},{18,26},{... | collective-permute-start | bytes 786440 | tf_op jit(solution)/shard_map/ppermute | solution.py:108
  86.5 8.3 %collective-permute-start.7 = (bf16[128,1024]{1,0:T(8,128)(2,1)S(1)}, bf16[128,1024]{1,0:T(8,128)(2,1)S(1)}, u32[]{:S(2)}, u32[]{:S(2)}) collective-permute-start(bf16[128,1024]{1,0:T(8,128)(2,1)S(1)} %collective-permute-done.6), channel_id=1, source_target_pairs={{8,0},{16,8},{24,16},{9,1},{17,9},{25,17},{10,2},{18,10},{26,18},{... | collective-permute-start | bytes 786440 | tf_op jit(solution)/shard_map/ppermute | solution.py:109

commit v2 on v1

--- a/solution.py
+++ b/solution.py
@@ -98,20 +98,14 @@
     return out.transpose(1, 2, 0, 3).reshape(recs, frame_rows, groups_here * group_out)
 
 
-def gather_ring(x, axis, rows):
+def gather_ring(x, axis, rows, offset):
     size = lax.axis_size(axis)
     place = lax.axis_index(axis)
-    ups = [(i, i + 1) for i in range(size - 1)]
-    downs = [(i + 1, i) for i in range(size - 1)]
-    from_below, from_above = [x], [x]
-    for step in range(1, size):
-        from_below.append(lax.ppermute(from_below[-1], axis, ups))
-        from_above.append(lax.ppermute(from_above[-1], axis, downs))
-    pieces, starts = [x], [place * rows]
-    for offset in range(1, size):
-        above = place + offset < size
-        pieces.append(jnp.where(above, from_above[offset], from_below[size - offset]))
-        starts.append(((place + offset) % size) * rows)
+    pieces, starts = [x], [place * rows + offset]
+    for shift in range(1, size):
+        pairs = [(i, (i + shift) % size) for i in range(size)]
+        pieces.append(lax.ppermute(x, axis, pairs))
+        starts.append(((place - shift) % size) * rows + offset)
     return pieces, starts
 
 
@@ -179,30 +173,44 @@
     groups_here, kernel_width, group_in, group_out = conv_weight.shape
     half_width = kernel_width // 2
     padded = padded_2(masked, (("ctx", 1),), half_width)
-    conv_out = grouped_conv(padded, conv_weight, frame_rows)
-    hidden = (
-        masked.astype(jnp.float32)
-        + jax.nn.gelu(conv_out + conv_bias.astype(jnp.float32), approximate=False)
-    ).astype(jnp.bfloat16)
-    record = lax.all_to_all(hidden, "fsdp", split_axis=0, concat_axis=2, tiled=True)
     own_length = lax.dynamic_index_in_dim(lengths, lax.axis_index("fsdp"), 0, keepdims=False)
-    flat = record[0].astype(jnp.float32)
-    centre = jnp.mean(flat, axis=1, keepdims=True)
-    spread = jnp.mean((flat - centre) ** 2, axis=1, keepdims=True)
-    normed = ((flat - centre) / jnp.sqrt(spread + 1e-05) * norm_gain + norm_shift).astype(
-        jnp.bfloat16
-    )
-    query_flat = jnp.dot(normed, w_query, preferred_element_type=jnp.float32).astype(jnp.bfloat16)
-    key_flat = jnp.dot(normed, w_key, preferred_element_type=jnp.float32).astype(jnp.bfloat16)
-    val_flat = jnp.dot(normed, w_value, preferred_element_type=jnp.float32).astype(jnp.bfloat16)
+    chunks = 2 if frame_rows % 16 == 0 else 1
+    rows = frame_rows // chunks
+    hidden_parts, query_parts, pieces, starts = [], [], [], []
+    size_of_ring = lax.axis_size("ctx")
+    for chunk in range(chunks):
+        low = chunk * rows
+        window = padded[:, low : low + rows + kernel_width - 1]
+        if pieces:
+            window, unused = lax.optimization_barrier((window, pieces[-size_of_ring]))
+        conv_out = grouped_conv(window, conv_weight, rows)
+        hidden_part = (
+            masked[:, low : low + rows].astype(jnp.float32)
+            + jax.nn.gelu(conv_out + conv_bias.astype(jnp.float32), approximate=False)
+        ).astype(jnp.bfloat16)
+        hidden_parts.append(hidden_part)
+        record = lax.all_to_all(hidden_part, "fsdp", split_axis=0, concat_axis=2, tiled=True)
+        flat = record[0].astype(jnp.float32)
+        centre = jnp.mean(flat, axis=1, keepdims=True)
+        spread = jnp.mean((flat - centre) ** 2, axis=1, keepdims=True)
+        normed = ((flat - centre) / jnp.sqrt(spread + 1e-05) * norm_gain + norm_shift).astype(
+            jnp.bfloat16
+        )
+        query_parts.append(
+            jnp.dot(normed, w_query, preferred_element_type=jnp.float32).astype(jnp.bfloat16)
+        )
+        key_flat = jnp.dot(normed, w_key, preferred_element_type=jnp.float32).astype(jnp.bfloat16)
+        val_flat = jnp.dot(normed, w_value, preferred_element_type=jnp.float32).astype(jnp.bfloat16)
+        width = key_flat.shape[1]
+        both = jnp.concatenate([key_flat, val_flat], axis=1)
+        got, at = gather_ring(both, "ctx", frame_rows, low)
+        pieces += got
+        starts += at
+    hidden = jnp.concatenate(hidden_parts, axis=1)
+    query_flat = jnp.concatenate(query_parts, axis=0)
     head_count = query_flat.shape[1] // HD
-    width = key_flat.shape[1]
-    both = jnp.concatenate([key_flat, val_flat], axis=1)
-    pieces, starts = gather_ring(both, "ctx", frame_rows)
     whole = jnp.concatenate(pieces, axis=0)
-    key_pos = jnp.concatenate(
-        [start + jnp.arange(frame_rows, dtype=jnp.int32) for start in starts]
-    )
+    key_pos = jnp.concatenate([start + jnp.arange(rows, dtype=jnp.int32) for start in starts])
     queries = query_flat.reshape(frame_rows, head_count, HD)
     keys = whole[:, :width].reshape(-1, head_count, HD)
     vals = whole[:, width:].reshape(-1, head_count, HD)

time: 106 us -> 121 us (1.14)
  Pallas kernels: 35 us -> 48.3 us
  blocking collectives: 7.92 us -> 0 us
  local copies, waits for them, and re-layouts: 9.21 us -> 13.8 us
  matrix products: 6.26 us -> 9.93 us
  other arithmetic: 6.67 us -> 8.81 us
    pallas_call x1 -> x2, Pallas kernels: 35 us -> 48.3 us  [hankel_conv(): pl.pallas_call(conv_body, grid=(groups,), in_specs=[pl.BlockSpec((1, recs...]
    ppermute x6, starting transfers between devices: 18.6 us -> 10.6 us  [gather_ring(): pieces.append(lax.ppermute(x, axis, pairs))]
    all_to_all x1 -> x0, blocking collectives: 7.92 us -> none  [per_device(): lax.all_to_all(hidden, 'fsdp', split_axis=0, concat_axis=2, tiled=True)]
    all_to_all x0 -> x2, starting transfers between devices: none -> 6.76 us  [per_device(): lax.all_to_all(hidden_part, 'fsdp', split_axis=0, concat_axis=2, tiled=True)]
    all_to_all x0 -> x2, waiting for transfers between devices: none -> 6.09 us  [per_device(): lax.all_to_all(hidden_part, 'fsdp', split_axis=0, concat_axis=2, tiled=True)]
    ppermute x1, waiting for transfers between devices: 4.33 us -> 0.01 us  [padded_2(): after = lax.ppermute(first, axis, down)]
    unnamed x17 -> x32, local copies, waits for them, and re-layouts: 2.86 us -> 6.12 us
    ppermute x6, waiting for transfers between devices: 7.89 us -> 5.21 us  [gather_ring(): pieces.append(lax.ppermute(x, axis, pairs))]
  transfers between devices with their start and end apart: 8 -> 10, of which waited for: 5 -> 5; matrix products, arithmetic and copies ran while one was open for 4% -> 15% of each run, Pallas kernels for 0% -> 40%
where the time goes in v2:
time: 121 us
  Pallas kernels  48.3 us (40%)
  starting transfers between devices  24.3 us (20%)
  waiting for transfers between devices  14.2 us (12%)
  local copies, waits for them, and re-layouts  13.8 us (11%)
  matrix products  9.93 us (8%)
  other arithmetic  8.81 us (7%)
  between operations  1.23 us (1%)
    pallas_call x2, Pallas kernels, hankel_conv(): pl.pallas_call(conv_body, grid=(groups,), in_specs=[pl.BlockSpec((1, recs...  48.3 us
    ppermute x6, starting transfers between devices, gather_ring(): pieces.append(lax.ppermute(x, axis, pairs))  10.6 us
    all_to_all x2, starting transfers between devices, per_device(): lax.all_to_all(hidden_part, 'fsdp', split_axis=0, concat_axis=2, tiled=True)  6.76 us
    unnamed x32, local copies, waits for them, and re-layouts  6.12 us
    all_to_all x2, waiting for transfers between devices, per_device(): lax.all_to_all(hidden_part, 'fsdp', split_axis=0, concat_axis=2, tiled=True)  6.09 us
    ppermute x1, starting transfers between devices, padded_2(): before = lax.ppermute(last, axis, up)  5.57 us
    ppermute x6, waiting for transfers between devices, gather_ring(): pieces.append(lax.ppermute(x, axis, pairs))  5.21 us
    ppermute x1, waiting for transfers between devices, padded_2(): before = lax.ppermute(last, axis, up)  2.93 us
  transfers between devices with their start and end apart: 10, of which 5 were waited for; matrix products, arithmetic and copies ran while one was open for 15% of the time, Pallas kernels for 40%

profile of v2, /device:TPU:0, one launch (start us, length us, event | category | flops | bytes accessed | tf_op | source)
XLA Modules:
  0.0 120.6 jit_solution(3155769169488737620)
XLA Ops:
  0.7 1.2 copy.29
  1.9 0.7 broadcast_compare_fusion.1
  2.8 1.3 %collective-permute-start.1 = (bf16[2,64,512]{1,2,0:T(8,128)(2,1)S(1)}, bf16[2,64,512]{1,2,0:T(8,128)(2,1)S(1)}, u32[]{:S(2)}, u32[]{:S(2)}) collective-permute-start(bf16[2,64,512]{1,2,0:T(8,128)(2,1)S(1)} %get-tuple-element.13), channel_id=1, source_target_pairs={{8,0},{16,8},{24,16},{9,1},{17,9},{25,17},{10,2},{18,10},{26,18},{... | collective-permute-start | bytes 393224 | tf_op jit(solution)/shard_map/ppermute | solution.py:21
  4.1 5.6 %collective-permute-start = (bf16[2,64,512]{1,2,0:T(8,128)(2,1)S(1)}, bf16[2,64,512]{1,2,0:T(8,128)(2,1)S(1)}, u32[]{:S(2)}, u32[]{:S(2)}) collective-permute-start(bf16[2,64,512]{1,2,0:T(8,128)(2,1)S(1)} %get-tuple-element.12), channel_id=1, source_target_pairs={{0,8},{8,16},{16,24},{1,9},{9,17},{17,25},{2,10},{10,18},{18,26},{... | collective-permute-start | bytes 393224 | tf_op jit(solution)/shard_map/ppermute | solution.py:20
  9.8 0.6 dynamic_slice.4
  10.5 0.6 broadcast_compare_fusion
  11.1 1.1 broadcast_compare_fusion.2
  12.3 2.9 %collective-permute-done = bf16[2,64,512]{1,2,0:T(8,128)(2,1)S(1)} collective-permute-done((bf16[2,64,512]{1,2,0:T(8,128)(2,1)S(1)}, bf16[2,64,512]{1,2,0:T(8,128)(2,1)S(1)}, u32[]{:S(2)}, u32[]{:S(2)}) %collective-permute-start) | collective-permute-done | bytes 131104 | tf_op jit(solution)/shard_map/ppermute | solution.py:20
  15.2 0.2 fusion.19
  15.6 1.1 copy_bitcast_fusion.1.x_ref
  16.7 24.1 %shard_map.104 = f32[8,2,64,64]{3,2,1,0:T(8,128)} custom-call(f32[8,2,64,256]{3,2,1,0:T(8,128)} %copy_bitcast_fusion.1.x_ref, bf16[8,64,64,128]{3,2,1,0:T(8,128)(2,1)} %bitcast.73), custom_call_target="tpu_custom_call" | custom-call | flops 1073741824 | bytes 9699328 | tf_op jit(solution)/shard_map/pallas_call | solution.py:75
  40.8 1.2 %copy.45 = f32[2,64,8,64]{1,3,2,0:T(8,128)S(1)} copy(f32[2,64,8,64]{3,1,0,2:T(8,128)} %bitcast.77) | data formatting | bytes 524288 | tf_op jit(solution)/shard_map/reshape | solution.py:98
  42.1 1.3 %fusion.14 = bf16[2,64,512]{1,2,0:T(8,128)(2,1)S(1)} fusion(f32[2,64,8,64]{1,3,2,0:T(8,128)S(1)} %copy.45, f32[512]{0:T(512)S(1)} %convert_element_type.118, bf16[2,128,512]{1,2,0:T(8,128)(2,1)S(1)} %broadcast_select_fusion), kind=kLoop, calls=%fused_computation.28 | loop fusion | flops 4456448 | bytes 526336 | tf_op jit(solution)/shard_map/convert_element_type | solution.py:190
  43.3 0.8 copy.33
  44.1 3.4 %all-to-all-start = ((bf16[2,64,512]{2,1,0:T(8,128)(2,1)}), bf16[2,64,512]{2,1,0:T(8,128)(2,1)S(1)}, u32[]{:S(2)}, u32[]{:S(2)}) async-start(bf16[2,64,512]{2,1,0:T(8,128)(2,1)} %copy.33), calls=%async_computation | async-start | bytes 262144 | tf_op jit(solution)/shard_map/all_to_all | solution.py:192
  47.6 4.3 %all-to-all-done = bf16[2,64,512]{2,1,0:T(8,128)(2,1)S(1)} async-done(((bf16[2,64,512]{2,1,0:T(8,128)(2,1)}), bf16[2,64,512]{2,1,0:T(8,128)(2,1)S(1)}, u32[]{:S(2)}, u32[]{:S(2)}) %all-to-all-start) | async-done | bytes 131104 | tf_op jit(solution)/shard_map/all_to_all | solution.py:192
  52.7 0.4 convolution_convert_fusion.4
  53.2 1.6 %convolution_convert_fusion.5 = bf16[64,512]{1,0:T(8,128)(2,1)S(1)} fusion(bf16[1024,512]{1,0:T(8,128)(2,1)} %param.16, f32[64,1024]{1,0:T(8,128)S(1)} %bitcast.88, f32[1024]{0:T(1024)S(1)} %copy-done.5, f32[1024]{0:T(1024)S(1)} %copy-done.6, f32[64]{0:T(128)S(1)} %add_sqrt_fusion.1, f32[64]{0:T(128)S(1)} %broadcast_multiply_fusion.1), kind=kOutput, calls=%fused_computation.13 | convolution fusion | flops 67469312 | bytes 1384960 | tf_op jit(solution)/shard_map/dot_general | solution.py:202
  54.8 0.2 pad_slice_fusion
  55.1 2.5 %collective-permute-start.2 = (bf16[64,1024]{1,0:T(8,128)(2,1)S(1)}, bf16[64,1024]{1,0:T(8,128)(2,1)}, u32[]{:S(2)}, u32[]{:S(2)}) collective-permute-start(bf16[64,1024]{1,0:T(8,128)(2,1)S(1)} %get-tuple-element.17), channel_id=1, source_target_pairs={{0,8},{8,16},{16,24},{24,0},{1,9},{9,17},{17,25},{25,1},{2,10},{10... | collective-permute-start | bytes 393224 | tf_op jit(solution)/shard_map/ppermute | solution.py:107
  57.6 2.8 %collective-permute-start.3 = (bf16[64,1024]{1,0:T(8,128)(2,1)S(1)}, bf16[64,1024]{1,0:T(8,128)(2,1)}, u32[]{:S(2)}, u32[]{:S(2)}) collective-permute-start(bf16[64,1024]{1,0:T(8,128)(2,1)S(1)} %get-tuple-element.17), channel_id=1, source_target_pairs={{0,16},{8,24},{16,0},{24,8},{1,17},{9,25},{17,1},{25,9},{2,18},{10... | collective-permute-start | bytes 393224 | tf_op jit(solution)/shard_map/ppermute | solution.py:107
  60.4 1.3 %collective-permute-start.4 = (bf16[64,1024]{1,0:T(8,128)(2,1)S(1)}, bf16[64,1024]{1,0:T(8,128)(2,1)}, u32[]{:S(2)}, u32[]{:S(2)}) collective-permute-start(bf16[64,1024]{1,0:T(8,128)(2,1)S(1)} %get-tuple-element.17), channel_id=1, source_target_pairs={{0,24},{8,0},{16,8},{24,16},{1,25},{9,1},{17,9},{25,17},{2,26},{10... | collective-permute-start | bytes 393224 | tf_op jit(solution)/shard_map/ppermute | solution.py:107
  61.9 1.1 copy_bitcast_fusion.x_ref
  63.0 24.1 %shard_map.105 = f32[8,2,64,64]{3,2,1,0:T(8,128)} custom-call(f32[8,2,64,256]{3,2,1,0:T(8,128)} %copy_bitcast_fusion.x_ref, bf16[8,64,64,128]{3,2,1,0:T(8,128)(2,1)} %bitcast.74), custom_call_target="tpu_custom_call" | custom-call | flops 1073741824 | bytes 9699328 | tf_op jit(solution)/shard_map/pallas_call | solution.py:75
  87.1 1.2 %copy.46 = f32[2,64,8,64]{1,3,2,0:T(8,128)S(1)} copy(f32[2,64,8,64]{3,1,0,2:T(8,128)} %bitcast.78) | data formatting | bytes 524288 | tf_op jit(solution)/shard_map/reshape | solution.py:98
  88.3 1.3 %fusion.18 = bf16[2,64,512]{1,2,0:T(8,128)(2,1)S(1)} fusion(f32[2,64,8,64]{1,3,2,0:T(8,128)S(1)} %copy.46, f32[512]{0:T(512)S(1)} %convert_element_type.118, bf16[2,128,512]{1,2,0:T(8,128)(2,1)S(1)} %broadcast_select_fusion), kind=kLoop, calls=%fused_computation.32 | loop fusion | flops 4456448 | bytes 526336 | tf_op jit(solution)/shard_map/convert_element_type | solution.py:190
  89.6 0.8 copy.38
  90.4 3.4 %all-to-all-start.1 = ((bf16[2,64,512]{2,1,0:T(8,128)(2,1)}), bf16[2,64,512]{2,1,0:T(8,128)(2,1)S(1)}, u32[]{:S(2)}, u32[]{:S(2)}) async-start(bf16[2,64,512]{2,1,0:T(8,128)(2,1)} %copy.38), calls=%async_computation.1 | async-start | bytes 262144 | tf_op jit(solution)/shard_map/all_to_all | solution.py:192
  93.8 1.7 %convolution_convert_fusion.3 = bf16[64,512]{1,0:T(8,128)(2,1)S(1)} fusion(bf16[1024,512]{1,0:T(8,128)(2,1)} %param.15, f32[64,1024]{1,0:T(8,128)} %bitcast.89, f32[1024]{0:T(1024)S(1)} %copy-done.5, f32[1024]{0:T(1024)} %param.13, f32[64]{0:T(128)} %copy-done.10, f32[64]{0:T(128)S(1)} %broadcast_multiply_fusion.1), kind=kOutput, calls=%fused_computation.11 | convolution fusion | flops 67469312 | bytes 1384960 | tf_op jit(solution)/shard_map/dot_general | solution.py:200
  95.6 0.9 copy.43
  96.5 1.7 %all-to-all-done.1 = bf16[2,64,512]{2,1,0:T(8,128)(2,1)S(1)} async-done(((bf16[2,64,512]{2,1,0:T(8,128)(2,1)}), bf16[2,64,512]{2,1,0:T(8,128)(2,1)S(1)}, u32[]{:S(2)}, u32[]{:S(2)}) %all-to-all-start.1) | async-done | bytes 131104 | tf_op jit(solution)/shard_map/all_to_all | solution.py:192
  98.9 0.4 convolution_convert_fusion
  99.5 0.3 convolution_convert_fusion.1
  99.8 0.9 constant_dynamic-update-slice_fusion.6
  100.8 0.9 constant_dynamic-update-slice_fusion.5
  101.7 0.9 constant_dynamic-update-slice_fusion.4
  102.6 0.8 collective-permute-start.5
  103.4 0.3 convolution_convert_fusion.2
  103.7 0.2 collective-permute-start.6
  104.1 3.0 %collective-permute-start.7 = (bf16[64,1024]{1,0:T(8,128)(2,1)S(1)}, bf16[64,1024]{1,0:T(8,128)(2,1)S(1)}, u32[]{:S(2)}, u32[]{:S(2)}) collective-permute-start(bf16[64,1024]{1,0:T(8,128)(2,1)S(1)} %get-tuple-element.14), channel_id=1, source_target_pairs={{0,24},{8,0},{16,8},{24,16},{1,25},{9,1},{17,9},{25,17},{2,26},{10... | collective-permute-start | bytes 393224 | tf_op jit(solution)/shard_map/ppermute | solution.py:107
  107.1 2.4 %collective-permute-done.5 = bf16[64,1024]{1,0:T(8,128)(2,1)S(1)} collective-permute-done((bf16[64,1024]{1,0:T(8,128)(2,1)S(1)}, bf16[64,1024]{1,0:T(8,128)(2,1)S(1)}, u32[]{:S(2)}, u32[]{:S(2)}) %collective-permute-start.5) | collective-permute-done | bytes 131104 | tf_op jit(solution)/shard_map/ppermute | solution.py:107
  109.6 2.8 %collective-permute-done.6 = bf16[64,1024]{1,0:T(8,128)(2,1)S(1)} collective-permute-done((bf16[64,1024]{1,0:T(8,128)(2,1)S(1)}, bf16[64,1024]{1,0:T(8,128)(2,1)S(1)}, u32[]{:S(2)}, u32[]{:S(2)}) %collective-permute-start.6) | collective-permute-done | bytes 131104 | tf_op jit(solution)/shard_map/ppermute | solution.py:107
  112.5 1.0 copy.42
  113.5 1.0 copy.41
  114.5 1.5 %fusion.53 = f32[8,128,512]{2,1,0:T(8,128)S(1)} fusion(bf16[128,8,64]{0,2,1:T(8,128)(2,1)S(1)} %bitcast.85, bf16[512,8,64]{0,2,1:T(8,128)(2,1)} %bitcast.79), kind=kOutput, calls=%fused_computation.123 | convolution fusion | flops 67108864 | bytes 2752512 | tf_op jit(solution)/shard_map/fhd,nhd->hfn/dot_general | solution.py:217
  116.0 2.0 %fusion.52 = f32[8,128]{1,0:T(8,128)S(1)} fusion(pred[512]{0:T(512)(128)(4,1)S(1)} %broadcast_compare_fusion, bf16[128,8,64]{0,2,1:T(8,128)(2,1)S(1)} %bitcast.86, bf16[512,8,64]{0,2,1:T(8,128)(2,1)} %bitcast.80), kind=kOutput, calls=%fused_computation.122 | convolution fusion | flops 69730816 | bytes 659968 | tf_op jit(solution)/shard_map/sub | solution.py:223
  118.0 1.8 %fusion.4 = bf16[128,8,64]{0,2,1:T(8,128)(2,1)S(1)} fusion(bf16[512,8,64]{0,2,1:T(8,128)(2,1)} %bitcast.84, f32[8,128,512]{2,1,0:T(8,128)S(1)} %fusion.53, pred[512]{0:T(512)(128)(4,1)S(1)} %broadcast_compare_fusion, f32[128,8]{0,1:T(8,128)S(1)} %bitcast.94, pred[128]{0:T(512)(128)(4,1)S(1)} %copy-done.9), kind=kOutput, calls=%fused_computation.7 | convolution fusion | flops 69928448 | bytes 2757248 | tf_op jit(solution)/shard_map/hfn,nhd->hfd/dot_general | solution.py:225
  119.8 0.8 copy.44
  (63 shorter events, 2.8 us)
Async XLA Ops:
  0.6 52.0 %copy-start = (bf16[1024,512]{1,0:T(8,128)(2,1)S(1)}, bf16[1024,512]{1,0:T(8,128)(2,1)}, u32[]{:S(2)}) copy-start(bf16[1024,512]{1,0:T(8,128)(2,1)} %param.17) | copy-start | bytes 3145732
  0.6 9.1 %copy-start.8 = (s32[2]{0:T(128)S(1)}, s32[2]{0:T(128)}, u32[]{:S(2)}) copy-start(s32[2]{0:T(128)} %param.10) | copy-start | bytes 28
  0.7 10.5 %copy-start.2 = (bf16[512]{0:T(512)(128)(2,1)S(1)}, bf16[512]{0:T(512)(128)(2,1)}, u32[]{:S(2)}) copy-start(bf16[512]{0:T(512)(128)(2,1)} %param.12) | copy-start | bytes 3076
  2.8 44.7 %collective-permute-start.1 = (bf16[2,64,512]{1,2,0:T(8,128)(2,1)S(1)}, bf16[2,64,512]{1,2,0:T(8,128)(2,1)S(1)}, u32[]{:S(2)}, u32[]{:S(2)}) collective-permute-start(bf16[2,64,512]{1,2,0:T(8,128)(2,1)S(1)} %get-tuple-element.13), channel_id=1, source_target_pairs={{8,0},{16,8},{24,16},{9,1},{17,9},{25,17},{10,2},{18,10},{26,18},{... | collective-permute-start | bytes 393224 | tf_op jit(solution)/shard_map/ppermute | solution.py:21
  4.1 11.1 %collective-permute-start = (bf16[2,64,512]{1,2,0:T(8,128)(2,1)S(1)}, bf16[2,64,512]{1,2,0:T(8,128)(2,1)S(1)}, u32[]{:S(2)}, u32[]{:S(2)}) collective-permute-start(bf16[2,64,512]{1,2,0:T(8,128)(2,1)S(1)} %get-tuple-element.12), channel_id=1, source_target_pairs={{0,8},{8,16},{16,24},{1,9},{9,17},{17,25},{2,10},{10,18},{18,26},{... | collective-permute-start | bytes 393224 | tf_op jit(solution)/shard_map/ppermute | solution.py:20
  42.1 10.6 %copy-start.5 = (f32[1024]{0:T(1024)S(1)}, f32[1024]{0:T(1024)}, u32[]{:S(2)}) copy-start(f32[1024]{0:T(1024)} %param.14) | copy-start | bytes 12292
  42.1 10.6 %copy-start.6 = (f32[1024]{0:T(1024)S(1)}, f32[1024]{0:T(1024)}, u32[]{:S(2)}) copy-start(f32[1024]{0:T(1024)} %param.13) | copy-start | bytes 12292
  44.1 7.8 %all-to-all-start = ((bf16[2,64,512]{2,1,0:T(8,128)(2,1)}), bf16[2,64,512]{2,1,0:T(8,128)(2,1)S(1)}, u32[]{:S(2)}, u32[]{:S(2)}) async-start(bf16[2,64,512]{2,1,0:T(8,128)(2,1)} %copy.33), calls=%async_computation | async-start | bytes 262144 | tf_op jit(solution)/shard_map/all_to_all | solution.py:192
  52.3 0.8 copy-start.1
  52.6 0.6 copy-start.10
  55.1 44.7 %collective-permute-start.2 = (bf16[64,1024]{1,0:T(8,128)(2,1)S(1)}, bf16[64,1024]{1,0:T(8,128)(2,1)}, u32[]{:S(2)}, u32[]{:S(2)}) collective-permute-start(bf16[64,1024]{1,0:T(8,128)(2,1)S(1)} %get-tuple-element.17), channel_id=1, source_target_pairs={{0,8},{8,16},{16,24},{24,0},{1,9},{9,17},{17,25},{25,1},{2,10},{10... | collective-permute-start | bytes 393224 | tf_op jit(solution)/shard_map/ppermute | solution.py:107
  57.6 43.1 %collective-permute-start.3 = (bf16[64,1024]{1,0:T(8,128)(2,1)S(1)}, bf16[64,1024]{1,0:T(8,128)(2,1)}, u32[]{:S(2)}, u32[]{:S(2)}) collective-permute-start(bf16[64,1024]{1,0:T(8,128)(2,1)S(1)} %get-tuple-element.17), channel_id=1, source_target_pairs={{0,16},{8,24},{16,0},{24,8},{1,17},{9,25},{17,1},{25,9},{2,18},{10... | collective-permute-start | bytes 393224 | tf_op jit(solution)/shard_map/ppermute | solution.py:107
  60.4 41.3 %collective-permute-start.4 = (bf16[64,1024]{1,0:T(8,128)(2,1)S(1)}, bf16[64,1024]{1,0:T(8,128)(2,1)}, u32[]{:S(2)}, u32[]{:S(2)}) collective-permute-start(bf16[64,1024]{1,0:T(8,128)(2,1)S(1)} %get-tuple-element.17), channel_id=1, source_target_pairs={{0,24},{8,0},{16,8},{24,16},{1,25},{9,1},{17,9},{25,17},{2,26},{10... | collective-permute-start | bytes 393224 | tf_op jit(solution)/shard_map/ppermute | solution.py:107
  90.4 7.8 %all-to-all-start.1 = ((bf16[2,64,512]{2,1,0:T(8,128)(2,1)}), bf16[2,64,512]{2,1,0:T(8,128)(2,1)S(1)}, u32[]{:S(2)}, u32[]{:S(2)}) async-start(bf16[2,64,512]{2,1,0:T(8,128)(2,1)} %copy.38), calls=%async_computation.1 | async-start | bytes 262144 | tf_op jit(solution)/shard_map/all_to_all | solution.py:192
  93.8 5.1 %copy-start.7 = (f32[1024]{0:T(1024)S(1)}, f32[1024]{0:T(1024)}, u32[]{:S(2)}) copy-start(f32[1024]{0:T(1024)} %param.13) | copy-start | bytes 12292
  98.2 1.2 %copy-start.3 = (bf16[1024,512]{1,0:T(8,128)(2,1)S(1)}, bf16[1024,512]{1,0:T(8,128)(2,1)}, u32[]{:S(2)}) copy-start(bf16[1024,512]{1,0:T(8,128)(2,1)} %param.16) | copy-start | bytes 3145732
  98.9 4.5 %copy-start.4 = (bf16[1024,512]{1,0:T(8,128)(2,1)S(1)}, bf16[1024,512]{1,0:T(8,128)(2,1)}, u32[]{:S(2)}) copy-start(bf16[1024,512]{1,0:T(8,128)(2,1)} %param.15) | copy-start | bytes 3145732
  102.6 7.0 %collective-permute-start.5 = (bf16[64,1024]{1,0:T(8,128)(2,1)S(1)}, bf16[64,1024]{1,0:T(8,128)(2,1)S(1)}, u32[]{:S(2)}, u32[]{:S(2)}) collective-permute-start(bf16[64,1024]{1,0:T(8,128)(2,1)S(1)} %get-tuple-element.14), channel_id=1, source_target_pairs={{0,8},{8,16},{16,24},{24,0},{1,9},{9,17},{17,25},{25,1},{2,10},{10... | collective-permute-start | bytes 393224 | tf_op jit(solution)/shard_map/ppermute | solution.py:107
  103.7 8.6 %collective-permute-start.6 = (bf16[64,1024]{1,0:T(8,128)(2,1)S(1)}, bf16[64,1024]{1,0:T(8,128)(2,1)S(1)}, u32[]{:S(2)}, u32[]{:S(2)}) collective-permute-start(bf16[64,1024]{1,0:T(8,128)(2,1)S(1)} %get-tuple-element.14), channel_id=1, source_target_pairs={{0,16},{8,24},{16,0},{24,8},{1,17},{9,25},{17,1},{25,9},{2,18},{10... | collective-permute-start | bytes 393224 | tf_op jit(solution)/shard_map/ppermute | solution.py:107
  104.1 8.3 %collective-permute-start.7 = (bf16[64,1024]{1,0:T(8,128)(2,1)S(1)}, bf16[64,1024]{1,0:T(8,128)(2,1)S(1)}, u32[]{:S(2)}, u32[]{:S(2)}) collective-permute-start(bf16[64,1024]{1,0:T(8,128)(2,1)S(1)} %get-tuple-element.14), channel_id=1, source_target_pairs={{0,24},{8,0},{16,8},{24,16},{1,25},{9,1},{17,9},{25,17},{2,26},{10... | collective-permute-start | bytes 393224 | tf_op jit(solution)/shard_map/ppermute | solution.py:107
  116.0 2.0 %copy-start.9 = (pred[128]{0:T(512)(128)(4,1)S(1)}, pred[128]{0:T(512)(128)(4,1)}, u32[]{:S(2)}) copy-start(pred[128]{0:T(512)(128)(4,1)} %broadcast_compare_fusion.2) | copy-start | bytes 388

commit v3 on v0

--- a/solution.py
+++ b/solution.py
@@ -36,25 +36,39 @@
             block = x_ref[0, r, pl.ds(base, 8), :]
             per_chan = []
             for c in range(8):
-                row = jnp.broadcast_to(block[c : c + 1, :], (rows, lanes))
+                row = jnp.broadcast_to(block[c : c + 1, :], (taps, lanes))
                 rolled = pltpu.roll(row, 0, 1, stride=1, stride_axis=0)
-                per_chan.append(rolled[:, :taps].astype(jnp.bfloat16))
+                per_chan.append(rolled[:, :rows].astype(jnp.bfloat16))
             hankels.append(per_chan)
         for pair in range(4):
-            lhs = jnp.concatenate(
-                [jnp.concatenate(hankels[r][2 * pair : 2 * pair + 2], axis=1) for r in range(recs)],
+            rhs = jnp.concatenate(
+                [
+                    jnp.concatenate([hankels[r][2 * pair + half] for r in range(recs)], axis=1)
+                    for half in range(2)
+                ],
                 axis=0,
             )
-            rhs = jnp.concatenate(
+            lhs = jnp.concatenate(
                 [w_ref[0, base + 2 * pair], w_ref[0, base + 2 * pair + 1]], axis=1
             )
-            acc = acc + lax.dot_general(
-                lhs, rhs, (((1,), (1,)), ((), ())), preferred_element_type=jnp.float32
-            )
+            acc = acc + jnp.dot(lhs, rhs, preferred_element_type=jnp.float32)
         return acc
 
-    acc = lax.fori_loop(0, chans // 8, octet_step, jnp.zeros((recs * rows, outs), jnp.float32))
-    out_ref[0] = acc.reshape(recs, rows, outs)
+    acc = lax.fori_loop(0, chans // 8, octet_step, jnp.zeros((outs, recs * rows), jnp.float32))
+    across = lax.broadcasted_iota(jnp.int32, (rows, rows), 0) + lax.broadcasted_iota(
+        jnp.int32, (rows, rows), 1
+    )
+    flip = jnp.where(across == rows - 1, 1.0, 0.0).astype(jnp.bfloat16)
+    dims = (((1,), (1,)), ((), ()))
+    for r in range(recs):
+        part = acc[:, r * rows : (r + 1) * rows]
+        high = part.astype(jnp.bfloat16)
+        rest = part - high.astype(jnp.float32)
+        middle = rest.astype(jnp.bfloat16)
+        low = (rest - middle.astype(jnp.float32)).astype(jnp.bfloat16)
+        total = lax.dot_general(flip, high, dims, preferred_element_type=jnp.float32)
+        total = total + lax.dot_general(flip, middle, dims, preferred_element_type=jnp.float32)
+        out_ref[0, r] = total + lax.dot_general(flip, low, dims, preferred_element_type=jnp.float32)
 
 
 def hankel_conv(xt, wv, rows):
@@ -80,10 +94,9 @@
     groups_here, taps, group_in, group_out = conv_weight.shape
     lanes = -(-(frame_rows + taps - 1) // 128) * 128
     grouped = jnp.pad(padded, ((0, 0), (0, lanes - span), (0, 0)))
-    grouped = jnp.roll(grouped, 1 - frame_rows, axis=1)
+    grouped = jnp.roll(jnp.flip(grouped, axis=1), frame_rows - lanes, axis=1)
     grouped = grouped.reshape(recs, lanes, groups_here, group_in).transpose(2, 0, 3, 1)
     out = hankel_conv(grouped.astype(jnp.float32), jnp.transpose(conv_weight, (0, 2, 3, 1)), frame_rows)
-    out = jnp.flip(out, axis=2)
     return out.transpose(1, 2, 0, 3).reshape(recs, frame_rows, groups_here * group_out)
 
 

time: 105 us -> 103 us (0.981)
  local copies, waits for them, and re-layouts: 15.7 us -> 11.7 us
  waiting for transfers between devices: 24.6 us -> 27 us
  starting transfers between devices: 16.2 us -> 14.3 us
  Pallas kernels: 33.4 us -> 35 us
    rev x1 -> x0, local copies, waits for them, and re-layouts: 6.83 us -> none  [grouped_conv(): out = jnp.flip(out, axis=2)]
    ppermute x1, waiting for transfers between devices: 1.18 us -> 3.62 us  [padded_2(): before = lax.ppermute(last, axis, up)]
    pallas_call x1, Pallas kernels: 33.4 us -> 35 us  [hankel_conv(): pl.pallas_call(conv_body, grid=(groups,), in_specs=[pl.BlockSpec((1, recs...]
    slice x1 -> x3, local copies, waits for them, and re-layouts: 0.14 us -> 1.7 us  [the longest x2 1.57 us: grouped_conv(): grouped = jnp.roll(jnp.flip(grouped, axis=1), frame_rows - lanes, axis=1)]
    transpose x1, local copies, waits for them, and re-layouts: 0.31 us -> 1.56 us  [grouped_conv(): out.transpose(1, 2, 0, 3).reshape(recs, frame_rows, groups_here * group_out)]
    ppermute x3, starting transfers between devices: 5.73 us -> 4.65 us  [gather_ring(): pieces.append(lax.ppermute(x, axis, pairs))]
  transfers between devices with their start and end apart: 6 -> 6, of which waited for: 5 -> 4; matrix products, arithmetic and copies ran while one was open for 5% -> 5% of each run, Pallas kernels for 0% -> 0%
where the time goes in v3:
time: 103 us
  Pallas kernels  35 us (34%)
  waiting for transfers between devices  27 us (26%)
  starting transfers between devices  14.3 us (14%)
  local copies, waits for them, and re-layouts  11.7 us (11%)
  matrix products  7.47 us (7%)
  other arithmetic  6.23 us (6%)
    pallas_call x1, Pallas kernels, hankel_conv(): pl.pallas_call(conv_body, grid=(groups,), in_specs=[pl.BlockSpec((1, recs...  35 us
    ppermute x3, waiting for transfers between devices, gather_ring(): pieces.append(lax.ppermute(x, axis, pairs))  14.8 us
    ppermute x1, starting transfers between devices, padded_2(): before = lax.ppermute(last, axis, up)  4.94 us
    ppermute x3, starting transfers between devices, gather_ring(): pieces.append(lax.ppermute(x, axis, pairs))  4.65 us
    all_to_all x1, waiting for transfers between devices, per_device(): lax.all_to_all(hidden, 'fsdp', split_axis=0, concat_axis=2, tiled=True)  4.45 us
    ppermute x1, waiting for transfers between devices, padded_2(): after = lax.ppermute(first, axis, down)  4.13 us
    unnamed x15, local copies, waits for them, and re-layouts  3.79 us
    ppermute x1, waiting for transfers between devices, padded_2(): before = lax.ppermute(last, axis, up)  3.62 us
  transfers between devices with their start and end apart: 6, of which 4 were waited for; matrix products, arithmetic and copies ran while one was open for 5% of the time, Pallas kernels for 0%

profile of v3, /device:TPU:0, one launch (start us, length us, event | category | flops | bytes accessed | tf_op | source)
XLA Modules:
  0.0 102.7 jit_solution(686843839562895506)
XLA Ops:
  0.6 0.0 copy-start
  0.6 0.0 copy-start.5
  0.7 0.0 copy-start.4
  0.7 1.2 %copy.15 = bf16[2,128,512]{1,2,0:T(8,128)(2,1)S(1)} copy(bf16[2,128,512]{2,1,0:T(8,128)(2,1)} %param.9) | data formatting | bytes 524288 | tf_op args[0]
  1.9 0.7 broadcast_compare_fusion
  2.7 0.1 fusion.37
  2.8 4.9 %collective-permute-start = (bf16[2,64,512]{1,2,0:T(8,128)(2,1)S(1)}, bf16[2,64,512]{1,2,0:T(8,128)(2,1)S(1)}, u32[]{:S(2)}, u32[]{:S(2)}) collective-permute-start(bf16[2,64,512]{1,2,0:T(8,128)(2,1)S(1)} %get-tuple-element.10), channel_id=1, source_target_pairs={{0,8},{8,16},{16,24},{1,9},{9,17},{17,25},{2,10},{10,18},{18,26},{... | collective-permute-start | bytes 393224 | tf_op jit(solution)/shard_map/ppermute | solution.py:20
  7.8 1.3 %collective-permute-start.1 = (bf16[2,64,512]{1,2,0:T(8,128)(2,1)S(1)}, bf16[2,64,512]{1,2,0:T(8,128)(2,1)S(1)}, u32[]{:S(2)}, u32[]{:S(2)}) collective-permute-start(bf16[2,64,512]{1,2,0:T(8,128)(2,1)S(1)} %get-tuple-element.11), channel_id=1, source_target_pairs={{8,0},{16,8},{24,16},{9,1},{17,9},{25,17},{10,2},{18,10},{26,18},{... | collective-permute-start | bytes 393224 | tf_op jit(solution)/shard_map/ppermute | solution.py:21
  9.1 0.0 copy-done.5
  9.1 0.6 dynamic_slice.4
  9.7 0.0 copy-done.4
  9.7 3.6 %collective-permute-done = bf16[2,64,512]{1,2,0:T(8,128)(2,1)S(1)} collective-permute-done((bf16[2,64,512]{1,2,0:T(8,128)(2,1)S(1)}, bf16[2,64,512]{1,2,0:T(8,128)(2,1)S(1)}, u32[]{:S(2)}, u32[]{:S(2)}) %collective-permute-start) | collective-permute-done | bytes 131104 | tf_op jit(solution)/shard_map/ppermute | solution.py:20
  13.3 4.1 %collective-permute-done.1 = bf16[2,64,512]{1,2,0:T(8,128)(2,1)S(1)} collective-permute-done((bf16[2,64,512]{1,2,0:T(8,128)(2,1)S(1)}, bf16[2,64,512]{1,2,0:T(8,128)(2,1)S(1)}, u32[]{:S(2)}, u32[]{:S(2)}) %collective-permute-start.1) | collective-permute-done | bytes 131104 | tf_op jit(solution)/shard_map/ppermute | solution.py:21
  17.4 0.3 pad_maximum_fusion.3
  17.7 0.8 slice.30
  18.5 0.8 slice.33
  19.3 0.1 pad_maximum_fusion.1
  19.4 1.1 %copy_bitcast_fusion.x_ref = f32[8,2,64,256]{3,2,1,0:T(8,128)} fusion(bf16[2,256,8,64]{1,3,2,0:T(8,128)(2,1)S(1)} %bitcast.56), kind=kLoop, calls=%fused_computation.12 | loop fusion | flops 262144 | bytes 1572864 | tf_op jit(solution)/shard_map/convert_element_type | solution.py:99
  20.5 35.0 %shard_map.104 = f32[8,2,128,64]{3,2,1,0:T(8,128)} custom-call(f32[8,2,64,256]{3,2,1,0:T(8,128)} %copy_bitcast_fusion.x_ref, bf16[8,64,64,128]{3,2,1,0:T(8,128)(2,1)} %bitcast.54), custom_call_target="tpu_custom_call" | custom-call | flops 2147483648 | bytes 9961472 | tf_op jit(solution)/shard_map/pallas_call | solution.py:77
  55.5 1.6 %copy.17 = f32[2,128,8,64]{1,3,2,0:T(8,128)S(1)} copy(f32[2,128,8,64]{3,1,0,2:T(8,128)} %bitcast.55) | data formatting | bytes 1048576 | tf_op jit(solution)/shard_map/transpose | solution.py:100
  57.0 0.0 copy-start.1
  57.1 2.0 %fusion.12 = bf16[2,128,512]{1,2,0:T(8,128)(2,1)} fusion(f32[2,128,8,64]{1,3,2,0:T(8,128)S(1)} %copy.17, f32[512]{0:T(512)S(1)} %convert_element_type.69, bf16[2,128,512]{1,2,0:T(8,128)(2,1)S(1)} %copy.15, pred[2,128]{1,0:T(4,128)(4,1)S(1)} %broadcast_compare_fusion), kind=kLoop, calls=%fused_computation.21 | loop fusion | flops 9043968 | bytes 1050880 | tf_op jit(solution)/shard_map/convert_element_type | solution.py:182
  59.0 3.4 %all-to-all-start = ((bf16[2,128,512]{1,2,0:T(8,128)(2,1)}), bf16[2,128,512]{1,2,0:T(8,128)(2,1)S(1)}, u32[]{:S(2)}, u32[]{:S(2)}) async-start(bf16[2,128,512]{1,2,0:T(8,128)(2,1)} %fusion.12), calls=%async_computation | async-start | bytes 524288 | tf_op jit(solution)/shard_map/all_to_all | solution.py:183
  62.5 0.7 broadcast_compare_fusion.1
  63.2 4.5 %all-to-all-done = bf16[2,128,512]{1,2,0:T(8,128)(2,1)S(1)} async-done(((bf16[2,128,512]{1,2,0:T(8,128)(2,1)}), bf16[2,128,512]{1,2,0:T(8,128)(2,1)S(1)}, u32[]{:S(2)}, u32[]{:S(2)}) %all-to-all-start) | async-done | bytes 262176 | tf_op jit(solution)/shard_map/all_to_all | solution.py:183
  67.6 0.2 convert_reduce_fusion
  67.8 0.2 fusion.17
  68.0 0.3 fusion.24
  68.3 0.3 convolution_convert_fusion
  68.7 0.3 convolution_convert_fusion.1
  69.0 1.6 %collective-permute-start.4 = (bf16[128,1024]{1,0:T(8,128)(2,1)S(1)}, bf16[128,1024]{1,0:T(8,128)(2,1)S(1)}, u32[]{:S(2)}, u32[]{:S(2)}) collective-permute-start(bf16[128,1024]{1,0:T(8,128)(2,1)S(1)} %pad_maximum_fusion.4), channel_id=1, source_target_pairs={{0,24},{8,0},{16,8},{24,16},{1,25},{9,1},{17,9},{25,17},{2,26},{10... | collective-permute-start | bytes 786440 | tf_op jit(solution)/shard_map/ppermute | solution.py:109
  70.7 1.5 %collective-permute-start.3 = (bf16[128,1024]{1,0:T(8,128)(2,1)S(1)}, bf16[128,1024]{1,0:T(8,128)(2,1)S(1)}, u32[]{:S(2)}, u32[]{:S(2)}) collective-permute-start(bf16[128,1024]{1,0:T(8,128)(2,1)S(1)} %pad_maximum_fusion.4), channel_id=1, source_target_pairs={{0,16},{8,24},{16,0},{24,8},{1,17},{9,25},{17,1},{25,9},{2,18},{10... | collective-permute-start | bytes 786440 | tf_op jit(solution)/shard_map/ppermute | solution.py:109
  72.1 1.6 %collective-permute-start.2 = (bf16[128,1024]{1,0:T(8,128)(2,1)S(1)}, bf16[128,1024]{1,0:T(8,128)(2,1)S(1)}, u32[]{:S(2)}, u32[]{:S(2)}) collective-permute-start(bf16[128,1024]{1,0:T(8,128)(2,1)S(1)} %pad_maximum_fusion.4), channel_id=1, source_target_pairs={{0,8},{8,16},{16,24},{24,0},{1,9},{9,17},{17,25},{25,1},{2,10},{10... | collective-permute-start | bytes 786440 | tf_op jit(solution)/shard_map/ppermute | solution.py:109
  73.7 0.7 add_compare_fusion
  74.4 1.8 %copy.21 = bf16[2,128,512]{2,1,0:T(8,128)(2,1)} copy(bf16[2,128,512]{1,2,0:T(8,128)(2,1)} %fusion.12) | data formatting | bytes 524288
  76.1 1.6 %convolution_convert_fusion.2 = bf16[128,512]{1,0:T(8,128)(2,1)S(1)} fusion(bf16[128,1024]{0,1:T(8,128)(2,1)S(1)} %fusion.24, bf16[1024,512]{1,0:T(8,128)(2,1)} %param.15), kind=kOutput, calls=%fused_computation.10 | convolution fusion | flops 134283264 | bytes 1441792 | tf_op jit(solution)/shard_map/dot_general | solution.py:191
  77.7 0.1 copy.18
  77.8 0.0 collective-permute-done.4
  77.8 14.8 %collective-permute-done.3 = bf16[128,1024]{1,0:T(8,128)(2,1)S(1)} collective-permute-done((bf16[128,1024]{1,0:T(8,128)(2,1)S(1)}, bf16[128,1024]{1,0:T(8,128)(2,1)S(1)}, u32[]{:S(2)}, u32[]{:S(2)}) %collective-permute-start.3) | collective-permute-done | bytes 262176 | tf_op jit(solution)/shard_map/ppermute | solution.py:109
  92.6 0.0 collective-permute-done.2
  92.6 0.1 pad_maximum_fusion
  92.7 0.9 fusion.36
  93.6 1.0 copy.19
  94.6 1.5 %fusion.39 = f32[8,128,512]{2,1,0:T(8,128)S(1)} fusion(bf16[128,8,64]{0,2,1:T(8,128)(2,1)S(1)} %bitcast.60, bf16[512,8,64]{0,2,1:T(8,128)(2,1)} %bitcast.57), kind=kOutput, calls=%fused_computation.71 | convolution fusion | flops 67108864 | bytes 2752512 | tf_op jit(solution)/shard_map/fhd,nhd->hfn/dot_general | solution.py:205
  96.1 2.0 %fusion.38 = f32[8,128]{1,0:T(8,128)S(1)} fusion(pred[512]{0:T(512)(128)(4,1)S(1)} %add_compare_fusion, bf16[128,8,64]{0,2,1:T(8,128)(2,1)S(1)} %bitcast.61, bf16[512,8,64]{0,2,1:T(8,128)(2,1)} %bitcast.58), kind=kOutput, calls=%fused_computation.70 | convolution fusion | flops 69730816 | bytes 659968 | tf_op jit(solution)/shard_map/sub | solution.py:211
  98.1 2.0 %copy.20 = bf16[512,512]{0,1:T(8,128)(2,1)} copy(bf16[512,512]{1,0:T(8,128)(2,1)} %get-tuple-element.7) | data formatting | bytes 1048576 | tf_op jit(solution)/shard_map/slice | solution.py:204
  100.1 1.8 %fusion.4 = bf16[128,8,64]{0,2,1:T(8,128)(2,1)S(1)} fusion(bf16[512,8,64]{0,2,1:T(8,128)(2,1)} %bitcast.59, f32[8,128,512]{2,1,0:T(8,128)S(1)} %fusion.39, pred[512]{0:T(512)(128)(4,1)S(1)} %add_compare_fusion, f32[128,8]{0,1:T(8,128)S(1)} %bitcast.63, pred[128]{0:T(512)(128)(4,1)S(1)} %broadcast_compare_fusion.1), kind=kOutput, calls=%fused_computation.7 | convolution fusion | flops 69928448 | bytes 2757248 | tf_op jit(solution)/shard_map/hfn,nhd->hfd/dot_general | solution.py:213
  101.9 0.8 copy.22
  (13 shorter events, 0.1 us)
Async XLA Ops:
  0.6 67.7 %copy-start = (bf16[1024,512]{1,0:T(8,128)(2,1)S(1)}, bf16[1024,512]{1,0:T(8,128)(2,1)}, u32[]{:S(2)}) copy-start(bf16[1024,512]{1,0:T(8,128)(2,1)} %param.17) | copy-start | bytes 3145732
  0.6 8.4 %copy-start.5 = (s32[2]{0:T(128)S(1)}, s32[2]{0:T(128)}, u32[]{:S(2)}) copy-start(s32[2]{0:T(128)} %param.10) | copy-start | bytes 28
  0.7 9.0 %copy-start.4 = (bf16[512]{0:T(512)(128)(2,1)S(1)}, bf16[512]{0:T(512)(128)(2,1)}, u32[]{:S(2)}) copy-start(bf16[512]{0:T(512)(128)(2,1)} %param.12) | copy-start | bytes 3076
  2.8 10.5 %collective-permute-start = (bf16[2,64,512]{1,2,0:T(8,128)(2,1)S(1)}, bf16[2,64,512]{1,2,0:T(8,128)(2,1)S(1)}, u32[]{:S(2)}, u32[]{:S(2)}) collective-permute-start(bf16[2,64,512]{1,2,0:T(8,128)(2,1)S(1)} %get-tuple-element.10), channel_id=1, source_target_pairs={{0,8},{8,16},{16,24},{1,9},{9,17},{17,25},{2,10},{10,18},{18,26},{... | collective-permute-start | bytes 393224 | tf_op jit(solution)/shard_map/ppermute | solution.py:20
  7.8 9.7 %collective-permute-start.1 = (bf16[2,64,512]{1,2,0:T(8,128)(2,1)S(1)}, bf16[2,64,512]{1,2,0:T(8,128)(2,1)S(1)}, u32[]{:S(2)}, u32[]{:S(2)}) collective-permute-start(bf16[2,64,512]{1,2,0:T(8,128)(2,1)S(1)} %get-tuple-element.11), channel_id=1, source_target_pairs={{8,0},{16,8},{24,16},{9,1},{17,9},{25,17},{10,2},{18,10},{26,18},{... | collective-permute-start | bytes 393224 | tf_op jit(solution)/shard_map/ppermute | solution.py:21
  55.5 12.5 %copy-start.2 = (f32[1024]{0:T(1024)S(1)}, f32[1024]{0:T(1024)}, u32[]{:S(2)}) copy-start(f32[1024]{0:T(1024)} %param.14) | copy-start | bytes 12292
  55.5 12.5 %copy-start.3 = (f32[1024]{0:T(1024)S(1)}, f32[1024]{0:T(1024)}, u32[]{:S(2)}) copy-start(f32[1024]{0:T(1024)} %param.13) | copy-start | bytes 12292
  57.0 11.6 %copy-start.1 = (bf16[1024,512]{1,0:T(8,128)(2,1)S(1)}, bf16[1024,512]{1,0:T(8,128)(2,1)}, u32[]{:S(2)}) copy-start(bf16[1024,512]{1,0:T(8,128)(2,1)} %param.16) | copy-start | bytes 3145732
  59.0 8.6 %all-to-all-start = ((bf16[2,128,512]{1,2,0:T(8,128)(2,1)}), bf16[2,128,512]{1,2,0:T(8,128)(2,1)S(1)}, u32[]{:S(2)}, u32[]{:S(2)}) async-start(bf16[2,128,512]{1,2,0:T(8,128)(2,1)} %fusion.12), calls=%async_computation | async-start | bytes 524288 | tf_op jit(solution)/shard_map/all_to_all | solution.py:183
  69.0 8.8 %collective-permute-start.4 = (bf16[128,1024]{1,0:T(8,128)(2,1)S(1)}, bf16[128,1024]{1,0:T(8,128)(2,1)S(1)}, u32[]{:S(2)}, u32[]{:S(2)}) collective-permute-start(bf16[128,1024]{1,0:T(8,128)(2,1)S(1)} %pad_maximum_fusion.4), channel_id=1, source_target_pairs={{0,24},{8,0},{16,8},{24,16},{1,25},{9,1},{17,9},{25,17},{2,26},{10... | collective-permute-start | bytes 786440 | tf_op jit(solution)/shard_map/ppermute | solution.py:109
  70.7 22.0 %collective-permute-start.3 = (bf16[128,1024]{1,0:T(8,128)(2,1)S(1)}, bf16[128,1024]{1,0:T(8,128)(2,1)S(1)}, u32[]{:S(2)}, u32[]{:S(2)}) collective-permute-start(bf16[128,1024]{1,0:T(8,128)(2,1)S(1)} %pad_maximum_fusion.4), channel_id=1, source_target_pairs={{0,16},{8,24},{16,0},{24,8},{1,17},{9,25},{17,1},{25,9},{2,18},{10... | collective-permute-start | bytes 786440 | tf_op jit(solution)/shard_map/ppermute | solution.py:109
  72.1 20.5 %collective-permute-start.2 = (bf16[128,1024]{1,0:T(8,128)(2,1)S(1)}, bf16[128,1024]{1,0:T(8,128)(2,1)S(1)}, u32[]{:S(2)}, u32[]{:S(2)}) collective-permute-start(bf16[128,1024]{1,0:T(8,128)(2,1)S(1)} %pad_maximum_fusion.4), channel_id=1, source_target_pairs={{0,8},{8,16},{16,24},{24,0},{1,9},{9,17},{17,25},{25,1},{2,10},{10... | collective-permute-start | bytes 786440 | tf_op jit(solution)/shard_map/ppermute | solution.py:109

commit v4 on v3

--- a/solution.py
+++ b/solution.py
@@ -100,6 +100,16 @@
     return out.transpose(1, 2, 0, 3).reshape(recs, frame_rows, groups_here * group_out)
 
 
+def swap_halves(hidden, axis):
+    if lax.axis_size(axis) != 2 or hidden.shape[0] != 2:
+        return lax.all_to_all(hidden, axis, split_axis=0, concat_axis=2, tiled=True)
+    place = lax.axis_index(axis)
+    mine = lax.dynamic_index_in_dim(hidden, place, 0, keepdims=True)
+    theirs = lax.dynamic_index_in_dim(hidden, 1 - place, 0, keepdims=True)
+    got = lax.ppermute(theirs, axis, [(0, 1), (1, 0)])
+    return jnp.where(place == 0, jnp.concatenate([mine, got], axis=2), jnp.concatenate([got, mine], axis=2))
+
+
 def gather_ring(x, axis, rows):
     size = lax.axis_size(axis)
     place = lax.axis_index(axis)
@@ -180,7 +190,7 @@
         masked.astype(jnp.float32)
         + jax.nn.gelu(conv_out + conv_bias.astype(jnp.float32), approximate=False)
     ).astype(jnp.bfloat16)
-    record = lax.all_to_all(hidden, "fsdp", split_axis=0, concat_axis=2, tiled=True)
+    record = swap_halves(hidden, "fsdp")
     own_length = lax.dynamic_index_in_dim(lengths, lax.axis_index("fsdp"), 0, keepdims=False)
     flat = record[0].astype(jnp.float32)
     centre = jnp.mean(flat, axis=1, keepdims=True)

time: 103 us -> 99.7 us (0.968)
  starting transfers between devices: 14.3 us -> 12.5 us
  matrix products: 7.47 us -> 8.64 us
  waiting for transfers between devices: 27 us -> 25.9 us
    all_to_all x1 -> x0, waiting for transfers between devices: 4.45 us -> none  [per_device(): lax.all_to_all(hidden, 'fsdp', split_axis=0, concat_axis=2, tiled=True)]
    all_to_all x1 -> x0, starting transfers between devices: 3.44 us -> none  [per_device(): lax.all_to_all(hidden, 'fsdp', split_axis=0, concat_axis=2, tiled=True)]
    ppermute x0 -> x1, waiting for transfers between devices: none -> 2.74 us  [swap_halves(): got = lax.ppermute(theirs, axis, [(0, 1), (1, 0)])]
    ppermute x0 -> x1, starting transfers between devices: none -> 1.58 us  [swap_halves(): got = lax.ppermute(theirs, axis, [(0, 1), (1, 0)])]
  transfers between devices with their start and end apart: 6 -> 6, of which waited for: 4 -> 5; matrix products, arithmetic and copies ran while one was open for 5% -> 5% of each run, Pallas kernels for 0% -> 0%
where the time goes in v4:
time: 99.7 us; the launch traced here: 99.2 us
  Pallas kernels  35 us (35%)
  waiting for transfers between devices  25.9 us (26%)
  starting transfers between devices  12.5 us (13%)
  local copies, waits for them, and re-layouts  11.1 us (11%)
  matrix products  8.64 us (9%)
  other arithmetic  5.23 us (5%)
    pallas_call x1, Pallas kernels, hankel_conv(): pl.pallas_call(conv_body, grid=(groups,), in_specs=[pl.BlockSpec((1, recs...  35 us
    ppermute x3, waiting for transfers between devices, gather_ring(): pieces.append(lax.ppermute(x, axis, pairs))  15.4 us
    ppermute x1, starting transfers between devices, padded_2(): before = lax.ppermute(last, axis, up)  4.94 us
    ppermute x3, starting transfers between devices, gather_ring(): pieces.append(lax.ppermute(x, axis, pairs))  4.65 us
    ppermute x1, waiting for transfers between devices, padded_2(): after = lax.ppermute(first, axis, down)  4.13 us
    ppermute x1, waiting for transfers between devices, padded_2(): before = lax.ppermute(last, axis, up)  3.62 us
    unnamed x15, local copies, waits for them, and re-layouts  3.14 us
    ppermute x1, waiting for transfers between devices, swap_halves(): got = lax.ppermute(theirs, axis, [(0, 1), (1, 0)])  2.74 us
  transfers between devices with their start and end apart: 6, of which 5 were waited for; matrix products, arithmetic and copies ran while one was open for 5% of the time, Pallas kernels for 0%

profile of v4, /device:TPU:0, one launch (start us, length us, event | category | flops | bytes accessed | tf_op | source)
XLA Modules:
  0.0 99.2 jit_solution(11558073572953000762)
XLA Ops:
  0.6 0.0 copy-start
  0.6 0.0 copy-start.5
  0.7 0.0 copy-start.1
  0.7 1.2 %copy.15 = bf16[2,128,512]{1,2,0:T(8,128)(2,1)S(1)} copy(bf16[2,128,512]{2,1,0:T(8,128)(2,1)} %param.9) | data formatting | bytes 524288 | tf_op args[0]
  1.9 0.7 broadcast_compare_fusion
  2.7 0.1 fusion.40
  2.8 4.9 %collective-permute-start = (bf16[2,64,512]{1,2,0:T(8,128)(2,1)S(1)}, bf16[2,64,512]{1,2,0:T(8,128)(2,1)S(1)}, u32[]{:S(2)}, u32[]{:S(2)}) collective-permute-start(bf16[2,64,512]{1,2,0:T(8,128)(2,1)S(1)} %get-tuple-element.12), channel_id=1, source_target_pairs={{0,8},{8,16},{16,24},{1,9},{9,17},{17,25},{2,10},{10,18},{18,26},{... | collective-permute-start | bytes 393224 | tf_op jit(solution)/shard_map/ppermute | solution.py:20
  7.8 1.3 %collective-permute-start.1 = (bf16[2,64,512]{1,2,0:T(8,128)(2,1)S(1)}, bf16[2,64,512]{1,2,0:T(8,128)(2,1)S(1)}, u32[]{:S(2)}, u32[]{:S(2)}) collective-permute-start(bf16[2,64,512]{1,2,0:T(8,128)(2,1)S(1)} %get-tuple-element.13), channel_id=1, source_target_pairs={{8,0},{16,8},{24,16},{9,1},{17,9},{25,17},{10,2},{18,10},{26,18},{... | collective-permute-start | bytes 393224 | tf_op jit(solution)/shard_map/ppermute | solution.py:21
  9.1 0.0 copy-done.5
  9.1 0.6 dynamic_slice.11
  9.7 0.0 copy-done.1
  9.7 3.6 %collective-permute-done = bf16[2,64,512]{1,2,0:T(8,128)(2,1)S(1)} collective-permute-done((bf16[2,64,512]{1,2,0:T(8,128)(2,1)S(1)}, bf16[2,64,512]{1,2,0:T(8,128)(2,1)S(1)}, u32[]{:S(2)}, u32[]{:S(2)}) %collective-permute-start) | collective-permute-done | bytes 131104 | tf_op jit(solution)/shard_map/ppermute | solution.py:20
  13.3 4.1 %collective-permute-done.1 = bf16[2,64,512]{1,2,0:T(8,128)(2,1)S(1)} collective-permute-done((bf16[2,64,512]{1,2,0:T(8,128)(2,1)S(1)}, bf16[2,64,512]{1,2,0:T(8,128)(2,1)S(1)}, u32[]{:S(2)}, u32[]{:S(2)}) %collective-permute-start.1) | collective-permute-done | bytes 131104 | tf_op jit(solution)/shard_map/ppermute | solution.py:21
  17.4 0.3 pad_maximum_fusion.3
  17.7 0.8 slice.30
  18.5 0.8 slice.33
  19.3 0.1 pad_maximum_fusion.1
  19.4 1.1 %copy_bitcast_fusion.x_ref = f32[8,2,64,256]{3,2,1,0:T(8,128)} fusion(bf16[2,256,8,64]{1,3,2,0:T(8,128)(2,1)S(1)} %bitcast.37), kind=kLoop, calls=%fused_computation.12 | loop fusion | flops 262144 | bytes 1572864 | tf_op jit(solution)/shard_map/convert_element_type | solution.py:99
  20.5 35.0 %shard_map.104 = f32[8,2,128,64]{3,2,1,0:T(8,128)} custom-call(f32[8,2,64,256]{3,2,1,0:T(8,128)} %copy_bitcast_fusion.x_ref, bf16[8,64,64,128]{3,2,1,0:T(8,128)(2,1)} %bitcast.35), custom_call_target="tpu_custom_call" | custom-call | flops 2147483648 | bytes 9961472 | tf_op jit(solution)/shard_map/pallas_call | solution.py:77
  55.5 1.6 %copy.17 = f32[2,128,8,64]{1,3,2,0:T(8,128)S(1)} copy(f32[2,128,8,64]{3,1,0,2:T(8,128)} %bitcast.36) | data formatting | bytes 1048576 | tf_op jit(solution)/shard_map/transpose | solution.py:100
  57.0 1.3 %fusion.18 = bf16[2,128,512]{1,2,0:T(8,128)(2,1)S(1)} fusion(f32[2,128,8,64]{1,3,2,0:T(8,128)S(1)} %copy.17, f32[512]{0:T(512)S(1)} %convert_element_type.52, bf16[2,128,512]{1,2,0:T(8,128)(2,1)S(1)} %copy.15, pred[2,128]{1,0:T(4,128)(4,1)S(1)} %broadcast_compare_fusion), kind=kLoop, calls=%fused_computation.29 | loop fusion | flops 9043968 | bytes 1050880 | tf_op jit(solution)/shard_map/convert_element_type | solution.py:192
  58.4 1.6 %collective-permute-start.2 = (bf16[1,128,512]{1,2,0:T(8,128)(2,1)S(1)}, bf16[1,128,512]{1,2,0:T(8,128)(2,1)S(1)}, u32[]{:S(2)}, u32[]{:S(2)}) collective-permute-start(bf16[1,128,512]{1,2,0:T(8,128)(2,1)S(1)} %get-tuple-element.8), channel_id=1, source_target_pairs={{0,4},{4,0},{1,5},{5,1},{2,6},{6,2},{3,7},{7,3},{8,12},{12,8},{9,1... | collective-permute-start | bytes 393224 | tf_op jit(solution)/shard_map/ppermute | solution.py:109
  59.9 0.7 broadcast_compare_fusion.1
  60.6 2.7 %collective-permute-done.2 = bf16[1,128,512]{1,2,0:T(8,128)(2,1)S(1)} collective-permute-done((bf16[1,128,512]{1,2,0:T(8,128)(2,1)S(1)}, bf16[1,128,512]{1,2,0:T(8,128)(2,1)S(1)}, u32[]{:S(2)}, u32[]{:S(2)}) %collective-permute-start.2) | collective-permute-done | bytes 131104 | tf_op jit(solution)/shard_map/ppermute | solution.py:109
  63.4 0.2 convert_reduce_fusion
  63.6 0.2 fusion.11
  63.7 0.0 copy-done
  63.8 0.7 convolution_convert_fusion.1
  64.5 0.3 copy-done.2
  64.8 0.7 convolution_convert_fusion
  65.5 1.6 %collective-permute-start.5 = (bf16[128,1024]{1,0:T(8,128)(2,1)S(1)}, bf16[128,1024]{1,0:T(8,128)(2,1)S(1)}, u32[]{:S(2)}, u32[]{:S(2)}) collective-permute-start(bf16[128,1024]{1,0:T(8,128)(2,1)S(1)} %pad_maximum_fusion.4), channel_id=1, source_target_pairs={{0,24},{8,0},{16,8},{24,16},{1,25},{9,1},{17,9},{25,17},{2,26},{10... | collective-permute-start | bytes 786440 | tf_op jit(solution)/shard_map/ppermute | solution.py:119
  67.2 1.5 %collective-permute-start.4 = (bf16[128,1024]{1,0:T(8,128)(2,1)S(1)}, bf16[128,1024]{1,0:T(8,128)(2,1)S(1)}, u32[]{:S(2)}, u32[]{:S(2)}) collective-permute-start(bf16[128,1024]{1,0:T(8,128)(2,1)S(1)} %pad_maximum_fusion.4), channel_id=1, source_target_pairs={{0,16},{8,24},{16,0},{24,8},{1,17},{9,25},{17,1},{25,9},{2,18},{10... | collective-permute-start | bytes 786440 | tf_op jit(solution)/shard_map/ppermute | solution.py:119
  68.6 1.6 %collective-permute-start.3 = (bf16[128,1024]{1,0:T(8,128)(2,1)S(1)}, bf16[128,1024]{1,0:T(8,128)(2,1)S(1)}, u32[]{:S(2)}, u32[]{:S(2)}) collective-permute-start(bf16[128,1024]{1,0:T(8,128)(2,1)S(1)} %pad_maximum_fusion.4), channel_id=1, source_target_pairs={{0,8},{8,16},{16,24},{24,0},{1,9},{9,17},{17,25},{25,1},{2,10},{10... | collective-permute-start | bytes 786440 | tf_op jit(solution)/shard_map/ppermute | solution.py:119
  70.2 0.7 add_compare_fusion
  70.9 0.9 copy.21
  71.7 1.9 %convolution_convert_fusion.2 = bf16[128,512]{1,0:T(8,128)(2,1)S(1)} fusion(bf16[1024,512]{1,0:T(8,128)(2,1)} %param.15, f32[1024]{0:T(1024)S(1)} %copy-done.3, f32[1024]{0:T(1024)S(1)} %copy-done.4, f32[128]{0:T(128)S(1)} %add_sqrt_fusion, f32[128]{0:T(128)S(1)} %broadcast_multiply_fusion, bf16[128,512]{0,1:T(8,128)(2,1)S(1)} %get-tuple-element.9, ...), kind=kOutput, calls=%fused_computation.10 | convolution fusion | flops 136249344 | bytes 1451009 | tf_op jit(solution)/shard_map/dot_general | solution.py:201
  73.7 0.1 copy.18
  73.8 0.1 collective-permute-done.5
  73.9 15.2 %collective-permute-done.4 = bf16[128,1024]{1,0:T(8,128)(2,1)S(1)} collective-permute-done((bf16[128,1024]{1,0:T(8,128)(2,1)S(1)}, bf16[128,1024]{1,0:T(8,128)(2,1)S(1)}, u32[]{:S(2)}, u32[]{:S(2)}) %collective-permute-start.4) | collective-permute-done | bytes 262176 | tf_op jit(solution)/shard_map/ppermute | solution.py:119
  89.2 0.0 collective-permute-done.3
  89.2 0.1 pad_maximum_fusion
  89.2 0.9 fusion.39
  90.1 1.0 %copy.19 = bf16[512,512]{0,1:T(8,128)(2,1)} copy(bf16[512,512]{1,0:T(8,128)(2,1)S(1)} %get-tuple-element.6) | data formatting | bytes 1048576 | tf_op jit(solution)/shard_map/slice | solution.py:213
  91.1 1.5 %fusion.42 = f32[8,128,512]{2,1,0:T(8,128)S(1)} fusion(bf16[128,8,64]{0,2,1:T(8,128)(2,1)S(1)} %bitcast.46, bf16[512,8,64]{0,2,1:T(8,128)(2,1)} %bitcast.38), kind=kOutput, calls=%fused_computation.73 | convolution fusion | flops 67108864 | bytes 2752512 | tf_op jit(solution)/shard_map/fhd,nhd->hfn/dot_general | solution.py:215
  92.6 2.0 %fusion.41 = f32[8,128]{1,0:T(8,128)S(1)} fusion(pred[512]{0:T(512)(128)(4,1)S(1)} %add_compare_fusion, bf16[128,8,64]{0,2,1:T(8,128)(2,1)S(1)} %bitcast.47, bf16[512,8,64]{0,2,1:T(8,128)(2,1)} %bitcast.39), kind=kOutput, calls=%fused_computation.72 | convolution fusion | flops 69730816 | bytes 659968 | tf_op jit(solution)/shard_map/sub | solution.py:221
  94.6 2.0 %copy.20 = bf16[512,512]{0,1:T(8,128)(2,1)} copy(bf16[512,512]{1,0:T(8,128)(2,1)} %get-tuple-element.7) | data formatting | bytes 1048576 | tf_op jit(solution)/shard_map/slice | solution.py:214
  96.6 1.8 %fusion.4 = bf16[128,8,64]{0,2,1:T(8,128)(2,1)S(1)} fusion(bf16[512,8,64]{0,2,1:T(8,128)(2,1)} %bitcast.40, f32[8,128,512]{2,1,0:T(8,128)S(1)} %fusion.42, pred[512]{0:T(512)(128)(4,1)S(1)} %add_compare_fusion, f32[128,8]{0,1:T(8,128)S(1)} %bitcast.49, pred[128]{0:T(512)(128)(4,1)S(1)} %broadcast_compare_fusion.1), kind=kOutput, calls=%fused_computation.7 | convolution fusion | flops 69928448 | bytes 2757248 | tf_op jit(solution)/shard_map/hfn,nhd->hfd/dot_general | solution.py:223
  98.4 0.8 copy.22
  (13 shorter events, 0.1 us)
Async XLA Ops:
  0.6 63.1 %copy-start = (bf16[1024,512]{1,0:T(8,128)(2,1)S(1)}, bf16[1024,512]{1,0:T(8,128)(2,1)}, u32[]{:S(2)}) copy-start(bf16[1024,512]{1,0:T(8,128)(2,1)} %param.16) | copy-start | bytes 3145732
  0.6 8.4 %copy-start.5 = (s32[2]{0:T(128)S(1)}, s32[2]{0:T(128)}, u32[]{:S(2)}) copy-start(s32[2]{0:T(128)} %param.10) | copy-start | bytes 28
  0.7 9.0 %copy-start.1 = (bf16[512]{0:T(512)(128)(2,1)S(1)}, bf16[512]{0:T(512)(128)(2,1)}, u32[]{:S(2)}) copy-start(bf16[512]{0:T(512)(128)(2,1)} %param.12) | copy-start | bytes 3076
  2.8 10.5 %collective-permute-start = (bf16[2,64,512]{1,2,0:T(8,128)(2,1)S(1)}, bf16[2,64,512]{1,2,0:T(8,128)(2,1)S(1)}, u32[]{:S(2)}, u32[]{:S(2)}) collective-permute-start(bf16[2,64,512]{1,2,0:T(8,128)(2,1)S(1)} %get-tuple-element.12), channel_id=1, source_target_pairs={{0,8},{8,16},{16,24},{1,9},{9,17},{17,25},{2,10},{10,18},{18,26},{... | collective-permute-start | bytes 393224 | tf_op jit(solution)/shard_map/ppermute | solution.py:20
  7.8 9.7 %collective-permute-start.1 = (bf16[2,64,512]{1,2,0:T(8,128)(2,1)S(1)}, bf16[2,64,512]{1,2,0:T(8,128)(2,1)S(1)}, u32[]{:S(2)}, u32[]{:S(2)}) collective-permute-start(bf16[2,64,512]{1,2,0:T(8,128)(2,1)S(1)} %get-tuple-element.13), channel_id=1, source_target_pairs={{8,0},{16,8},{24,16},{9,1},{17,9},{25,17},{10,2},{18,10},{26,18},{... | collective-permute-start | bytes 393224 | tf_op jit(solution)/shard_map/ppermute | solution.py:21
  55.5 8.3 %copy-start.3 = (f32[1024]{0:T(1024)S(1)}, f32[1024]{0:T(1024)}, u32[]{:S(2)}) copy-start(f32[1024]{0:T(1024)} %param.14) | copy-start | bytes 12292
  55.5 8.3 %copy-start.4 = (f32[1024]{0:T(1024)S(1)}, f32[1024]{0:T(1024)}, u32[]{:S(2)}) copy-start(f32[1024]{0:T(1024)} %param.13) | copy-start | bytes 12292
  58.4 5.0 %collective-permute-start.2 = (bf16[1,128,512]{1,2,0:T(8,128)(2,1)S(1)}, bf16[1,128,512]{1,2,0:T(8,128)(2,1)S(1)}, u32[]{:S(2)}, u32[]{:S(2)}) collective-permute-start(bf16[1,128,512]{1,2,0:T(8,128)(2,1)S(1)} %get-tuple-element.8), channel_id=1, source_target_pairs={{0,4},{4,0},{1,5},{5,1},{2,6},{6,2},{3,7},{7,3},{8,12},{12,8},{9,1... | collective-permute-start | bytes 393224 | tf_op jit(solution)/shard_map/ppermute | solution.py:109
  63.6 1.2 %copy-start.2 = (bf16[1024,512]{1,0:T(8,128)(2,1)S(1)}, bf16[1024,512]{1,0:T(8,128)(2,1)}, u32[]{:S(2)}) copy-start(bf16[1024,512]{1,0:T(8,128)(2,1)} %param.17) | copy-start | bytes 3145732
  65.5 8.4 %collective-permute-start.5 = (bf16[128,1024]{1,0:T(8,128)(2,1)S(1)}, bf16[128,1024]{1,0:T(8,128)(2,1)S(1)}, u32[]{:S(2)}, u32[]{:S(2)}) collective-permute-start(bf16[128,1024]{1,0:T(8,128)(2,1)S(1)} %pad_maximum_fusion.4), channel_id=1, source_target_pairs={{0,24},{8,0},{16,8},{24,16},{1,25},{9,1},{17,9},{25,17},{2,26},{10... | collective-permute-start | bytes 786440 | tf_op jit(solution)/shard_map/ppermute | solution.py:119
  67.2 22.0 %collective-permute-start.4 = (bf16[128,1024]{1,0:T(8,128)(2,1)S(1)}, bf16[128,1024]{1,0:T(8,128)(2,1)S(1)}, u32[]{:S(2)}, u32[]{:S(2)}) collective-permute-start(bf16[128,1024]{1,0:T(8,128)(2,1)S(1)} %pad_maximum_fusion.4), channel_id=1, source_target_pairs={{0,16},{8,24},{16,0},{24,8},{1,17},{9,25},{17,1},{25,9},{2,18},{10... | collective-permute-start | bytes 786440 | tf_op jit(solution)/shard_map/ppermute | solution.py:119
  68.6 20.5 %collective-permute-start.3 = (bf16[128,1024]{1,0:T(8,128)(2,1)S(1)}, bf16[128,1024]{1,0:T(8,128)(2,1)S(1)}, u32[]{:S(2)}, u32[]{:S(2)}) collective-permute-start(bf16[128,1024]{1,0:T(8,128)(2,1)S(1)} %pad_maximum_fusion.4), channel_id=1, source_target_pairs={{0,8},{8,16},{16,24},{24,0},{1,9},{9,17},{17,25},{25,1},{2,10},{10... | collective-permute-start | bytes 786440 | tf_op jit(solution)/shard_map/ppermute | solution.py:119

commit v5 on v4

--- a/solution.py
+++ b/solution.py
@@ -100,6 +100,38 @@
     return out.transpose(1, 2, 0, 3).reshape(recs, frame_rows, groups_here * group_out)
 
 
+def conv_block(masked, conv_weight, conv_bias, half_width, frame_rows, after=None):
+    padded = padded_2(masked, (("ctx", 1),), half_width)
+    if after is not None:
+        padded, unused = lax.optimization_barrier((padded, after))
+    conv_out = grouped_conv(padded, conv_weight, frame_rows)
+    return (
+        masked.astype(jnp.float32)
+        + jax.nn.gelu(conv_out + conv_bias.astype(jnp.float32), approximate=False)
+    ).astype(jnp.bfloat16)
+
+
+def conv_by_record(masked, conv_weight, conv_bias, half_width, frame_rows):
+    place = lax.axis_index("fsdp")
+    given = lax.dynamic_index_in_dim(masked, 1 - place, 0, keepdims=True)
+    kept = lax.dynamic_index_in_dim(masked, place, 0, keepdims=True)
+    hidden_given = conv_block(given, conv_weight, conv_bias, half_width, frame_rows)
+    got = lax.ppermute(hidden_given, "fsdp", [(0, 1), (1, 0)])
+    hidden_kept = conv_block(kept, conv_weight, conv_bias, half_width, frame_rows, hidden_given)
+    first = place == 0
+    hidden = jnp.where(
+        first,
+        jnp.concatenate([hidden_kept, hidden_given], axis=0),
+        jnp.concatenate([hidden_given, hidden_kept], axis=0),
+    )
+    record = jnp.where(
+        first,
+        jnp.concatenate([hidden_kept, got], axis=2),
+        jnp.concatenate([got, hidden_kept], axis=2),
+    )
+    return hidden, record
+
+
 def swap_halves(hidden, axis):
     if lax.axis_size(axis) != 2 or hidden.shape[0] != 2:
         return lax.all_to_all(hidden, axis, split_axis=0, concat_axis=2, tiled=True)
@@ -184,13 +216,11 @@
     masked = jnp.where(live[:, :, None], frames_in, jnp.zeros((), frames_in.dtype))
     groups_here, kernel_width, group_in, group_out = conv_weight.shape
     half_width = kernel_width // 2
-    padded = padded_2(masked, (("ctx", 1),), half_width)
-    conv_out = grouped_conv(padded, conv_weight, frame_rows)
-    hidden = (
-        masked.astype(jnp.float32)
-        + jax.nn.gelu(conv_out + conv_bias.astype(jnp.float32), approximate=False)
-    ).astype(jnp.bfloat16)
-    record = swap_halves(hidden, "fsdp")
+    if lax.axis_size("fsdp") == 2 and record_count == 2:
+        hidden, record = conv_by_record(masked, conv_weight, conv_bias, half_width, frame_rows)
+    else:
+        hidden = conv_block(masked, conv_weight, conv_bias, half_width, frame_rows)
+        record = swap_halves(hidden, "fsdp")
     own_length = lax.dynamic_index_in_dim(lengths, lax.axis_index("fsdp"), 0, keepdims=False)
     flat = record[0].astype(jnp.float32)
     centre = jnp.mean(flat, axis=1, keepdims=True)

time: 99.7 us -> 116 us (1.16)
  Pallas kernels: 35 us -> 51.7 us
  waiting for transfers between devices: 25.9 us -> 16.9 us
  starting transfers between devices: 12.5 us -> 19.4 us
    pallas_call x1 -> x2, Pallas kernels: 35 us -> 51.7 us  [hankel_conv(): pl.pallas_call(conv_body, grid=(groups,), in_specs=[pl.BlockSpec((1, recs...]
    ppermute x1 -> x2, starting transfers between devices: 4.94 us -> 9.49 us  [padded_2(): before = lax.ppermute(last, axis, up)]
    ppermute x1 -> x2, waiting for transfers between devices: 4.13 us -> 0.01 us  [padded_2(): after = lax.ppermute(first, axis, down)]
    ppermute x1 -> x2, waiting for transfers between devices: 3.62 us -> 0.01 us  [padded_2(): before = lax.ppermute(last, axis, up)]
    ppermute x1, waiting for transfers between devices: 2.74 us -> 0.01 us  [conv_by_record(): got = lax.ppermute(hidden_given, 'fsdp', [(0, 1), (1, 0)])]
    ppermute x3, waiting for transfers between devices: 15.4 us -> 16.9 us  [gather_ring(): pieces.append(lax.ppermute(x, axis, pairs))]
    ppermute x1 -> x2, starting transfers between devices: 1.29 us -> 2.58 us  [padded_2(): after = lax.ppermute(first, axis, down)]
    transpose x1 -> x2, local copies, waits for them, and re-layouts: 1.56 us -> 2.44 us  [grouped_conv(): out.transpose(1, 2, 0, 3).reshape(recs, frame_rows, groups_here * group_out)]
  transfers between devices with their start and end apart: 6 -> 8, of which waited for: 5 -> 2; matrix products, arithmetic and copies ran while one was open for 5% -> 11% of each run, Pallas kernels for 0% -> 45%
where the time goes in v5:
time: 116 us
  Pallas kernels  51.7 us (45%)
  starting transfers between devices  19.4 us (17%)
  waiting for transfers between devices  16.9 us (15%)
  local copies, waits for them, and re-layouts  12 us (10%)
  matrix products  8.7 us (7%)
  other arithmetic  5.97 us (5%)
    pallas_call x2, Pallas kernels, hankel_conv(): pl.pallas_call(conv_body, grid=(groups,), in_specs=[pl.BlockSpec((1, recs...  51.7 us
    ppermute x3, waiting for transfers between devices, gather_ring(): pieces.append(lax.ppermute(x, axis, pairs))  16.9 us
    ppermute x2, starting transfers between devices, padded_2(): before = lax.ppermute(last, axis, up)  9.49 us
    ppermute x3, starting transfers between devices, gather_ring(): pieces.append(lax.ppermute(x, axis, pairs))  5.73 us
    unnamed x15, local copies, waits for them, and re-layouts  3.14 us
    ppermute x2, starting transfers between devices, padded_2(): after = lax.ppermute(first, axis, down)  2.58 us
    transpose x2, local copies, waits for them, and re-layouts, grouped_conv(): out.transpose(1, 2, 0, 3).reshape(recs, frame_rows, groups_here * group_out)  2.44 us
  transfers between devices with their start and end apart: 8, of which 2 were waited for; matrix products, arithmetic and copies ran while one was open for 11% of the time, Pallas kernels for 45%

profile of v5, /device:TPU:0, one launch (start us, length us, event | category | flops | bytes accessed | tf_op | source)
XLA Modules:
  0.0 115.8 jit_solution(17397417583715322521)
XLA Ops:
  0.6 0.0 copy-start
  0.6 0.0 copy-start.5
  0.7 1.2 %copy.17 = bf16[2,128,512]{1,2,0:T(8,128)(2,1)S(1)} copy(bf16[2,128,512]{2,1,0:T(8,128)(2,1)} %param.9) | data formatting | bytes 524288 | tf_op args[0]
  1.9 0.7 broadcast_compare_fusion
  2.7 0.1 constant_dynamic-slice_fusion
  2.8 4.9 %collective-permute-start = (bf16[1,64,512]{1,2,0:T(8,128)(2,1)S(1)}, bf16[1,64,512]{1,2,0:T(8,128)(2,1)S(1)}, u32[]{:S(2)}, u32[]{:S(2)}) collective-permute-start(bf16[1,64,512]{1,2,0:T(8,128)(2,1)S(1)} %get-tuple-element.12), channel_id=1, source_target_pairs={{0,8},{8,16},{16,24},{1,9},{9,17},{17,25},{2,10},{10,18},{18,26},{... | collective-permute-start | bytes 196616 | tf_op jit(solution)/shard_map/ppermute | solution.py:20
  7.8 1.3 %collective-permute-start.3 = (bf16[1,64,512]{1,2,0:T(8,128)(2,1)S(1)}, bf16[1,64,512]{1,2,0:T(8,128)(2,1)S(1)}, u32[]{:S(2)}, u32[]{:S(2)}) collective-permute-start(bf16[1,64,512]{1,2,0:T(8,128)(2,1)S(1)} %get-tuple-element.13), channel_id=1, source_target_pairs={{8,0},{16,8},{24,16},{9,1},{17,9},{25,17},{10,2},{18,10},{26,18},{... | collective-permute-start | bytes 196616 | tf_op jit(solution)/shard_map/ppermute | solution.py:21
  9.1 4.6 %collective-permute-start.2 = (bf16[1,64,512]{1,2,0:T(8,128)(2,1)S(1)}, bf16[1,64,512]{1,2,0:T(8,128)(2,1)S(1)}, u32[]{:S(2)}, u32[]{:S(2)}) collective-permute-start(bf16[1,64,512]{1,2,0:T(8,128)(2,1)S(1)} %get-tuple-element.14), channel_id=1, source_target_pairs={{0,8},{8,16},{16,24},{1,9},{9,17},{17,25},{2,10},{10,18},{18,26},{... | collective-permute-start | bytes 196616 | tf_op jit(solution)/shard_map/ppermute | solution.py:20
  13.6 1.3 %collective-permute-start.1 = (bf16[1,64,512]{1,2,0:T(8,128)(2,1)S(1)}, bf16[1,64,512]{1,2,0:T(8,128)(2,1)S(1)}, u32[]{:S(2)}, u32[]{:S(2)}) collective-permute-start(bf16[1,64,512]{1,2,0:T(8,128)(2,1)S(1)} %get-tuple-element.15), channel_id=1, source_target_pairs={{8,0},{16,8},{24,16},{9,1},{17,9},{25,17},{10,2},{18,10},{26,18},{... | collective-permute-start | bytes 196616 | tf_op jit(solution)/shard_map/ppermute | solution.py:21
  15.0 0.6 dynamic_slice.13
  15.6 0.7 broadcast_compare_fusion.1
  16.3 0.7 add_compare_fusion
  17.0 0.0 collective-permute-done.2
  17.0 0.2 pad_maximum_fusion.6
  17.2 0.4 slice.50
  17.6 0.4 slice.53
  18.0 0.8 convert_bitcast_fusion.1.x_ref
  18.9 25.9 %shard_map.104 = f32[8,1,128,64]{3,2,1,0:T(8,128)} custom-call(f32[8,1,64,256]{3,2,1,0:T(8,128)} %convert_bitcast_fusion.1.x_ref, bf16[8,64,64,128]{3,2,1,0:T(8,128)(2,1)} %bitcast.43), custom_call_target="tpu_custom_call" | custom-call | flops 1073741824 | bytes 9175040 | tf_op jit(solution)/shard_map/pallas_call | solution.py:77
  44.7 1.2 %copy.18 = f32[1,128,8,64]{1,3,2,0:T(8,128)S(1)} copy(f32[1,128,8,64]{3,1,0,2:T(8,128)} %bitcast.45) | data formatting | bytes 524288 | tf_op jit(solution)/shard_map/transpose | solution.py:100
  45.9 0.7 fusion.18
  46.6 1.6 %collective-permute-start.4 = (bf16[1,128,512]{1,2,0:T(8,128)(2,1)S(1)}, bf16[1,128,512]{1,2,0:T(8,128)(2,1)S(1)}, u32[]{:S(2)}, u32[]{:S(2)}) collective-permute-start(bf16[1,128,512]{1,2,0:T(8,128)(2,1)S(1)} %fusion.18), channel_id=1, source_target_pairs={{0,4},{4,0},{1,5},{5,1},{2,6},{6,2},{3,7},{7,3},{8,12},{12,8},{9,1... | collective-permute-start | bytes 393224 | tf_op jit(solution)/shard_map/ppermute | solution.py:119
  48.2 0.2 pad_maximum_fusion.1
  48.4 0.4 slice.55
  48.8 0.4 slice.57
  49.3 0.8 convert_bitcast_fusion.x_ref
  50.1 25.9 %shard_map.105 = f32[8,1,128,64]{3,2,1,0:T(8,128)} custom-call(f32[8,1,64,256]{3,2,1,0:T(8,128)} %convert_bitcast_fusion.x_ref, bf16[8,64,64,128]{3,2,1,0:T(8,128)(2,1)} %bitcast.44), custom_call_target="tpu_custom_call" | custom-call | flops 1073741824 | bytes 9175040 | tf_op jit(solution)/shard_map/pallas_call | solution.py:77
  76.0 1.2 %copy.19 = f32[1,128,8,64]{1,3,2,0:T(8,128)S(1)} copy(f32[1,128,8,64]{3,1,0,2:T(8,128)} %bitcast.46) | data formatting | bytes 524288 | tf_op jit(solution)/shard_map/transpose | solution.py:100
  77.2 0.7 fusion.22
  77.9 0.2 convert_reduce_fusion
  78.1 0.2 fusion.11
  78.3 0.7 convolution_convert_fusion.1
  79.0 0.3 copy-done.2
  79.3 0.7 convolution_convert_fusion
  80.1 4.7 %collective-permute-start.7 = (bf16[128,1024]{1,0:T(8,128)(2,1)S(1)}, bf16[128,1024]{1,0:T(8,128)(2,1)S(1)}, u32[]{:S(2)}, u32[]{:S(2)}) collective-permute-start(bf16[128,1024]{1,0:T(8,128)(2,1)S(1)} %pad_maximum_fusion.4), channel_id=1, source_target_pairs={{0,24},{8,0},{16,8},{24,16},{1,25},{9,1},{17,9},{25,17},{2,26},{10... | collective-permute-start | bytes 786440 | tf_op jit(solution)/shard_map/ppermute | solution.py:151
  84.8 1.0 collective-permute-start.5
  85.8 0.9 copy.23
  86.7 2.0 %convolution_convert_fusion.2 = bf16[128,512]{1,0:T(8,128)(2,1)S(1)} fusion(bf16[1024,512]{1,0:T(8,128)(2,1)} %param.15, f32[1024]{0:T(1024)S(1)} %copy-done.3, f32[1024]{0:T(1024)S(1)} %copy-done.4, f32[128]{0:T(128)S(1)} %add_sqrt_fusion, f32[128]{0:T(128)S(1)} %broadcast_multiply_fusion, bf16[128,512]{0,1:T(8,128)(2,1)S(1)} %bitcast.51, ...), kind=kOutput, calls=%fused_computation.10 | convolution fusion | flops 136249344 | bytes 1451009 | tf_op jit(solution)/shard_map/dot_general | solution.py:231
  88.6 0.1 copy.20
  88.8 2.8 %collective-permute-done.7 = bf16[128,1024]{1,0:T(8,128)(2,1)S(1)} collective-permute-done((bf16[128,1024]{1,0:T(8,128)(2,1)S(1)}, bf16[128,1024]{1,0:T(8,128)(2,1)S(1)}, u32[]{:S(2)}, u32[]{:S(2)}) %collective-permute-start.7) | collective-permute-done | bytes 262176 | tf_op jit(solution)/shard_map/ppermute | solution.py:151
  91.6 14.1 %collective-permute-done.6 = bf16[128,1024]{1,0:T(8,128)(2,1)S(1)} collective-permute-done((bf16[128,1024]{1,0:T(8,128)(2,1)S(1)}, bf16[128,1024]{1,0:T(8,128)(2,1)S(1)}, u32[]{:S(2)}, u32[]{:S(2)}) %collective-permute-start.6) | collective-permute-done | bytes 262176 | tf_op jit(solution)/shard_map/ppermute | solution.py:151
  105.7 0.1 pad_maximum_fusion
  105.8 0.9 fusion.50
  106.6 1.0 copy.21
  107.6 1.5 %fusion.53 = f32[8,128,512]{2,1,0:T(8,128)S(1)} fusion(bf16[128,8,64]{0,2,1:T(8,128)(2,1)S(1)} %bitcast.62, bf16[512,8,64]{0,2,1:T(8,128)(2,1)} %bitcast.52), kind=kOutput, calls=%fused_computation.102 | convolution fusion | flops 67108864 | bytes 2752512 | tf_op jit(solution)/shard_map/fhd,nhd->hfn/dot_general | solution.py:245
  109.2 2.0 %fusion.52 = f32[8,128]{1,0:T(8,128)S(1)} fusion(pred[512]{0:T(512)(128)(4,1)S(1)} %add_compare_fusion, bf16[128,8,64]{0,2,1:T(8,128)(2,1)S(1)} %bitcast.63, bf16[512,8,64]{0,2,1:T(8,128)(2,1)} %bitcast.53), kind=kOutput, calls=%fused_computation.101 | convolution fusion | flops 69730816 | bytes 659968 | tf_op jit(solution)/shard_map/sub | solution.py:251
  111.1 2.1 %copy.22 = bf16[512,512]{0,1:T(8,128)(2,1)} copy(bf16[512,512]{1,0:T(8,128)(2,1)} %get-tuple-element.9) | data formatting | bytes 1048576 | tf_op jit(solution)/shard_map/slice | solution.py:244
  113.2 1.8 %fusion.4 = bf16[128,8,64]{0,2,1:T(8,128)(2,1)S(1)} fusion(bf16[512,8,64]{0,2,1:T(8,128)(2,1)} %bitcast.56, f32[8,128,512]{2,1,0:T(8,128)S(1)} %fusion.53, pred[512]{0:T(512)(128)(4,1)S(1)} %add_compare_fusion, f32[128,8]{0,1:T(8,128)S(1)} %bitcast.65, pred[128]{0:T(512)(128)(4,1)S(1)} %broadcast_compare_fusion.1), kind=kOutput, calls=%fused_computation.7 | convolution fusion | flops 69928448 | bytes 2757248 | tf_op jit(solution)/shard_map/hfn,nhd->hfd/dot_general | solution.py:253
  115.0 0.8 copy.24
  (27 shorter events, 0.2 us)
Async XLA Ops:
  0.6 77.6 %copy-start = (bf16[1024,512]{1,0:T(8,128)(2,1)S(1)}, bf16[1024,512]{1,0:T(8,128)(2,1)}, u32[]{:S(2)}) copy-start(bf16[1024,512]{1,0:T(8,128)(2,1)} %param.16) | copy-start | bytes 3145732
  0.6 14.3 %copy-start.5 = (s32[2]{0:T(128)S(1)}, s32[2]{0:T(128)}, u32[]{:S(2)}) copy-start(s32[2]{0:T(128)} %param.10) | copy-start | bytes 28
  0.7 15.6 %copy-start.1 = (bf16[512]{0:T(512)(128)(2,1)S(1)}, bf16[512]{0:T(512)(128)(2,1)}, u32[]{:S(2)}) copy-start(bf16[512]{0:T(512)(128)(2,1)} %param.12) | copy-start | bytes 3076
  2.8 45.4 %collective-permute-start = (bf16[1,64,512]{1,2,0:T(8,128)(2,1)S(1)}, bf16[1,64,512]{1,2,0:T(8,128)(2,1)S(1)}, u32[]{:S(2)}, u32[]{:S(2)}) collective-permute-start(bf16[1,64,512]{1,2,0:T(8,128)(2,1)S(1)} %get-tuple-element.12), channel_id=1, source_target_pairs={{0,8},{8,16},{16,24},{1,9},{9,17},{17,25},{2,10},{10,18},{18,26},{... | collective-permute-start | bytes 196616 | tf_op jit(solution)/shard_map/ppermute | solution.py:20
  7.8 9.2 %collective-permute-start.3 = (bf16[1,64,512]{1,2,0:T(8,128)(2,1)S(1)}, bf16[1,64,512]{1,2,0:T(8,128)(2,1)S(1)}, u32[]{:S(2)}, u32[]{:S(2)}) collective-permute-start(bf16[1,64,512]{1,2,0:T(8,128)(2,1)S(1)} %get-tuple-element.13), channel_id=1, source_target_pairs={{8,0},{16,8},{24,16},{9,1},{17,9},{25,17},{10,2},{18,10},{26,18},{... | collective-permute-start | bytes 196616 | tf_op jit(solution)/shard_map/ppermute | solution.py:21
  9.1 7.9 %collective-permute-start.2 = (bf16[1,64,512]{1,2,0:T(8,128)(2,1)S(1)}, bf16[1,64,512]{1,2,0:T(8,128)(2,1)S(1)}, u32[]{:S(2)}, u32[]{:S(2)}) collective-permute-start(bf16[1,64,512]{1,2,0:T(8,128)(2,1)S(1)} %get-tuple-element.14), channel_id=1, source_target_pairs={{0,8},{8,16},{16,24},{1,9},{9,17},{17,25},{2,10},{10,18},{18,26},{... | collective-permute-start | bytes 196616 | tf_op jit(solution)/shard_map/ppermute | solution.py:20
  13.6 34.6 %collective-permute-start.1 = (bf16[1,64,512]{1,2,0:T(8,128)(2,1)S(1)}, bf16[1,64,512]{1,2,0:T(8,128)(2,1)S(1)}, u32[]{:S(2)}, u32[]{:S(2)}) collective-permute-start(bf16[1,64,512]{1,2,0:T(8,128)(2,1)S(1)} %get-tuple-element.15), channel_id=1, source_target_pairs={{8,0},{16,8},{24,16},{9,1},{17,9},{25,17},{10,2},{18,10},{26,18},{... | collective-permute-start | bytes 196616 | tf_op jit(solution)/shard_map/ppermute | solution.py:21
  46.6 31.3 %collective-permute-start.4 = (bf16[1,128,512]{1,2,0:T(8,128)(2,1)S(1)}, bf16[1,128,512]{1,2,0:T(8,128)(2,1)S(1)}, u32[]{:S(2)}, u32[]{:S(2)}) collective-permute-start(bf16[1,128,512]{1,2,0:T(8,128)(2,1)S(1)} %fusion.18), channel_id=1, source_target_pairs={{0,4},{4,0},{1,5},{5,1},{2,6},{6,2},{3,7},{7,3},{8,12},{12,8},{9,1... | collective-permute-start | bytes 393224 | tf_op jit(solution)/shard_map/ppermute | solution.py:119
  50.1 28.2 %copy-start.3 = (f32[1024]{0:T(1024)S(1)}, f32[1024]{0:T(1024)}, u32[]{:S(2)}) copy-start(f32[1024]{0:T(1024)} %param.14) | copy-start | bytes 12292
  50.1 28.2 %copy-start.4 = (f32[1024]{0:T(1024)S(1)}, f32[1024]{0:T(1024)}, u32[]{:S(2)}) copy-start(f32[1024]{0:T(1024)} %param.13) | copy-start | bytes 12292
  78.1 1.2 %copy-start.2 = (bf16[1024,512]{1,0:T(8,128)(2,1)S(1)}, bf16[1024,512]{1,0:T(8,128)(2,1)}, u32[]{:S(2)}) copy-start(bf16[1024,512]{1,0:T(8,128)(2,1)} %param.17) | copy-start | bytes 3145732
  80.1 11.5 %collective-permute-start.7 = (bf16[128,1024]{1,0:T(8,128)(2,1)S(1)}, bf16[128,1024]{1,0:T(8,128)(2,1)S(1)}, u32[]{:S(2)}, u32[]{:S(2)}) collective-permute-start(bf16[128,1024]{1,0:T(8,128)(2,1)S(1)} %pad_maximum_fusion.4), channel_id=1, source_target_pairs={{0,24},{8,0},{16,8},{24,16},{1,25},{9,1},{17,9},{25,17},{2,26},{10... | collective-permute-start | bytes 786440 | tf_op jit(solution)/shard_map/ppermute | solution.py:151
  84.8 20.9 %collective-permute-start.6 = (bf16[128,1024]{1,0:T(8,128)(2,1)S(1)}, bf16[128,1024]{1,0:T(8,128)(2,1)S(1)}, u32[]{:S(2)}, u32[]{:S(2)}) collective-permute-start(bf16[128,1024]{1,0:T(8,128)(2,1)S(1)} %pad_maximum_fusion.4), channel_id=1, source_target_pairs={{0,16},{8,24},{16,0},{24,8},{1,17},{9,25},{17,1},{25,9},{2,18},{10... | collective-permute-start | bytes 786440 | tf_op jit(solution)/shard_map/ppermute | solution.py:151
  84.8 20.9 %collective-permute-start.5 = (bf16[128,1024]{1,0:T(8,128)(2,1)S(1)}, bf16[128,1024]{1,0:T(8,128)(2,1)S(1)}, u32[]{:S(2)}, u32[]{:S(2)}) collective-permute-start(bf16[128,1024]{1,0:T(8,128)(2,1)S(1)} %pad_maximum_fusion.4), channel_id=1, source_target_pairs={{0,8},{8,16},{16,24},{24,0},{1,9},{9,17},{17,25},{25,1},{2,10},{10... | collective-permute-start | bytes 786440 | tf_op jit(solution)/shard_map/ppermute | solution.py:151

commit v6 on v4

--- a/solution.py
+++ b/solution.py
@@ -38,7 +38,7 @@
             for c in range(8):
                 row = jnp.broadcast_to(block[c : c + 1, :], (taps, lanes))
                 rolled = pltpu.roll(row, 0, 1, stride=1, stride_axis=0)
-                per_chan.append(rolled[:, :rows].astype(jnp.bfloat16))
+                per_chan.append(rolled[:, :rows])
             hankels.append(per_chan)
         for pair in range(4):
             rhs = jnp.concatenate(
@@ -54,7 +54,7 @@
             acc = acc + jnp.dot(lhs, rhs, preferred_element_type=jnp.float32)
         return acc
 
-    acc = lax.fori_loop(0, chans // 8, octet_step, jnp.zeros((outs, recs * rows), jnp.float32))
+    acc = lax.fori_loop(0, chans // 8, octet_step, jnp.zeros((outs, recs * rows), jnp.float32), unroll=2)
     across = lax.broadcasted_iota(jnp.int32, (rows, rows), 0) + lax.broadcasted_iota(
         jnp.int32, (rows, rows), 1
     )
@@ -83,7 +83,7 @@
         out_shape=jax.ShapeDtypeStruct((groups, recs, rows, outs), jnp.float32),
         cost_estimate=pl.CostEstimate(
             flops=2 * groups * recs * rows * taps * chans * outs,
-            bytes_accessed=xt.size * 4 + wv.size * 2 + groups * recs * rows * outs * 4,
+            bytes_accessed=xt.size * 2 + wv.size * 2 + groups * recs * rows * outs * 4,
             transcendentals=0,
         ),
     )(xt, wv)
@@ -96,7 +96,7 @@
     grouped = jnp.pad(padded, ((0, 0), (0, lanes - span), (0, 0)))
     grouped = jnp.roll(jnp.flip(grouped, axis=1), frame_rows - lanes, axis=1)
     grouped = grouped.reshape(recs, lanes, groups_here, group_in).transpose(2, 0, 3, 1)
-    out = hankel_conv(grouped.astype(jnp.float32), jnp.transpose(conv_weight, (0, 2, 3, 1)), frame_rows)
+    out = hankel_conv(grouped, jnp.transpose(conv_weight, (0, 2, 3, 1)), frame_rows)
     return out.transpose(1, 2, 0, 3).reshape(recs, frame_rows, groups_here * group_out)
 
 

time: 99.7 us -> 92.4 us (0.927)
  Pallas kernels: 35 us -> 27.9 us
  other arithmetic: 5.23 us -> 4.15 us
    pallas_call x1, Pallas kernels: 35 us -> 27.9 us  [hankel_conv(): pl.pallas_call(conv_body, grid=(groups,), in_specs=[pl.BlockSpec((1, recs...]
    convert_element_type x1 -> x0, other arithmetic: 1.08 us -> none  [grouped_conv(): grouped.astype(jnp.float32)]
where the time goes in v6:
time: 92.4 us; the launch traced here: 91.8 us
  Pallas kernels  27.9 us (30%)
  waiting for transfers between devices  25.9 us (28%)
  starting transfers between devices  12.5 us (14%)
  local copies, waits for them, and re-layouts  11.9 us (13%)
  matrix products  8.64 us (9%)
  other arithmetic  4.15 us (4%)
    pallas_call x1, Pallas kernels, hankel_conv(): pl.pallas_call(conv_body, grid=(groups,), in_specs=[pl.BlockSpec((1, recs...  27.9 us
    ppermute x3, waiting for transfers between devices, gather_ring(): pieces.append(lax.ppermute(x, axis, pairs))  15.4 us
    ppermute x1, starting transfers between devices, padded_2(): before = lax.ppermute(last, axis, up)  4.94 us
    ppermute x3, starting transfers between devices, gather_ring(): pieces.append(lax.ppermute(x, axis, pairs))  4.66 us
    ppermute x1, waiting for transfers between devices, padded_2(): after = lax.ppermute(first, axis, down)  4.13 us
    ppermute x1, waiting for transfers between devices, padded_2(): before = lax.ppermute(last, axis, up)  3.62 us
    unnamed x15, local copies, waits for them, and re-layouts  3.14 us
    ppermute x1, waiting for transfers between devices, swap_halves(): got = lax.ppermute(theirs, axis, [(0, 1), (1, 0)])  2.74 us
  transfers between devices with their start and end apart: 6, of which 5 were waited for; matrix products, arithmetic and copies ran while one was open for 5% of the time, Pallas kernels for 0%

profile of v6, /device:TPU:0, one launch (start us, length us, event | category | flops | bytes accessed | tf_op | source)
XLA Modules:
  0.0 91.8 jit_solution(6062635240930098194)
XLA Ops:
  0.6 0.0 copy-start
  0.6 0.0 copy-start.5
  0.7 0.0 copy-start.1
  0.7 1.2 %copy.15 = bf16[2,128,512]{1,2,0:T(8,128)(2,1)S(1)} copy(bf16[2,128,512]{2,1,0:T(8,128)(2,1)} %param.9) | data formatting | bytes 524288 | tf_op args[0]
  1.9 0.7 broadcast_compare_fusion
  2.7 0.1 fusion.40
  2.8 4.9 %collective-permute-start = (bf16[2,64,512]{1,2,0:T(8,128)(2,1)S(1)}, bf16[2,64,512]{1,2,0:T(8,128)(2,1)S(1)}, u32[]{:S(2)}, u32[]{:S(2)}) collective-permute-start(bf16[2,64,512]{1,2,0:T(8,128)(2,1)S(1)} %get-tuple-element.12), channel_id=1, source_target_pairs={{0,8},{8,16},{16,24},{1,9},{9,17},{17,25},{2,10},{10,18},{18,26},{... | collective-permute-start | bytes 393224 | tf_op jit(solution)/shard_map/ppermute | solution.py:20
  7.8 1.3 %collective-permute-start.1 = (bf16[2,64,512]{1,2,0:T(8,128)(2,1)S(1)}, bf16[2,64,512]{1,2,0:T(8,128)(2,1)S(1)}, u32[]{:S(2)}, u32[]{:S(2)}) collective-permute-start(bf16[2,64,512]{1,2,0:T(8,128)(2,1)S(1)} %get-tuple-element.13), channel_id=1, source_target_pairs={{8,0},{16,8},{24,16},{9,1},{17,9},{25,17},{10,2},{18,10},{26,18},{... | collective-permute-start | bytes 393224 | tf_op jit(solution)/shard_map/ppermute | solution.py:21
  9.1 0.0 copy-done.5
  9.1 0.6 dynamic_slice.11
  9.7 0.0 copy-done.1
  9.7 3.6 %collective-permute-done = bf16[2,64,512]{1,2,0:T(8,128)(2,1)S(1)} collective-permute-done((bf16[2,64,512]{1,2,0:T(8,128)(2,1)S(1)}, bf16[2,64,512]{1,2,0:T(8,128)(2,1)S(1)}, u32[]{:S(2)}, u32[]{:S(2)}) %collective-permute-start) | collective-permute-done | bytes 131104 | tf_op jit(solution)/shard_map/ppermute | solution.py:20
  13.3 4.1 %collective-permute-done.1 = bf16[2,64,512]{1,2,0:T(8,128)(2,1)S(1)} collective-permute-done((bf16[2,64,512]{1,2,0:T(8,128)(2,1)S(1)}, bf16[2,64,512]{1,2,0:T(8,128)(2,1)S(1)}, u32[]{:S(2)}, u32[]{:S(2)}) %collective-permute-start.1) | collective-permute-done | bytes 131104 | tf_op jit(solution)/shard_map/ppermute | solution.py:21
  17.4 0.3 pad_maximum_fusion.3
  17.7 0.8 slice.30
  18.5 0.8 slice.33
  19.3 0.1 pad_maximum_fusion.1
  19.4 0.8 copy.24
  20.2 27.9 %shard_map.104 = f32[8,2,128,64]{3,2,1,0:T(8,128)} custom-call(bf16[8,2,64,256]{3,2,1,0:T(8,128)(2,1)} %bitcast.37, bf16[8,64,64,128]{3,2,1,0:T(8,128)(2,1)} %bitcast.35), custom_call_target="tpu_custom_call" | custom-call | flops 2147483648 | bytes 9437184 | tf_op jit(solution)/shard_map/pallas_call | solution.py:77
  48.1 1.6 %copy.17 = f32[2,128,8,64]{1,3,2,0:T(8,128)S(1)} copy(f32[2,128,8,64]{3,1,0,2:T(8,128)} %bitcast.36) | data formatting | bytes 1048576 | tf_op jit(solution)/shard_map/transpose | solution.py:100
  49.7 1.3 %fusion.18 = bf16[2,128,512]{1,2,0:T(8,128)(2,1)S(1)} fusion(f32[2,128,8,64]{1,3,2,0:T(8,128)S(1)} %copy.17, f32[512]{0:T(512)S(1)} %convert_element_type.42, bf16[2,128,512]{1,2,0:T(8,128)(2,1)S(1)} %copy.15, pred[2,128]{1,0:T(4,128)(4,1)S(1)} %broadcast_compare_fusion), kind=kLoop, calls=%fused_computation.28 | loop fusion | flops 9043968 | bytes 1050880 | tf_op jit(solution)/shard_map/convert_element_type | solution.py:192
  51.0 1.6 %collective-permute-start.2 = (bf16[1,128,512]{1,2,0:T(8,128)(2,1)S(1)}, bf16[1,128,512]{1,2,0:T(8,128)(2,1)S(1)}, u32[]{:S(2)}, u32[]{:S(2)}) collective-permute-start(bf16[1,128,512]{1,2,0:T(8,128)(2,1)S(1)} %get-tuple-element.8), channel_id=1, source_target_pairs={{0,4},{4,0},{1,5},{5,1},{2,6},{6,2},{3,7},{7,3},{8,12},{12,8},{9,1... | collective-permute-start | bytes 393224 | tf_op jit(solution)/shard_map/ppermute | solution.py:109
  52.6 0.7 broadcast_compare_fusion.1
  53.3 2.7 %collective-permute-done.2 = bf16[1,128,512]{1,2,0:T(8,128)(2,1)S(1)} collective-permute-done((bf16[1,128,512]{1,2,0:T(8,128)(2,1)S(1)}, bf16[1,128,512]{1,2,0:T(8,128)(2,1)S(1)}, u32[]{:S(2)}, u32[]{:S(2)}) %collective-permute-start.2) | collective-permute-done | bytes 131104 | tf_op jit(solution)/shard_map/ppermute | solution.py:109
  56.0 0.2 convert_reduce_fusion
  56.2 0.2 fusion.11
  56.4 0.0 copy-done
  56.4 0.7 convolution_convert_fusion.1
  57.1 0.3 copy-done.2
  57.4 0.7 convolution_convert_fusion
  58.2 1.6 %collective-permute-start.5 = (bf16[128,1024]{1,0:T(8,128)(2,1)S(1)}, bf16[128,1024]{1,0:T(8,128)(2,1)S(1)}, u32[]{:S(2)}, u32[]{:S(2)}) collective-permute-start(bf16[128,1024]{1,0:T(8,128)(2,1)S(1)} %pad_maximum_fusion.4), channel_id=1, source_target_pairs={{0,24},{8,0},{16,8},{24,16},{1,25},{9,1},{17,9},{25,17},{2,26},{10... | collective-permute-start | bytes 786440 | tf_op jit(solution)/shard_map/ppermute | solution.py:119
  59.8 1.5 %collective-permute-start.4 = (bf16[128,1024]{1,0:T(8,128)(2,1)S(1)}, bf16[128,1024]{1,0:T(8,128)(2,1)S(1)}, u32[]{:S(2)}, u32[]{:S(2)}) collective-permute-start(bf16[128,1024]{1,0:T(8,128)(2,1)S(1)} %pad_maximum_fusion.4), channel_id=1, source_target_pairs={{0,16},{8,24},{16,0},{24,8},{1,17},{9,25},{17,1},{25,9},{2,18},{10... | collective-permute-start | bytes 786440 | tf_op jit(solution)/shard_map/ppermute | solution.py:119
  61.3 1.6 %collective-permute-start.3 = (bf16[128,1024]{1,0:T(8,128)(2,1)S(1)}, bf16[128,1024]{1,0:T(8,128)(2,1)S(1)}, u32[]{:S(2)}, u32[]{:S(2)}) collective-permute-start(bf16[128,1024]{1,0:T(8,128)(2,1)S(1)} %pad_maximum_fusion.4), channel_id=1, source_target_pairs={{0,8},{8,16},{16,24},{24,0},{1,9},{9,17},{17,25},{25,1},{2,10},{10... | collective-permute-start | bytes 786440 | tf_op jit(solution)/shard_map/ppermute | solution.py:119
  62.9 0.7 add_compare_fusion
  63.5 0.9 copy.21
  64.4 1.9 %convolution_convert_fusion.2 = bf16[128,512]{1,0:T(8,128)(2,1)S(1)} fusion(bf16[1024,512]{1,0:T(8,128)(2,1)} %param.15, f32[1024]{0:T(1024)S(1)} %copy-done.3, f32[1024]{0:T(1024)S(1)} %copy-done.4, f32[128]{0:T(128)S(1)} %add_sqrt_fusion, f32[128]{0:T(128)S(1)} %broadcast_multiply_fusion, bf16[128,512]{0,1:T(8,128)(2,1)S(1)} %get-tuple-element.9, ...), kind=kOutput, calls=%fused_computation.10 | convolution fusion | flops 136249344 | bytes 1451009 | tf_op jit(solution)/shard_map/dot_general | solution.py:201
  66.3 0.1 copy.18
  66.4 0.1 collective-permute-done.5
  66.6 15.2 %collective-permute-done.4 = bf16[128,1024]{1,0:T(8,128)(2,1)S(1)} collective-permute-done((bf16[128,1024]{1,0:T(8,128)(2,1)S(1)}, bf16[128,1024]{1,0:T(8,128)(2,1)S(1)}, u32[]{:S(2)}, u32[]{:S(2)}) %collective-permute-start.4) | collective-permute-done | bytes 262176 | tf_op jit(solution)/shard_map/ppermute | solution.py:119
  81.8 0.0 collective-permute-done.3
  81.8 0.1 pad_maximum_fusion
  81.9 0.9 fusion.39
  82.8 1.0 %copy.19 = bf16[512,512]{0,1:T(8,128)(2,1)} copy(bf16[512,512]{1,0:T(8,128)(2,1)S(1)} %get-tuple-element.6) | data formatting | bytes 1048576 | tf_op jit(solution)/shard_map/slice | solution.py:213
  83.8 1.5 %fusion.42 = f32[8,128,512]{2,1,0:T(8,128)S(1)} fusion(bf16[128,8,64]{0,2,1:T(8,128)(2,1)S(1)} %bitcast.47, bf16[512,8,64]{0,2,1:T(8,128)(2,1)} %bitcast.39), kind=kOutput, calls=%fused_computation.73 | convolution fusion | flops 67108864 | bytes 2752512 | tf_op jit(solution)/shard_map/fhd,nhd->hfn/dot_general | solution.py:215
  85.3 2.0 %fusion.41 = f32[8,128]{1,0:T(8,128)S(1)} fusion(pred[512]{0:T(512)(128)(4,1)S(1)} %add_compare_fusion, bf16[128,8,64]{0,2,1:T(8,128)(2,1)S(1)} %bitcast.48, bf16[512,8,64]{0,2,1:T(8,128)(2,1)} %bitcast.40), kind=kOutput, calls=%fused_computation.72 | convolution fusion | flops 69730816 | bytes 659968 | tf_op jit(solution)/shard_map/sub | solution.py:221
  87.2 2.0 %copy.20 = bf16[512,512]{0,1:T(8,128)(2,1)} copy(bf16[512,512]{1,0:T(8,128)(2,1)} %get-tuple-element.7) | data formatting | bytes 1048576 | tf_op jit(solution)/shard_map/slice | solution.py:214
  89.3 1.8 %fusion.4 = bf16[128,8,64]{0,2,1:T(8,128)(2,1)S(1)} fusion(bf16[512,8,64]{0,2,1:T(8,128)(2,1)} %bitcast.41, f32[8,128,512]{2,1,0:T(8,128)S(1)} %fusion.42, pred[512]{0:T(512)(128)(4,1)S(1)} %add_compare_fusion, f32[128,8]{0,1:T(8,128)S(1)} %bitcast.50, pred[128]{0:T(512)(128)(4,1)S(1)} %broadcast_compare_fusion.1), kind=kOutput, calls=%fused_computation.7 | convolution fusion | flops 69928448 | bytes 2757248 | tf_op jit(solution)/shard_map/hfn,nhd->hfd/dot_general | solution.py:223
  91.1 0.8 copy.22
  (13 shorter events, 0.1 us)
Async XLA Ops:
  0.6 55.8 %copy-start = (bf16[1024,512]{1,0:T(8,128)(2,1)S(1)}, bf16[1024,512]{1,0:T(8,128)(2,1)}, u32[]{:S(2)}) copy-start(bf16[1024,512]{1,0:T(8,128)(2,1)} %param.16) | copy-start | bytes 3145732
  0.6 8.4 %copy-start.5 = (s32[2]{0:T(128)S(1)}, s32[2]{0:T(128)}, u32[]{:S(2)}) copy-start(s32[2]{0:T(128)} %param.10) | copy-start | bytes 28
  0.7 9.0 %copy-start.1 = (bf16[512]{0:T(512)(128)(2,1)S(1)}, bf16[512]{0:T(512)(128)(2,1)}, u32[]{:S(2)}) copy-start(bf16[512]{0:T(512)(128)(2,1)} %param.12) | copy-start | bytes 3076
  2.8 10.5 %collective-permute-start = (bf16[2,64,512]{1,2,0:T(8,128)(2,1)S(1)}, bf16[2,64,512]{1,2,0:T(8,128)(2,1)S(1)}, u32[]{:S(2)}, u32[]{:S(2)}) collective-permute-start(bf16[2,64,512]{1,2,0:T(8,128)(2,1)S(1)} %get-tuple-element.12), channel_id=1, source_target_pairs={{0,8},{8,16},{16,24},{1,9},{9,17},{17,25},{2,10},{10,18},{18,26},{... | collective-permute-start | bytes 393224 | tf_op jit(solution)/shard_map/ppermute | solution.py:20
  7.8 9.7 %collective-permute-start.1 = (bf16[2,64,512]{1,2,0:T(8,128)(2,1)S(1)}, bf16[2,64,512]{1,2,0:T(8,128)(2,1)S(1)}, u32[]{:S(2)}, u32[]{:S(2)}) collective-permute-start(bf16[2,64,512]{1,2,0:T(8,128)(2,1)S(1)} %get-tuple-element.13), channel_id=1, source_target_pairs={{8,0},{16,8},{24,16},{9,1},{17,9},{25,17},{10,2},{18,10},{26,18},{... | collective-permute-start | bytes 393224 | tf_op jit(solution)/shard_map/ppermute | solution.py:21
  48.1 8.3 %copy-start.3 = (f32[1024]{0:T(1024)S(1)}, f32[1024]{0:T(1024)}, u32[]{:S(2)}) copy-start(f32[1024]{0:T(1024)} %param.14) | copy-start | bytes 12292
  48.1 8.3 %copy-start.4 = (f32[1024]{0:T(1024)S(1)}, f32[1024]{0:T(1024)}, u32[]{:S(2)}) copy-start(f32[1024]{0:T(1024)} %param.13) | copy-start | bytes 12292
  51.0 5.0 %collective-permute-start.2 = (bf16[1,128,512]{1,2,0:T(8,128)(2,1)S(1)}, bf16[1,128,512]{1,2,0:T(8,128)(2,1)S(1)}, u32[]{:S(2)}, u32[]{:S(2)}) collective-permute-start(bf16[1,128,512]{1,2,0:T(8,128)(2,1)S(1)} %get-tuple-element.8), channel_id=1, source_target_pairs={{0,4},{4,0},{1,5},{5,1},{2,6},{6,2},{3,7},{7,3},{8,12},{12,8},{9,1... | collective-permute-start | bytes 393224 | tf_op jit(solution)/shard_map/ppermute | solution.py:109
  56.2 1.2 %copy-start.2 = (bf16[1024,512]{1,0:T(8,128)(2,1)S(1)}, bf16[1024,512]{1,0:T(8,128)(2,1)}, u32[]{:S(2)}) copy-start(bf16[1024,512]{1,0:T(8,128)(2,1)} %param.17) | copy-start | bytes 3145732
  58.2 8.4 %collective-permute-start.5 = (bf16[128,1024]{1,0:T(8,128)(2,1)S(1)}, bf16[128,1024]{1,0:T(8,128)(2,1)S(1)}, u32[]{:S(2)}, u32[]{:S(2)}) collective-permute-start(bf16[128,1024]{1,0:T(8,128)(2,1)S(1)} %pad_maximum_fusion.4), channel_id=1, source_target_pairs={{0,24},{8,0},{16,8},{24,16},{1,25},{9,1},{17,9},{25,17},{2,26},{10... | collective-permute-start | bytes 786440 | tf_op jit(solution)/shard_map/ppermute | solution.py:119
  59.8 22.0 %collective-permute-start.4 = (bf16[128,1024]{1,0:T(8,128)(2,1)S(1)}, bf16[128,1024]{1,0:T(8,128)(2,1)S(1)}, u32[]{:S(2)}, u32[]{:S(2)}) collective-permute-start(bf16[128,1024]{1,0:T(8,128)(2,1)S(1)} %pad_maximum_fusion.4), channel_id=1, source_target_pairs={{0,16},{8,24},{16,0},{24,8},{1,17},{9,25},{17,1},{25,9},{2,18},{10... | collective-permute-start | bytes 786440 | tf_op jit(solution)/shard_map/ppermute | solution.py:119
  61.3 20.5 %collective-permute-start.3 = (bf16[128,1024]{1,0:T(8,128)(2,1)S(1)}, bf16[128,1024]{1,0:T(8,128)(2,1)S(1)}, u32[]{:S(2)}, u32[]{:S(2)}) collective-permute-start(bf16[128,1024]{1,0:T(8,128)(2,1)S(1)} %pad_maximum_fusion.4), channel_id=1, source_target_pairs={{0,8},{8,16},{16,24},{24,0},{1,9},{9,17},{17,25},{25,1},{2,10},{10... | collective-permute-start | bytes 786440 | tf_op jit(solution)/shard_map/ppermute | solution.py:119

commit v7 on v6

--- a/solution.py
+++ b/solution.py
@@ -54,7 +54,7 @@
             acc = acc + jnp.dot(lhs, rhs, preferred_element_type=jnp.float32)
         return acc
 
-    acc = lax.fori_loop(0, chans // 8, octet_step, jnp.zeros((outs, recs * rows), jnp.float32), unroll=2)
+    acc = lax.fori_loop(0, chans // 8, octet_step, jnp.zeros((outs, recs * rows), jnp.float32), unroll=4)
     across = lax.broadcasted_iota(jnp.int32, (rows, rows), 0) + lax.broadcasted_iota(
         jnp.int32, (rows, rows), 1
     )
@@ -108,6 +108,55 @@
     theirs = lax.dynamic_index_in_dim(hidden, 1 - place, 0, keepdims=True)
     got = lax.ppermute(theirs, axis, [(0, 1), (1, 0)])
     return jnp.where(place == 0, jnp.concatenate([mine, got], axis=2), jnp.concatenate([got, mine], axis=2))
+
+
+def attend_body(*refs):
+    q_ref, valid_ref, live_ref = refs[0], refs[1], refs[2]
+    out_ref = refs[-1]
+    block_refs = refs[3:-1]
+    rows, width = q_ref.shape
+    valid = valid_ref[...] > 0.0
+    live = live_ref[...] > 0.0
+    lanes = lax.broadcasted_iota(jnp.int32, (1, 128), 1)
+    for pair in range(width // 128):
+        cols = slice(pair * 128, (pair + 1) * 128)
+        vcols = slice(width + pair * 128, width + (pair + 1) * 128)
+        keys = jnp.concatenate([block[:, cols] for block in block_refs], axis=0)
+        vals = jnp.concatenate([block[:, vcols] for block in block_refs], axis=0)
+        query = q_ref[:, cols]
+        results = []
+        for half in range(2):
+            mine = (lanes // HD) == half
+            scores = lax.dot_general(
+                jnp.where(mine, query, jnp.zeros_like(query)),
+                keys,
+                (((1,), (1,)), ((), ())),
+                preferred_element_type=jnp.float32,
+            ) / math.sqrt(HD)
+            scores = jnp.where(valid, scores, -1e30)
+            rowmax = jnp.max(scores, axis=1, keepdims=True)
+            weights = jnp.where(valid, jnp.exp(scores - rowmax), 0.0)
+            total = jnp.sum(weights, axis=1, keepdims=True)
+            summed = jnp.dot(weights.astype(jnp.bfloat16), vals, preferred_element_type=jnp.float32)
+            results.append(summed / total)
+        both = jnp.where((lanes // HD) == 0, results[0], results[1])
+        out_ref[:, cols] = jnp.where(live, both, 0.0).astype(out_ref.dtype)
+
+
+def fused_attention(query_flat, pieces, key_pos, own_length, query_pos):
+    rows, width = query_flat.shape
+    keys_total = key_pos.shape[0]
+    valid = (key_pos < own_length).astype(jnp.float32).reshape(1, keys_total)
+    live = (query_pos < own_length).astype(jnp.float32).reshape(rows, 1)
+    return pl.pallas_call(
+        attend_body,
+        out_shape=jax.ShapeDtypeStruct((rows, width), jnp.bfloat16),
+        cost_estimate=pl.CostEstimate(
+            flops=8 * rows * keys_total * width,
+            bytes_accessed=2 * (rows * width * 2 + keys_total * width * 2),
+            transcendentals=2 * rows * keys_total * (width // HD),
+        ),
+    )(query_flat, valid, live, *pieces)
 
 
 def gather_ring(x, axis, rows):
@@ -205,28 +254,11 @@
     width = key_flat.shape[1]
     both = jnp.concatenate([key_flat, val_flat], axis=1)
     pieces, starts = gather_ring(both, "ctx", frame_rows)
-    whole = jnp.concatenate(pieces, axis=0)
     key_pos = jnp.concatenate(
         [start + jnp.arange(frame_rows, dtype=jnp.int32) for start in starts]
     )
-    queries = query_flat.reshape(frame_rows, head_count, HD)
-    keys = whole[:, :width].reshape(-1, head_count, HD)
-    vals = whole[:, width:].reshape(-1, head_count, HD)
-    scores = jnp.einsum(
-        "fhd,nhd->hfn", queries, keys, preferred_element_type=jnp.float32
-    ) / math.sqrt(HD)
-    valid = (key_pos < own_length)[None, None, :]
-    scores = jnp.where(valid, scores, -1e30)
-    rowmax = jnp.max(scores, axis=2, keepdims=True)
-    weights = jnp.where(valid, jnp.exp(scores - rowmax), 0.0)
-    total = jnp.sum(weights, axis=2, keepdims=True)
-    summed = jnp.einsum(
-        "hfn,nhd->hfd", weights.astype(jnp.bfloat16), vals, preferred_element_type=jnp.float32
-    )
-    out = summed / total
-    query_live = (positions < own_length)[None, :, None]
-    out = jnp.where(query_live, out, 0.0).transpose(1, 0, 2)
-    result = out.reshape(1, frame_rows, head_count * HD).astype(jnp.bfloat16)
+    result = fused_attention(query_flat, pieces, key_pos, own_length, positions)
+    result = result.reshape(1, frame_rows, query_flat.shape[1])
     return (hidden, result)
 
 

time: 92.4 us -> 83.6 us (0.905)
  the two profiles are of different devices: /device:TPU:0 before, /device:TPU:9 now
where the time goes in v7:
time: 83.6 us; the launch traced here: 83.2 us
  Pallas kernels  29 us (35%)
  waiting for transfers between devices  25.4 us (30%)
  starting transfers between devices  9.2 us (11%)
  local copies, waits for them, and re-layouts  7.52 us (9%)
  other arithmetic  5.95 us (7%)
  matrix products  5.27 us (6%)
  between operations  0.87 us (1%)
    pallas_call x1, Pallas kernels, hankel_conv(): pl.pallas_call(conv_body, grid=(groups,), in_specs=[pl.BlockSpec((1, recs...  24.9 us
    ppermute x3, waiting for transfers between devices, gather_ring(): pieces.append(lax.ppermute(x, axis, pairs))  18.7 us
    pallas_call x1, Pallas kernels, fused_attention(): pl.pallas_call(attend_body, out_shape=jax.ShapeDtypeStruct((rows, width),...  4.18 us
    ppermute x1, starting transfers between devices, padded_2(): before = lax.ppermute(last, axis, up)  3.2 us
    ppermute x1, waiting for transfers between devices, padded_2(): before = lax.ppermute(last, axis, up)  3.02 us
    ppermute x1, waiting for transfers between devices, padded_2(): after = lax.ppermute(first, axis, down)  2.89 us
    unnamed x18, local copies, waits for them, and re-layouts  2.8 us
    ppermute x3, starting transfers between devices, gather_ring(): pieces.append(lax.ppermute(x, axis, pairs))  2.6 us
  transfers between devices with their start and end apart: 6, of which 5 were waited for; matrix products, arithmetic and copies ran while one was open for 9% of the time, Pallas kernels for 0%

profile of v7, /device:TPU:9, one launch (start us, length us, event | category | flops | bytes accessed | tf_op | source)
XLA Modules:
  0.0 83.2 jit_solution(4712045169818898324)
XLA Ops:
  0.6 0.0 copy-start
  0.7 1.2 %copy.15 = bf16[2,128,512]{1,2,0:T(8,128)(2,1)S(1)} copy(bf16[2,128,512]{2,1,0:T(8,128)(2,1)} %param.9) | data formatting | bytes 524288 | tf_op args[0]
  1.9 0.7 broadcast_compare_fusion
  2.6 0.1 fusion.22
  2.8 3.2 %collective-permute-start = (bf16[2,64,512]{1,2,0:T(8,128)(2,1)S(1)}, bf16[2,64,512]{1,2,0:T(8,128)(2,1)S(1)}, u32[]{:S(2)}, u32[]{:S(2)}) collective-permute-start(bf16[2,64,512]{1,2,0:T(8,128)(2,1)S(1)} %get-tuple-element.10), channel_id=1, source_target_pairs={{0,8},{8,16},{16,24},{1,9},{9,17},{17,25},{2,10},{10,18},{18,26},{... | collective-permute-start | bytes 393224 | tf_op jit(solution)/shard_map/ppermute | solution.py:20
  6.0 2.1 %collective-permute-start.1 = (bf16[2,64,512]{1,2,0:T(8,128)(2,1)S(1)}, bf16[2,64,512]{1,2,0:T(8,128)(2,1)S(1)}, u32[]{:S(2)}, u32[]{:S(2)}) collective-permute-start(bf16[2,64,512]{1,2,0:T(8,128)(2,1)S(1)} %get-tuple-element.11), channel_id=1, source_target_pairs={{8,0},{16,8},{24,16},{9,1},{17,9},{25,17},{10,2},{18,10},{26,18},{... | collective-permute-start | bytes 393224 | tf_op jit(solution)/shard_map/ppermute | solution.py:21
  8.1 0.7 convert_element_type.45
  8.8 3.0 %collective-permute-done = bf16[2,64,512]{1,2,0:T(8,128)(2,1)S(1)} collective-permute-done((bf16[2,64,512]{1,2,0:T(8,128)(2,1)S(1)}, bf16[2,64,512]{1,2,0:T(8,128)(2,1)S(1)}, u32[]{:S(2)}, u32[]{:S(2)}) %collective-permute-start) | collective-permute-done | bytes 131104 | tf_op jit(solution)/shard_map/ppermute | solution.py:20
  11.8 2.9 %collective-permute-done.1 = bf16[2,64,512]{1,2,0:T(8,128)(2,1)S(1)} collective-permute-done((bf16[2,64,512]{1,2,0:T(8,128)(2,1)S(1)}, bf16[2,64,512]{1,2,0:T(8,128)(2,1)S(1)}, u32[]{:S(2)}, u32[]{:S(2)}) %collective-permute-start.1) | collective-permute-done | bytes 131104 | tf_op jit(solution)/shard_map/ppermute | solution.py:21
  14.7 0.3 pad_maximum_fusion.2
  15.0 0.0 copy-start.7
  15.1 0.0 copy-start.5
  15.1 0.0 copy-start.6
  15.1 0.8 slice.24
  15.9 0.8 slice.27
  16.7 0.1 pad_maximum_fusion
  16.7 0.9 %copy.21 = bf16[2,256,8,64]{1,3,0,2:T(8,128)(2,1)} copy(bf16[2,256,8,64]{1,3,2,0:T(8,128)(2,1)S(1)} %bitcast.29) | data formatting | bytes 1048576 | tf_op jit(solution)/shard_map/reshape | solution.py:98
  17.6 24.9 %shard_map.104 = f32[8,2,128,64]{3,2,1,0:T(8,128)} custom-call(bf16[8,2,64,256]{3,2,1,0:T(8,128)(2,1)} %bitcast.28, bf16[8,64,64,128]{3,2,1,0:T(8,128)(2,1)} %bitcast.26), custom_call_target="tpu_custom_call" | custom-call | flops 2147483648 | bytes 9437184 | tf_op jit(solution)/shard_map/pallas_call | solution.py:77
  42.5 1.5 %copy.17 = f32[2,128,8,64]{1,3,2,0:T(8,128)S(1)} copy(f32[2,128,8,64]{3,1,0,2:T(8,128)} %bitcast.27) | data formatting | bytes 1048576 | tf_op jit(solution)/shard_map/transpose | solution.py:100
  44.0 1.3 %fusion.9 = bf16[2,128,512]{1,2,0:T(8,128)(2,1)S(1)} fusion(f32[2,128,8,64]{1,3,2,0:T(8,128)S(1)} %copy.17, f32[512]{0:T(512)S(1)} %convert_element_type.45, bf16[2,128,512]{1,2,0:T(8,128)(2,1)S(1)} %copy.15, pred[2,128]{1,0:T(4,128)(4,1)S(1)} %broadcast_compare_fusion), kind=kLoop, calls=%fused_computation.15 | loop fusion | flops 9043968 | bytes 1050880 | tf_op jit(solution)/shard_map/convert_element_type | solution.py:241
  45.3 1.3 %collective-permute-start.2 = (bf16[1,128,512]{1,2,0:T(8,128)(2,1)S(1)}, bf16[1,128,512]{1,2,0:T(8,128)(2,1)S(1)}, u32[]{:S(2)}, u32[]{:S(2)}) collective-permute-start(bf16[1,128,512]{1,2,0:T(8,128)(2,1)S(1)} %get-tuple-element.6), channel_id=1, source_target_pairs={{0,4},{4,0},{1,5},{5,1},{2,6},{6,2},{3,7},{7,3},{8,12},{12,8},{9,1... | collective-permute-start | bytes 393224 | tf_op jit(solution)/shard_map/ppermute | solution.py:109
  46.6 0.0 copy-done.7
  46.6 0.6 dynamic_slice.13
  47.2 1.3 %fusion.17.refs_2_ = f32[128,1]{1,0:T(8,128)} fusion(s32[]{:T(128)S(6)} %mul.36, s32[]{:T(128)} %bitcast.11), kind=kLoop, calls=%fused_computation.41 | loop fusion | flops 384 | bytes 520 | tf_op jit(solution)/shard_map/convert_element_type | solution.py:150
  48.5 0.7 collective-permute-done.2
  49.2 0.2 convert_reduce_fusion
  49.4 0.2 fusion.2
  49.5 0.0 copy-done
  49.6 0.0 copy-done.5
  49.6 0.0 copy-done.6
  49.6 0.7 convolution_convert_fusion.1
  50.3 2.0 %convolution_convert_fusion = bf16[128,512]{1,0:T(8,128)(2,1)S(1)} fusion(bf16[1024,512]{1,0:T(8,128)(2,1)} %param.17, f32[1024]{0:T(1024)S(1)} %copy-done.5, f32[1024]{0:T(1024)S(1)} %copy-done.6, f32[128]{0:T(128)S(1)} %add_sqrt_fusion, f32[128]{0:T(128)S(1)} %broadcast_multiply_fusion, bf16[128,512]{0,1:T(8,128)(2,1)S(1)} %get-tuple-element.7, ...), kind=kOutput, calls=%fused_computation | convolution fusion | flops 136249344 | bytes 1451009 | tf_op jit(solution)/shard_map/dot_general | solution.py:252
  52.3 0.0 copy-start.1
  52.3 1.3 %collective-permute-start.3 = (bf16[128,1024]{1,0:T(8,128)(2,1)S(1)}, bf16[128,1024]{1,0:T(8,128)(2,1)S(1)}, u32[]{:S(2)}, u32[]{:S(2)}) collective-permute-start(bf16[128,1024]{1,0:T(8,128)(2,1)S(1)} %pad_maximum_fusion.3.refs_3_), channel_id=1, source_target_pairs={{0,8},{8,16},{16,24},{24,0},{1,9},{9,17},{17,25},{25,1},{2,10},{10... | collective-permute-start | bytes 786440 | tf_op jit(solution)/shard_map/ppermute | solution.py:168
  53.6 1.0 %collective-permute-start.4 = (bf16[128,1024]{1,0:T(8,128)(2,1)S(1)}, bf16[128,1024]{1,0:T(8,128)(2,1)S(1)}, u32[]{:S(2)}, u32[]{:S(2)}) collective-permute-start(bf16[128,1024]{1,0:T(8,128)(2,1)S(1)} %pad_maximum_fusion.3.refs_3_), channel_id=1, source_target_pairs={{0,16},{8,24},{16,0},{24,8},{1,17},{9,25},{17,1},{25,9},{2,18},{10... | collective-permute-start | bytes 786440 | tf_op jit(solution)/shard_map/ppermute | solution.py:168
  54.6 0.3 collective-permute-start.5
  54.9 1.2 %compare_convert_fusion.refs_1_ = f32[1,512]{1,0:T(1,128)} fusion(s32[1,128]{1,0:T(1,128)S(1)} %get-tuple-element.12, s32[1,128]{1,0:T(1,128)S(1)} %get-tuple-element.13, s32[1,128]{1,0:T(1,128)S(1)} %get-tuple-element.14, s32[1,128]{1,0:T(1,128)S(1)} %get-tuple-element.15, s32[]{:T(128)} %bitcast.11), kind=kLoop, calls=%fused_computation.42 | loop fusion | flops 2560 | bytes 4100 | tf_op jit(solution)/shard_map/convert_element_type | solution.py:149
  56.1 0.9 %copy.19 = bf16[2,128,512]{2,1,0:T(8,128)(2,1)} copy(bf16[2,128,512]{1,2,0:T(8,128)(2,1)S(1)} %fusion.9) | data formatting | bytes 524288
  57.0 2.6 %convolution_convert_fusion.2.refs_0_ = bf16[128,512]{1,0:T(8,128)(2,1)} fusion(bf16[1024,512]{1,0:T(8,128)(2,1)} %param.15, f32[1024]{0:T(1024)S(1)} %copy-done.5, f32[1024]{0:T(1024)S(1)} %copy-done.6, f32[128]{0:T(128)S(1)} %add_sqrt_fusion, f32[128]{0:T(128)S(1)} %broadcast_multiply_fusion, bf16[128,512]{0,1:T(8,128)(2,1)S(1)} %get-tuple-element.7, ...), kind=kOutput, calls=%fused_computation.2 | convolution fusion | flops 136249344 | bytes 1451009 | tf_op jit(solution)/shard_map/dot_general | solution.py:250
  59.6 0.0 collective-permute-done.3.refs_4_
  59.6 14.2 %collective-permute-done.4.refs_5_ = bf16[128,1024]{1,0:T(8,128)(2,1)S(1)} collective-permute-done((bf16[128,1024]{1,0:T(8,128)(2,1)S(1)}, bf16[128,1024]{1,0:T(8,128)(2,1)S(1)}, u32[]{:S(2)}, u32[]{:S(2)}) %collective-permute-start.4) | collective-permute-done | bytes 262176 | tf_op jit(solution)/shard_map/ppermute | solution.py:168
  73.7 4.6 %collective-permute-done.5.refs_6_ = bf16[128,1024]{1,0:T(8,128)(2,1)S(1)} collective-permute-done((bf16[128,1024]{1,0:T(8,128)(2,1)S(1)}, bf16[128,1024]{1,0:T(8,128)(2,1)S(1)}, u32[]{:S(2)}, u32[]{:S(2)}) %collective-permute-start.5) | collective-permute-done | bytes 262176 | tf_op jit(solution)/shard_map/ppermute | solution.py:168
  78.3 0.0 copy-done.1
  78.3 0.0 copy-done.2
  78.3 0.0 copy-done.3
  78.3 0.0 copy-start.4
  78.3 0.7 copy-done.4
  79.0 4.2 %shard_map.105 = bf16[128,512]{1,0:T(8,128)(2,1)} custom-call(bf16[128,512]{1,0:T(8,128)(2,1)} %convolution_convert_fusion.2.refs_0_, f32[1,512]{1,0:T(1,128)} %compare_convert_fusion.refs_1_, f32[128,1]{1,0:T(8,128)} %fusion.17.refs_2_, bf16[128,1024]{1,0:T(8,128)(2,1)} %copy-done.1, bf16[128,1024]{1,0:T(8,128)(2,1)} %copy-done.2, ...), custom_call_target="tpu_custom_call" | custom-call | flops 268435456 | bytes 1310720 | tf_op jit(solution)/shard_map/pallas_call | solution.py:151
  (10 shorter events, 0.1 us)
Async XLA Ops:
  0.6 48.9 %copy-start = (bf16[1024,512]{1,0:T(8,128)(2,1)S(1)}, bf16[1024,512]{1,0:T(8,128)(2,1)}, u32[]{:S(2)}) copy-start(bf16[1024,512]{1,0:T(8,128)(2,1)} %param.16) | copy-start | bytes 3145732
  2.8 9.1 %collective-permute-start = (bf16[2,64,512]{1,2,0:T(8,128)(2,1)S(1)}, bf16[2,64,512]{1,2,0:T(8,128)(2,1)S(1)}, u32[]{:S(2)}, u32[]{:S(2)}) collective-permute-start(bf16[2,64,512]{1,2,0:T(8,128)(2,1)S(1)} %get-tuple-element.10), channel_id=1, source_target_pairs={{0,8},{8,16},{16,24},{1,9},{9,17},{17,25},{2,10},{10,18},{18,26},{... | collective-permute-start | bytes 393224 | tf_op jit(solution)/shard_map/ppermute | solution.py:20
  6.0 8.8 %collective-permute-start.1 = (bf16[2,64,512]{1,2,0:T(8,128)(2,1)S(1)}, bf16[2,64,512]{1,2,0:T(8,128)(2,1)S(1)}, u32[]{:S(2)}, u32[]{:S(2)}) collective-permute-start(bf16[2,64,512]{1,2,0:T(8,128)(2,1)S(1)} %get-tuple-element.11), channel_id=1, source_target_pairs={{8,0},{16,8},{24,16},{9,1},{17,9},{25,17},{10,2},{18,10},{26,18},{... | collective-permute-start | bytes 393224 | tf_op jit(solution)/shard_map/ppermute | solution.py:21
  15.0 31.6 %copy-start.7 = (s32[2]{0:T(128)S(1)}, s32[2]{0:T(128)}, u32[]{:S(2)}) copy-start(s32[2]{0:T(128)} %param.10) | copy-start | bytes 28
  15.1 34.5 %copy-start.5 = (f32[1024]{0:T(1024)S(1)}, f32[1024]{0:T(1024)}, u32[]{:S(2)}) copy-start(f32[1024]{0:T(1024)} %param.14) | copy-start | bytes 12292
  15.1 34.5 %copy-start.6 = (f32[1024]{0:T(1024)S(1)}, f32[1024]{0:T(1024)}, u32[]{:S(2)}) copy-start(f32[1024]{0:T(1024)} %param.13) | copy-start | bytes 12292
  45.3 3.9 %collective-permute-start.2 = (bf16[1,128,512]{1,2,0:T(8,128)(2,1)S(1)}, bf16[1,128,512]{1,2,0:T(8,128)(2,1)S(1)}, u32[]{:S(2)}, u32[]{:S(2)}) collective-permute-start(bf16[1,128,512]{1,2,0:T(8,128)(2,1)S(1)} %get-tuple-element.6), channel_id=1, source_target_pairs={{0,4},{4,0},{1,5},{5,1},{2,6},{6,2},{3,7},{7,3},{8,12},{12,8},{9,1... | collective-permute-start | bytes 393224 | tf_op jit(solution)/shard_map/ppermute | solution.py:109
  52.3 26.0 %copy-start.1 = (bf16[128,1024]{1,0:T(8,128)(2,1)}, bf16[128,1024]{1,0:T(8,128)(2,1)S(1)}, u32[]{:S(2)}) copy-start(bf16[128,1024]{1,0:T(8,128)(2,1)S(1)} %pad_maximum_fusion.3.refs_3_) | copy-start | bytes 786436
  52.3 7.3 %collective-permute-start.3 = (bf16[128,1024]{1,0:T(8,128)(2,1)S(1)}, bf16[128,1024]{1,0:T(8,128)(2,1)S(1)}, u32[]{:S(2)}, u32[]{:S(2)}) collective-permute-start(bf16[128,1024]{1,0:T(8,128)(2,1)S(1)} %pad_maximum_fusion.3.refs_3_), channel_id=1, source_target_pairs={{0,8},{8,16},{16,24},{24,0},{1,9},{9,17},{17,25},{25,1},{2,10},{10... | collective-permute-start | bytes 786440 | tf_op jit(solution)/shard_map/ppermute | solution.py:168
  53.6 20.1 %collective-permute-start.4 = (bf16[128,1024]{1,0:T(8,128)(2,1)S(1)}, bf16[128,1024]{1,0:T(8,128)(2,1)S(1)}, u32[]{:S(2)}, u32[]{:S(2)}) collective-permute-start(bf16[128,1024]{1,0:T(8,128)(2,1)S(1)} %pad_maximum_fusion.3.refs_3_), channel_id=1, source_target_pairs={{0,16},{8,24},{16,0},{24,8},{1,17},{9,25},{17,1},{25,9},{2,18},{10... | collective-permute-start | bytes 786440 | tf_op jit(solution)/shard_map/ppermute | solution.py:168
  54.6 23.7 %collective-permute-start.5 = (bf16[128,1024]{1,0:T(8,128)(2,1)S(1)}, bf16[128,1024]{1,0:T(8,128)(2,1)S(1)}, u32[]{:S(2)}, u32[]{:S(2)}) collective-permute-start(bf16[128,1024]{1,0:T(8,128)(2,1)S(1)} %pad_maximum_fusion.3.refs_3_), channel_id=1, source_target_pairs={{0,24},{8,0},{16,8},{24,16},{1,25},{9,1},{17,9},{25,17},{2,26},{10... | collective-permute-start | bytes 786440 | tf_op jit(solution)/shard_map/ppermute | solution.py:168
  59.6 18.7 %copy-start.2 = (bf16[128,1024]{1,0:T(8,128)(2,1)}, bf16[128,1024]{1,0:T(8,128)(2,1)S(1)}, u32[]{:S(2)}) copy-start(bf16[128,1024]{1,0:T(8,128)(2,1)S(1)} %collective-permute-done.3.refs_4_) | copy-start | bytes 786436
  73.7 4.6 %copy-start.3 = (bf16[128,1024]{1,0:T(8,128)(2,1)}, bf16[128,1024]{1,0:T(8,128)(2,1)S(1)}, u32[]{:S(2)}) copy-start(bf16[128,1024]{1,0:T(8,128)(2,1)S(1)} %collective-permute-done.4.refs_5_) | copy-start | bytes 786436
  78.3 0.7 copy-start.4

commit v8 on v7

--- a/solution.py
+++ b/solution.py
@@ -159,8 +159,26 @@
     )(query_flat, valid, live, *pieces)
 
 
+def gather_line4(x, axis, rows):
+    place = lax.axis_index(axis)
+    from_below = lax.ppermute(x, axis, [(0, 1), (1, 2), (2, 3)])
+    from_above = lax.ppermute(x, axis, [(1, 0), (2, 1), (3, 2)])
+    across = lax.ppermute(x, axis, [(0, 2), (1, 3), (2, 0), (3, 1)])
+    passed = lax.ppermute(across, axis, [(2, 3), (1, 0)])
+    pieces = [
+        x,
+        across,
+        jnp.where(place >= 1, from_below, passed),
+        jnp.where(place <= 2, from_above, passed),
+    ]
+    starts = [place * rows, ((place + 2) % 4) * rows, ((place + 3) % 4) * rows, ((place + 1) % 4) * rows]
+    return pieces, starts
+
+
 def gather_ring(x, axis, rows):
     size = lax.axis_size(axis)
+    if size == 4:
+        return gather_line4(x, axis, rows)
     place = lax.axis_index(axis)
     pieces, starts = [x], [place * rows]
     for shift in range(1, size):

time: 83.6 us -> 82.1 us (0.982)
  the two profiles are of different devices: /device:TPU:9 before, /device:TPU:0 now
where the time goes in v8:
time: 82.1 us; the launch traced here: 81.7 us
  Pallas kernels  29.1 us (35%)
  starting transfers between devices  17.6 us (21%)
  waiting for transfers between devices  16.5 us (20%)
  local copies, waits for them, and re-layouts  6.82 us (8%)
  other arithmetic  6.81 us (8%)
  matrix products  4.06 us (5%)
  between operations  0.84 us (1%)
    pallas_call x1, Pallas kernels, hankel_conv(): pl.pallas_call(conv_body, grid=(groups,), in_specs=[pl.BlockSpec((1, recs...  25 us
    ppermute x1, starting transfers between devices, padded_2(): before = lax.ppermute(last, axis, up)  4.94 us
    ppermute x1, starting transfers between devices, gather_line4(): from_below = lax.ppermute(x, axis, [(0, 1), (1, 2), (2, 3)])  4.56 us
    pallas_call x1, Pallas kernels, fused_attention(): pl.pallas_call(attend_body, out_shape=jax.ShapeDtypeStruct((rows, width),...  4.18 us
    ppermute x1, waiting for transfers between devices, padded_2(): after = lax.ppermute(first, axis, down)  4.13 us
    ppermute x1, waiting for transfers between devices, padded_2(): before = lax.ppermute(last, axis, up)  3.54 us
    ppermute x1, waiting for transfers between devices, swap_halves(): got = lax.ppermute(theirs, axis, [(0, 1), (1, 0)])  3.45 us
    ppermute x1, waiting for transfers between devices, gather_line4(): across = lax.ppermute(x, axis, [(0, 2), (1, 3), (2, 0), (3, 1)])  3.08 us
  transfers between devices with their start and end apart: 7, of which 5 were waited for; matrix products, arithmetic and copies ran while one was open for 9% of the time, Pallas kernels for 0%

profile of v8, /device:TPU:0, one launch (start us, length us, event | category | flops | bytes accessed | tf_op | source)
XLA Modules:
  0.0 81.7 jit_solution(4920208342514315141)
XLA Ops:
  0.6 0.0 copy-start
  0.7 1.2 %copy.15 = bf16[2,128,512]{1,2,0:T(8,128)(2,1)S(1)} copy(bf16[2,128,512]{2,1,0:T(8,128)(2,1)} %param.9) | data formatting | bytes 524288 | tf_op args[0]
  1.9 0.7 broadcast_compare_fusion
  2.6 0.1 fusion.22
  2.8 4.9 %collective-permute-start = (bf16[2,64,512]{1,2,0:T(8,128)(2,1)S(1)}, bf16[2,64,512]{1,2,0:T(8,128)(2,1)S(1)}, u32[]{:S(2)}, u32[]{:S(2)}) collective-permute-start(bf16[2,64,512]{1,2,0:T(8,128)(2,1)S(1)} %get-tuple-element.12), channel_id=1, source_target_pairs={{0,8},{8,16},{16,24},{1,9},{9,17},{17,25},{2,10},{10,18},{18,26},{... | collective-permute-start | bytes 393224 | tf_op jit(solution)/shard_map/ppermute | solution.py:20
  7.7 1.3 %collective-permute-start.1 = (bf16[2,64,512]{1,2,0:T(8,128)(2,1)S(1)}, bf16[2,64,512]{1,2,0:T(8,128)(2,1)S(1)}, u32[]{:S(2)}, u32[]{:S(2)}) collective-permute-start(bf16[2,64,512]{1,2,0:T(8,128)(2,1)S(1)} %get-tuple-element.13), channel_id=1, source_target_pairs={{8,0},{16,8},{24,16},{9,1},{17,9},{25,17},{10,2},{18,10},{26,18},{... | collective-permute-start | bytes 393224 | tf_op jit(solution)/shard_map/ppermute | solution.py:21
  9.0 0.7 convert_element_type.45
  9.7 3.5 %collective-permute-done = bf16[2,64,512]{1,2,0:T(8,128)(2,1)S(1)} collective-permute-done((bf16[2,64,512]{1,2,0:T(8,128)(2,1)S(1)}, bf16[2,64,512]{1,2,0:T(8,128)(2,1)S(1)}, u32[]{:S(2)}, u32[]{:S(2)}) %collective-permute-start) | collective-permute-done | bytes 131104 | tf_op jit(solution)/shard_map/ppermute | solution.py:20
  13.3 4.1 %collective-permute-done.1 = bf16[2,64,512]{1,2,0:T(8,128)(2,1)S(1)} collective-permute-done((bf16[2,64,512]{1,2,0:T(8,128)(2,1)S(1)}, bf16[2,64,512]{1,2,0:T(8,128)(2,1)S(1)}, u32[]{:S(2)}, u32[]{:S(2)}) %collective-permute-start.1) | collective-permute-done | bytes 131104 | tf_op jit(solution)/shard_map/ppermute | solution.py:21
  17.4 0.3 pad_maximum_fusion.2
  17.7 0.0 copy-start.4
  17.7 0.0 copy-start.5
  17.7 0.8 slice.24
  18.5 0.8 slice.27
  19.3 0.1 pad_maximum_fusion
  19.4 0.9 %copy.21 = bf16[2,256,8,64]{1,3,0,2:T(8,128)(2,1)} copy(bf16[2,256,8,64]{1,3,2,0:T(8,128)(2,1)S(1)} %bitcast.29) | data formatting | bytes 1048576 | tf_op jit(solution)/shard_map/reshape | solution.py:98
  20.2 25.0 %shard_map.104 = f32[8,2,128,64]{3,2,1,0:T(8,128)} custom-call(bf16[8,2,64,256]{3,2,1,0:T(8,128)(2,1)} %bitcast.28, bf16[8,64,64,128]{3,2,1,0:T(8,128)(2,1)} %bitcast.26), custom_call_target="tpu_custom_call" | custom-call | flops 2147483648 | bytes 9437184 | tf_op jit(solution)/shard_map/pallas_call | solution.py:77
  45.2 1.6 %copy.17 = f32[2,128,8,64]{1,3,2,0:T(8,128)S(1)} copy(f32[2,128,8,64]{3,1,0,2:T(8,128)} %bitcast.27) | data formatting | bytes 1048576 | tf_op jit(solution)/shard_map/transpose | solution.py:100
  46.8 1.3 %fusion.9 = bf16[2,128,512]{1,2,0:T(8,128)(2,1)S(1)} fusion(f32[2,128,8,64]{1,3,2,0:T(8,128)S(1)} %copy.17, f32[512]{0:T(512)S(1)} %convert_element_type.45, bf16[2,128,512]{1,2,0:T(8,128)(2,1)S(1)} %copy.15, pred[2,128]{1,0:T(4,128)(4,1)S(1)} %broadcast_compare_fusion), kind=kLoop, calls=%fused_computation.15 | loop fusion | flops 9043968 | bytes 1050880 | tf_op jit(solution)/shard_map/convert_element_type | solution.py:259
  48.1 1.6 %collective-permute-start.2 = (bf16[1,128,512]{1,2,0:T(8,128)(2,1)S(1)}, bf16[1,128,512]{1,2,0:T(8,128)(2,1)S(1)}, u32[]{:S(2)}, u32[]{:S(2)}) collective-permute-start(bf16[1,128,512]{1,2,0:T(8,128)(2,1)S(1)} %get-tuple-element.8), channel_id=1, source_target_pairs={{0,4},{4,0},{1,5},{5,1},{2,6},{6,2},{3,7},{7,3},{8,12},{12,8},{9,1... | collective-permute-start | bytes 393224 | tf_op jit(solution)/shard_map/ppermute | solution.py:109
  49.7 3.4 %collective-permute-done.2 = bf16[1,128,512]{1,2,0:T(8,128)(2,1)S(1)} collective-permute-done((bf16[1,128,512]{1,2,0:T(8,128)(2,1)S(1)}, bf16[1,128,512]{1,2,0:T(8,128)(2,1)S(1)}, u32[]{:S(2)}, u32[]{:S(2)}) %collective-permute-start.2) | collective-permute-done | bytes 131104 | tf_op jit(solution)/shard_map/ppermute | solution.py:109
  53.1 0.2 convert_reduce_fusion
  53.3 0.2 fusion.2
  53.5 0.0 copy-done
  53.5 0.0 copy-done.4
  53.5 0.0 copy-done.5
  53.5 0.7 convolution_convert_fusion.1
  54.2 0.0 copy-done.2
  54.2 0.7 convolution_convert_fusion
  55.0 0.0 copy-start.1
  55.0 2.6 %collective-permute-start.3 = (bf16[128,1024]{1,0:T(8,128)(2,1)S(1)}, bf16[128,1024]{1,0:T(8,128)(2,1)S(1)}, u32[]{:S(2)}, u32[]{:S(2)}) collective-permute-start(bf16[128,1024]{1,0:T(8,128)(2,1)S(1)} %pad_maximum_fusion.3.refs_3_), channel_id=1, source_target_pairs={{0,16},{8,24},{16,0},{24,8},{1,17},{9,25},{17,1},{25,9},{2,18},{10... | collective-permute-start | bytes 786440 | tf_op jit(solution)/shard_map/ppermute | solution.py:166
  57.6 0.0 copy-done.6
  57.6 0.6 dynamic_slice.13
  58.2 1.3 %fusion.17.refs_2_ = f32[128,1]{1,0:T(8,128)} fusion(s32[]{:T(128)S(6)} %mul.36, s32[]{:T(128)} %bitcast.11), kind=kLoop, calls=%fused_computation.43 | loop fusion | flops 384 | bytes 520 | tf_op jit(solution)/shard_map/convert_element_type | solution.py:150
  59.5 1.3 %collective-permute-start.6 = (bf16[128,1024]{1,0:T(8,128)(2,1)S(1)}, bf16[128,1024]{1,0:T(8,128)(2,1)S(1)}, u32[]{:S(2)}, u32[]{:S(2)}) collective-permute-start(bf16[128,1024]{1,0:T(8,128)(2,1)S(1)} %pad_maximum_fusion.3.refs_3_), channel_id=1, source_target_pairs={{8,0},{16,8},{24,16},{9,1},{17,9},{25,17},{10,2},{18,10},{26,18},{... | collective-permute-start | bytes 786440 | tf_op jit(solution)/shard_map/ppermute | solution.py:165
  60.8 4.6 %collective-permute-start.4 = (bf16[128,1024]{1,0:T(8,128)(2,1)S(1)}, bf16[128,1024]{1,0:T(8,128)(2,1)S(1)}, u32[]{:S(2)}, u32[]{:S(2)}) collective-permute-start(bf16[128,1024]{1,0:T(8,128)(2,1)S(1)} %pad_maximum_fusion.3.refs_3_), channel_id=1, source_target_pairs={{0,8},{8,16},{16,24},{1,9},{9,17},{17,25},{2,10},{10,18},{18,26},{... | collective-permute-start | bytes 786440 | tf_op jit(solution)/shard_map/ppermute | solution.py:164
  65.4 3.1 %collective-permute-done.3.refs_4_ = bf16[128,1024]{1,0:T(8,128)(2,1)S(1)} collective-permute-done((bf16[128,1024]{1,0:T(8,128)(2,1)S(1)}, bf16[128,1024]{1,0:T(8,128)(2,1)S(1)}, u32[]{:S(2)}, u32[]{:S(2)}) %collective-permute-start.3) | collective-permute-done | bytes 262176 | tf_op jit(solution)/shard_map/ppermute | solution.py:166
  68.4 1.3 %collective-permute-start.5 = (bf16[128,1024]{1,0:T(8,128)(2,1)S(1)}, bf16[128,1024]{1,0:T(8,128)(2,1)S(1)}, u32[]{:S(2)}, u32[]{:S(2)}) collective-permute-start(bf16[128,1024]{1,0:T(8,128)(2,1)S(1)} %collective-permute-done.3.refs_4_), channel_id=1, source_target_pairs={{16,24},{8,0},{17,25},{9,1},{18,26},{10,2},{19,27},{11,3},{20,28},... | collective-permute-start | bytes 786440 | tf_op jit(solution)/shard_map/ppermute | solution.py:167
  69.7 1.2 %compare_convert_fusion.refs_1_ = f32[1,512]{1,0:T(1,128)} fusion(s32[1,128]{1,0:T(1,128)S(1)} %get-tuple-element.14, s32[1,128]{1,0:T(1,128)S(1)} %get-tuple-element.15, s32[1,128]{1,0:T(1,128)S(1)} %get-tuple-element.16, s32[1,128]{1,0:T(1,128)S(1)} %get-tuple-element.17, s32[]{:T(128)} %bitcast.11), kind=kLoop, calls=%fused_computation.44 | loop fusion | flops 2560 | bytes 4100 | tf_op jit(solution)/shard_map/convert_element_type | solution.py:149
  71.0 0.8 %copy.19 = bf16[2,128,512]{2,1,0:T(8,128)(2,1)} copy(bf16[2,128,512]{1,2,0:T(8,128)(2,1)S(1)} %fusion.9) | data formatting | bytes 524288
  71.8 2.6 %convolution_convert_fusion.2.refs_0_ = bf16[128,512]{1,0:T(8,128)(2,1)} fusion(bf16[1024,512]{1,0:T(8,128)(2,1)} %param.15, f32[1024]{0:T(1024)S(1)} %copy-done.4, f32[1024]{0:T(1024)S(1)} %copy-done.5, f32[128]{0:T(128)S(1)} %add_sqrt_fusion, f32[128]{0:T(128)S(1)} %broadcast_multiply_fusion, bf16[128,512]{0,1:T(8,128)(2,1)S(1)} %get-tuple-element.9, ...), kind=kOutput, calls=%fused_computation.2 | convolution fusion | flops 136249344 | bytes 1451009 | tf_op jit(solution)/shard_map/dot_general | solution.py:268
  74.4 0.0 collective-permute-done.6
  74.4 0.0 collective-permute-done.4
  74.4 2.3 %collective-permute-done.5 = bf16[128,1024]{1,0:T(8,128)(2,1)S(1)} collective-permute-done((bf16[128,1024]{1,0:T(8,128)(2,1)S(1)}, bf16[128,1024]{1,0:T(8,128)(2,1)S(1)}, u32[]{:S(2)}, u32[]{:S(2)}) %collective-permute-start.5) | collective-permute-done | bytes 262176 | tf_op jit(solution)/shard_map/ppermute | solution.py:167
  76.7 0.8 %broadcast_select_fusion = (bf16[128,1024]{1,0:T(8,128)(2,1)}, bf16[128,1024]{1,0:T(8,128)(2,1)}) fusion(bf16[128,1024]{1,0:T(8,128)(2,1)S(1)} %collective-permute-done.6, bf16[128,1024]{1,0:T(8,128)(2,1)S(1)} %collective-permute-done.5, pred[]{:T(512)S(6)} %le.3, bf16[128,1024]{1,0:T(8,128)(2,1)S(1)} %collective-permute-done.4, pred[]{:T(512)S(6)} %ge.3), kind=kLoop, calls=%fused_computation.38 | loop fusion | flops 262144 | bytes 1310722 | tf_op jit(solution)/shard_map/jit(_where)/select_n | solution.py:172
  77.6 0.0 copy-done.1
  77.6 0.0 copy-done.3
  77.6 4.2 %shard_map.105 = bf16[128,512]{1,0:T(8,128)(2,1)} custom-call(bf16[128,512]{1,0:T(8,128)(2,1)} %convolution_convert_fusion.2.refs_0_, f32[1,512]{1,0:T(1,128)} %compare_convert_fusion.refs_1_, f32[128,1]{1,0:T(8,128)} %fusion.17.refs_2_, bf16[128,1024]{1,0:T(8,128)(2,1)} %copy-done.1, bf16[128,1024]{1,0:T(8,128)(2,1)} %copy-done.3, ...), custom_call_target="tpu_custom_call" | custom-call | flops 268435456 | bytes 1310720 | tf_op jit(solution)/shard_map/pallas_call | solution.py:151
  (11 shorter events, 0.1 us)
Async XLA Ops:
  0.6 52.8 %copy-start = (bf16[1024,512]{1,0:T(8,128)(2,1)S(1)}, bf16[1024,512]{1,0:T(8,128)(2,1)}, u32[]{:S(2)}) copy-start(bf16[1024,512]{1,0:T(8,128)(2,1)} %param.16) | copy-start | bytes 3145732
  2.8 10.5 %collective-permute-start = (bf16[2,64,512]{1,2,0:T(8,128)(2,1)S(1)}, bf16[2,64,512]{1,2,0:T(8,128)(2,1)S(1)}, u32[]{:S(2)}, u32[]{:S(2)}) collective-permute-start(bf16[2,64,512]{1,2,0:T(8,128)(2,1)S(1)} %get-tuple-element.12), channel_id=1, source_target_pairs={{0,8},{8,16},{16,24},{1,9},{9,17},{17,25},{2,10},{10,18},{18,26},{... | collective-permute-start | bytes 393224 | tf_op jit(solution)/shard_map/ppermute | solution.py:20
  7.7 9.7 %collective-permute-start.1 = (bf16[2,64,512]{1,2,0:T(8,128)(2,1)S(1)}, bf16[2,64,512]{1,2,0:T(8,128)(2,1)S(1)}, u32[]{:S(2)}, u32[]{:S(2)}) collective-permute-start(bf16[2,64,512]{1,2,0:T(8,128)(2,1)S(1)} %get-tuple-element.13), channel_id=1, source_target_pairs={{8,0},{16,8},{24,16},{9,1},{17,9},{25,17},{10,2},{18,10},{26,18},{... | collective-permute-start | bytes 393224 | tf_op jit(solution)/shard_map/ppermute | solution.py:21
  17.7 35.8 %copy-start.4 = (f32[1024]{0:T(1024)S(1)}, f32[1024]{0:T(1024)}, u32[]{:S(2)}) copy-start(f32[1024]{0:T(1024)} %param.14) | copy-start | bytes 12292
  17.7 35.8 %copy-start.5 = (f32[1024]{0:T(1024)S(1)}, f32[1024]{0:T(1024)}, u32[]{:S(2)}) copy-start(f32[1024]{0:T(1024)} %param.13) | copy-start | bytes 12292
  20.2 34.0 %copy-start.2 = (bf16[1024,512]{1,0:T(8,128)(2,1)S(1)}, bf16[1024,512]{1,0:T(8,128)(2,1)}, u32[]{:S(2)}) copy-start(bf16[1024,512]{1,0:T(8,128)(2,1)} %param.17) | copy-start | bytes 3145732
  45.2 12.4 %copy-start.6 = (s32[2]{0:T(128)S(1)}, s32[2]{0:T(128)}, u32[]{:S(2)}) copy-start(s32[2]{0:T(128)} %param.10) | copy-start | bytes 28
  48.1 5.0 %collective-permute-start.2 = (bf16[1,128,512]{1,2,0:T(8,128)(2,1)S(1)}, bf16[1,128,512]{1,2,0:T(8,128)(2,1)S(1)}, u32[]{:S(2)}, u32[]{:S(2)}) collective-permute-start(bf16[1,128,512]{1,2,0:T(8,128)(2,1)S(1)} %get-tuple-element.8), channel_id=1, source_target_pairs={{0,4},{4,0},{1,5},{5,1},{2,6},{6,2},{3,7},{7,3},{8,12},{12,8},{9,1... | collective-permute-start | bytes 393224 | tf_op jit(solution)/shard_map/ppermute | solution.py:109
  55.0 22.6 %copy-start.1 = (bf16[128,1024]{1,0:T(8,128)(2,1)}, bf16[128,1024]{1,0:T(8,128)(2,1)S(1)}, u32[]{:S(2)}) copy-start(bf16[128,1024]{1,0:T(8,128)(2,1)S(1)} %pad_maximum_fusion.3.refs_3_) | copy-start | bytes 786436
  55.0 13.5 %collective-permute-start.3 = (bf16[128,1024]{1,0:T(8,128)(2,1)S(1)}, bf16[128,1024]{1,0:T(8,128)(2,1)S(1)}, u32[]{:S(2)}, u32[]{:S(2)}) collective-permute-start(bf16[128,1024]{1,0:T(8,128)(2,1)S(1)} %pad_maximum_fusion.3.refs_3_), channel_id=1, source_target_pairs={{0,16},{8,24},{16,0},{24,8},{1,17},{9,25},{17,1},{25,9},{2,18},{10... | collective-permute-start | bytes 786440 | tf_op jit(solution)/shard_map/ppermute | solution.py:166
  59.5 14.9 %collective-permute-start.6 = (bf16[128,1024]{1,0:T(8,128)(2,1)S(1)}, bf16[128,1024]{1,0:T(8,128)(2,1)S(1)}, u32[]{:S(2)}, u32[]{:S(2)}) collective-permute-start(bf16[128,1024]{1,0:T(8,128)(2,1)S(1)} %pad_maximum_fusion.3.refs_3_), channel_id=1, source_target_pairs={{8,0},{16,8},{24,16},{9,1},{17,9},{25,17},{10,2},{18,10},{26,18},{... | collective-permute-start | bytes 786440 | tf_op jit(solution)/shard_map/ppermute | solution.py:165
  60.8 13.6 %collective-permute-start.4 = (bf16[128,1024]{1,0:T(8,128)(2,1)S(1)}, bf16[128,1024]{1,0:T(8,128)(2,1)S(1)}, u32[]{:S(2)}, u32[]{:S(2)}) collective-permute-start(bf16[128,1024]{1,0:T(8,128)(2,1)S(1)} %pad_maximum_fusion.3.refs_3_), channel_id=1, source_target_pairs={{0,8},{8,16},{16,24},{1,9},{9,17},{17,25},{2,10},{10,18},{18,26},{... | collective-permute-start | bytes 786440 | tf_op jit(solution)/shard_map/ppermute | solution.py:164
  68.4 9.1 %copy-start.3 = (bf16[128,1024]{1,0:T(8,128)(2,1)}, bf16[128,1024]{1,0:T(8,128)(2,1)S(1)}, u32[]{:S(2)}) copy-start(bf16[128,1024]{1,0:T(8,128)(2,1)S(1)} %collective-permute-done.3.refs_4_) | copy-start | bytes 786436
  68.4 8.3 %collective-permute-start.5 = (bf16[128,1024]{1,0:T(8,128)(2,1)S(1)}, bf16[128,1024]{1,0:T(8,128)(2,1)S(1)}, u32[]{:S(2)}, u32[]{:S(2)}) collective-permute-start(bf16[128,1024]{1,0:T(8,128)(2,1)S(1)} %collective-permute-done.3.refs_4_), channel_id=1, source_target_pairs={{16,24},{8,0},{17,25},{9,1},{18,26},{10,2},{19,27},{11,3},{20,28},... | collective-permute-start | bytes 786440 | tf_op jit(solution)/shard_map/ppermute | solution.py:167

commit v9 on v8

--- a/solution.py
+++ b/solution.py
@@ -24,37 +24,41 @@
 
 
 def conv_body(x_ref, w_ref, out_ref):
-    recs, chans, lanes = x_ref.shape[1], x_ref.shape[2], x_ref.shape[3]
+    pair_groups, recs, chans, lanes = x_ref.shape
     taps = w_ref.shape[3]
-    rows = out_ref.shape[2]
+    rows = out_ref.shape[1]
     outs = w_ref.shape[2]
 
-    def octet_step(q, acc):
-        base = pl.multiple_of(q * 8, 8)
-        hankels = []
-        for r in range(recs):
-            block = x_ref[0, r, pl.ds(base, 8), :]
-            per_chan = []
-            for c in range(8):
-                row = jnp.broadcast_to(block[c : c + 1, :], (taps, lanes))
-                rolled = pltpu.roll(row, 0, 1, stride=1, stride_axis=0)
-                per_chan.append(rolled[:, :rows])
-            hankels.append(per_chan)
-        for pair in range(4):
-            rhs = jnp.concatenate(
-                [
-                    jnp.concatenate([hankels[r][2 * pair + half] for r in range(recs)], axis=1)
-                    for half in range(2)
-                ],
-                axis=0,
-            )
-            lhs = jnp.concatenate(
-                [w_ref[0, base + 2 * pair], w_ref[0, base + 2 * pair + 1]], axis=1
-            )
-            acc = acc + jnp.dot(lhs, rhs, preferred_element_type=jnp.float32)
-        return acc
-
-    acc = lax.fori_loop(0, chans // 8, octet_step, jnp.zeros((outs, recs * rows), jnp.float32), unroll=4)
+    def one_group(group):
+        def octet_step(q, acc):
+            base = pl.multiple_of(q * 8, 8)
+            hankels = []
+            for r in range(recs):
+                block = x_ref[group, r, pl.ds(base, 8), :]
+                per_chan = []
+                for c in range(8):
+                    row = jnp.broadcast_to(block[c : c + 1, :], (taps, lanes))
+                    rolled = pltpu.roll(row, 0, 1, stride=1, stride_axis=0)
+                    per_chan.append(rolled[:, :rows])
+                hankels.append(per_chan)
+            for pair in range(4):
+                rhs = jnp.concatenate(
+                    [
+                        jnp.concatenate([hankels[r][2 * pair + half] for r in range(recs)], axis=1)
+                        for half in range(2)
+                    ],
+                    axis=0,
+                )
+                lhs = jnp.concatenate(
+                    [w_ref[group, base + 2 * pair], w_ref[group, base + 2 * pair + 1]], axis=1
+                )
+                acc = acc + jnp.dot(lhs, rhs, preferred_element_type=jnp.float32)
+            return acc
+
+        start = jnp.zeros((outs, recs * rows), jnp.float32)
+        return lax.fori_loop(0, chans // 8, octet_step, start, unroll=4)
+
+    acc = jnp.concatenate([one_group(group) for group in range(pair_groups)], axis=0)
     across = lax.broadcasted_iota(jnp.int32, (rows, rows), 0) + lax.broadcasted_iota(
         jnp.int32, (rows, rows), 1
     )
@@ -68,7 +72,7 @@
         low = (rest - middle.astype(jnp.float32)).astype(jnp.bfloat16)
         total = lax.dot_general(flip, high, dims, preferred_element_type=jnp.float32)
         total = total + lax.dot_general(flip, middle, dims, preferred_element_type=jnp.float32)
-        out_ref[0, r] = total + lax.dot_general(flip, low, dims, preferred_element_type=jnp.float32)
+        out_ref[r] = total + lax.dot_general(flip, low, dims, preferred_element_type=jnp.float32)
 
 
 def hankel_conv(xt, wv, rows):
@@ -76,11 +80,13 @@
     taps, outs = wv.shape[3], wv.shape[2]
     return pl.pallas_call(
         conv_body,
-        grid=(groups,),
-        in_specs=[pl.BlockSpec((1, recs, chans, lanes), lambda g: (g, 0, 0, 0)),
-                  pl.BlockSpec((1, chans, outs, taps), lambda g: (g, 0, 0, 0))],
-        out_specs=pl.BlockSpec((1, recs, rows, outs), lambda g: (g, 0, 0, 0)),
-        out_shape=jax.ShapeDtypeStruct((groups, recs, rows, outs), jnp.float32),
+        grid=(groups // 2,),
+        in_specs=[
+            pl.BlockSpec((2, recs, chans, lanes), lambda g: (g, 0, 0, 0)),
+            pl.BlockSpec((2, chans, outs, taps), lambda g: (g, 0, 0, 0)),
+        ],
+        out_specs=pl.BlockSpec((recs, rows, 2 * outs), lambda g: (0, 0, g)),
+        out_shape=jax.ShapeDtypeStruct((recs, rows, groups * outs), jnp.float32),
         cost_estimate=pl.CostEstimate(
             flops=2 * groups * recs * rows * taps * chans * outs,
             bytes_accessed=xt.size * 2 + wv.size * 2 + groups * recs * rows * outs * 4,
@@ -96,8 +102,7 @@
     grouped = jnp.pad(padded, ((0, 0), (0, lanes - span), (0, 0)))
     grouped = jnp.roll(jnp.flip(grouped, axis=1), frame_rows - lanes, axis=1)
     grouped = grouped.reshape(recs, lanes, groups_here, group_in).transpose(2, 0, 3, 1)
-    out = hankel_conv(grouped, jnp.transpose(conv_weight, (0, 2, 3, 1)), frame_rows)
-    return out.transpose(1, 2, 0, 3).reshape(recs, frame_rows, groups_here * group_out)
+    return hankel_conv(grouped, jnp.transpose(conv_weight, (0, 2, 3, 1)), frame_rows)
 
 
 def swap_halves(hidden, axis):

time: 82.1 us -> 76.4 us (0.931)
  local copies, waits for them, and re-layouts: 6.82 us -> 2.38 us
  other arithmetic: 6.81 us -> 8.67 us
  waiting for transfers between devices: 16.5 us -> 14.7 us
  matrix products: 4.06 us -> 2.98 us
    ppermute x1, waiting for transfers between devices: 3.54 us -> 0.74 us  [padded_2(): before = lax.ppermute(last, axis, up)]
    unnamed x16 -> x18, local copies, waits for them, and re-layouts: 2.09 us -> 0.05 us
    transpose x1 -> x0, local copies, waits for them, and re-layouts: 1.55 us -> none  [grouped_conv(): out.transpose(1, 2, 0, 3).reshape(recs, frame_rows, groups_here * group_out)]
    ppermute x1, waiting for transfers between devices: 2.28 us -> 3.5 us  [gather_line4(): passed = lax.ppermute(across, axis, [(2, 3), (1, 0)])]
    convert_element_type x1, other arithmetic: 1.27 us -> 2.3 us  [per_device(): hidden = (masked.astype(jnp.float32) + jax.nn.gelu(conv_out + conv_bias.a...]
    select_n x1, other arithmetic: 0.03 us -> 1.05 us  [per_device(): jnp.where(live[:, :, None], frames_in, jnp.zeros((), frames_in.dtype))]
    slice x2, local copies, waits for them, and re-layouts: 1.57 us -> 0.66 us  [grouped_conv(): grouped = jnp.roll(jnp.flip(grouped, axis=1), frame_rows - lanes, axis=1)]
  transfers between devices with their start and end apart: 7 -> 7, of which waited for: 5 -> 5; matrix products, arithmetic and copies ran while one was open for 9% -> 8% of each run, Pallas kernels for 0% -> 0%
where the time goes in v9:
time: 76.4 us; the launch traced here: 76 us
  Pallas kernels  28.9 us (38%)
  starting transfers between devices  17.6 us (23%)
  waiting for transfers between devices  14.7 us (19%)
  other arithmetic  8.67 us (11%)
  matrix products  2.98 us (4%)
  local copies, waits for them, and re-layouts  2.38 us (3%)
  between operations  0.86 us (1%)
    pallas_call x1, Pallas kernels, hankel_conv(): pl.pallas_call(conv_body, grid=(groups // 2,), in_specs=[pl.BlockSpec((2,...  24.7 us
    ppermute x1, starting transfers between devices, padded_2(): before = lax.ppermute(last, axis, up)  4.94 us
    ppermute x1, starting transfers between devices, gather_line4(): from_below = lax.ppermute(x, axis, [(0, 1), (1, 2), (2, 3)])  4.56 us
    pallas_call x1, Pallas kernels, fused_attention(): pl.pallas_call(attend_body, out_shape=jax.ShapeDtypeStruct((rows, width),...  4.18 us
    ppermute x1, waiting for transfers between devices, padded_2(): after = lax.ppermute(first, axis, down)  4.13 us
    ppermute x1, waiting for transfers between devices, gather_line4(): passed = lax.ppermute(across, axis, [(2, 3), (1, 0)])  3.5 us
    ppermute x1, waiting for transfers between devices, swap_halves(): got = lax.ppermute(theirs, axis, [(0, 1), (1, 0)])  3.45 us
    ppermute x1, waiting for transfers between devices, gather_line4(): across = lax.ppermute(x, axis, [(0, 2), (1, 3), (2, 0), (3, 1)])  2.83 us
  transfers between devices with their start and end apart: 7, of which 5 were waited for; matrix products, arithmetic and copies ran while one was open for 8% of the time, Pallas kernels for 0%

profile of v9, /device:TPU:0, one launch (start us, length us, event | category | flops | bytes accessed | tf_op | source)
XLA Modules:
  0.0 76.0 jit_solution(7610135913330154155)
XLA Ops:
  0.6 0.0 copy-start
  0.6 0.0 copy-start.1
  0.7 0.8 %broadcast_compare_fusion = pred[2,128]{1,0:T(4,128)(4,1)S(1)} fusion(s32[128]{0:T(128)S(1)} %iota_add_fusion, s32[2]{0:T(128)} %param.10), kind=kLoop, calls=%fused_computation.49 | loop fusion | flops 256 | bytes 776 | tf_op jit(solution)/shard_map/lt | solution.py:255
  1.5 1.0 %broadcast_select_fusion.2 = bf16[2,128,512]{2,1,0:T(8,128)(2,1)S(1)} fusion(bf16[2,128,512]{2,1,0:T(8,128)(2,1)} %param.9, pred[2,128]{1,0:T(4,128)(4,1)S(1)} %broadcast_compare_fusion), kind=kLoop, calls=%fused_computation.39 | loop fusion | flops 131072 | bytes 524544 | tf_op jit(solution)/shard_map/jit(_where)/select_n | solution.py:256
  2.6 4.9 %collective-permute-start = (bf16[2,64,512]{2,1,0:T(8,128)(2,1)S(1)}, bf16[2,64,512]{2,1,0:T(8,128)(2,1)S(1)}, u32[]{:S(2)}, u32[]{:S(2)}) collective-permute-start(bf16[2,64,512]{2,1,0:T(8,128)(2,1)S(1)} %get-tuple-element.8), channel_id=1, source_target_pairs={{0,8},{8,16},{16,24},{1,9},{9,17},{17,25},{2,10},{10,18},{18,26},{... | collective-permute-start | bytes 393224 | tf_op jit(solution)/shard_map/ppermute | solution.py:20
  7.5 1.3 %collective-permute-start.1 = (bf16[2,64,512]{2,1,0:T(8,128)(2,1)S(1)}, bf16[2,64,512]{2,1,0:T(8,128)(2,1)S(1)}, u32[]{:S(2)}, u32[]{:S(2)}) collective-permute-start(bf16[2,64,512]{2,1,0:T(8,128)(2,1)S(1)} %get-tuple-element.9), channel_id=1, source_target_pairs={{8,0},{16,8},{24,16},{9,1},{17,9},{25,17},{10,2},{18,10},{26,18},{... | collective-permute-start | bytes 393224 | tf_op jit(solution)/shard_map/ppermute | solution.py:21
  8.8 0.7 convert_element_type.45
  9.5 0.0 copy-start.6
  9.5 0.7 collective-permute-done
  10.3 4.1 %collective-permute-done.1 = bf16[2,64,512]{2,1,0:T(8,128)(2,1)S(1)} collective-permute-done((bf16[2,64,512]{2,1,0:T(8,128)(2,1)S(1)}, bf16[2,64,512]{2,1,0:T(8,128)(2,1)S(1)}, u32[]{:S(2)}, u32[]{:S(2)}) %collective-permute-start.1) | collective-permute-done | bytes 131104 | tf_op jit(solution)/shard_map/ppermute | solution.py:21
  14.4 0.3 slice.24
  14.8 0.3 slice.27
  15.2 0.2 copy.13
  15.4 0.0 copy-start.4
  15.4 0.8 %copy.17 = bf16[2,256,8,64]{1,3,0,2:T(8,128)(2,1)} copy(bf16[2,256,8,64]{1,3,2,0:T(8,128)(2,1)S(1)} %bitcast.23) | data formatting | bytes 1048576 | tf_op jit(solution)/shard_map/reshape | solution.py:104
  16.2 24.7 %shard_map.104 = f32[2,128,512]{2,1,0:T(8,128)} custom-call(bf16[8,2,64,256]{3,2,1,0:T(8,128)(2,1)} %bitcast.22, bf16[8,64,64,128]{3,2,1,0:T(8,128)(2,1)} %bitcast.21), custom_call_target="tpu_custom_call" | custom-call | flops 2147483648 | bytes 9437184 | tf_op jit(solution)/shard_map/pallas_call | solution.py:81
  40.9 0.0 copy-done.1
  40.9 2.3 %fusion.9 = bf16[2,128,512]{2,1,0:T(8,128)(2,1)S(1)} fusion(f32[2,128,512]{2,1,0:T(8,128)} %shard_map.104, f32[512]{0:T(512)S(1)} %convert_element_type.45, bf16[2,128,512]{2,1,0:T(8,128)(2,1)S(1)} %copy-done.1, pred[2,128]{1,0:T(4,128)(4,1)S(1)} %broadcast_compare_fusion), kind=kLoop, calls=%fused_computation.15 | loop fusion | flops 9043968 | bytes 1050880 | tf_op jit(solution)/shard_map/convert_element_type | solution.py:264
  43.2 0.0 copy-start.2
  43.3 1.6 %collective-permute-start.2 = (bf16[1,128,512]{2,1,0:T(8,128)(2,1)S(1)}, bf16[1,128,512]{2,1,0:T(8,128)(2,1)S(1)}, u32[]{:S(2)}, u32[]{:S(2)}) collective-permute-start(bf16[1,128,512]{2,1,0:T(8,128)(2,1)S(1)} %get-tuple-element.4), channel_id=1, source_target_pairs={{0,4},{4,0},{1,5},{5,1},{2,6},{6,2},{3,7},{7,3},{8,12},{12,8},{9,1... | collective-permute-start | bytes 393224 | tf_op jit(solution)/shard_map/ppermute | solution.py:114
  44.8 3.4 %collective-permute-done.2 = bf16[1,128,512]{2,1,0:T(8,128)(2,1)S(1)} collective-permute-done((bf16[1,128,512]{2,1,0:T(8,128)(2,1)S(1)}, bf16[1,128,512]{2,1,0:T(8,128)(2,1)S(1)}, u32[]{:S(2)}, u32[]{:S(2)}) %collective-permute-start.2) | collective-permute-done | bytes 131104 | tf_op jit(solution)/shard_map/ppermute | solution.py:114
  48.3 0.1 convert_reduce_fusion
  48.4 0.2 fusion.2
  48.7 0.0 copy-done
  48.7 0.0 copy-done.6
  48.7 0.0 copy-done.7
  48.7 0.4 convolution_convert_fusion.1
  49.0 0.0 copy-done.4
  49.1 0.4 convolution_convert_fusion
  49.5 0.0 copy-start.3
  49.5 2.6 %collective-permute-start.3 = (bf16[128,1024]{1,0:T(8,128)(2,1)S(1)}, bf16[128,1024]{1,0:T(8,128)(2,1)S(1)}, u32[]{:S(2)}, u32[]{:S(2)}) collective-permute-start(bf16[128,1024]{1,0:T(8,128)(2,1)S(1)} %pad_maximum_fusion.3.refs_3_), channel_id=1, source_target_pairs={{0,16},{8,24},{16,0},{24,8},{1,17},{9,25},{17,1},{25,9},{2,18},{10... | collective-permute-start | bytes 786440 | tf_op jit(solution)/shard_map/ppermute | solution.py:171
  52.1 0.0 copy-done.8
  52.1 0.6 dynamic_slice.13
  52.7 1.3 %fusion.17.refs_2_ = f32[128,1]{1,0:T(8,128)} fusion(s32[]{:T(128)S(6)} %mul.36, s32[]{:T(128)} %bitcast.9), kind=kLoop, calls=%fused_computation.42 | loop fusion | flops 384 | bytes 520 | tf_op jit(solution)/shard_map/convert_element_type | solution.py:155
  54.0 1.3 %collective-permute-start.6 = (bf16[128,1024]{1,0:T(8,128)(2,1)S(1)}, bf16[128,1024]{1,0:T(8,128)(2,1)S(1)}, u32[]{:S(2)}, u32[]{:S(2)}) collective-permute-start(bf16[128,1024]{1,0:T(8,128)(2,1)S(1)} %pad_maximum_fusion.3.refs_3_), channel_id=1, source_target_pairs={{8,0},{16,8},{24,16},{9,1},{17,9},{25,17},{10,2},{18,10},{26,18},{... | collective-permute-start | bytes 786440 | tf_op jit(solution)/shard_map/ppermute | solution.py:170
  55.3 4.6 %collective-permute-start.4 = (bf16[128,1024]{1,0:T(8,128)(2,1)S(1)}, bf16[128,1024]{1,0:T(8,128)(2,1)S(1)}, u32[]{:S(2)}, u32[]{:S(2)}) collective-permute-start(bf16[128,1024]{1,0:T(8,128)(2,1)S(1)} %pad_maximum_fusion.3.refs_3_), channel_id=1, source_target_pairs={{0,8},{8,16},{16,24},{1,9},{9,17},{17,25},{2,10},{10,18},{18,26},{... | collective-permute-start | bytes 786440 | tf_op jit(solution)/shard_map/ppermute | solution.py:169
  59.9 2.8 %collective-permute-done.3.refs_4_ = bf16[128,1024]{1,0:T(8,128)(2,1)S(1)} collective-permute-done((bf16[128,1024]{1,0:T(8,128)(2,1)S(1)}, bf16[128,1024]{1,0:T(8,128)(2,1)S(1)}, u32[]{:S(2)}, u32[]{:S(2)}) %collective-permute-start.3) | collective-permute-done | bytes 262176 | tf_op jit(solution)/shard_map/ppermute | solution.py:171
  62.7 1.3 %collective-permute-start.5 = (bf16[128,1024]{1,0:T(8,128)(2,1)S(1)}, bf16[128,1024]{1,0:T(8,128)(2,1)S(1)}, u32[]{:S(2)}, u32[]{:S(2)}) collective-permute-start(bf16[128,1024]{1,0:T(8,128)(2,1)S(1)} %collective-permute-done.3.refs_4_), channel_id=1, source_target_pairs={{16,24},{8,0},{17,25},{9,1},{18,26},{10,2},{19,27},{11,3},{20,28},... | collective-permute-start | bytes 786440 | tf_op jit(solution)/shard_map/ppermute | solution.py:172
  64.0 1.2 %compare_convert_fusion.refs_1_ = f32[1,512]{1,0:T(1,128)} fusion(s32[1,128]{1,0:T(1,128)S(1)} %get-tuple-element.10, s32[1,128]{1,0:T(1,128)S(1)} %get-tuple-element.11, s32[1,128]{1,0:T(1,128)S(1)} %get-tuple-element.12, s32[1,128]{1,0:T(1,128)S(1)} %get-tuple-element.13, s32[]{:T(128)} %bitcast.9), kind=kLoop, calls=%fused_computation.43 | loop fusion | flops 2560 | bytes 4100 | tf_op jit(solution)/shard_map/convert_element_type | solution.py:154
  65.2 2.2 %convolution_convert_fusion.2.refs_0_ = bf16[128,512]{1,0:T(8,128)(2,1)} fusion(bf16[1024,512]{1,0:T(8,128)(2,1)} %param.15, f32[1024]{0:T(1024)S(1)} %copy-done.6, f32[1024]{0:T(1024)S(1)} %copy-done.7, f32[128]{0:T(128)S(1)} %add_sqrt_fusion, f32[128]{0:T(128)S(1)} %broadcast_multiply_fusion, bf16[128,512]{1,0:T(8,128)(2,1)S(1)} %get-tuple-element.5, ...), kind=kOutput, calls=%fused_computation.2 | convolution fusion | flops 136249344 | bytes 1451009 | tf_op jit(solution)/shard_map/dot_general | solution.py:273
  67.4 0.0 collective-permute-done.6
  67.5 0.0 collective-permute-done.4
  67.5 3.5 %collective-permute-done.5 = bf16[128,1024]{1,0:T(8,128)(2,1)S(1)} collective-permute-done((bf16[128,1024]{1,0:T(8,128)(2,1)S(1)}, bf16[128,1024]{1,0:T(8,128)(2,1)S(1)}, u32[]{:S(2)}, u32[]{:S(2)}) %collective-permute-start.5) | collective-permute-done | bytes 262176 | tf_op jit(solution)/shard_map/ppermute | solution.py:172
  71.0 0.8 %broadcast_select_fusion = (bf16[128,1024]{1,0:T(8,128)(2,1)}, bf16[128,1024]{1,0:T(8,128)(2,1)}) fusion(bf16[128,1024]{1,0:T(8,128)(2,1)S(1)} %collective-permute-done.6, bf16[128,1024]{1,0:T(8,128)(2,1)S(1)} %collective-permute-done.5, pred[]{:T(512)S(6)} %le.3, bf16[128,1024]{1,0:T(8,128)(2,1)S(1)} %collective-permute-done.4, pred[]{:T(512)S(6)} %ge.3), kind=kLoop, calls=%fused_computation.37 | loop fusion | flops 262144 | bytes 1310722 | tf_op jit(solution)/shard_map/jit(_where)/select_n | solution.py:177
  71.8 0.0 copy-done.3
  71.8 0.0 copy-done.5
  71.8 4.2 %shard_map.105 = bf16[128,512]{1,0:T(8,128)(2,1)} custom-call(bf16[128,512]{1,0:T(8,128)(2,1)} %convolution_convert_fusion.2.refs_0_, f32[1,512]{1,0:T(1,128)} %compare_convert_fusion.refs_1_, f32[128,1]{1,0:T(8,128)} %fusion.17.refs_2_, bf16[128,1024]{1,0:T(8,128)(2,1)} %copy-done.3, bf16[128,1024]{1,0:T(8,128)(2,1)} %copy-done.5, ...), custom_call_target="tpu_custom_call" | custom-call | flops 268435456 | bytes 1310720 | tf_op jit(solution)/shard_map/pallas_call | solution.py:156
  76.0 0.0 copy-done.2
  (13 shorter events, 0.2 us)
Async XLA Ops:
  0.6 48.0 %copy-start = (bf16[1024,512]{1,0:T(8,128)(2,1)S(1)}, bf16[1024,512]{1,0:T(8,128)(2,1)}, u32[]{:S(2)}) copy-start(bf16[1024,512]{1,0:T(8,128)(2,1)} %param.16) | copy-start | bytes 3145732
  0.6 40.3 %copy-start.1 = (bf16[2,128,512]{2,1,0:T(8,128)(2,1)S(1)}, bf16[2,128,512]{2,1,0:T(8,128)(2,1)}, u32[]{:S(2)}) copy-start(bf16[2,128,512]{2,1,0:T(8,128)(2,1)} %param.9) | copy-start | bytes 786436
  2.6 7.7 %collective-permute-start = (bf16[2,64,512]{2,1,0:T(8,128)(2,1)S(1)}, bf16[2,64,512]{2,1,0:T(8,128)(2,1)S(1)}, u32[]{:S(2)}, u32[]{:S(2)}) collective-permute-start(bf16[2,64,512]{2,1,0:T(8,128)(2,1)S(1)} %get-tuple-element.8), channel_id=1, source_target_pairs={{0,8},{8,16},{16,24},{1,9},{9,17},{17,25},{2,10},{10,18},{18,26},{... | collective-permute-start | bytes 393224 | tf_op jit(solution)/shard_map/ppermute | solution.py:20
  7.5 6.9 %collective-permute-start.1 = (bf16[2,64,512]{2,1,0:T(8,128)(2,1)S(1)}, bf16[2,64,512]{2,1,0:T(8,128)(2,1)S(1)}, u32[]{:S(2)}, u32[]{:S(2)}) collective-permute-start(bf16[2,64,512]{2,1,0:T(8,128)(2,1)S(1)} %get-tuple-element.9), channel_id=1, source_target_pairs={{8,0},{16,8},{24,16},{9,1},{17,9},{25,17},{10,2},{18,10},{26,18},{... | collective-permute-start | bytes 393224 | tf_op jit(solution)/shard_map/ppermute | solution.py:21
  9.5 39.1 %copy-start.6 = (f32[1024]{0:T(1024)S(1)}, f32[1024]{0:T(1024)}, u32[]{:S(2)}) copy-start(f32[1024]{0:T(1024)} %param.14) | copy-start | bytes 12292
  9.5 39.1 %copy-start.7 = (f32[1024]{0:T(1024)S(1)}, f32[1024]{0:T(1024)}, u32[]{:S(2)}) copy-start(f32[1024]{0:T(1024)} %param.13) | copy-start | bytes 12292
  15.4 33.7 %copy-start.4 = (bf16[1024,512]{1,0:T(8,128)(2,1)S(1)}, bf16[1024,512]{1,0:T(8,128)(2,1)}, u32[]{:S(2)}) copy-start(bf16[1024,512]{1,0:T(8,128)(2,1)} %param.17) | copy-start | bytes 3145732
  16.2 35.9 %copy-start.8 = (s32[2]{0:T(128)S(1)}, s32[2]{0:T(128)}, u32[]{:S(2)}) copy-start(s32[2]{0:T(128)} %param.10) | copy-start | bytes 28
  43.2 32.8 %copy-start.2 = (bf16[2,128,512]{2,1,0:T(8,128)(2,1)}, bf16[2,128,512]{2,1,0:T(8,128)(2,1)S(1)}, u32[]{:S(2)}) copy-start(bf16[2,128,512]{2,1,0:T(8,128)(2,1)S(1)} %fusion.9) | copy-start | bytes 786436
  43.3 5.0 %collective-permute-start.2 = (bf16[1,128,512]{2,1,0:T(8,128)(2,1)S(1)}, bf16[1,128,512]{2,1,0:T(8,128)(2,1)S(1)}, u32[]{:S(2)}, u32[]{:S(2)}) collective-permute-start(bf16[1,128,512]{2,1,0:T(8,128)(2,1)S(1)} %get-tuple-element.4), channel_id=1, source_target_pairs={{0,4},{4,0},{1,5},{5,1},{2,6},{6,2},{3,7},{7,3},{8,12},{12,8},{9,1... | collective-permute-start | bytes 393224 | tf_op jit(solution)/shard_map/ppermute | solution.py:114
  49.5 22.3 %copy-start.3 = (bf16[128,1024]{1,0:T(8,128)(2,1)}, bf16[128,1024]{1,0:T(8,128)(2,1)S(1)}, u32[]{:S(2)}) copy-start(bf16[128,1024]{1,0:T(8,128)(2,1)S(1)} %pad_maximum_fusion.3.refs_3_) | copy-start | bytes 786436
  49.5 13.2 %collective-permute-start.3 = (bf16[128,1024]{1,0:T(8,128)(2,1)S(1)}, bf16[128,1024]{1,0:T(8,128)(2,1)S(1)}, u32[]{:S(2)}, u32[]{:S(2)}) collective-permute-start(bf16[128,1024]{1,0:T(8,128)(2,1)S(1)} %pad_maximum_fusion.3.refs_3_), channel_id=1, source_target_pairs={{0,16},{8,24},{16,0},{24,8},{1,17},{9,25},{17,1},{25,9},{2,18},{10... | collective-permute-start | bytes 786440 | tf_op jit(solution)/shard_map/ppermute | solution.py:171
  54.0 13.5 %collective-permute-start.6 = (bf16[128,1024]{1,0:T(8,128)(2,1)S(1)}, bf16[128,1024]{1,0:T(8,128)(2,1)S(1)}, u32[]{:S(2)}, u32[]{:S(2)}) collective-permute-start(bf16[128,1024]{1,0:T(8,128)(2,1)S(1)} %pad_maximum_fusion.3.refs_3_), channel_id=1, source_target_pairs={{8,0},{16,8},{24,16},{9,1},{17,9},{25,17},{10,2},{18,10},{26,18},{... | collective-permute-start | bytes 786440 | tf_op jit(solution)/shard_map/ppermute | solution.py:170
  55.3 12.2 %collective-permute-start.4 = (bf16[128,1024]{1,0:T(8,128)(2,1)S(1)}, bf16[128,1024]{1,0:T(8,128)(2,1)S(1)}, u32[]{:S(2)}, u32[]{:S(2)}) collective-permute-start(bf16[128,1024]{1,0:T(8,128)(2,1)S(1)} %pad_maximum_fusion.3.refs_3_), channel_id=1, source_target_pairs={{0,8},{8,16},{16,24},{1,9},{9,17},{17,25},{2,10},{10,18},{18,26},{... | collective-permute-start | bytes 786440 | tf_op jit(solution)/shard_map/ppermute | solution.py:169
  62.7 9.1 %copy-start.5 = (bf16[128,1024]{1,0:T(8,128)(2,1)}, bf16[128,1024]{1,0:T(8,128)(2,1)S(1)}, u32[]{:S(2)}) copy-start(bf16[128,1024]{1,0:T(8,128)(2,1)S(1)} %collective-permute-done.3.refs_4_) | copy-start | bytes 786436
  62.7 8.3 %collective-permute-start.5 = (bf16[128,1024]{1,0:T(8,128)(2,1)S(1)}, bf16[128,1024]{1,0:T(8,128)(2,1)S(1)}, u32[]{:S(2)}, u32[]{:S(2)}) collective-permute-start(bf16[128,1024]{1,0:T(8,128)(2,1)S(1)} %collective-permute-done.3.refs_4_), channel_id=1, source_target_pairs={{16,24},{8,0},{17,25},{9,1},{18,26},{10,2},{19,27},{11,3},{20,28},... | collective-permute-start | bytes 786440 | tf_op jit(solution)/shard_map/ppermute | solution.py:172

commit v10 on v9

--- a/solution.py
+++ b/solution.py
@@ -23,7 +23,7 @@
     return x
 
 
-def conv_body(x_ref, w_ref, out_ref):
+def conv_body(x_ref, w_ref, res_ref, bias_ref, out_ref):
     pair_groups, recs, chans, lanes = x_ref.shape
     taps = w_ref.shape[3]
     rows = out_ref.shape[1]
@@ -72,10 +72,14 @@
         low = (rest - middle.astype(jnp.float32)).astype(jnp.bfloat16)
         total = lax.dot_general(flip, high, dims, preferred_element_type=jnp.float32)
         total = total + lax.dot_general(flip, middle, dims, preferred_element_type=jnp.float32)
-        out_ref[r] = total + lax.dot_general(flip, low, dims, preferred_element_type=jnp.float32)
-
-
-def hankel_conv(xt, wv, rows):
+        conv = total + lax.dot_general(flip, low, dims, preferred_element_type=jnp.float32)
+        shifted = conv + bias_ref[...]
+        gelu = 0.5 * shifted * (1.0 + lax.erf(shifted * (1.0 / math.sqrt(2.0))))
+        hidden = res_ref[r].astype(jnp.float32) + gelu
+        out_ref[r] = hidden.astype(out_ref.dtype)
+
+
+def hankel_conv(xt, wv, residual, bias, rows):
     groups, recs, chans, lanes = xt.shape
     taps, outs = wv.shape[3], wv.shape[2]
     return pl.pallas_call(
@@ -84,25 +88,28 @@
         in_specs=[
             pl.BlockSpec((2, recs, chans, lanes), lambda g: (g, 0, 0, 0)),
             pl.BlockSpec((2, chans, outs, taps), lambda g: (g, 0, 0, 0)),
+            pl.BlockSpec((recs, rows, 2 * outs), lambda g: (0, 0, g)),
+            pl.BlockSpec((1, 2 * outs), lambda g: (0, g)),
         ],
         out_specs=pl.BlockSpec((recs, rows, 2 * outs), lambda g: (0, 0, g)),
-        out_shape=jax.ShapeDtypeStruct((recs, rows, groups * outs), jnp.float32),
+        out_shape=jax.ShapeDtypeStruct((recs, rows, groups * outs), jnp.bfloat16),
         cost_estimate=pl.CostEstimate(
             flops=2 * groups * recs * rows * taps * chans * outs,
             bytes_accessed=xt.size * 2 + wv.size * 2 + groups * recs * rows * outs * 4,
-            transcendentals=0,
+            transcendentals=recs * rows * groups * outs,
         ),
-    )(xt, wv)
-
-
-def grouped_conv(padded, conv_weight, frame_rows):
+    )(xt, wv, residual, bias)
+
+
+def grouped_conv(padded, conv_weight, masked, conv_bias, frame_rows):
     recs, span = padded.shape[0], padded.shape[1]
     groups_here, taps, group_in, group_out = conv_weight.shape
     lanes = -(-(frame_rows + taps - 1) // 128) * 128
     grouped = jnp.pad(padded, ((0, 0), (0, lanes - span), (0, 0)))
     grouped = jnp.roll(jnp.flip(grouped, axis=1), frame_rows - lanes, axis=1)
     grouped = grouped.reshape(recs, lanes, groups_here, group_in).transpose(2, 0, 3, 1)
-    return hankel_conv(grouped, jnp.transpose(conv_weight, (0, 2, 3, 1)), frame_rows)
+    bias = conv_bias.astype(jnp.float32).reshape(1, -1)
+    return hankel_conv(grouped, jnp.transpose(conv_weight, (0, 2, 3, 1)), masked, bias, frame_rows)
 
 
 def swap_halves(hidden, axis):
@@ -257,11 +264,7 @@
     groups_here, kernel_width, group_in, group_out = conv_weight.shape
     half_width = kernel_width // 2
     padded = padded_2(masked, (("ctx", 1),), half_width)
-    conv_out = grouped_conv(padded, conv_weight, frame_rows)
-    hidden = (
-        masked.astype(jnp.float32)
-        + jax.nn.gelu(conv_out + conv_bias.astype(jnp.float32), approximate=False)
-    ).astype(jnp.bfloat16)
+    hidden = grouped_conv(padded, conv_weight, masked, conv_bias, frame_rows)
     record = swap_halves(hidden, "fsdp")
     own_length = lax.dynamic_index_in_dim(lengths, lax.axis_index("fsdp"), 0, keepdims=False)
     flat = record[0].astype(jnp.float32)

time: 76.4 us -> 75 us (0.982)
  other arithmetic: 8.67 us -> 6.95 us
  local copies, waits for them, and re-layouts: 2.38 us -> 3.32 us
    convert_element_type x2 -> x0, other arithmetic: 2.99 us -> none  [the longest x1 2.3 us: per_device(): hidden = (masked.astype(jnp.float32) + jax.nn.gelu(conv_out + conv_bias.a...]
    reshape x0 -> x1, other arithmetic: none -> 1.26 us  [grouped_conv(): bias = conv_bias.astype(jnp.float32).reshape(1, -1)]
    dynamic_slice x1, local copies, waits for them, and re-layouts: 0.03 us -> 0.98 us  [swap_halves(): theirs = lax.dynamic_index_in_dim(hidden, 1 - place, 0, keepdims=True)]
  transfers between devices with their start and end apart: 7 -> 7, of which waited for: 5 -> 5; matrix products, arithmetic and copies ran while one was open for 8% -> 9% of each run, Pallas kernels for 0% -> 0%
where the time goes in v10:
time: 75 us; the launch traced here: 74.6 us
  Pallas kernels  28.9 us (39%)
  starting transfers between devices  17.6 us (23%)
  waiting for transfers between devices  14.1 us (19%)
  other arithmetic  6.95 us (9%)
  local copies, waits for them, and re-layouts  3.32 us (4%)
  matrix products  2.95 us (4%)
  between operations  0.84 us (1%)
    pallas_call x1, Pallas kernels, hankel_conv(): pl.pallas_call(conv_body, grid=(groups // 2,), in_specs=[pl.BlockSpec((2,...  24.7 us
    ppermute x1, starting transfers between devices, padded_2(): before = lax.ppermute(last, axis, up)  4.94 us
    ppermute x1, starting transfers between devices, gather_line4(): from_below = lax.ppermute(x, axis, [(0, 1), (1, 2), (2, 3)])  4.56 us
    pallas_call x1, Pallas kernels, fused_attention(): pl.pallas_call(attend_body, out_shape=jax.ShapeDtypeStruct((rows, width),...  4.19 us
    ppermute x1, waiting for transfers between devices, padded_2(): after = lax.ppermute(first, axis, down)  4.13 us
    ppermute x1, waiting for transfers between devices, gather_line4(): passed = lax.ppermute(across, axis, [(2, 3), (1, 0)])  3.5 us
    ppermute x1, waiting for transfers between devices, swap_halves(): got = lax.ppermute(theirs, axis, [(0, 1), (1, 0)])  3.45 us
    ppermute x1, waiting for transfers between devices, gather_line4(): across = lax.ppermute(x, axis, [(0, 2), (1, 3), (2, 0), (3, 1)])  2.83 us
  transfers between devices with their start and end apart: 7, of which 5 were waited for; matrix products, arithmetic and copies ran while one was open for 9% of the time, Pallas kernels for 0%

profile of v10, /device:TPU:0, one launch (start us, length us, event | category | flops | bytes accessed | tf_op | source)
XLA Modules:
  0.0 74.6 jit_solution(14494237882498824107)
XLA Ops:
  0.6 0.0 copy-start
  0.7 0.8 %broadcast_compare_fusion = pred[2,128]{1,0:T(4,128)(4,1)S(1)} fusion(s32[128]{0:T(128)S(1)} %iota_add_fusion, s32[2]{0:T(128)} %param.10), kind=kLoop, calls=%fused_computation.29 | loop fusion | flops 256 | bytes 776 | tf_op jit(solution)/shard_map/lt | solution.py:262
  1.5 0.0 copy-start.5
  1.5 0.0 copy-start.6
  1.5 1.1 %broadcast_select_fusion.2.res_ref = bf16[2,128,512]{2,1,0:T(8,128)(2,1)S(1)} fusion(bf16[2,128,512]{2,1,0:T(8,128)(2,1)} %param.9, pred[2,128]{1,0:T(4,128)(4,1)S(1)} %broadcast_compare_fusion), kind=kLoop, calls=%fused_computation.19 | loop fusion | flops 131072 | bytes 524544 | tf_op jit(solution)/shard_map/jit(_where)/select_n | solution.py:263
  2.6 0.0 copy-start.1
  2.6 4.9 %collective-permute-start = (bf16[2,64,512]{2,1,0:T(8,128)(2,1)S(1)}, bf16[2,64,512]{2,1,0:T(8,128)(2,1)S(1)}, u32[]{:S(2)}, u32[]{:S(2)}) collective-permute-start(bf16[2,64,512]{2,1,0:T(8,128)(2,1)S(1)} %get-tuple-element.8), channel_id=1, source_target_pairs={{0,8},{8,16},{16,24},{1,9},{9,17},{17,25},{2,10},{10,18},{18,26},{... | collective-permute-start | bytes 393224 | tf_op jit(solution)/shard_map/ppermute | solution.py:20
  7.5 1.3 %collective-permute-start.1 = (bf16[2,64,512]{2,1,0:T(8,128)(2,1)S(1)}, bf16[2,64,512]{2,1,0:T(8,128)(2,1)S(1)}, u32[]{:S(2)}, u32[]{:S(2)}) collective-permute-start(bf16[2,64,512]{2,1,0:T(8,128)(2,1)S(1)} %get-tuple-element.9), channel_id=1, source_target_pairs={{8,0},{16,8},{24,16},{9,1},{17,9},{25,17},{10,2},{18,10},{26,18},{... | collective-permute-start | bytes 393224 | tf_op jit(solution)/shard_map/ppermute | solution.py:21
  8.9 1.3 %reshape.147 = f32[512]{0:T(512)} convert(bf16[512]{0:T(512)(128)(2,1)} %param.12) | non-fusion elementwise | flops 512 | bytes 3072 | tf_op jit(solution)/shard_map/reshape | solution.py:111
  10.1 0.2 collective-permute-done
  10.3 4.1 %collective-permute-done.1 = bf16[2,64,512]{2,1,0:T(8,128)(2,1)S(1)} collective-permute-done((bf16[2,64,512]{2,1,0:T(8,128)(2,1)S(1)}, bf16[2,64,512]{2,1,0:T(8,128)(2,1)S(1)}, u32[]{:S(2)}, u32[]{:S(2)}) %collective-permute-start.1) | collective-permute-done | bytes 131104 | tf_op jit(solution)/shard_map/ppermute | solution.py:21
  14.4 0.3 slice.24
  14.8 0.3 slice.27
  15.2 0.0 copy-start.3
  15.2 0.2 copy.14
  15.4 0.8 %copy.18 = bf16[2,256,8,64]{1,3,0,2:T(8,128)(2,1)} copy(bf16[2,256,8,64]{1,3,2,0:T(8,128)(2,1)S(1)} %bitcast.24) | data formatting | bytes 1048576 | tf_op jit(solution)/shard_map/reshape | solution.py:110
  16.2 0.0 copy-done.1
  16.2 0.0 copy-start.7
  16.2 24.7 %shard_map.104 = bf16[2,128,512]{2,1,0:T(8,128)(2,1)} custom-call(bf16[8,2,64,256]{3,2,1,0:T(8,128)(2,1)} %bitcast.23, bf16[8,64,64,128]{3,2,1,0:T(8,128)(2,1)} %bitcast.22, bf16[2,128,512]{2,1,0:T(8,128)(2,1)} %copy-done.1, f32[1,512]{1,0:T(1,128)} %bitcast.30), custom_call_target="tpu_custom_call" | custom-call | flops 2147483648 | bytes 9437184 | tf_op jit(solution)/shard_map/pallas_call | solution.py:85
  40.9 1.0 %constant_dynamic-slice_fusion = (bf16[1,128,512]{2,1,0:T(8,128)(2,1)S(1)}, bf16[128,512]{1,0:T(8,128)(2,1)S(1)}) fusion(bf16[2,128,512]{2,1,0:T(8,128)(2,1)} %shard_map.104, s32[]{:T(128)S(6)} %select_n.56, s32[]{:T(128)S(6)} %select_n.55), kind=kLoop, calls=%fused_computation.28 | loop fusion | bytes 524296 | tf_op jit(solution)/shard_map/jit(dynamic_index_in_dim)/dynamic_slice | solution.py:120
  41.9 1.6 %collective-permute-start.2 = (bf16[1,128,512]{2,1,0:T(8,128)(2,1)S(1)}, bf16[1,128,512]{2,1,0:T(8,128)(2,1)S(1)}, u32[]{:S(2)}, u32[]{:S(2)}) collective-permute-start(bf16[1,128,512]{2,1,0:T(8,128)(2,1)S(1)} %get-tuple-element.4), channel_id=1, source_target_pairs={{0,4},{4,0},{1,5},{5,1},{2,6},{6,2},{3,7},{7,3},{8,12},{12,8},{9,1... | collective-permute-start | bytes 393224 | tf_op jit(solution)/shard_map/ppermute | solution.py:121
  43.5 3.4 %collective-permute-done.2 = bf16[1,128,512]{2,1,0:T(8,128)(2,1)S(1)} collective-permute-done((bf16[1,128,512]{2,1,0:T(8,128)(2,1)S(1)}, bf16[1,128,512]{2,1,0:T(8,128)(2,1)S(1)}, u32[]{:S(2)}, u32[]{:S(2)}) %collective-permute-start.2) | collective-permute-done | bytes 131104 | tf_op jit(solution)/shard_map/ppermute | solution.py:121
  46.9 0.1 convert_reduce_fusion
  47.1 0.2 fusion.2
  47.3 0.0 copy-done
  47.3 0.0 copy-done.5
  47.3 0.0 copy-done.6
  47.3 0.4 convolution_convert_fusion.1
  47.7 0.0 copy-done.3
  47.7 0.4 convolution_convert_fusion
  48.1 0.0 copy-start.2
  48.1 2.7 %collective-permute-start.3 = (bf16[128,1024]{1,0:T(8,128)(2,1)S(1)}, bf16[128,1024]{1,0:T(8,128)(2,1)S(1)}, u32[]{:S(2)}, u32[]{:S(2)}) collective-permute-start(bf16[128,1024]{1,0:T(8,128)(2,1)S(1)} %pad_maximum_fusion.3.refs_3_), channel_id=1, source_target_pairs={{0,16},{8,24},{16,0},{24,8},{1,17},{9,25},{17,1},{25,9},{2,18},{10... | collective-permute-start | bytes 786440 | tf_op jit(solution)/shard_map/ppermute | solution.py:178
  50.8 0.0 copy-done.7
  50.8 0.6 dynamic_slice.13
  51.4 1.3 %fusion.6.refs_2_ = f32[128,1]{1,0:T(8,128)} fusion(s32[]{:T(128)S(6)} %mul.21, s32[]{:T(128)} %bitcast.10), kind=kLoop, calls=%fused_computation.22 | loop fusion | flops 384 | bytes 520 | tf_op jit(solution)/shard_map/convert_element_type | solution.py:162
  52.6 1.3 %collective-permute-start.6 = (bf16[128,1024]{1,0:T(8,128)(2,1)S(1)}, bf16[128,1024]{1,0:T(8,128)(2,1)S(1)}, u32[]{:S(2)}, u32[]{:S(2)}) collective-permute-start(bf16[128,1024]{1,0:T(8,128)(2,1)S(1)} %pad_maximum_fusion.3.refs_3_), channel_id=1, source_target_pairs={{8,0},{16,8},{24,16},{9,1},{17,9},{25,17},{10,2},{18,10},{26,18},{... | collective-permute-start | bytes 786440 | tf_op jit(solution)/shard_map/ppermute | solution.py:177
  53.9 4.6 %collective-permute-start.4 = (bf16[128,1024]{1,0:T(8,128)(2,1)S(1)}, bf16[128,1024]{1,0:T(8,128)(2,1)S(1)}, u32[]{:S(2)}, u32[]{:S(2)}) collective-permute-start(bf16[128,1024]{1,0:T(8,128)(2,1)S(1)} %pad_maximum_fusion.3.refs_3_), channel_id=1, source_target_pairs={{0,8},{8,16},{16,24},{1,9},{9,17},{17,25},{2,10},{10,18},{18,26},{... | collective-permute-start | bytes 786440 | tf_op jit(solution)/shard_map/ppermute | solution.py:176
  58.5 2.8 %collective-permute-done.3.refs_4_ = bf16[128,1024]{1,0:T(8,128)(2,1)S(1)} collective-permute-done((bf16[128,1024]{1,0:T(8,128)(2,1)S(1)}, bf16[128,1024]{1,0:T(8,128)(2,1)S(1)}, u32[]{:S(2)}, u32[]{:S(2)}) %collective-permute-start.3) | collective-permute-done | bytes 262176 | tf_op jit(solution)/shard_map/ppermute | solution.py:178
  61.3 1.3 %collective-permute-start.5 = (bf16[128,1024]{1,0:T(8,128)(2,1)S(1)}, bf16[128,1024]{1,0:T(8,128)(2,1)S(1)}, u32[]{:S(2)}, u32[]{:S(2)}) collective-permute-start(bf16[128,1024]{1,0:T(8,128)(2,1)S(1)} %collective-permute-done.3.refs_4_), channel_id=1, source_target_pairs={{16,24},{8,0},{17,25},{9,1},{18,26},{10,2},{19,27},{11,3},{20,28},... | collective-permute-start | bytes 786440 | tf_op jit(solution)/shard_map/ppermute | solution.py:179
  62.6 1.2 %compare_convert_fusion.refs_1_ = f32[1,512]{1,0:T(1,128)} fusion(s32[1,128]{1,0:T(1,128)S(1)} %get-tuple-element.10, s32[1,128]{1,0:T(1,128)S(1)} %get-tuple-element.11, s32[1,128]{1,0:T(1,128)S(1)} %get-tuple-element.12, s32[1,128]{1,0:T(1,128)S(1)} %get-tuple-element.13, s32[]{:T(128)} %bitcast.10), kind=kLoop, calls=%fused_computation.23 | loop fusion | flops 2560 | bytes 4100 | tf_op jit(solution)/shard_map/convert_element_type | solution.py:161
  63.8 2.2 %convolution_convert_fusion.2.refs_0_ = bf16[128,512]{1,0:T(8,128)(2,1)} fusion(bf16[1024,512]{1,0:T(8,128)(2,1)} %param.15, f32[1024]{0:T(1024)S(1)} %copy-done.5, f32[1024]{0:T(1024)S(1)} %copy-done.6, f32[128]{0:T(128)S(1)} %add_sqrt_fusion, f32[128]{0:T(128)S(1)} %broadcast_multiply_fusion, bf16[128,512]{1,0:T(8,128)(2,1)S(1)} %get-tuple-element.5, ...), kind=kOutput, calls=%fused_computation.2 | convolution fusion | flops 136249344 | bytes 1451009 | tf_op jit(solution)/shard_map/dot_general | solution.py:276
  66.1 0.0 collective-permute-done.6
  66.1 0.0 collective-permute-done.4
  66.1 3.5 %collective-permute-done.5 = bf16[128,1024]{1,0:T(8,128)(2,1)S(1)} collective-permute-done((bf16[128,1024]{1,0:T(8,128)(2,1)S(1)}, bf16[128,1024]{1,0:T(8,128)(2,1)S(1)}, u32[]{:S(2)}, u32[]{:S(2)}) %collective-permute-start.5) | collective-permute-done | bytes 262176 | tf_op jit(solution)/shard_map/ppermute | solution.py:179
  69.6 0.8 %broadcast_select_fusion = (bf16[128,1024]{1,0:T(8,128)(2,1)}, bf16[128,1024]{1,0:T(8,128)(2,1)}) fusion(bf16[128,1024]{1,0:T(8,128)(2,1)S(1)} %collective-permute-done.6, bf16[128,1024]{1,0:T(8,128)(2,1)S(1)} %collective-permute-done.5, pred[]{:T(512)S(6)} %le.3, bf16[128,1024]{1,0:T(8,128)(2,1)S(1)} %collective-permute-done.4, pred[]{:T(512)S(6)} %ge.3), kind=kLoop, calls=%fused_computation.17 | loop fusion | flops 262144 | bytes 1310722 | tf_op jit(solution)/shard_map/jit(_where)/select_n | solution.py:184
  70.4 0.0 copy-done.2
  70.4 0.0 copy-done.4
  70.4 4.2 %shard_map.105 = bf16[128,512]{1,0:T(8,128)(2,1)} custom-call(bf16[128,512]{1,0:T(8,128)(2,1)} %convolution_convert_fusion.2.refs_0_, f32[1,512]{1,0:T(1,128)} %compare_convert_fusion.refs_1_, f32[128,1]{1,0:T(8,128)} %fusion.6.refs_2_, bf16[128,1024]{1,0:T(8,128)(2,1)} %copy-done.2, bf16[128,1024]{1,0:T(8,128)(2,1)} %copy-done.4, ...), custom_call_target="tpu_custom_call" | custom-call | flops 268435456 | bytes 1310720 | tf_op jit(solution)/shard_map/pallas_call | solution.py:163
  (10 shorter events, 0.1 us)
Async XLA Ops:
  0.6 46.7 %copy-start = (bf16[1024,512]{1,0:T(8,128)(2,1)S(1)}, bf16[1024,512]{1,0:T(8,128)(2,1)}, u32[]{:S(2)}) copy-start(bf16[1024,512]{1,0:T(8,128)(2,1)} %param.16) | copy-start | bytes 3145732
  1.5 45.8 %copy-start.5 = (f32[1024]{0:T(1024)S(1)}, f32[1024]{0:T(1024)}, u32[]{:S(2)}) copy-start(f32[1024]{0:T(1024)} %param.14) | copy-start | bytes 12292
  1.5 45.8 %copy-start.6 = (f32[1024]{0:T(1024)S(1)}, f32[1024]{0:T(1024)}, u32[]{:S(2)}) copy-start(f32[1024]{0:T(1024)} %param.13) | copy-start | bytes 12292
  2.6 13.7 %copy-start.1 = (bf16[2,128,512]{2,1,0:T(8,128)(2,1)}, bf16[2,128,512]{2,1,0:T(8,128)(2,1)S(1)}, u32[]{:S(2)}) copy-start(bf16[2,128,512]{2,1,0:T(8,128)(2,1)S(1)} %broadcast_select_fusion.2.res_ref) | copy-start | bytes 786436
  2.6 7.7 %collective-permute-start = (bf16[2,64,512]{2,1,0:T(8,128)(2,1)S(1)}, bf16[2,64,512]{2,1,0:T(8,128)(2,1)S(1)}, u32[]{:S(2)}, u32[]{:S(2)}) collective-permute-start(bf16[2,64,512]{2,1,0:T(8,128)(2,1)S(1)} %get-tuple-element.8), channel_id=1, source_target_pairs={{0,8},{8,16},{16,24},{1,9},{9,17},{17,25},{2,10},{10,18},{18,26},{... | collective-permute-start | bytes 393224 | tf_op jit(solution)/shard_map/ppermute | solution.py:20
  7.5 6.9 %collective-permute-start.1 = (bf16[2,64,512]{2,1,0:T(8,128)(2,1)S(1)}, bf16[2,64,512]{2,1,0:T(8,128)(2,1)S(1)}, u32[]{:S(2)}, u32[]{:S(2)}) collective-permute-start(bf16[2,64,512]{2,1,0:T(8,128)(2,1)S(1)} %get-tuple-element.9), channel_id=1, source_target_pairs={{8,0},{16,8},{24,16},{9,1},{17,9},{25,17},{10,2},{18,10},{26,18},{... | collective-permute-start | bytes 393224 | tf_op jit(solution)/shard_map/ppermute | solution.py:21
  15.2 32.5 %copy-start.3 = (bf16[1024,512]{1,0:T(8,128)(2,1)S(1)}, bf16[1024,512]{1,0:T(8,128)(2,1)}, u32[]{:S(2)}) copy-start(bf16[1024,512]{1,0:T(8,128)(2,1)} %param.17) | copy-start | bytes 3145732
  16.2 34.6 %copy-start.7 = (s32[2]{0:T(128)S(1)}, s32[2]{0:T(128)}, u32[]{:S(2)}) copy-start(s32[2]{0:T(128)} %param.10) | copy-start | bytes 28
  41.9 5.0 %collective-permute-start.2 = (bf16[1,128,512]{2,1,0:T(8,128)(2,1)S(1)}, bf16[1,128,512]{2,1,0:T(8,128)(2,1)S(1)}, u32[]{:S(2)}, u32[]{:S(2)}) collective-permute-start(bf16[1,128,512]{2,1,0:T(8,128)(2,1)S(1)} %get-tuple-element.4), channel_id=1, source_target_pairs={{0,4},{4,0},{1,5},{5,1},{2,6},{6,2},{3,7},{7,3},{8,12},{12,8},{9,1... | collective-permute-start | bytes 393224 | tf_op jit(solution)/shard_map/ppermute | solution.py:121
  48.1 22.3 %copy-start.2 = (bf16[128,1024]{1,0:T(8,128)(2,1)}, bf16[128,1024]{1,0:T(8,128)(2,1)S(1)}, u32[]{:S(2)}) copy-start(bf16[128,1024]{1,0:T(8,128)(2,1)S(1)} %pad_maximum_fusion.3.refs_3_) | copy-start | bytes 786436
  48.1 13.2 %collective-permute-start.3 = (bf16[128,1024]{1,0:T(8,128)(2,1)S(1)}, bf16[128,1024]{1,0:T(8,128)(2,1)S(1)}, u32[]{:S(2)}, u32[]{:S(2)}) collective-permute-start(bf16[128,1024]{1,0:T(8,128)(2,1)S(1)} %pad_maximum_fusion.3.refs_3_), channel_id=1, source_target_pairs={{0,16},{8,24},{16,0},{24,8},{1,17},{9,25},{17,1},{25,9},{2,18},{10... | collective-permute-start | bytes 786440 | tf_op jit(solution)/shard_map/ppermute | solution.py:178
  52.6 13.4 %collective-permute-start.6 = (bf16[128,1024]{1,0:T(8,128)(2,1)S(1)}, bf16[128,1024]{1,0:T(8,128)(2,1)S(1)}, u32[]{:S(2)}, u32[]{:S(2)}) collective-permute-start(bf16[128,1024]{1,0:T(8,128)(2,1)S(1)} %pad_maximum_fusion.3.refs_3_), channel_id=1, source_target_pairs={{8,0},{16,8},{24,16},{9,1},{17,9},{25,17},{10,2},{18,10},{26,18},{... | collective-permute-start | bytes 786440 | tf_op jit(solution)/shard_map/ppermute | solution.py:177
  53.9 12.2 %collective-permute-start.4 = (bf16[128,1024]{1,0:T(8,128)(2,1)S(1)}, bf16[128,1024]{1,0:T(8,128)(2,1)S(1)}, u32[]{:S(2)}, u32[]{:S(2)}) collective-permute-start(bf16[128,1024]{1,0:T(8,128)(2,1)S(1)} %pad_maximum_fusion.3.refs_3_), channel_id=1, source_target_pairs={{0,8},{8,16},{16,24},{1,9},{9,17},{17,25},{2,10},{10,18},{18,26},{... | collective-permute-start | bytes 786440 | tf_op jit(solution)/shard_map/ppermute | solution.py:176
  61.3 9.1 %copy-start.4 = (bf16[128,1024]{1,0:T(8,128)(2,1)}, bf16[128,1024]{1,0:T(8,128)(2,1)S(1)}, u32[]{:S(2)}) copy-start(bf16[128,1024]{1,0:T(8,128)(2,1)S(1)} %collective-permute-done.3.refs_4_) | copy-start | bytes 786436
  61.3 8.3 %collective-permute-start.5 = (bf16[128,1024]{1,0:T(8,128)(2,1)S(1)}, bf16[128,1024]{1,0:T(8,128)(2,1)S(1)}, u32[]{:S(2)}, u32[]{:S(2)}) collective-permute-start(bf16[128,1024]{1,0:T(8,128)(2,1)S(1)} %collective-permute-done.3.refs_4_), channel_id=1, source_target_pairs={{16,24},{8,0},{17,25},{9,1},{18,26},{10,2},{19,27},{11,3},{20,28},... | collective-permute-start | bytes 786440 | tf_op jit(solution)/shard_map/ppermute | solution.py:179

commit v11 on v10

--- a/solution.py
+++ b/solution.py
@@ -8,6 +8,22 @@
 from jax.experimental.pallas import tpu as pltpu
 
 HD = 64
+
+
+def halo_masked(frames_in, masked, lengths, axis, width):
+    size, place = lax.axis_size(axis), lax.axis_index(axis)
+    rows = frames_in.shape[1]
+    up = [(i, i + 1) for i in range(size - 1)]
+    down = [(i + 1, i) for i in range(size - 1)]
+    before = lax.ppermute(frames_in[:, rows - width :], axis, up)
+    after = lax.ppermute(frames_in[:, :width], axis, down)
+    steps = jnp.arange(width, dtype=jnp.int32)
+    keep_before = (place * rows - width + steps)[None, :] < lengths[:, None]
+    keep_after = ((place + 1) * rows + steps)[None, :] < lengths[:, None]
+    zero = jnp.zeros((), frames_in.dtype)
+    before = jnp.where(keep_before[:, :, None], before, zero)
+    after = jnp.where(keep_after[:, :, None], after, zero)
+    return jnp.concatenate([before, masked, after], axis=1)
 
 
 def padded_2(x, sides, width):
@@ -263,7 +279,7 @@
     masked = jnp.where(live[:, :, None], frames_in, jnp.zeros((), frames_in.dtype))
     groups_here, kernel_width, group_in, group_out = conv_weight.shape
     half_width = kernel_width // 2
-    padded = padded_2(masked, (("ctx", 1),), half_width)
+    padded = halo_masked(frames_in, masked, lengths, "ctx", half_width)
     hidden = grouped_conv(padded, conv_weight, masked, conv_bias, frame_rows)
     record = swap_halves(hidden, "fsdp")
     own_length = lax.dynamic_index_in_dim(lengths, lax.axis_index("fsdp"), 0, keepdims=False)

time: 75 us -> 74.9 us (level)
  waiting for transfers between devices: 14.1 us -> 11.7 us
  local copies, waits for them, and re-layouts: 3.32 us -> 4.38 us
  other arithmetic: 6.95 us -> 7.82 us
    ppermute x2, waiting for transfers between devices: 4.3 us -> 1.57 us  [the longest x1 1.57 us: halo_masked(): after = lax.ppermute(frames_in[:, :width], axis, down)]
    slice x1, local copies, waits for them, and re-layouts: 0.02 us -> 1.08 us  [halo_masked(): before = lax.ppermute(frames_in[:, rows - width:], axis, up)]
    lt x0 -> x1, other arithmetic: none -> 0.77 us  [halo_masked(): keep_before = (place * rows - width + steps)[None, :] < lengths[:, None]]
  transfers between devices with their start and end apart: 7 -> 7, of which waited for: 5 -> 4; matrix products, arithmetic and copies ran while one was open for 9% -> 12% of each run, Pallas kernels for 0% -> 0%
where the time goes in v11:
time: 74.9 us; the launch traced here: 74.2 us
  Pallas kernels  28.9 us (39%)
  starting transfers between devices  17.6 us (23%)
  waiting for transfers between devices  11.7 us (16%)
  other arithmetic  7.82 us (10%)
  local copies, waits for them, and re-layouts  4.38 us (6%)
  matrix products  2.97 us (4%)
  between operations  0.86 us (1%)
    pallas_call x1, Pallas kernels, hankel_conv(): pl.pallas_call(conv_body, grid=(groups // 2,), in_specs=[pl.BlockSpec((2,...  24.7 us
    ppermute x1, starting transfers between devices, halo_masked(): before = lax.ppermute(frames_in[:, rows - width:], axis, up)  4.94 us
    ppermute x1, starting transfers between devices, gather_line4(): from_below = lax.ppermute(x, axis, [(0, 1), (1, 2), (2, 3)])  4.56 us
    pallas_call x1, Pallas kernels, fused_attention(): pl.pallas_call(attend_body, out_shape=jax.ShapeDtypeStruct((rows, width),...  4.18 us
    ppermute x1, waiting for transfers between devices, gather_line4(): passed = lax.ppermute(across, axis, [(2, 3), (1, 0)])  3.49 us
    ppermute x1, waiting for transfers between devices, swap_halves(): got = lax.ppermute(theirs, axis, [(0, 1), (1, 0)])  3.45 us
    ppermute x1, waiting for transfers between devices, gather_line4(): across = lax.ppermute(x, axis, [(0, 2), (1, 3), (2, 0), (3, 1)])  3.23 us
    ppermute x1, starting transfers between devices, gather_line4(): across = lax.ppermute(x, axis, [(0, 2), (1, 3), (2, 0), (3, 1)])  2.66 us
  transfers between devices with their start and end apart: 7, of which 4 were waited for; matrix products, arithmetic and copies ran while one was open for 12% of the time, Pallas kernels for 0%

profile of v11, /device:TPU:0, one launch (start us, length us, event | category | flops | bytes accessed | tf_op | source)
XLA Modules:
  0.0 74.2 jit_solution(11815808461292311937)
XLA Ops:
  0.6 0.0 copy-start
  0.6 1.1 %fusion.11 = (bf16[2,64,512]{2,1,0:T(8,128)(2,1)S(1)}, bf16[2,64,512]{2,1,0:T(8,128)(2,1)S(1)}) fusion(bf16[2,128,512]{2,1,0:T(8,128)(2,1)} %param.9), kind=kLoop, calls=%fused_computation.39 | loop fusion | bytes 524288 | tf_op jit(solution)/shard_map/slice | solution.py:18
  1.7 4.9 %collective-permute-start = (bf16[2,64,512]{2,1,0:T(8,128)(2,1)S(1)}, bf16[2,64,512]{2,1,0:T(8,128)(2,1)S(1)}, u32[]{:S(2)}, u32[]{:S(2)}) collective-permute-start(bf16[2,64,512]{2,1,0:T(8,128)(2,1)S(1)} %get-tuple-element.8), channel_id=1, source_target_pairs={{0,8},{8,16},{16,24},{1,9},{9,17},{17,25},{2,10},{10,18},{18,26},{... | collective-permute-start | bytes 393224 | tf_op jit(solution)/shard_map/ppermute | solution.py:18
  6.7 1.3 %collective-permute-start.1 = (bf16[2,64,512]{2,1,0:T(8,128)(2,1)S(1)}, bf16[2,64,512]{2,1,0:T(8,128)(2,1)S(1)}, u32[]{:S(2)}, u32[]{:S(2)}) collective-permute-start(bf16[2,64,512]{2,1,0:T(8,128)(2,1)S(1)} %get-tuple-element.9), channel_id=1, source_target_pairs={{8,0},{16,8},{24,16},{9,1},{17,9},{25,17},{10,2},{18,10},{26,18},{... | collective-permute-start | bytes 393224 | tf_op jit(solution)/shard_map/ppermute | solution.py:19
  8.0 1.3 %reshape.207 = f32[512]{0:T(512)} convert(bf16[512]{0:T(512)(128)(2,1)} %param.12) | non-fusion elementwise | flops 512 | bytes 3072 | tf_op jit(solution)/shard_map/reshape | solution.py:127
  9.3 0.7 broadcast_compare_fusion.1
  10.0 1.1 %broadcast_select_fusion.2.res_ref = bf16[2,128,512]{2,1,0:T(8,128)(2,1)S(1)} fusion(bf16[2,128,512]{2,1,0:T(8,128)(2,1)} %param.9, pred[2,128]{1,0:T(4,128)(4,1)S(1)} %broadcast_compare_fusion.1), kind=kLoop, calls=%fused_computation.19 | loop fusion | flops 131072 | bytes 524544 | tf_op jit(solution)/shard_map/jit(_where)/select_n | solution.py:279
  11.1 0.0 copy-start.1
  11.1 0.8 %broadcast_compare_fusion.2 = (pred[2,64]{1,0:T(4,128)(4,1)S(1)}, pred[2,64]{1,0:T(4,128)(4,1)S(1)}) fusion(s32[64]{0:T(128)S(1)} %get-tuple-element.13, s32[2]{0:T(128)} %param.10, s32[64]{0:T(128)S(1)} %get-tuple-element.12), kind=kLoop, calls=%fused_computation.35 | loop fusion | flops 256 | bytes 776 | tf_op jit(solution)/shard_map/lt | solution.py:21
  11.9 0.0 collective-permute-done
  11.9 0.1 broadcast_select_fusion.4
  12.0 1.6 %collective-permute-done.1 = bf16[2,64,512]{2,1,0:T(8,128)(2,1)S(1)} collective-permute-done((bf16[2,64,512]{2,1,0:T(8,128)(2,1)S(1)}, bf16[2,64,512]{2,1,0:T(8,128)(2,1)S(1)}, u32[]{:S(2)}, u32[]{:S(2)}) %collective-permute-start.1) | collective-permute-done | bytes 131104 | tf_op jit(solution)/shard_map/ppermute | solution.py:19
  13.5 0.1 broadcast_select_fusion.3
  13.7 0.3 slice.24
  14.0 0.3 slice.27
  14.4 0.0 copy-start.4
  14.4 0.2 copy.14
  14.6 0.8 %copy.19 = bf16[2,256,8,64]{1,3,0,2:T(8,128)(2,1)} copy(bf16[2,256,8,64]{1,3,2,0:T(8,128)(2,1)S(1)} %bitcast.24) | data formatting | bytes 1048576 | tf_op jit(solution)/shard_map/reshape | solution.py:126
  15.4 0.0 copy-done.1
  15.4 24.7 %shard_map.104 = bf16[2,128,512]{2,1,0:T(8,128)(2,1)} custom-call(bf16[8,2,64,256]{3,2,1,0:T(8,128)(2,1)} %bitcast.23, bf16[8,64,64,128]{3,2,1,0:T(8,128)(2,1)} %bitcast.22, bf16[2,128,512]{2,1,0:T(8,128)(2,1)} %copy-done.1, f32[1,512]{1,0:T(1,128)} %bitcast.30), custom_call_target="tpu_custom_call" | custom-call | flops 2147483648 | bytes 9437184 | tf_op jit(solution)/shard_map/pallas_call | solution.py:101
  40.1 1.0 %constant_dynamic-slice_fusion = (bf16[1,128,512]{2,1,0:T(8,128)(2,1)S(1)}, bf16[128,512]{1,0:T(8,128)(2,1)S(1)}) fusion(bf16[2,128,512]{2,1,0:T(8,128)(2,1)} %shard_map.104, s32[]{:T(128)S(6)} %select_n.65, s32[]{:T(128)S(6)} %select_n.64), kind=kLoop, calls=%fused_computation.30 | loop fusion | bytes 524296 | tf_op jit(solution)/shard_map/jit(dynamic_index_in_dim)/dynamic_slice | solution.py:136
  41.1 1.6 %collective-permute-start.2 = (bf16[1,128,512]{2,1,0:T(8,128)(2,1)S(1)}, bf16[1,128,512]{2,1,0:T(8,128)(2,1)S(1)}, u32[]{:S(2)}, u32[]{:S(2)}) collective-permute-start(bf16[1,128,512]{2,1,0:T(8,128)(2,1)S(1)} %get-tuple-element.4), channel_id=1, source_target_pairs={{0,4},{4,0},{1,5},{5,1},{2,6},{6,2},{3,7},{7,3},{8,12},{12,8},{9,1... | collective-permute-start | bytes 393224 | tf_op jit(solution)/shard_map/ppermute | solution.py:137
  42.7 3.4 %collective-permute-done.2 = bf16[1,128,512]{2,1,0:T(8,128)(2,1)S(1)} collective-permute-done((bf16[1,128,512]{2,1,0:T(8,128)(2,1)S(1)}, bf16[1,128,512]{2,1,0:T(8,128)(2,1)S(1)}, u32[]{:S(2)}, u32[]{:S(2)}) %collective-permute-start.2) | collective-permute-done | bytes 131104 | tf_op jit(solution)/shard_map/ppermute | solution.py:137
  46.2 0.1 convert_reduce_fusion
  46.3 0.2 fusion.2
  46.5 0.0 copy-done
  46.5 0.0 copy-done.6
  46.5 0.0 copy-done.7
  46.6 0.4 convolution_convert_fusion.1
  46.9 0.0 copy-done.4
  46.9 0.4 convolution_convert_fusion
  47.3 0.0 copy-start.2
  47.3 2.7 %collective-permute-start.3 = (bf16[128,1024]{1,0:T(8,128)(2,1)S(1)}, bf16[128,1024]{1,0:T(8,128)(2,1)S(1)}, u32[]{:S(2)}, u32[]{:S(2)}) collective-permute-start(bf16[128,1024]{1,0:T(8,128)(2,1)S(1)} %pad_maximum_fusion.3.refs_3_), channel_id=1, source_target_pairs={{0,16},{8,24},{16,0},{24,8},{1,17},{9,25},{17,1},{25,9},{2,18},{10... | collective-permute-start | bytes 786440 | tf_op jit(solution)/shard_map/ppermute | solution.py:194
  50.0 0.0 copy-done.3
  50.0 0.6 dynamic_slice.13
  50.6 1.3 %fusion.6.refs_2_ = f32[128,1]{1,0:T(8,128)} fusion(s32[]{:T(128)S(6)} %mul.25, s32[]{:T(128)} %bitcast.10), kind=kLoop, calls=%fused_computation.24 | loop fusion | flops 384 | bytes 520 | tf_op jit(solution)/shard_map/convert_element_type | solution.py:178
  51.9 1.3 %collective-permute-start.6 = (bf16[128,1024]{1,0:T(8,128)(2,1)S(1)}, bf16[128,1024]{1,0:T(8,128)(2,1)S(1)}, u32[]{:S(2)}, u32[]{:S(2)}) collective-permute-start(bf16[128,1024]{1,0:T(8,128)(2,1)S(1)} %pad_maximum_fusion.3.refs_3_), channel_id=1, source_target_pairs={{8,0},{16,8},{24,16},{9,1},{17,9},{25,17},{10,2},{18,10},{26,18},{... | collective-permute-start | bytes 786440 | tf_op jit(solution)/shard_map/ppermute | solution.py:193
  53.2 4.6 %collective-permute-start.4 = (bf16[128,1024]{1,0:T(8,128)(2,1)S(1)}, bf16[128,1024]{1,0:T(8,128)(2,1)S(1)}, u32[]{:S(2)}, u32[]{:S(2)}) collective-permute-start(bf16[128,1024]{1,0:T(8,128)(2,1)S(1)} %pad_maximum_fusion.3.refs_3_), channel_id=1, source_target_pairs={{0,8},{8,16},{16,24},{1,9},{9,17},{17,25},{2,10},{10,18},{18,26},{... | collective-permute-start | bytes 786440 | tf_op jit(solution)/shard_map/ppermute | solution.py:192
  57.7 3.2 %collective-permute-done.3.refs_4_ = bf16[128,1024]{1,0:T(8,128)(2,1)S(1)} collective-permute-done((bf16[128,1024]{1,0:T(8,128)(2,1)S(1)}, bf16[128,1024]{1,0:T(8,128)(2,1)S(1)}, u32[]{:S(2)}, u32[]{:S(2)}) %collective-permute-start.3) | collective-permute-done | bytes 262176 | tf_op jit(solution)/shard_map/ppermute | solution.py:194
  61.0 1.3 %collective-permute-start.5 = (bf16[128,1024]{1,0:T(8,128)(2,1)S(1)}, bf16[128,1024]{1,0:T(8,128)(2,1)S(1)}, u32[]{:S(2)}, u32[]{:S(2)}) collective-permute-start(bf16[128,1024]{1,0:T(8,128)(2,1)S(1)} %collective-permute-done.3.refs_4_), channel_id=1, source_target_pairs={{16,24},{8,0},{17,25},{9,1},{18,26},{10,2},{19,27},{11,3},{20,28},... | collective-permute-start | bytes 786440 | tf_op jit(solution)/shard_map/ppermute | solution.py:195
  62.2 1.2 %compare_convert_fusion.refs_1_ = f32[1,512]{1,0:T(1,128)} fusion(s32[1,128]{1,0:T(1,128)S(1)} %get-tuple-element.14, s32[1,128]{1,0:T(1,128)S(1)} %get-tuple-element.15, s32[1,128]{1,0:T(1,128)S(1)} %get-tuple-element.16, s32[1,128]{1,0:T(1,128)S(1)} %get-tuple-element.17, s32[]{:T(128)} %bitcast.10), kind=kLoop, calls=%fused_computation.25 | loop fusion | flops 2560 | bytes 4100 | tf_op jit(solution)/shard_map/convert_element_type | solution.py:177
  63.5 2.2 %convolution_convert_fusion.2.refs_0_ = bf16[128,512]{1,0:T(8,128)(2,1)} fusion(bf16[1024,512]{1,0:T(8,128)(2,1)} %param.15, f32[1024]{0:T(1024)S(1)} %copy-done.6, f32[1024]{0:T(1024)S(1)} %copy-done.7, f32[128]{0:T(128)S(1)} %add_sqrt_fusion, f32[128]{0:T(128)S(1)} %broadcast_multiply_fusion, bf16[128,512]{1,0:T(8,128)(2,1)S(1)} %get-tuple-element.5, ...), kind=kOutput, calls=%fused_computation.2 | convolution fusion | flops 136249344 | bytes 1451009 | tf_op jit(solution)/shard_map/dot_general | solution.py:292
  65.7 0.0 collective-permute-done.6
  65.7 0.0 collective-permute-done.4
  65.7 3.5 %collective-permute-done.5 = bf16[128,1024]{1,0:T(8,128)(2,1)S(1)} collective-permute-done((bf16[128,1024]{1,0:T(8,128)(2,1)S(1)}, bf16[128,1024]{1,0:T(8,128)(2,1)S(1)}, u32[]{:S(2)}, u32[]{:S(2)}) %collective-permute-start.5) | collective-permute-done | bytes 262176 | tf_op jit(solution)/shard_map/ppermute | solution.py:195
  69.2 0.9 %broadcast_select_fusion = (bf16[128,1024]{1,0:T(8,128)(2,1)}, bf16[128,1024]{1,0:T(8,128)(2,1)}) fusion(bf16[128,1024]{1,0:T(8,128)(2,1)S(1)} %collective-permute-done.6, bf16[128,1024]{1,0:T(8,128)(2,1)S(1)} %collective-permute-done.5, pred[]{:T(512)S(6)} %le.3, bf16[128,1024]{1,0:T(8,128)(2,1)S(1)} %collective-permute-done.4, pred[]{:T(512)S(6)} %ge.3), kind=kLoop, calls=%fused_computation.17 | loop fusion | flops 262144 | bytes 1310722 | tf_op jit(solution)/shard_map/jit(_where)/select_n | solution.py:200
  70.1 0.0 copy-done.2
  70.1 4.2 %shard_map.105 = bf16[128,512]{1,0:T(8,128)(2,1)} custom-call(bf16[128,512]{1,0:T(8,128)(2,1)} %convolution_convert_fusion.2.refs_0_, f32[1,512]{1,0:T(1,128)} %compare_convert_fusion.refs_1_, f32[128,1]{1,0:T(8,128)} %fusion.6.refs_2_, bf16[128,1024]{1,0:T(8,128)(2,1)} %copy-done.2, bf16[128,1024]{1,0:T(8,128)(2,1)} %copy-done.5, ...), custom_call_target="tpu_custom_call" | custom-call | flops 268435456 | bytes 1310720 | tf_op jit(solution)/shard_map/pallas_call | solution.py:179
  (14 shorter events, 0.1 us)
Async XLA Ops:
  0.6 45.9 %copy-start = (bf16[1024,512]{1,0:T(8,128)(2,1)S(1)}, bf16[1024,512]{1,0:T(8,128)(2,1)}, u32[]{:S(2)}) copy-start(bf16[1024,512]{1,0:T(8,128)(2,1)} %param.16) | copy-start | bytes 3145732
  1.7 10.1 %collective-permute-start = (bf16[2,64,512]{2,1,0:T(8,128)(2,1)S(1)}, bf16[2,64,512]{2,1,0:T(8,128)(2,1)S(1)}, u32[]{:S(2)}, u32[]{:S(2)}) collective-permute-start(bf16[2,64,512]{2,1,0:T(8,128)(2,1)S(1)} %get-tuple-element.8), channel_id=1, source_target_pairs={{0,8},{8,16},{16,24},{1,9},{9,17},{17,25},{2,10},{10,18},{18,26},{... | collective-permute-start | bytes 393224 | tf_op jit(solution)/shard_map/ppermute | solution.py:18
  6.7 6.9 %collective-permute-start.1 = (bf16[2,64,512]{2,1,0:T(8,128)(2,1)S(1)}, bf16[2,64,512]{2,1,0:T(8,128)(2,1)S(1)}, u32[]{:S(2)}, u32[]{:S(2)}) collective-permute-start(bf16[2,64,512]{2,1,0:T(8,128)(2,1)S(1)} %get-tuple-element.9), channel_id=1, source_target_pairs={{8,0},{16,8},{24,16},{9,1},{17,9},{25,17},{10,2},{18,10},{26,18},{... | collective-permute-start | bytes 393224 | tf_op jit(solution)/shard_map/ppermute | solution.py:19
  10.0 36.6 %copy-start.6 = (f32[1024]{0:T(1024)S(1)}, f32[1024]{0:T(1024)}, u32[]{:S(2)}) copy-start(f32[1024]{0:T(1024)} %param.14) | copy-start | bytes 12292
  10.0 36.6 %copy-start.7 = (f32[1024]{0:T(1024)S(1)}, f32[1024]{0:T(1024)}, u32[]{:S(2)}) copy-start(f32[1024]{0:T(1024)} %param.13) | copy-start | bytes 12292
  11.1 4.4 %copy-start.1 = (bf16[2,128,512]{2,1,0:T(8,128)(2,1)}, bf16[2,128,512]{2,1,0:T(8,128)(2,1)S(1)}, u32[]{:S(2)}) copy-start(bf16[2,128,512]{2,1,0:T(8,128)(2,1)S(1)} %broadcast_select_fusion.2.res_ref) | copy-start | bytes 786436
  14.4 32.5 %copy-start.4 = (bf16[1024,512]{1,0:T(8,128)(2,1)S(1)}, bf16[1024,512]{1,0:T(8,128)(2,1)}, u32[]{:S(2)}) copy-start(bf16[1024,512]{1,0:T(8,128)(2,1)} %param.17) | copy-start | bytes 3145732
  15.4 34.6 %copy-start.3 = (s32[2]{0:T(128)S(1)}, s32[2]{0:T(128)}, u32[]{:S(2)}) copy-start(s32[2]{0:T(128)} %param.10) | copy-start | bytes 28
  41.1 5.0 %collective-permute-start.2 = (bf16[1,128,512]{2,1,0:T(8,128)(2,1)S(1)}, bf16[1,128,512]{2,1,0:T(8,128)(2,1)S(1)}, u32[]{:S(2)}, u32[]{:S(2)}) collective-permute-start(bf16[1,128,512]{2,1,0:T(8,128)(2,1)S(1)} %get-tuple-element.4), channel_id=1, source_target_pairs={{0,4},{4,0},{1,5},{5,1},{2,6},{6,2},{3,7},{7,3},{8,12},{12,8},{9,1... | collective-permute-start | bytes 393224 | tf_op jit(solution)/shard_map/ppermute | solution.py:137
  47.3 22.7 %copy-start.2 = (bf16[128,1024]{1,0:T(8,128)(2,1)}, bf16[128,1024]{1,0:T(8,128)(2,1)S(1)}, u32[]{:S(2)}) copy-start(bf16[128,1024]{1,0:T(8,128)(2,1)S(1)} %pad_maximum_fusion.3.refs_3_) | copy-start | bytes 786436
  47.3 13.6 %collective-permute-start.3 = (bf16[128,1024]{1,0:T(8,128)(2,1)S(1)}, bf16[128,1024]{1,0:T(8,128)(2,1)S(1)}, u32[]{:S(2)}, u32[]{:S(2)}) collective-permute-start(bf16[128,1024]{1,0:T(8,128)(2,1)S(1)} %pad_maximum_fusion.3.refs_3_), channel_id=1, source_target_pairs={{0,16},{8,24},{16,0},{24,8},{1,17},{9,25},{17,1},{25,9},{2,18},{10... | collective-permute-start | bytes 786440 | tf_op jit(solution)/shard_map/ppermute | solution.py:194
  51.9 13.9 %collective-permute-start.6 = (bf16[128,1024]{1,0:T(8,128)(2,1)S(1)}, bf16[128,1024]{1,0:T(8,128)(2,1)S(1)}, u32[]{:S(2)}, u32[]{:S(2)}) collective-permute-start(bf16[128,1024]{1,0:T(8,128)(2,1)S(1)} %pad_maximum_fusion.3.refs_3_), channel_id=1, source_target_pairs={{8,0},{16,8},{24,16},{9,1},{17,9},{25,17},{10,2},{18,10},{26,18},{... | collective-permute-start | bytes 786440 | tf_op jit(solution)/shard_map/ppermute | solution.py:193
  53.2 12.6 %collective-permute-start.4 = (bf16[128,1024]{1,0:T(8,128)(2,1)S(1)}, bf16[128,1024]{1,0:T(8,128)(2,1)S(1)}, u32[]{:S(2)}, u32[]{:S(2)}) collective-permute-start(bf16[128,1024]{1,0:T(8,128)(2,1)S(1)} %pad_maximum_fusion.3.refs_3_), channel_id=1, source_target_pairs={{0,8},{8,16},{16,24},{1,9},{9,17},{17,25},{2,10},{10,18},{18,26},{... | collective-permute-start | bytes 786440 | tf_op jit(solution)/shard_map/ppermute | solution.py:192
  61.0 9.1 %copy-start.5 = (bf16[128,1024]{1,0:T(8,128)(2,1)}, bf16[128,1024]{1,0:T(8,128)(2,1)S(1)}, u32[]{:S(2)}) copy-start(bf16[128,1024]{1,0:T(8,128)(2,1)S(1)} %collective-permute-done.3.refs_4_) | copy-start | bytes 786436
  61.0 8.3 %collective-permute-start.5 = (bf16[128,1024]{1,0:T(8,128)(2,1)S(1)}, bf16[128,1024]{1,0:T(8,128)(2,1)S(1)}, u32[]{:S(2)}, u32[]{:S(2)}) collective-permute-start(bf16[128,1024]{1,0:T(8,128)(2,1)S(1)} %collective-permute-done.3.refs_4_), channel_id=1, source_target_pairs={{16,24},{8,0},{17,25},{9,1},{18,26},{10,2},{19,27},{11,3},{20,28},... | collective-permute-start | bytes 786440 | tf_op jit(solution)/shard_map/ppermute | solution.py:195

commit v12 on v8

--- a/solution.py
+++ b/solution.py
@@ -23,17 +23,17 @@
     return x
 
 
-def conv_body(x_ref, w_ref, out_ref):
-    recs, chans, lanes = x_ref.shape[1], x_ref.shape[2], x_ref.shape[3]
+def conv_body(x_ref, w_ref, res_ref, bias_ref, out_ref):
+    pair_groups, recs, chans, lanes = x_ref.shape
     taps = w_ref.shape[3]
-    rows = out_ref.shape[2]
+    rows = out_ref.shape[1]
     outs = w_ref.shape[2]
 
-    def octet_step(q, acc):
+    def octet_step(group, q, acc):
         base = pl.multiple_of(q * 8, 8)
         hankels = []
         for r in range(recs):
-            block = x_ref[0, r, pl.ds(base, 8), :]
+            block = x_ref[group, r, pl.ds(base, 8), :]
             per_chan = []
             for c in range(8):
                 row = jnp.broadcast_to(block[c : c + 1, :], (taps, lanes))
@@ -49,12 +49,17 @@
                 axis=0,
             )
             lhs = jnp.concatenate(
-                [w_ref[0, base + 2 * pair], w_ref[0, base + 2 * pair + 1]], axis=1
+                [w_ref[group, base + 2 * pair], w_ref[group, base + 2 * pair + 1]], axis=1
             )
             acc = acc + jnp.dot(lhs, rhs, preferred_element_type=jnp.float32)
         return acc
 
-    acc = lax.fori_loop(0, chans // 8, octet_step, jnp.zeros((outs, recs * rows), jnp.float32), unroll=4)
+    def both_groups(q, accs):
+        return tuple(octet_step(group, q, acc) for group, acc in enumerate(accs))
+
+    start = tuple(jnp.zeros((outs, recs * rows), jnp.float32) for _ in range(pair_groups))
+    accs = lax.fori_loop(0, chans // 8, both_groups, start, unroll=2)
+    acc = jnp.concatenate(accs, axis=0)
     across = lax.broadcasted_iota(jnp.int32, (rows, rows), 0) + lax.broadcasted_iota(
         jnp.int32, (rows, rows), 1
     )
@@ -68,36 +73,44 @@
         low = (rest - middle.astype(jnp.float32)).astype(jnp.bfloat16)
         total = lax.dot_general(flip, high, dims, preferred_element_type=jnp.float32)
         total = total + lax.dot_general(flip, middle, dims, preferred_element_type=jnp.float32)
-        out_ref[0, r] = total + lax.dot_general(flip, low, dims, preferred_element_type=jnp.float32)
-
-
-def hankel_conv(xt, wv, rows):
+        conv = total + lax.dot_general(flip, low, dims, preferred_element_type=jnp.float32)
+        shifted = conv + bias_ref[...]
+        gelu = 0.5 * shifted * (1.0 + lax.erf(shifted * (1.0 / math.sqrt(2.0))))
+        hidden = res_ref[r].astype(jnp.float32) + gelu
+        out_ref[r] = hidden.astype(out_ref.dtype)
+
+
+def hankel_conv(xt, wv, residual, bias, rows):
     groups, recs, chans, lanes = xt.shape
     taps, outs = wv.shape[3], wv.shape[2]
     return pl.pallas_call(
         conv_body,
-        grid=(groups,),
-        in_specs=[pl.BlockSpec((1, recs, chans, lanes), lambda g: (g, 0, 0, 0)),
-                  pl.BlockSpec((1, chans, outs, taps), lambda g: (g, 0, 0, 0))],
-        out_specs=pl.BlockSpec((1, recs, rows, outs), lambda g: (g, 0, 0, 0)),
-        out_shape=jax.ShapeDtypeStruct((groups, recs, rows, outs), jnp.float32),
+        grid=(groups // 2,),
+        in_specs=[
+            pl.BlockSpec((2, recs, chans, lanes), lambda g: (g, 0, 0, 0)),
+            pl.BlockSpec((2, chans, outs, taps), lambda g: (g, 0, 0, 0)),
+            pl.BlockSpec((recs, rows, 2 * outs), lambda g: (0, 0, g)),
+            pl.BlockSpec((1, 2 * outs), lambda g: (0, g)),
+        ],
+        out_specs=pl.BlockSpec((recs, rows, 2 * outs), lambda g: (0, 0, g)),
+        out_shape=jax.ShapeDtypeStruct((recs, rows, groups * outs), jnp.bfloat16),
         cost_estimate=pl.CostEstimate(
             flops=2 * groups * recs * rows * taps * chans * outs,
             bytes_accessed=xt.size * 2 + wv.size * 2 + groups * recs * rows * outs * 4,
-            transcendentals=0,
+            transcendentals=recs * rows * groups * outs,
         ),
-    )(xt, wv)
-
-
-def grouped_conv(padded, conv_weight, frame_rows):
+    )(xt, wv, residual, bias)
+
+
+def grouped_conv(padded, conv_weight, masked, conv_bias, frame_rows):
     recs, span = padded.shape[0], padded.shape[1]
     groups_here, taps, group_in, group_out = conv_weight.shape
     lanes = -(-(frame_rows + taps - 1) // 128) * 128
     grouped = jnp.pad(padded, ((0, 0), (0, lanes - span), (0, 0)))
     grouped = jnp.roll(jnp.flip(grouped, axis=1), frame_rows - lanes, axis=1)
     grouped = grouped.reshape(recs, lanes, groups_here, group_in).transpose(2, 0, 3, 1)
-    out = hankel_conv(grouped, jnp.transpose(conv_weight, (0, 2, 3, 1)), frame_rows)
-    return out.transpose(1, 2, 0, 3).reshape(recs, frame_rows, groups_here * group_out)
+    bias = conv_bias.astype(jnp.float32).reshape(1, -1)
+    return hankel_conv(grouped, jnp.transpose(conv_weight, (0, 2, 3, 1)), masked, bias, frame_rows)
 
 
 def swap_halves(hidden, axis):
@@ -252,11 +265,7 @@
     groups_here, kernel_width, group_in, group_out = conv_weight.shape
     half_width = kernel_width // 2
     padded = padded_2(masked, (("ctx", 1),), half_width)
-    conv_out = grouped_conv(padded, conv_weight, frame_rows)
-    hidden = (
-        masked.astype(jnp.float32)
-        + jax.nn.gelu(conv_out + conv_bias.astype(jnp.float32), approximate=False)
-    ).astype(jnp.bfloat16)
+    hidden = grouped_conv(padded, conv_weight, masked, conv_bias, frame_rows)
     record = swap_halves(hidden, "fsdp")
     own_length = lax.dynamic_index_in_dim(lengths, lax.axis_index("fsdp"), 0, keepdims=False)
     flat = record[0].astype(jnp.float32)

time: 82.1 us -> 74.8 us (0.911)
  local copies, waits for them, and re-layouts: 6.82 us -> 3.32 us
  waiting for transfers between devices: 16.5 us -> 14.1 us
  matrix products: 4.06 us -> 2.95 us
    ppermute x1, waiting for transfers between devices: 3.54 us -> 0.16 us  [padded_2(): before = lax.ppermute(last, axis, up)]
    unnamed x16, local copies, waits for them, and re-layouts: 2.09 us -> 0.04 us
    convert_element_type x2 -> x0, other arithmetic: 1.95 us -> none  [the longest x1 1.27 us: per_device(): hidden = (masked.astype(jnp.float32) + jax.nn.gelu(conv_out + conv_bias.a...]
    transpose x1 -> x0, local copies, waits for them, and re-layouts: 1.55 us -> none  [grouped_conv(): out.transpose(1, 2, 0, 3).reshape(recs, frame_rows, groups_here * group_out)]
    reshape x0 -> x1, other arithmetic: none -> 1.26 us  [grouped_conv(): bias = conv_bias.astype(jnp.float32).reshape(1, -1)]
    ppermute x1, waiting for transfers between devices: 2.28 us -> 3.5 us  [gather_line4(): passed = lax.ppermute(across, axis, [(2, 3), (1, 0)])]
    select_n x1, other arithmetic: 0.03 us -> 1.08 us  [per_device(): jnp.where(live[:, :, None], frames_in, jnp.zeros((), frames_in.dtype))]
    dynamic_slice x1, local copies, waits for them, and re-layouts: 0.03 us -> 0.98 us  [swap_halves(): theirs = lax.dynamic_index_in_dim(hidden, 1 - place, 0, keepdims=True)]
where the time goes in v12:
time: 74.8 us; the launch traced here: 74.4 us
  Pallas kernels  28.7 us (38%)
  starting transfers between devices  17.6 us (24%)
  waiting for transfers between devices  14.1 us (19%)
  other arithmetic  6.95 us (9%)
  local copies, waits for them, and re-layouts  3.32 us (4%)
  matrix products  2.95 us (4%)
  between operations  0.84 us (1%)
    pallas_call x1, Pallas kernels, hankel_conv(): pl.pallas_call(conv_body, grid=(groups // 2,), in_specs=[pl.BlockSpec((2,...  24.5 us
    ppermute x1, starting transfers between devices, padded_2(): before = lax.ppermute(last, axis, up)  4.94 us
    ppermute x1, starting transfers between devices, gather_line4(): from_below = lax.ppermute(x, axis, [(0, 1), (1, 2), (2, 3)])  4.56 us
    pallas_call x1, Pallas kernels, fused_attention(): pl.pallas_call(attend_body, out_shape=jax.ShapeDtypeStruct((rows, width),...  4.18 us
    ppermute x1, waiting for transfers between devices, padded_2(): after = lax.ppermute(first, axis, down)  4.13 us
    ppermute x1, waiting for transfers between devices, gather_line4(): passed = lax.ppermute(across, axis, [(2, 3), (1, 0)])  3.5 us
    ppermute x1, waiting for transfers between devices, swap_halves(): got = lax.ppermute(theirs, axis, [(0, 1), (1, 0)])  3.45 us
    ppermute x1, waiting for transfers between devices, gather_line4(): across = lax.ppermute(x, axis, [(0, 2), (1, 3), (2, 0), (3, 1)])  2.85 us
  transfers between devices with their start and end apart: 7, of which 5 were waited for; matrix products, arithmetic and copies ran while one was open for 9% of the time, Pallas kernels for 0%

profile of v12, /device:TPU:0, one launch (start us, length us, event | category | flops | bytes accessed | tf_op | source)
XLA Modules:
  0.0 74.4 jit_solution(17123003826345473603)
XLA Ops:
  0.6 0.0 copy-start
  0.7 0.8 %broadcast_compare_fusion = pred[2,128]{1,0:T(4,128)(4,1)S(1)} fusion(s32[128]{0:T(128)S(1)} %iota_add_fusion, s32[2]{0:T(128)} %param.10), kind=kLoop, calls=%fused_computation.29 | loop fusion | flops 256 | bytes 776 | tf_op jit(solution)/shard_map/lt | solution.py:263
  1.5 0.0 copy-start.5
  1.5 0.0 copy-start.6
  1.5 1.1 %broadcast_select_fusion.2.res_ref = bf16[2,128,512]{2,1,0:T(8,128)(2,1)S(1)} fusion(bf16[2,128,512]{2,1,0:T(8,128)(2,1)} %param.9, pred[2,128]{1,0:T(4,128)(4,1)S(1)} %broadcast_compare_fusion), kind=kLoop, calls=%fused_computation.19 | loop fusion | flops 131072 | bytes 524544 | tf_op jit(solution)/shard_map/jit(_where)/select_n | solution.py:264
  2.6 0.0 copy-start.1
  2.6 4.9 %collective-permute-start = (bf16[2,64,512]{2,1,0:T(8,128)(2,1)S(1)}, bf16[2,64,512]{2,1,0:T(8,128)(2,1)S(1)}, u32[]{:S(2)}, u32[]{:S(2)}) collective-permute-start(bf16[2,64,512]{2,1,0:T(8,128)(2,1)S(1)} %get-tuple-element.8), channel_id=1, source_target_pairs={{0,8},{8,16},{16,24},{1,9},{9,17},{17,25},{2,10},{10,18},{18,26},{... | collective-permute-start | bytes 393224 | tf_op jit(solution)/shard_map/ppermute | solution.py:20
  7.5 1.3 %collective-permute-start.1 = (bf16[2,64,512]{2,1,0:T(8,128)(2,1)S(1)}, bf16[2,64,512]{2,1,0:T(8,128)(2,1)S(1)}, u32[]{:S(2)}, u32[]{:S(2)}) collective-permute-start(bf16[2,64,512]{2,1,0:T(8,128)(2,1)S(1)} %get-tuple-element.9), channel_id=1, source_target_pairs={{8,0},{16,8},{24,16},{9,1},{17,9},{25,17},{10,2},{18,10},{26,18},{... | collective-permute-start | bytes 393224 | tf_op jit(solution)/shard_map/ppermute | solution.py:21
  8.9 1.3 %reshape.147 = f32[512]{0:T(512)} convert(bf16[512]{0:T(512)(128)(2,1)} %param.12) | non-fusion elementwise | flops 512 | bytes 3072 | tf_op jit(solution)/shard_map/reshape | solution.py:112
  10.1 0.2 collective-permute-done
  10.3 4.1 %collective-permute-done.1 = bf16[2,64,512]{2,1,0:T(8,128)(2,1)S(1)} collective-permute-done((bf16[2,64,512]{2,1,0:T(8,128)(2,1)S(1)}, bf16[2,64,512]{2,1,0:T(8,128)(2,1)S(1)}, u32[]{:S(2)}, u32[]{:S(2)}) %collective-permute-start.1) | collective-permute-done | bytes 131104 | tf_op jit(solution)/shard_map/ppermute | solution.py:21
  14.4 0.3 slice.24
  14.8 0.3 slice.27
  15.2 0.0 copy-start.3
  15.2 0.2 copy.14
  15.4 0.8 %copy.18 = bf16[2,256,8,64]{1,3,0,2:T(8,128)(2,1)} copy(bf16[2,256,8,64]{1,3,2,0:T(8,128)(2,1)S(1)} %bitcast.24) | data formatting | bytes 1048576 | tf_op jit(solution)/shard_map/reshape | solution.py:111
  16.2 0.0 copy-done.1
  16.2 0.0 copy-start.7
  16.2 24.5 %shard_map.104 = bf16[2,128,512]{2,1,0:T(8,128)(2,1)} custom-call(bf16[8,2,64,256]{3,2,1,0:T(8,128)(2,1)} %bitcast.23, bf16[8,64,64,128]{3,2,1,0:T(8,128)(2,1)} %bitcast.22, bf16[2,128,512]{2,1,0:T(8,128)(2,1)} %copy-done.1, f32[1,512]{1,0:T(1,128)} %bitcast.30), custom_call_target="tpu_custom_call" | custom-call | flops 2147483648 | bytes 9437184 | tf_op jit(solution)/shard_map/pallas_call | solution.py:86
  40.7 1.0 %constant_dynamic-slice_fusion = (bf16[1,128,512]{2,1,0:T(8,128)(2,1)S(1)}, bf16[128,512]{1,0:T(8,128)(2,1)S(1)}) fusion(bf16[2,128,512]{2,1,0:T(8,128)(2,1)} %shard_map.104, s32[]{:T(128)S(6)} %select_n.56, s32[]{:T(128)S(6)} %select_n.55), kind=kLoop, calls=%fused_computation.28 | loop fusion | bytes 524296 | tf_op jit(solution)/shard_map/jit(dynamic_index_in_dim)/dynamic_slice | solution.py:121
  41.7 1.6 %collective-permute-start.2 = (bf16[1,128,512]{2,1,0:T(8,128)(2,1)S(1)}, bf16[1,128,512]{2,1,0:T(8,128)(2,1)S(1)}, u32[]{:S(2)}, u32[]{:S(2)}) collective-permute-start(bf16[1,128,512]{2,1,0:T(8,128)(2,1)S(1)} %get-tuple-element.4), channel_id=1, source_target_pairs={{0,4},{4,0},{1,5},{5,1},{2,6},{6,2},{3,7},{7,3},{8,12},{12,8},{9,1... | collective-permute-start | bytes 393224 | tf_op jit(solution)/shard_map/ppermute | solution.py:122
  43.3 3.4 %collective-permute-done.2 = bf16[1,128,512]{2,1,0:T(8,128)(2,1)S(1)} collective-permute-done((bf16[1,128,512]{2,1,0:T(8,128)(2,1)S(1)}, bf16[1,128,512]{2,1,0:T(8,128)(2,1)S(1)}, u32[]{:S(2)}, u32[]{:S(2)}) %collective-permute-start.2) | collective-permute-done | bytes 131104 | tf_op jit(solution)/shard_map/ppermute | solution.py:122
  46.7 0.1 convert_reduce_fusion
  46.9 0.2 fusion.2
  47.1 0.0 copy-done
  47.1 0.0 copy-done.5
  47.1 0.0 copy-done.6
  47.1 0.4 convolution_convert_fusion.1
  47.5 0.0 copy-done.3
  47.5 0.4 convolution_convert_fusion
  47.9 0.0 copy-start.2
  47.9 2.6 %collective-permute-start.3 = (bf16[128,1024]{1,0:T(8,128)(2,1)S(1)}, bf16[128,1024]{1,0:T(8,128)(2,1)S(1)}, u32[]{:S(2)}, u32[]{:S(2)}) collective-permute-start(bf16[128,1024]{1,0:T(8,128)(2,1)S(1)} %pad_maximum_fusion.3.refs_3_), channel_id=1, source_target_pairs={{0,16},{8,24},{16,0},{24,8},{1,17},{9,25},{17,1},{25,9},{2,18},{10... | collective-permute-start | bytes 786440 | tf_op jit(solution)/shard_map/ppermute | solution.py:179
  50.6 0.0 copy-done.7
  50.6 0.6 dynamic_slice.13
  51.2 1.3 %fusion.6.refs_2_ = f32[128,1]{1,0:T(8,128)} fusion(s32[]{:T(128)S(6)} %mul.21, s32[]{:T(128)} %bitcast.10), kind=kLoop, calls=%fused_computation.22 | loop fusion | flops 384 | bytes 520 | tf_op jit(solution)/shard_map/convert_element_type | solution.py:163
  52.4 1.3 %collective-permute-start.6 = (bf16[128,1024]{1,0:T(8,128)(2,1)S(1)}, bf16[128,1024]{1,0:T(8,128)(2,1)S(1)}, u32[]{:S(2)}, u32[]{:S(2)}) collective-permute-start(bf16[128,1024]{1,0:T(8,128)(2,1)S(1)} %pad_maximum_fusion.3.refs_3_), channel_id=1, source_target_pairs={{8,0},{16,8},{24,16},{9,1},{17,9},{25,17},{10,2},{18,10},{26,18},{... | collective-permute-start | bytes 786440 | tf_op jit(solution)/shard_map/ppermute | solution.py:178
  53.7 4.6 %collective-permute-start.4 = (bf16[128,1024]{1,0:T(8,128)(2,1)S(1)}, bf16[128,1024]{1,0:T(8,128)(2,1)S(1)}, u32[]{:S(2)}, u32[]{:S(2)}) collective-permute-start(bf16[128,1024]{1,0:T(8,128)(2,1)S(1)} %pad_maximum_fusion.3.refs_3_), channel_id=1, source_target_pairs={{0,8},{8,16},{16,24},{1,9},{9,17},{17,25},{2,10},{10,18},{18,26},{... | collective-permute-start | bytes 786440 | tf_op jit(solution)/shard_map/ppermute | solution.py:177
  58.3 2.9 %collective-permute-done.3.refs_4_ = bf16[128,1024]{1,0:T(8,128)(2,1)S(1)} collective-permute-done((bf16[128,1024]{1,0:T(8,128)(2,1)S(1)}, bf16[128,1024]{1,0:T(8,128)(2,1)S(1)}, u32[]{:S(2)}, u32[]{:S(2)}) %collective-permute-start.3) | collective-permute-done | bytes 262176 | tf_op jit(solution)/shard_map/ppermute | solution.py:179
  61.1 1.3 %collective-permute-start.5 = (bf16[128,1024]{1,0:T(8,128)(2,1)S(1)}, bf16[128,1024]{1,0:T(8,128)(2,1)S(1)}, u32[]{:S(2)}, u32[]{:S(2)}) collective-permute-start(bf16[128,1024]{1,0:T(8,128)(2,1)S(1)} %collective-permute-done.3.refs_4_), channel_id=1, source_target_pairs={{16,24},{8,0},{17,25},{9,1},{18,26},{10,2},{19,27},{11,3},{20,28},... | collective-permute-start | bytes 786440 | tf_op jit(solution)/shard_map/ppermute | solution.py:180
  62.4 1.2 %compare_convert_fusion.refs_1_ = f32[1,512]{1,0:T(1,128)} fusion(s32[1,128]{1,0:T(1,128)S(1)} %get-tuple-element.10, s32[1,128]{1,0:T(1,128)S(1)} %get-tuple-element.11, s32[1,128]{1,0:T(1,128)S(1)} %get-tuple-element.12, s32[1,128]{1,0:T(1,128)S(1)} %get-tuple-element.13, s32[]{:T(128)} %bitcast.10), kind=kLoop, calls=%fused_computation.23 | loop fusion | flops 2560 | bytes 4100 | tf_op jit(solution)/shard_map/convert_element_type | solution.py:162
  63.7 2.2 %convolution_convert_fusion.2.refs_0_ = bf16[128,512]{1,0:T(8,128)(2,1)} fusion(bf16[1024,512]{1,0:T(8,128)(2,1)} %param.15, f32[1024]{0:T(1024)S(1)} %copy-done.5, f32[1024]{0:T(1024)S(1)} %copy-done.6, f32[128]{0:T(128)S(1)} %add_sqrt_fusion, f32[128]{0:T(128)S(1)} %broadcast_multiply_fusion, bf16[128,512]{1,0:T(8,128)(2,1)S(1)} %get-tuple-element.5, ...), kind=kOutput, calls=%fused_computation.2 | convolution fusion | flops 136249344 | bytes 1451009 | tf_op jit(solution)/shard_map/dot_general | solution.py:277
  65.9 0.0 collective-permute-done.6
  65.9 0.0 collective-permute-done.4
  65.9 3.5 %collective-permute-done.5 = bf16[128,1024]{1,0:T(8,128)(2,1)S(1)} collective-permute-done((bf16[128,1024]{1,0:T(8,128)(2,1)S(1)}, bf16[128,1024]{1,0:T(8,128)(2,1)S(1)}, u32[]{:S(2)}, u32[]{:S(2)}) %collective-permute-start.5) | collective-permute-done | bytes 262176 | tf_op jit(solution)/shard_map/ppermute | solution.py:180
  69.4 0.8 %broadcast_select_fusion = (bf16[128,1024]{1,0:T(8,128)(2,1)}, bf16[128,1024]{1,0:T(8,128)(2,1)}) fusion(bf16[128,1024]{1,0:T(8,128)(2,1)S(1)} %collective-permute-done.6, bf16[128,1024]{1,0:T(8,128)(2,1)S(1)} %collective-permute-done.5, pred[]{:T(512)S(6)} %le.3, bf16[128,1024]{1,0:T(8,128)(2,1)S(1)} %collective-permute-done.4, pred[]{:T(512)S(6)} %ge.3), kind=kLoop, calls=%fused_computation.17 | loop fusion | flops 262144 | bytes 1310722 | tf_op jit(solution)/shard_map/jit(_where)/select_n | solution.py:185
  70.2 0.0 copy-done.2
  70.2 0.0 copy-done.4
  70.2 4.2 %shard_map.105 = bf16[128,512]{1,0:T(8,128)(2,1)} custom-call(bf16[128,512]{1,0:T(8,128)(2,1)} %convolution_convert_fusion.2.refs_0_, f32[1,512]{1,0:T(1,128)} %compare_convert_fusion.refs_1_, f32[128,1]{1,0:T(8,128)} %fusion.6.refs_2_, bf16[128,1024]{1,0:T(8,128)(2,1)} %copy-done.2, bf16[128,1024]{1,0:T(8,128)(2,1)} %copy-done.4, ...), custom_call_target="tpu_custom_call" | custom-call | flops 268435456 | bytes 1310720 | tf_op jit(solution)/shard_map/pallas_call | solution.py:164
  (10 shorter events, 0.1 us)
Async XLA Ops:
  0.6 46.5 %copy-start = (bf16[1024,512]{1,0:T(8,128)(2,1)S(1)}, bf16[1024,512]{1,0:T(8,128)(2,1)}, u32[]{:S(2)}) copy-start(bf16[1024,512]{1,0:T(8,128)(2,1)} %param.16) | copy-start | bytes 3145732
  1.5 45.6 %copy-start.5 = (f32[1024]{0:T(1024)S(1)}, f32[1024]{0:T(1024)}, u32[]{:S(2)}) copy-start(f32[1024]{0:T(1024)} %param.14) | copy-start | bytes 12292
  1.5 45.6 %copy-start.6 = (f32[1024]{0:T(1024)S(1)}, f32[1024]{0:T(1024)}, u32[]{:S(2)}) copy-start(f32[1024]{0:T(1024)} %param.13) | copy-start | bytes 12292
  2.6 13.7 %copy-start.1 = (bf16[2,128,512]{2,1,0:T(8,128)(2,1)}, bf16[2,128,512]{2,1,0:T(8,128)(2,1)S(1)}, u32[]{:S(2)}) copy-start(bf16[2,128,512]{2,1,0:T(8,128)(2,1)S(1)} %broadcast_select_fusion.2.res_ref) | copy-start | bytes 786436
  2.6 7.7 %collective-permute-start = (bf16[2,64,512]{2,1,0:T(8,128)(2,1)S(1)}, bf16[2,64,512]{2,1,0:T(8,128)(2,1)S(1)}, u32[]{:S(2)}, u32[]{:S(2)}) collective-permute-start(bf16[2,64,512]{2,1,0:T(8,128)(2,1)S(1)} %get-tuple-element.8), channel_id=1, source_target_pairs={{0,8},{8,16},{16,24},{1,9},{9,17},{17,25},{2,10},{10,18},{18,26},{... | collective-permute-start | bytes 393224 | tf_op jit(solution)/shard_map/ppermute | solution.py:20
  7.5 6.9 %collective-permute-start.1 = (bf16[2,64,512]{2,1,0:T(8,128)(2,1)S(1)}, bf16[2,64,512]{2,1,0:T(8,128)(2,1)S(1)}, u32[]{:S(2)}, u32[]{:S(2)}) collective-permute-start(bf16[2,64,512]{2,1,0:T(8,128)(2,1)S(1)} %get-tuple-element.9), channel_id=1, source_target_pairs={{8,0},{16,8},{24,16},{9,1},{17,9},{25,17},{10,2},{18,10},{26,18},{... | collective-permute-start | bytes 393224 | tf_op jit(solution)/shard_map/ppermute | solution.py:21
  15.2 32.3 %copy-start.3 = (bf16[1024,512]{1,0:T(8,128)(2,1)S(1)}, bf16[1024,512]{1,0:T(8,128)(2,1)}, u32[]{:S(2)}) copy-start(bf16[1024,512]{1,0:T(8,128)(2,1)} %param.17) | copy-start | bytes 3145732
  16.2 34.3 %copy-start.7 = (s32[2]{0:T(128)S(1)}, s32[2]{0:T(128)}, u32[]{:S(2)}) copy-start(s32[2]{0:T(128)} %param.10) | copy-start | bytes 28
  41.7 5.0 %collective-permute-start.2 = (bf16[1,128,512]{2,1,0:T(8,128)(2,1)S(1)}, bf16[1,128,512]{2,1,0:T(8,128)(2,1)S(1)}, u32[]{:S(2)}, u32[]{:S(2)}) collective-permute-start(bf16[1,128,512]{2,1,0:T(8,128)(2,1)S(1)} %get-tuple-element.4), channel_id=1, source_target_pairs={{0,4},{4,0},{1,5},{5,1},{2,6},{6,2},{3,7},{7,3},{8,12},{12,8},{9,1... | collective-permute-start | bytes 393224 | tf_op jit(solution)/shard_map/ppermute | solution.py:122
  47.9 22.3 %copy-start.2 = (bf16[128,1024]{1,0:T(8,128)(2,1)}, bf16[128,1024]{1,0:T(8,128)(2,1)S(1)}, u32[]{:S(2)}) copy-start(bf16[128,1024]{1,0:T(8,128)(2,1)S(1)} %pad_maximum_fusion.3.refs_3_) | copy-start | bytes 786436
  47.9 13.2 %collective-permute-start.3 = (bf16[128,1024]{1,0:T(8,128)(2,1)S(1)}, bf16[128,1024]{1,0:T(8,128)(2,1)S(1)}, u32[]{:S(2)}, u32[]{:S(2)}) collective-permute-start(bf16[128,1024]{1,0:T(8,128)(2,1)S(1)} %pad_maximum_fusion.3.refs_3_), channel_id=1, source_target_pairs={{0,16},{8,24},{16,0},{24,8},{1,17},{9,25},{17,1},{25,9},{2,18},{10... | collective-permute-start | bytes 786440 | tf_op jit(solution)/shard_map/ppermute | solution.py:179
  52.4 13.5 %collective-permute-start.6 = (bf16[128,1024]{1,0:T(8,128)(2,1)S(1)}, bf16[128,1024]{1,0:T(8,128)(2,1)S(1)}, u32[]{:S(2)}, u32[]{:S(2)}) collective-permute-start(bf16[128,1024]{1,0:T(8,128)(2,1)S(1)} %pad_maximum_fusion.3.refs_3_), channel_id=1, source_target_pairs={{8,0},{16,8},{24,16},{9,1},{17,9},{25,17},{10,2},{18,10},{26,18},{... | collective-permute-start | bytes 786440 | tf_op jit(solution)/shard_map/ppermute | solution.py:178
  53.7 12.2 %collective-permute-start.4 = (bf16[128,1024]{1,0:T(8,128)(2,1)S(1)}, bf16[128,1024]{1,0:T(8,128)(2,1)S(1)}, u32[]{:S(2)}, u32[]{:S(2)}) collective-permute-start(bf16[128,1024]{1,0:T(8,128)(2,1)S(1)} %pad_maximum_fusion.3.refs_3_), channel_id=1, source_target_pairs={{0,8},{8,16},{16,24},{1,9},{9,17},{17,25},{2,10},{10,18},{18,26},{... | collective-permute-start | bytes 786440 | tf_op jit(solution)/shard_map/ppermute | solution.py:177
  61.1 9.1 %copy-start.4 = (bf16[128,1024]{1,0:T(8,128)(2,1)}, bf16[128,1024]{1,0:T(8,128)(2,1)S(1)}, u32[]{:S(2)}) copy-start(bf16[128,1024]{1,0:T(8,128)(2,1)S(1)} %collective-permute-done.3.refs_4_) | copy-start | bytes 786436
  61.1 8.3 %collective-permute-start.5 = (bf16[128,1024]{1,0:T(8,128)(2,1)S(1)}, bf16[128,1024]{1,0:T(8,128)(2,1)S(1)}, u32[]{:S(2)}, u32[]{:S(2)}) collective-permute-start(bf16[128,1024]{1,0:T(8,128)(2,1)S(1)} %collective-permute-done.3.refs_4_), channel_id=1, source_target_pairs={{16,24},{8,0},{17,25},{9,1},{18,26},{10,2},{19,27},{11,3},{20,28},... | collective-permute-start | bytes 786440 | tf_op jit(solution)/shard_map/ppermute | solution.py:180

commit v13 on v12

--- a/solution.py
+++ b/solution.py
@@ -58,7 +58,7 @@
         return tuple(octet_step(group, q, acc) for group, acc in enumerate(accs))
 
     start = tuple(jnp.zeros((outs, recs * rows), jnp.float32) for _ in range(pair_groups))
-    accs = lax.fori_loop(0, chans // 8, both_groups, start, unroll=2)
+    accs = lax.fori_loop(0, chans // 8, both_groups, start, unroll=4)
     acc = jnp.concatenate(accs, axis=0)
     across = lax.broadcasted_iota(jnp.int32, (rows, rows), 0) + lax.broadcasted_iota(
         jnp.int32, (rows, rows), 1

time: 74.8 us -> 73.1 us (0.977)
  Pallas kernels: 28.7 us -> 27 us
    pallas_call x1, Pallas kernels: 24.5 us -> 22.9 us  [hankel_conv(): pl.pallas_call(conv_body, grid=(groups // 2,), in_specs=[pl.BlockSpec((2,...]
where the time goes in v13:
time: 73.1 us; the launch traced here: 72.8 us
  Pallas kernels  27 us (37%)
  starting transfers between devices  17.6 us (24%)
  waiting for transfers between devices  14.1 us (19%)
  other arithmetic  6.95 us (10%)
  local copies, waits for them, and re-layouts  3.32 us (5%)
  matrix products  2.96 us (4%)
  between operations  0.84 us (1%)
    pallas_call x1, Pallas kernels, hankel_conv(): pl.pallas_call(conv_body, grid=(groups // 2,), in_specs=[pl.BlockSpec((2,...  22.9 us
    ppermute x1, starting transfers between devices, padded_2(): before = lax.ppermute(last, axis, up)  4.94 us
    ppermute x1, starting transfers between devices, gather_line4(): from_below = lax.ppermute(x, axis, [(0, 1), (1, 2), (2, 3)])  4.56 us
    pallas_call x1, Pallas kernels, fused_attention(): pl.pallas_call(attend_body, out_shape=jax.ShapeDtypeStruct((rows, width),...  4.18 us
    ppermute x1, waiting for transfers between devices, padded_2(): after = lax.ppermute(first, axis, down)  4.13 us
    ppermute x1, waiting for transfers between devices, gather_line4(): passed = lax.ppermute(across, axis, [(2, 3), (1, 0)])  3.49 us
    ppermute x1, waiting for transfers between devices, swap_halves(): got = lax.ppermute(theirs, axis, [(0, 1), (1, 0)])  3.45 us
    ppermute x1, waiting for transfers between devices, gather_line4(): across = lax.ppermute(x, axis, [(0, 2), (1, 3), (2, 0), (3, 1)])  2.85 us
  transfers between devices with their start and end apart: 7, of which 5 were waited for; matrix products, arithmetic and copies ran while one was open for 9% of the time, Pallas kernels for 0%

profile of v13, /device:TPU:0, one launch (start us, length us, event | category | flops | bytes accessed | tf_op | source)
XLA Modules:
  0.0 72.8 jit_solution(7405618654292038017)
XLA Ops:
  0.6 0.0 copy-start
  0.7 0.8 %broadcast_compare_fusion = pred[2,128]{1,0:T(4,128)(4,1)S(1)} fusion(s32[128]{0:T(128)S(1)} %iota_add_fusion, s32[2]{0:T(128)} %param.10), kind=kLoop, calls=%fused_computation.29 | loop fusion | flops 256 | bytes 776 | tf_op jit(solution)/shard_map/lt | solution.py:263
  1.5 0.0 copy-start.5
  1.5 0.0 copy-start.6
  1.5 1.1 %broadcast_select_fusion.2.res_ref = bf16[2,128,512]{2,1,0:T(8,128)(2,1)S(1)} fusion(bf16[2,128,512]{2,1,0:T(8,128)(2,1)} %param.9, pred[2,128]{1,0:T(4,128)(4,1)S(1)} %broadcast_compare_fusion), kind=kLoop, calls=%fused_computation.19 | loop fusion | flops 131072 | bytes 524544 | tf_op jit(solution)/shard_map/jit(_where)/select_n | solution.py:264
  2.6 0.0 copy-start.1
  2.6 4.9 %collective-permute-start = (bf16[2,64,512]{2,1,0:T(8,128)(2,1)S(1)}, bf16[2,64,512]{2,1,0:T(8,128)(2,1)S(1)}, u32[]{:S(2)}, u32[]{:S(2)}) collective-permute-start(bf16[2,64,512]{2,1,0:T(8,128)(2,1)S(1)} %get-tuple-element.8), channel_id=1, source_target_pairs={{0,8},{8,16},{16,24},{1,9},{9,17},{17,25},{2,10},{10,18},{18,26},{... | collective-permute-start | bytes 393224 | tf_op jit(solution)/shard_map/ppermute | solution.py:20
  7.5 1.3 %collective-permute-start.1 = (bf16[2,64,512]{2,1,0:T(8,128)(2,1)S(1)}, bf16[2,64,512]{2,1,0:T(8,128)(2,1)S(1)}, u32[]{:S(2)}, u32[]{:S(2)}) collective-permute-start(bf16[2,64,512]{2,1,0:T(8,128)(2,1)S(1)} %get-tuple-element.9), channel_id=1, source_target_pairs={{8,0},{16,8},{24,16},{9,1},{17,9},{25,17},{10,2},{18,10},{26,18},{... | collective-permute-start | bytes 393224 | tf_op jit(solution)/shard_map/ppermute | solution.py:21
  8.9 1.3 %reshape.147 = f32[512]{0:T(512)} convert(bf16[512]{0:T(512)(128)(2,1)} %param.12) | non-fusion elementwise | flops 512 | bytes 3072 | tf_op jit(solution)/shard_map/reshape | solution.py:112
  10.1 0.2 collective-permute-done
  10.3 4.1 %collective-permute-done.1 = bf16[2,64,512]{2,1,0:T(8,128)(2,1)S(1)} collective-permute-done((bf16[2,64,512]{2,1,0:T(8,128)(2,1)S(1)}, bf16[2,64,512]{2,1,0:T(8,128)(2,1)S(1)}, u32[]{:S(2)}, u32[]{:S(2)}) %collective-permute-start.1) | collective-permute-done | bytes 131104 | tf_op jit(solution)/shard_map/ppermute | solution.py:21
  14.4 0.3 slice.24
  14.8 0.3 slice.27
  15.2 0.0 copy-start.3
  15.2 0.2 copy.14
  15.4 0.8 %copy.18 = bf16[2,256,8,64]{1,3,0,2:T(8,128)(2,1)} copy(bf16[2,256,8,64]{1,3,2,0:T(8,128)(2,1)S(1)} %bitcast.24) | data formatting | bytes 1048576 | tf_op jit(solution)/shard_map/reshape | solution.py:111
  16.2 0.0 copy-done.1
  16.2 0.0 copy-start.7
  16.2 22.9 %shard_map.104 = bf16[2,128,512]{2,1,0:T(8,128)(2,1)} custom-call(bf16[8,2,64,256]{3,2,1,0:T(8,128)(2,1)} %bitcast.23, bf16[8,64,64,128]{3,2,1,0:T(8,128)(2,1)} %bitcast.22, bf16[2,128,512]{2,1,0:T(8,128)(2,1)} %copy-done.1, f32[1,512]{1,0:T(1,128)} %bitcast.30), custom_call_target="tpu_custom_call" | custom-call | flops 2147483648 | bytes 9437184 | tf_op jit(solution)/shard_map/pallas_call | solution.py:86
  39.1 1.0 %constant_dynamic-slice_fusion = (bf16[1,128,512]{2,1,0:T(8,128)(2,1)S(1)}, bf16[128,512]{1,0:T(8,128)(2,1)S(1)}) fusion(bf16[2,128,512]{2,1,0:T(8,128)(2,1)} %shard_map.104, s32[]{:T(128)S(6)} %select_n.56, s32[]{:T(128)S(6)} %select_n.55), kind=kLoop, calls=%fused_computation.28 | loop fusion | bytes 524296 | tf_op jit(solution)/shard_map/jit(dynamic_index_in_dim)/dynamic_slice | solution.py:121
  40.1 1.6 %collective-permute-start.2 = (bf16[1,128,512]{2,1,0:T(8,128)(2,1)S(1)}, bf16[1,128,512]{2,1,0:T(8,128)(2,1)S(1)}, u32[]{:S(2)}, u32[]{:S(2)}) collective-permute-start(bf16[1,128,512]{2,1,0:T(8,128)(2,1)S(1)} %get-tuple-element.4), channel_id=1, source_target_pairs={{0,4},{4,0},{1,5},{5,1},{2,6},{6,2},{3,7},{7,3},{8,12},{12,8},{9,1... | collective-permute-start | bytes 393224 | tf_op jit(solution)/shard_map/ppermute | solution.py:122
  41.6 3.4 %collective-permute-done.2 = bf16[1,128,512]{2,1,0:T(8,128)(2,1)S(1)} collective-permute-done((bf16[1,128,512]{2,1,0:T(8,128)(2,1)S(1)}, bf16[1,128,512]{2,1,0:T(8,128)(2,1)S(1)}, u32[]{:S(2)}, u32[]{:S(2)}) %collective-permute-start.2) | collective-permute-done | bytes 131104 | tf_op jit(solution)/shard_map/ppermute | solution.py:122
  45.1 0.1 convert_reduce_fusion
  45.2 0.2 fusion.2
  45.5 0.0 copy-done
  45.5 0.0 copy-done.5
  45.5 0.0 copy-done.6
  45.5 0.4 convolution_convert_fusion.1
  45.9 0.0 copy-done.3
  45.9 0.4 convolution_convert_fusion
  46.3 0.0 copy-start.2
  46.3 2.6 %collective-permute-start.3 = (bf16[128,1024]{1,0:T(8,128)(2,1)S(1)}, bf16[128,1024]{1,0:T(8,128)(2,1)S(1)}, u32[]{:S(2)}, u32[]{:S(2)}) collective-permute-start(bf16[128,1024]{1,0:T(8,128)(2,1)S(1)} %pad_maximum_fusion.3.refs_3_), channel_id=1, source_target_pairs={{0,16},{8,24},{16,0},{24,8},{1,17},{9,25},{17,1},{25,9},{2,18},{10... | collective-permute-start | bytes 786440 | tf_op jit(solution)/shard_map/ppermute | solution.py:179
  48.9 0.0 copy-done.7
  48.9 0.6 dynamic_slice.13
  49.5 1.3 %fusion.6.refs_2_ = f32[128,1]{1,0:T(8,128)} fusion(s32[]{:T(128)S(6)} %mul.21, s32[]{:T(128)} %bitcast.10), kind=kLoop, calls=%fused_computation.22 | loop fusion | flops 384 | bytes 520 | tf_op jit(solution)/shard_map/convert_element_type | solution.py:163
  50.8 1.3 %collective-permute-start.6 = (bf16[128,1024]{1,0:T(8,128)(2,1)S(1)}, bf16[128,1024]{1,0:T(8,128)(2,1)S(1)}, u32[]{:S(2)}, u32[]{:S(2)}) collective-permute-start(bf16[128,1024]{1,0:T(8,128)(2,1)S(1)} %pad_maximum_fusion.3.refs_3_), channel_id=1, source_target_pairs={{8,0},{16,8},{24,16},{9,1},{17,9},{25,17},{10,2},{18,10},{26,18},{... | collective-permute-start | bytes 786440 | tf_op jit(solution)/shard_map/ppermute | solution.py:178
  52.1 4.6 %collective-permute-start.4 = (bf16[128,1024]{1,0:T(8,128)(2,1)S(1)}, bf16[128,1024]{1,0:T(8,128)(2,1)S(1)}, u32[]{:S(2)}, u32[]{:S(2)}) collective-permute-start(bf16[128,1024]{1,0:T(8,128)(2,1)S(1)} %pad_maximum_fusion.3.refs_3_), channel_id=1, source_target_pairs={{0,8},{8,16},{16,24},{1,9},{9,17},{17,25},{2,10},{10,18},{18,26},{... | collective-permute-start | bytes 786440 | tf_op jit(solution)/shard_map/ppermute | solution.py:177
  56.6 2.9 %collective-permute-done.3.refs_4_ = bf16[128,1024]{1,0:T(8,128)(2,1)S(1)} collective-permute-done((bf16[128,1024]{1,0:T(8,128)(2,1)S(1)}, bf16[128,1024]{1,0:T(8,128)(2,1)S(1)}, u32[]{:S(2)}, u32[]{:S(2)}) %collective-permute-start.3) | collective-permute-done | bytes 262176 | tf_op jit(solution)/shard_map/ppermute | solution.py:179
  59.5 1.3 %collective-permute-start.5 = (bf16[128,1024]{1,0:T(8,128)(2,1)S(1)}, bf16[128,1024]{1,0:T(8,128)(2,1)S(1)}, u32[]{:S(2)}, u32[]{:S(2)}) collective-permute-start(bf16[128,1024]{1,0:T(8,128)(2,1)S(1)} %collective-permute-done.3.refs_4_), channel_id=1, source_target_pairs={{16,24},{8,0},{17,25},{9,1},{18,26},{10,2},{19,27},{11,3},{20,28},... | collective-permute-start | bytes 786440 | tf_op jit(solution)/shard_map/ppermute | solution.py:180
  60.8 1.2 %compare_convert_fusion.refs_1_ = f32[1,512]{1,0:T(1,128)} fusion(s32[1,128]{1,0:T(1,128)S(1)} %get-tuple-element.10, s32[1,128]{1,0:T(1,128)S(1)} %get-tuple-element.11, s32[1,128]{1,0:T(1,128)S(1)} %get-tuple-element.12, s32[1,128]{1,0:T(1,128)S(1)} %get-tuple-element.13, s32[]{:T(128)} %bitcast.10), kind=kLoop, calls=%fused_computation.23 | loop fusion | flops 2560 | bytes 4100 | tf_op jit(solution)/shard_map/convert_element_type | solution.py:162
  62.0 2.2 %convolution_convert_fusion.2.refs_0_ = bf16[128,512]{1,0:T(8,128)(2,1)} fusion(bf16[1024,512]{1,0:T(8,128)(2,1)} %param.15, f32[1024]{0:T(1024)S(1)} %copy-done.5, f32[1024]{0:T(1024)S(1)} %copy-done.6, f32[128]{0:T(128)S(1)} %add_sqrt_fusion, f32[128]{0:T(128)S(1)} %broadcast_multiply_fusion, bf16[128,512]{1,0:T(8,128)(2,1)S(1)} %get-tuple-element.5, ...), kind=kOutput, calls=%fused_computation.2 | convolution fusion | flops 136249344 | bytes 1451009 | tf_op jit(solution)/shard_map/dot_general | solution.py:277
  64.2 0.0 collective-permute-done.6
  64.2 0.0 collective-permute-done.4
  64.2 3.5 %collective-permute-done.5 = bf16[128,1024]{1,0:T(8,128)(2,1)S(1)} collective-permute-done((bf16[128,1024]{1,0:T(8,128)(2,1)S(1)}, bf16[128,1024]{1,0:T(8,128)(2,1)S(1)}, u32[]{:S(2)}, u32[]{:S(2)}) %collective-permute-start.5) | collective-permute-done | bytes 262176 | tf_op jit(solution)/shard_map/ppermute | solution.py:180
  67.7 0.8 %broadcast_select_fusion = (bf16[128,1024]{1,0:T(8,128)(2,1)}, bf16[128,1024]{1,0:T(8,128)(2,1)}) fusion(bf16[128,1024]{1,0:T(8,128)(2,1)S(1)} %collective-permute-done.6, bf16[128,1024]{1,0:T(8,128)(2,1)S(1)} %collective-permute-done.5, pred[]{:T(512)S(6)} %le.3, bf16[128,1024]{1,0:T(8,128)(2,1)S(1)} %collective-permute-done.4, pred[]{:T(512)S(6)} %ge.3), kind=kLoop, calls=%fused_computation.17 | loop fusion | flops 262144 | bytes 1310722 | tf_op jit(solution)/shard_map/jit(_where)/select_n | solution.py:185
  68.6 0.0 copy-done.2
  68.6 0.0 copy-done.4
  68.6 4.2 %shard_map.105 = bf16[128,512]{1,0:T(8,128)(2,1)} custom-call(bf16[128,512]{1,0:T(8,128)(2,1)} %convolution_convert_fusion.2.refs_0_, f32[1,512]{1,0:T(1,128)} %compare_convert_fusion.refs_1_, f32[128,1]{1,0:T(8,128)} %fusion.6.refs_2_, bf16[128,1024]{1,0:T(8,128)(2,1)} %copy-done.2, bf16[128,1024]{1,0:T(8,128)(2,1)} %copy-done.4, ...), custom_call_target="tpu_custom_call" | custom-call | flops 268435456 | bytes 1310720 | tf_op jit(solution)/shard_map/pallas_call | solution.py:164
  (10 shorter events, 0.1 us)
Async XLA Ops:
  0.6 44.8 %copy-start = (bf16[1024,512]{1,0:T(8,128)(2,1)S(1)}, bf16[1024,512]{1,0:T(8,128)(2,1)}, u32[]{:S(2)}) copy-start(bf16[1024,512]{1,0:T(8,128)(2,1)} %param.16) | copy-start | bytes 3145732
  1.5 44.0 %copy-start.5 = (f32[1024]{0:T(1024)S(1)}, f32[1024]{0:T(1024)}, u32[]{:S(2)}) copy-start(f32[1024]{0:T(1024)} %param.14) | copy-start | bytes 12292
  1.5 44.0 %copy-start.6 = (f32[1024]{0:T(1024)S(1)}, f32[1024]{0:T(1024)}, u32[]{:S(2)}) copy-start(f32[1024]{0:T(1024)} %param.13) | copy-start | bytes 12292
  2.6 13.7 %copy-start.1 = (bf16[2,128,512]{2,1,0:T(8,128)(2,1)}, bf16[2,128,512]{2,1,0:T(8,128)(2,1)S(1)}, u32[]{:S(2)}) copy-start(bf16[2,128,512]{2,1,0:T(8,128)(2,1)S(1)} %broadcast_select_fusion.2.res_ref) | copy-start | bytes 786436
  2.6 7.7 %collective-permute-start = (bf16[2,64,512]{2,1,0:T(8,128)(2,1)S(1)}, bf16[2,64,512]{2,1,0:T(8,128)(2,1)S(1)}, u32[]{:S(2)}, u32[]{:S(2)}) collective-permute-start(bf16[2,64,512]{2,1,0:T(8,128)(2,1)S(1)} %get-tuple-element.8), channel_id=1, source_target_pairs={{0,8},{8,16},{16,24},{1,9},{9,17},{17,25},{2,10},{10,18},{18,26},{... | collective-permute-start | bytes 393224 | tf_op jit(solution)/shard_map/ppermute | solution.py:20
  7.5 6.9 %collective-permute-start.1 = (bf16[2,64,512]{2,1,0:T(8,128)(2,1)S(1)}, bf16[2,64,512]{2,1,0:T(8,128)(2,1)S(1)}, u32[]{:S(2)}, u32[]{:S(2)}) collective-permute-start(bf16[2,64,512]{2,1,0:T(8,128)(2,1)S(1)} %get-tuple-element.9), channel_id=1, source_target_pairs={{8,0},{16,8},{24,16},{9,1},{17,9},{25,17},{10,2},{18,10},{26,18},{... | collective-permute-start | bytes 393224 | tf_op jit(solution)/shard_map/ppermute | solution.py:21
  15.2 30.7 %copy-start.3 = (bf16[1024,512]{1,0:T(8,128)(2,1)S(1)}, bf16[1024,512]{1,0:T(8,128)(2,1)}, u32[]{:S(2)}) copy-start(bf16[1024,512]{1,0:T(8,128)(2,1)} %param.17) | copy-start | bytes 3145732
  16.2 32.7 %copy-start.7 = (s32[2]{0:T(128)S(1)}, s32[2]{0:T(128)}, u32[]{:S(2)}) copy-start(s32[2]{0:T(128)} %param.10) | copy-start | bytes 28
  40.1 5.0 %collective-permute-start.2 = (bf16[1,128,512]{2,1,0:T(8,128)(2,1)S(1)}, bf16[1,128,512]{2,1,0:T(8,128)(2,1)S(1)}, u32[]{:S(2)}, u32[]{:S(2)}) collective-permute-start(bf16[1,128,512]{2,1,0:T(8,128)(2,1)S(1)} %get-tuple-element.4), channel_id=1, source_target_pairs={{0,4},{4,0},{1,5},{5,1},{2,6},{6,2},{3,7},{7,3},{8,12},{12,8},{9,1... | collective-permute-start | bytes 393224 | tf_op jit(solution)/shard_map/ppermute | solution.py:122
  46.3 22.3 %copy-start.2 = (bf16[128,1024]{1,0:T(8,128)(2,1)}, bf16[128,1024]{1,0:T(8,128)(2,1)S(1)}, u32[]{:S(2)}) copy-start(bf16[128,1024]{1,0:T(8,128)(2,1)S(1)} %pad_maximum_fusion.3.refs_3_) | copy-start | bytes 786436
  46.3 13.2 %collective-permute-start.3 = (bf16[128,1024]{1,0:T(8,128)(2,1)S(1)}, bf16[128,1024]{1,0:T(8,128)(2,1)S(1)}, u32[]{:S(2)}, u32[]{:S(2)}) collective-permute-start(bf16[128,1024]{1,0:T(8,128)(2,1)S(1)} %pad_maximum_fusion.3.refs_3_), channel_id=1, source_target_pairs={{0,16},{8,24},{16,0},{24,8},{1,17},{9,25},{17,1},{25,9},{2,18},{10... | collective-permute-start | bytes 786440 | tf_op jit(solution)/shard_map/ppermute | solution.py:179
  50.8 13.5 %collective-permute-start.6 = (bf16[128,1024]{1,0:T(8,128)(2,1)S(1)}, bf16[128,1024]{1,0:T(8,128)(2,1)S(1)}, u32[]{:S(2)}, u32[]{:S(2)}) collective-permute-start(bf16[128,1024]{1,0:T(8,128)(2,1)S(1)} %pad_maximum_fusion.3.refs_3_), channel_id=1, source_target_pairs={{8,0},{16,8},{24,16},{9,1},{17,9},{25,17},{10,2},{18,10},{26,18},{... | collective-permute-start | bytes 786440 | tf_op jit(solution)/shard_map/ppermute | solution.py:178
  52.1 12.2 %collective-permute-start.4 = (bf16[128,1024]{1,0:T(8,128)(2,1)S(1)}, bf16[128,1024]{1,0:T(8,128)(2,1)S(1)}, u32[]{:S(2)}, u32[]{:S(2)}) collective-permute-start(bf16[128,1024]{1,0:T(8,128)(2,1)S(1)} %pad_maximum_fusion.3.refs_3_), channel_id=1, source_target_pairs={{0,8},{8,16},{16,24},{1,9},{9,17},{17,25},{2,10},{10,18},{18,26},{... | collective-permute-start | bytes 786440 | tf_op jit(solution)/shard_map/ppermute | solution.py:177
  59.5 9.1 %copy-start.4 = (bf16[128,1024]{1,0:T(8,128)(2,1)}, bf16[128,1024]{1,0:T(8,128)(2,1)S(1)}, u32[]{:S(2)}) copy-start(bf16[128,1024]{1,0:T(8,128)(2,1)S(1)} %collective-permute-done.3.refs_4_) | copy-start | bytes 786436
  59.5 8.3 %collective-permute-start.5 = (bf16[128,1024]{1,0:T(8,128)(2,1)S(1)}, bf16[128,1024]{1,0:T(8,128)(2,1)S(1)}, u32[]{:S(2)}, u32[]{:S(2)}) collective-permute-start(bf16[128,1024]{1,0:T(8,128)(2,1)S(1)} %collective-permute-done.3.refs_4_), channel_id=1, source_target_pairs={{16,24},{8,0},{17,25},{9,1},{18,26},{10,2},{19,27},{11,3},{20,28},... | collective-permute-start | bytes 786440 | tf_op jit(solution)/shard_map/ppermute | solution.py:180

commit v14 on v13

--- a/solution.py
+++ b/solution.py
@@ -58,7 +58,7 @@
         return tuple(octet_step(group, q, acc) for group, acc in enumerate(accs))
 
     start = tuple(jnp.zeros((outs, recs * rows), jnp.float32) for _ in range(pair_groups))
-    accs = lax.fori_loop(0, chans // 8, both_groups, start, unroll=4)
+    accs = lax.fori_loop(0, chans // 8, both_groups, start, unroll=8)
     acc = jnp.concatenate(accs, axis=0)
     across = lax.broadcasted_iota(jnp.int32, (rows, rows), 0) + lax.broadcasted_iota(
         jnp.int32, (rows, rows), 1

time: 73.1 us -> 72.2 us (0.988)
  Pallas kernels: 27 us -> 26.1 us
    pallas_call x1, Pallas kernels: 22.9 us -> 21.9 us  [hankel_conv(): pl.pallas_call(conv_body, grid=(groups // 2,), in_specs=[pl.BlockSpec((2,...]
where the time goes in v14:
time: 72.2 us; the launch traced here: 71.8 us
  Pallas kernels  26.1 us (36%)
  starting transfers between devices  17.6 us (24%)
  waiting for transfers between devices  14.1 us (20%)
  other arithmetic  6.95 us (10%)
  local copies, waits for them, and re-layouts  3.32 us (5%)
  matrix products  2.96 us (4%)
  between operations  0.84 us (1%)
    pallas_call x1, Pallas kernels, hankel_conv(): pl.pallas_call(conv_body, grid=(groups // 2,), in_specs=[pl.BlockSpec((2,...  21.9 us
    ppermute x1, starting transfers between devices, padded_2(): before = lax.ppermute(last, axis, up)  4.94 us
    ppermute x1, starting transfers between devices, gather_line4(): from_below = lax.ppermute(x, axis, [(0, 1), (1, 2), (2, 3)])  4.56 us
    pallas_call x1, Pallas kernels, fused_attention(): pl.pallas_call(attend_body, out_shape=jax.ShapeDtypeStruct((rows, width),...  4.18 us
    ppermute x1, waiting for transfers between devices, padded_2(): after = lax.ppermute(first, axis, down)  4.13 us
    ppermute x1, waiting for transfers between devices, gather_line4(): passed = lax.ppermute(across, axis, [(2, 3), (1, 0)])  3.5 us
    ppermute x1, waiting for transfers between devices, swap_halves(): got = lax.ppermute(theirs, axis, [(0, 1), (1, 0)])  3.45 us
    ppermute x1, waiting for transfers between devices, gather_line4(): across = lax.ppermute(x, axis, [(0, 2), (1, 3), (2, 0), (3, 1)])  2.84 us
  transfers between devices with their start and end apart: 7, of which 5 were waited for; matrix products, arithmetic and copies ran while one was open for 9% of the time, Pallas kernels for 0%

profile of v14, /device:TPU:0, one launch (start us, length us, event | category | flops | bytes accessed | tf_op | source)
XLA Modules:
  0.0 71.8 jit_solution(7582665304014827178)
XLA Ops:
  0.6 0.0 copy-start
  0.7 0.8 %broadcast_compare_fusion = pred[2,128]{1,0:T(4,128)(4,1)S(1)} fusion(s32[128]{0:T(128)S(1)} %iota_add_fusion, s32[2]{0:T(128)} %param.10), kind=kLoop, calls=%fused_computation.29 | loop fusion | flops 256 | bytes 776 | tf_op jit(solution)/shard_map/lt | solution.py:263
  1.5 0.0 copy-start.5
  1.5 0.0 copy-start.6
  1.5 1.1 %broadcast_select_fusion.2.res_ref = bf16[2,128,512]{2,1,0:T(8,128)(2,1)S(1)} fusion(bf16[2,128,512]{2,1,0:T(8,128)(2,1)} %param.9, pred[2,128]{1,0:T(4,128)(4,1)S(1)} %broadcast_compare_fusion), kind=kLoop, calls=%fused_computation.19 | loop fusion | flops 131072 | bytes 524544 | tf_op jit(solution)/shard_map/jit(_where)/select_n | solution.py:264
  2.6 0.0 copy-start.1
  2.6 4.9 %collective-permute-start = (bf16[2,64,512]{2,1,0:T(8,128)(2,1)S(1)}, bf16[2,64,512]{2,1,0:T(8,128)(2,1)S(1)}, u32[]{:S(2)}, u32[]{:S(2)}) collective-permute-start(bf16[2,64,512]{2,1,0:T(8,128)(2,1)S(1)} %get-tuple-element.8), channel_id=1, source_target_pairs={{0,8},{8,16},{16,24},{1,9},{9,17},{17,25},{2,10},{10,18},{18,26},{... | collective-permute-start | bytes 393224 | tf_op jit(solution)/shard_map/ppermute | solution.py:20
  7.5 1.3 %collective-permute-start.1 = (bf16[2,64,512]{2,1,0:T(8,128)(2,1)S(1)}, bf16[2,64,512]{2,1,0:T(8,128)(2,1)S(1)}, u32[]{:S(2)}, u32[]{:S(2)}) collective-permute-start(bf16[2,64,512]{2,1,0:T(8,128)(2,1)S(1)} %get-tuple-element.9), channel_id=1, source_target_pairs={{8,0},{16,8},{24,16},{9,1},{17,9},{25,17},{10,2},{18,10},{26,18},{... | collective-permute-start | bytes 393224 | tf_op jit(solution)/shard_map/ppermute | solution.py:21
  8.9 1.3 %reshape.147 = f32[512]{0:T(512)} convert(bf16[512]{0:T(512)(128)(2,1)} %param.12) | non-fusion elementwise | flops 512 | bytes 3072 | tf_op jit(solution)/shard_map/reshape | solution.py:112
  10.1 0.2 collective-permute-done
  10.3 4.1 %collective-permute-done.1 = bf16[2,64,512]{2,1,0:T(8,128)(2,1)S(1)} collective-permute-done((bf16[2,64,512]{2,1,0:T(8,128)(2,1)S(1)}, bf16[2,64,512]{2,1,0:T(8,128)(2,1)S(1)}, u32[]{:S(2)}, u32[]{:S(2)}) %collective-permute-start.1) | collective-permute-done | bytes 131104 | tf_op jit(solution)/shard_map/ppermute | solution.py:21
  14.4 0.3 slice.24
  14.8 0.3 slice.27
  15.2 0.0 copy-start.3
  15.2 0.2 copy.14
  15.4 0.8 %copy.18 = bf16[2,256,8,64]{1,3,0,2:T(8,128)(2,1)} copy(bf16[2,256,8,64]{1,3,2,0:T(8,128)(2,1)S(1)} %bitcast.24) | data formatting | bytes 1048576 | tf_op jit(solution)/shard_map/reshape | solution.py:111
  16.2 0.0 copy-done.1
  16.2 0.0 copy-start.7
  16.2 21.9 %shard_map.104 = bf16[2,128,512]{2,1,0:T(8,128)(2,1)} custom-call(bf16[8,2,64,256]{3,2,1,0:T(8,128)(2,1)} %bitcast.23, bf16[8,64,64,128]{3,2,1,0:T(8,128)(2,1)} %bitcast.22, bf16[2,128,512]{2,1,0:T(8,128)(2,1)} %copy-done.1, f32[1,512]{1,0:T(1,128)} %bitcast.30), custom_call_target="tpu_custom_call" | custom-call | flops 2147483648 | bytes 9437184 | tf_op jit(solution)/shard_map/pallas_call | solution.py:86
  38.1 1.0 %constant_dynamic-slice_fusion = (bf16[1,128,512]{2,1,0:T(8,128)(2,1)S(1)}, bf16[128,512]{1,0:T(8,128)(2,1)S(1)}) fusion(bf16[2,128,512]{2,1,0:T(8,128)(2,1)} %shard_map.104, s32[]{:T(128)S(6)} %select_n.56, s32[]{:T(128)S(6)} %select_n.55), kind=kLoop, calls=%fused_computation.28 | loop fusion | bytes 524296 | tf_op jit(solution)/shard_map/jit(dynamic_index_in_dim)/dynamic_slice | solution.py:121
  39.1 1.6 %collective-permute-start.2 = (bf16[1,128,512]{2,1,0:T(8,128)(2,1)S(1)}, bf16[1,128,512]{2,1,0:T(8,128)(2,1)S(1)}, u32[]{:S(2)}, u32[]{:S(2)}) collective-permute-start(bf16[1,128,512]{2,1,0:T(8,128)(2,1)S(1)} %get-tuple-element.4), channel_id=1, source_target_pairs={{0,4},{4,0},{1,5},{5,1},{2,6},{6,2},{3,7},{7,3},{8,12},{12,8},{9,1... | collective-permute-start | bytes 393224 | tf_op jit(solution)/shard_map/ppermute | solution.py:122
  40.7 3.4 %collective-permute-done.2 = bf16[1,128,512]{2,1,0:T(8,128)(2,1)S(1)} collective-permute-done((bf16[1,128,512]{2,1,0:T(8,128)(2,1)S(1)}, bf16[1,128,512]{2,1,0:T(8,128)(2,1)S(1)}, u32[]{:S(2)}, u32[]{:S(2)}) %collective-permute-start.2) | collective-permute-done | bytes 131104 | tf_op jit(solution)/shard_map/ppermute | solution.py:122
  44.1 0.1 convert_reduce_fusion
  44.3 0.2 fusion.2
  44.5 0.0 copy-done
  44.5 0.0 copy-done.5
  44.5 0.0 copy-done.6
  44.5 0.4 convolution_convert_fusion.1
  44.9 0.0 copy-done.3
  44.9 0.4 convolution_convert_fusion
  45.3 0.0 copy-start.2
  45.3 2.6 %collective-permute-start.3 = (bf16[128,1024]{1,0:T(8,128)(2,1)S(1)}, bf16[128,1024]{1,0:T(8,128)(2,1)S(1)}, u32[]{:S(2)}, u32[]{:S(2)}) collective-permute-start(bf16[128,1024]{1,0:T(8,128)(2,1)S(1)} %pad_maximum_fusion.3.refs_3_), channel_id=1, source_target_pairs={{0,16},{8,24},{16,0},{24,8},{1,17},{9,25},{17,1},{25,9},{2,18},{10... | collective-permute-start | bytes 786440 | tf_op jit(solution)/shard_map/ppermute | solution.py:179
  47.9 0.0 copy-done.7
  47.9 0.6 dynamic_slice.13
  48.5 1.3 %fusion.6.refs_2_ = f32[128,1]{1,0:T(8,128)} fusion(s32[]{:T(128)S(6)} %mul.21, s32[]{:T(128)} %bitcast.10), kind=kLoop, calls=%fused_computation.22 | loop fusion | flops 384 | bytes 520 | tf_op jit(solution)/shard_map/convert_element_type | solution.py:163
  49.8 1.3 %collective-permute-start.6 = (bf16[128,1024]{1,0:T(8,128)(2,1)S(1)}, bf16[128,1024]{1,0:T(8,128)(2,1)S(1)}, u32[]{:S(2)}, u32[]{:S(2)}) collective-permute-start(bf16[128,1024]{1,0:T(8,128)(2,1)S(1)} %pad_maximum_fusion.3.refs_3_), channel_id=1, source_target_pairs={{8,0},{16,8},{24,16},{9,1},{17,9},{25,17},{10,2},{18,10},{26,18},{... | collective-permute-start | bytes 786440 | tf_op jit(solution)/shard_map/ppermute | solution.py:178
  51.1 4.6 %collective-permute-start.4 = (bf16[128,1024]{1,0:T(8,128)(2,1)S(1)}, bf16[128,1024]{1,0:T(8,128)(2,1)S(1)}, u32[]{:S(2)}, u32[]{:S(2)}) collective-permute-start(bf16[128,1024]{1,0:T(8,128)(2,1)S(1)} %pad_maximum_fusion.3.refs_3_), channel_id=1, source_target_pairs={{0,8},{8,16},{16,24},{1,9},{9,17},{17,25},{2,10},{10,18},{18,26},{... | collective-permute-start | bytes 786440 | tf_op jit(solution)/shard_map/ppermute | solution.py:177
  55.7 2.8 %collective-permute-done.3.refs_4_ = bf16[128,1024]{1,0:T(8,128)(2,1)S(1)} collective-permute-done((bf16[128,1024]{1,0:T(8,128)(2,1)S(1)}, bf16[128,1024]{1,0:T(8,128)(2,1)S(1)}, u32[]{:S(2)}, u32[]{:S(2)}) %collective-permute-start.3) | collective-permute-done | bytes 262176 | tf_op jit(solution)/shard_map/ppermute | solution.py:179
  58.5 1.3 %collective-permute-start.5 = (bf16[128,1024]{1,0:T(8,128)(2,1)S(1)}, bf16[128,1024]{1,0:T(8,128)(2,1)S(1)}, u32[]{:S(2)}, u32[]{:S(2)}) collective-permute-start(bf16[128,1024]{1,0:T(8,128)(2,1)S(1)} %collective-permute-done.3.refs_4_), channel_id=1, source_target_pairs={{16,24},{8,0},{17,25},{9,1},{18,26},{10,2},{19,27},{11,3},{20,28},... | collective-permute-start | bytes 786440 | tf_op jit(solution)/shard_map/ppermute | solution.py:180
  59.8 1.2 %compare_convert_fusion.refs_1_ = f32[1,512]{1,0:T(1,128)} fusion(s32[1,128]{1,0:T(1,128)S(1)} %get-tuple-element.10, s32[1,128]{1,0:T(1,128)S(1)} %get-tuple-element.11, s32[1,128]{1,0:T(1,128)S(1)} %get-tuple-element.12, s32[1,128]{1,0:T(1,128)S(1)} %get-tuple-element.13, s32[]{:T(128)} %bitcast.10), kind=kLoop, calls=%fused_computation.23 | loop fusion | flops 2560 | bytes 4100 | tf_op jit(solution)/shard_map/convert_element_type | solution.py:162
  61.0 2.2 %convolution_convert_fusion.2.refs_0_ = bf16[128,512]{1,0:T(8,128)(2,1)} fusion(bf16[1024,512]{1,0:T(8,128)(2,1)} %param.15, f32[1024]{0:T(1024)S(1)} %copy-done.5, f32[1024]{0:T(1024)S(1)} %copy-done.6, f32[128]{0:T(128)S(1)} %add_sqrt_fusion, f32[128]{0:T(128)S(1)} %broadcast_multiply_fusion, bf16[128,512]{1,0:T(8,128)(2,1)S(1)} %get-tuple-element.5, ...), kind=kOutput, calls=%fused_computation.2 | convolution fusion | flops 136249344 | bytes 1451009 | tf_op jit(solution)/shard_map/dot_general | solution.py:277
  63.3 0.0 collective-permute-done.6
  63.3 0.0 collective-permute-done.4
  63.3 3.5 %collective-permute-done.5 = bf16[128,1024]{1,0:T(8,128)(2,1)S(1)} collective-permute-done((bf16[128,1024]{1,0:T(8,128)(2,1)S(1)}, bf16[128,1024]{1,0:T(8,128)(2,1)S(1)}, u32[]{:S(2)}, u32[]{:S(2)}) %collective-permute-start.5) | collective-permute-done | bytes 262176 | tf_op jit(solution)/shard_map/ppermute | solution.py:180
  66.8 0.8 %broadcast_select_fusion = (bf16[128,1024]{1,0:T(8,128)(2,1)}, bf16[128,1024]{1,0:T(8,128)(2,1)}) fusion(bf16[128,1024]{1,0:T(8,128)(2,1)S(1)} %collective-permute-done.6, bf16[128,1024]{1,0:T(8,128)(2,1)S(1)} %collective-permute-done.5, pred[]{:T(512)S(6)} %le.3, bf16[128,1024]{1,0:T(8,128)(2,1)S(1)} %collective-permute-done.4, pred[]{:T(512)S(6)} %ge.3), kind=kLoop, calls=%fused_computation.17 | loop fusion | flops 262144 | bytes 1310722 | tf_op jit(solution)/shard_map/jit(_where)/select_n | solution.py:185
  67.6 0.0 copy-done.2
  67.6 0.0 copy-done.4
  67.6 4.2 %shard_map.105 = bf16[128,512]{1,0:T(8,128)(2,1)} custom-call(bf16[128,512]{1,0:T(8,128)(2,1)} %convolution_convert_fusion.2.refs_0_, f32[1,512]{1,0:T(1,128)} %compare_convert_fusion.refs_1_, f32[128,1]{1,0:T(8,128)} %fusion.6.refs_2_, bf16[128,1024]{1,0:T(8,128)(2,1)} %copy-done.2, bf16[128,1024]{1,0:T(8,128)(2,1)} %copy-done.4, ...), custom_call_target="tpu_custom_call" | custom-call | flops 268435456 | bytes 1310720 | tf_op jit(solution)/shard_map/pallas_call | solution.py:164
  (10 shorter events, 0.1 us)
Async XLA Ops:
  0.6 43.8 %copy-start = (bf16[1024,512]{1,0:T(8,128)(2,1)S(1)}, bf16[1024,512]{1,0:T(8,128)(2,1)}, u32[]{:S(2)}) copy-start(bf16[1024,512]{1,0:T(8,128)(2,1)} %param.16) | copy-start | bytes 3145732
  1.5 43.0 %copy-start.5 = (f32[1024]{0:T(1024)S(1)}, f32[1024]{0:T(1024)}, u32[]{:S(2)}) copy-start(f32[1024]{0:T(1024)} %param.14) | copy-start | bytes 12292
  1.5 43.0 %copy-start.6 = (f32[1024]{0:T(1024)S(1)}, f32[1024]{0:T(1024)}, u32[]{:S(2)}) copy-start(f32[1024]{0:T(1024)} %param.13) | copy-start | bytes 12292
  2.6 13.7 %copy-start.1 = (bf16[2,128,512]{2,1,0:T(8,128)(2,1)}, bf16[2,128,512]{2,1,0:T(8,128)(2,1)S(1)}, u32[]{:S(2)}) copy-start(bf16[2,128,512]{2,1,0:T(8,128)(2,1)S(1)} %broadcast_select_fusion.2.res_ref) | copy-start | bytes 786436
  2.6 7.7 %collective-permute-start = (bf16[2,64,512]{2,1,0:T(8,128)(2,1)S(1)}, bf16[2,64,512]{2,1,0:T(8,128)(2,1)S(1)}, u32[]{:S(2)}, u32[]{:S(2)}) collective-permute-start(bf16[2,64,512]{2,1,0:T(8,128)(2,1)S(1)} %get-tuple-element.8), channel_id=1, source_target_pairs={{0,8},{8,16},{16,24},{1,9},{9,17},{17,25},{2,10},{10,18},{18,26},{... | collective-permute-start | bytes 393224 | tf_op jit(solution)/shard_map/ppermute | solution.py:20
  7.5 6.9 %collective-permute-start.1 = (bf16[2,64,512]{2,1,0:T(8,128)(2,1)S(1)}, bf16[2,64,512]{2,1,0:T(8,128)(2,1)S(1)}, u32[]{:S(2)}, u32[]{:S(2)}) collective-permute-start(bf16[2,64,512]{2,1,0:T(8,128)(2,1)S(1)} %get-tuple-element.9), channel_id=1, source_target_pairs={{8,0},{16,8},{24,16},{9,1},{17,9},{25,17},{10,2},{18,10},{26,18},{... | collective-permute-start | bytes 393224 | tf_op jit(solution)/shard_map/ppermute | solution.py:21
  15.2 29.7 %copy-start.3 = (bf16[1024,512]{1,0:T(8,128)(2,1)S(1)}, bf16[1024,512]{1,0:T(8,128)(2,1)}, u32[]{:S(2)}) copy-start(bf16[1024,512]{1,0:T(8,128)(2,1)} %param.17) | copy-start | bytes 3145732
  16.2 31.7 %copy-start.7 = (s32[2]{0:T(128)S(1)}, s32[2]{0:T(128)}, u32[]{:S(2)}) copy-start(s32[2]{0:T(128)} %param.10) | copy-start | bytes 28
  39.1 5.0 %collective-permute-start.2 = (bf16[1,128,512]{2,1,0:T(8,128)(2,1)S(1)}, bf16[1,128,512]{2,1,0:T(8,128)(2,1)S(1)}, u32[]{:S(2)}, u32[]{:S(2)}) collective-permute-start(bf16[1,128,512]{2,1,0:T(8,128)(2,1)S(1)} %get-tuple-element.4), channel_id=1, source_target_pairs={{0,4},{4,0},{1,5},{5,1},{2,6},{6,2},{3,7},{7,3},{8,12},{12,8},{9,1... | collective-permute-start | bytes 393224 | tf_op jit(solution)/shard_map/ppermute | solution.py:122
  45.3 22.3 %copy-start.2 = (bf16[128,1024]{1,0:T(8,128)(2,1)}, bf16[128,1024]{1,0:T(8,128)(2,1)S(1)}, u32[]{:S(2)}) copy-start(bf16[128,1024]{1,0:T(8,128)(2,1)S(1)} %pad_maximum_fusion.3.refs_3_) | copy-start | bytes 786436
  45.3 13.2 %collective-permute-start.3 = (bf16[128,1024]{1,0:T(8,128)(2,1)S(1)}, bf16[128,1024]{1,0:T(8,128)(2,1)S(1)}, u32[]{:S(2)}, u32[]{:S(2)}) collective-permute-start(bf16[128,1024]{1,0:T(8,128)(2,1)S(1)} %pad_maximum_fusion.3.refs_3_), channel_id=1, source_target_pairs={{0,16},{8,24},{16,0},{24,8},{1,17},{9,25},{17,1},{25,9},{2,18},{10... | collective-permute-start | bytes 786440 | tf_op jit(solution)/shard_map/ppermute | solution.py:179
  49.8 13.5 %collective-permute-start.6 = (bf16[128,1024]{1,0:T(8,128)(2,1)S(1)}, bf16[128,1024]{1,0:T(8,128)(2,1)S(1)}, u32[]{:S(2)}, u32[]{:S(2)}) collective-permute-start(bf16[128,1024]{1,0:T(8,128)(2,1)S(1)} %pad_maximum_fusion.3.refs_3_), channel_id=1, source_target_pairs={{8,0},{16,8},{24,16},{9,1},{17,9},{25,17},{10,2},{18,10},{26,18},{... | collective-permute-start | bytes 786440 | tf_op jit(solution)/shard_map/ppermute | solution.py:178
  51.1 12.2 %collective-permute-start.4 = (bf16[128,1024]{1,0:T(8,128)(2,1)S(1)}, bf16[128,1024]{1,0:T(8,128)(2,1)S(1)}, u32[]{:S(2)}, u32[]{:S(2)}) collective-permute-start(bf16[128,1024]{1,0:T(8,128)(2,1)S(1)} %pad_maximum_fusion.3.refs_3_), channel_id=1, source_target_pairs={{0,8},{8,16},{16,24},{1,9},{9,17},{17,25},{2,10},{10,18},{18,26},{... | collective-permute-start | bytes 786440 | tf_op jit(solution)/shard_map/ppermute | solution.py:177
  58.5 9.1 %copy-start.4 = (bf16[128,1024]{1,0:T(8,128)(2,1)}, bf16[128,1024]{1,0:T(8,128)(2,1)S(1)}, u32[]{:S(2)}) copy-start(bf16[128,1024]{1,0:T(8,128)(2,1)S(1)} %collective-permute-done.3.refs_4_) | copy-start | bytes 786436
  58.5 8.3 %collective-permute-start.5 = (bf16[128,1024]{1,0:T(8,128)(2,1)S(1)}, bf16[128,1024]{1,0:T(8,128)(2,1)S(1)}, u32[]{:S(2)}, u32[]{:S(2)}) collective-permute-start(bf16[128,1024]{1,0:T(8,128)(2,1)S(1)} %collective-permute-done.3.refs_4_), channel_id=1, source_target_pairs={{16,24},{8,0},{17,25},{9,1},{18,26},{10,2},{19,27},{11,3},{20,28},... | collective-permute-start | bytes 786440 | tf_op jit(solution)/shard_map/ppermute | solution.py:180

commit v15 on v14

--- a/solution.py
+++ b/solution.py
@@ -83,16 +83,17 @@
 def hankel_conv(xt, wv, residual, bias, rows):
     groups, recs, chans, lanes = xt.shape
     taps, outs = wv.shape[3], wv.shape[2]
+    step = 4 if groups % 4 == 0 else 2
     return pl.pallas_call(
         conv_body,
-        grid=(groups // 2,),
+        grid=(groups // step,),
         in_specs=[
-            pl.BlockSpec((2, recs, chans, lanes), lambda g: (g, 0, 0, 0)),
-            pl.BlockSpec((2, chans, outs, taps), lambda g: (g, 0, 0, 0)),
-            pl.BlockSpec((recs, rows, 2 * outs), lambda g: (0, 0, g)),
-            pl.BlockSpec((1, 2 * outs), lambda g: (0, g)),
+            pl.BlockSpec((step, recs, chans, lanes), lambda g: (g, 0, 0, 0)),
+            pl.BlockSpec((step, chans, outs, taps), lambda g: (g, 0, 0, 0)),
+            pl.BlockSpec((recs, rows, step * outs), lambda g: (0, 0, g)),
+            pl.BlockSpec((1, step * outs), lambda g: (0, g)),
         ],
-        out_specs=pl.BlockSpec((recs, rows, 2 * outs), lambda g: (0, 0, g)),
+        out_specs=pl.BlockSpec((recs, rows, step * outs), lambda g: (0, 0, g)),
         out_shape=jax.ShapeDtypeStruct((recs, rows, groups * outs), jnp.bfloat16),
         cost_estimate=pl.CostEstimate(
             flops=2 * groups * recs * rows * taps * chans * outs,

time: 72.2 us -> 72 us (level)
  no operation moved by 1% of the time
where the time goes in v15:
time: 72 us; the launch traced here: 71.7 us
  Pallas kernels  25.9 us (36%)
  starting transfers between devices  17.6 us (24%)
  waiting for transfers between devices  14.1 us (20%)
  other arithmetic  6.95 us (10%)
  local copies, waits for them, and re-layouts  3.32 us (5%)
  matrix products  2.95 us (4%)
  between operations  0.84 us (1%)
    pallas_call x1, Pallas kernels, hankel_conv(): pl.pallas_call(conv_body, grid=(groups // step,), in_specs=[pl.BlockSpec(...  21.7 us
    ppermute x1, starting transfers between devices, padded_2(): before = lax.ppermute(last, axis, up)  4.94 us
    ppermute x1, starting transfers between devices, gather_line4(): from_below = lax.ppermute(x, axis, [(0, 1), (1, 2), (2, 3)])  4.56 us
    pallas_call x1, Pallas kernels, fused_attention(): pl.pallas_call(attend_body, out_shape=jax.ShapeDtypeStruct((rows, width),...  4.18 us
    ppermute x1, waiting for transfers between devices, padded_2(): after = lax.ppermute(first, axis, down)  4.13 us
    ppermute x1, waiting for transfers between devices, gather_line4(): passed = lax.ppermute(across, axis, [(2, 3), (1, 0)])  3.5 us
    ppermute x1, waiting for transfers between devices, swap_halves(): got = lax.ppermute(theirs, axis, [(0, 1), (1, 0)])  3.44 us
    ppermute x1, waiting for transfers between devices, gather_line4(): across = lax.ppermute(x, axis, [(0, 2), (1, 3), (2, 0), (3, 1)])  2.85 us
  transfers between devices with their start and end apart: 7, of which 5 were waited for; matrix products, arithmetic and copies ran while one was open for 9% of the time, Pallas kernels for 0%

profile of v15, /device:TPU:0, one launch (start us, length us, event | category | flops | bytes accessed | tf_op | source)
XLA Modules:
  0.0 71.7 jit_solution(18054912688882350045)
XLA Ops:
  0.6 0.0 copy-start
  0.7 0.8 %broadcast_compare_fusion = pred[2,128]{1,0:T(4,128)(4,1)S(1)} fusion(s32[128]{0:T(128)S(1)} %iota_add_fusion, s32[2]{0:T(128)} %param.10), kind=kLoop, calls=%fused_computation.29 | loop fusion | flops 256 | bytes 776 | tf_op jit(solution)/shard_map/lt | solution.py:264
  1.5 0.0 copy-start.6
  1.5 1.1 %broadcast_select_fusion.2.res_ref = bf16[2,128,512]{2,1,0:T(8,128)(2,1)S(1)} fusion(bf16[2,128,512]{2,1,0:T(8,128)(2,1)} %param.9, pred[2,128]{1,0:T(4,128)(4,1)S(1)} %broadcast_compare_fusion), kind=kLoop, calls=%fused_computation.19 | loop fusion | flops 131072 | bytes 524544 | tf_op jit(solution)/shard_map/jit(_where)/select_n | solution.py:265
  2.6 0.0 copy-start.1
  2.6 4.9 %collective-permute-start = (bf16[2,64,512]{2,1,0:T(8,128)(2,1)S(1)}, bf16[2,64,512]{2,1,0:T(8,128)(2,1)S(1)}, u32[]{:S(2)}, u32[]{:S(2)}) collective-permute-start(bf16[2,64,512]{2,1,0:T(8,128)(2,1)S(1)} %get-tuple-element.8), channel_id=1, source_target_pairs={{0,8},{8,16},{16,24},{1,9},{9,17},{17,25},{2,10},{10,18},{18,26},{... | collective-permute-start | bytes 393224 | tf_op jit(solution)/shard_map/ppermute | solution.py:20
  7.5 1.3 %collective-permute-start.1 = (bf16[2,64,512]{2,1,0:T(8,128)(2,1)S(1)}, bf16[2,64,512]{2,1,0:T(8,128)(2,1)S(1)}, u32[]{:S(2)}, u32[]{:S(2)}) collective-permute-start(bf16[2,64,512]{2,1,0:T(8,128)(2,1)S(1)} %get-tuple-element.9), channel_id=1, source_target_pairs={{8,0},{16,8},{24,16},{9,1},{17,9},{25,17},{10,2},{18,10},{26,18},{... | collective-permute-start | bytes 393224 | tf_op jit(solution)/shard_map/ppermute | solution.py:21
  8.9 1.3 %reshape.147 = f32[512]{0:T(512)} convert(bf16[512]{0:T(512)(128)(2,1)} %param.12) | non-fusion elementwise | flops 512 | bytes 3072 | tf_op jit(solution)/shard_map/reshape | solution.py:113
  10.1 0.2 collective-permute-done
  10.3 4.1 %collective-permute-done.1 = bf16[2,64,512]{2,1,0:T(8,128)(2,1)S(1)} collective-permute-done((bf16[2,64,512]{2,1,0:T(8,128)(2,1)S(1)}, bf16[2,64,512]{2,1,0:T(8,128)(2,1)S(1)}, u32[]{:S(2)}, u32[]{:S(2)}) %collective-permute-start.1) | collective-permute-done | bytes 131104 | tf_op jit(solution)/shard_map/ppermute | solution.py:21
  14.4 0.3 slice.24
  14.8 0.3 slice.27
  15.2 0.0 copy-start.3
  15.2 0.2 copy.14
  15.4 0.8 %copy.18 = bf16[2,256,8,64]{1,3,0,2:T(8,128)(2,1)} copy(bf16[2,256,8,64]{1,3,2,0:T(8,128)(2,1)S(1)} %bitcast.24) | data formatting | bytes 1048576 | tf_op jit(solution)/shard_map/reshape | solution.py:112
  16.2 0.0 copy-done.1
  16.2 0.0 copy-start.7
  16.2 21.7 %shard_map.104 = bf16[2,128,512]{2,1,0:T(8,128)(2,1)} custom-call(bf16[8,2,64,256]{3,2,1,0:T(8,128)(2,1)} %bitcast.23, bf16[8,64,64,128]{3,2,1,0:T(8,128)(2,1)} %bitcast.22, bf16[2,128,512]{2,1,0:T(8,128)(2,1)} %copy-done.1, f32[1,512]{1,0:T(1,128)} %bitcast.30), custom_call_target="tpu_custom_call" | custom-call | flops 2147483648 | bytes 9437184 | tf_op jit(solution)/shard_map/pallas_call | solution.py:87
  38.0 1.0 %constant_dynamic-slice_fusion = (bf16[1,128,512]{2,1,0:T(8,128)(2,1)S(1)}, bf16[128,512]{1,0:T(8,128)(2,1)S(1)}) fusion(bf16[2,128,512]{2,1,0:T(8,128)(2,1)} %shard_map.104, s32[]{:T(128)S(6)} %select_n.56, s32[]{:T(128)S(6)} %select_n.55), kind=kLoop, calls=%fused_computation.28 | loop fusion | bytes 524296 | tf_op jit(solution)/shard_map/jit(dynamic_index_in_dim)/dynamic_slice | solution.py:122
  38.9 1.6 %collective-permute-start.2 = (bf16[1,128,512]{2,1,0:T(8,128)(2,1)S(1)}, bf16[1,128,512]{2,1,0:T(8,128)(2,1)S(1)}, u32[]{:S(2)}, u32[]{:S(2)}) collective-permute-start(bf16[1,128,512]{2,1,0:T(8,128)(2,1)S(1)} %get-tuple-element.4), channel_id=1, source_target_pairs={{0,4},{4,0},{1,5},{5,1},{2,6},{6,2},{3,7},{7,3},{8,12},{12,8},{9,1... | collective-permute-start | bytes 393224 | tf_op jit(solution)/shard_map/ppermute | solution.py:123
  40.5 3.4 %collective-permute-done.2 = bf16[1,128,512]{2,1,0:T(8,128)(2,1)S(1)} collective-permute-done((bf16[1,128,512]{2,1,0:T(8,128)(2,1)S(1)}, bf16[1,128,512]{2,1,0:T(8,128)(2,1)S(1)}, u32[]{:S(2)}, u32[]{:S(2)}) %collective-permute-start.2) | collective-permute-done | bytes 131104 | tf_op jit(solution)/shard_map/ppermute | solution.py:123
  44.0 0.1 convert_reduce_fusion
  44.1 0.2 fusion.2
  44.3 0.0 copy-done
  44.3 0.0 copy-done.5
  44.4 0.0 copy-done.6
  44.4 0.4 convolution_convert_fusion.1
  44.7 0.0 copy-done.3
  44.7 0.4 convolution_convert_fusion
  45.1 0.0 copy-start.2
  45.1 2.7 %collective-permute-start.3 = (bf16[128,1024]{1,0:T(8,128)(2,1)S(1)}, bf16[128,1024]{1,0:T(8,128)(2,1)S(1)}, u32[]{:S(2)}, u32[]{:S(2)}) collective-permute-start(bf16[128,1024]{1,0:T(8,128)(2,1)S(1)} %pad_maximum_fusion.3.refs_3_), channel_id=1, source_target_pairs={{0,16},{8,24},{16,0},{24,8},{1,17},{9,25},{17,1},{25,9},{2,18},{10... | collective-permute-start | bytes 786440 | tf_op jit(solution)/shard_map/ppermute | solution.py:180
  47.8 0.0 copy-done.7
  47.8 0.6 dynamic_slice.13
  48.4 1.3 %fusion.6.refs_2_ = f32[128,1]{1,0:T(8,128)} fusion(s32[]{:T(128)S(6)} %mul.21, s32[]{:T(128)} %bitcast.10), kind=kLoop, calls=%fused_computation.22 | loop fusion | flops 384 | bytes 520 | tf_op jit(solution)/shard_map/convert_element_type | solution.py:164
  49.7 1.3 %collective-permute-start.6 = (bf16[128,1024]{1,0:T(8,128)(2,1)S(1)}, bf16[128,1024]{1,0:T(8,128)(2,1)S(1)}, u32[]{:S(2)}, u32[]{:S(2)}) collective-permute-start(bf16[128,1024]{1,0:T(8,128)(2,1)S(1)} %pad_maximum_fusion.3.refs_3_), channel_id=1, source_target_pairs={{8,0},{16,8},{24,16},{9,1},{17,9},{25,17},{10,2},{18,10},{26,18},{... | collective-permute-start | bytes 786440 | tf_op jit(solution)/shard_map/ppermute | solution.py:179
  51.0 4.6 %collective-permute-start.4 = (bf16[128,1024]{1,0:T(8,128)(2,1)S(1)}, bf16[128,1024]{1,0:T(8,128)(2,1)S(1)}, u32[]{:S(2)}, u32[]{:S(2)}) collective-permute-start(bf16[128,1024]{1,0:T(8,128)(2,1)S(1)} %pad_maximum_fusion.3.refs_3_), channel_id=1, source_target_pairs={{0,8},{8,16},{16,24},{1,9},{9,17},{17,25},{2,10},{10,18},{18,26},{... | collective-permute-start | bytes 786440 | tf_op jit(solution)/shard_map/ppermute | solution.py:178
  55.5 2.8 %collective-permute-done.3.refs_4_ = bf16[128,1024]{1,0:T(8,128)(2,1)S(1)} collective-permute-done((bf16[128,1024]{1,0:T(8,128)(2,1)S(1)}, bf16[128,1024]{1,0:T(8,128)(2,1)S(1)}, u32[]{:S(2)}, u32[]{:S(2)}) %collective-permute-start.3) | collective-permute-done | bytes 262176 | tf_op jit(solution)/shard_map/ppermute | solution.py:180
  58.4 0.0 copy-start.4
  58.4 1.3 %collective-permute-start.5 = (bf16[128,1024]{1,0:T(8,128)(2,1)S(1)}, bf16[128,1024]{1,0:T(8,128)(2,1)S(1)}, u32[]{:S(2)}, u32[]{:S(2)}) collective-permute-start(bf16[128,1024]{1,0:T(8,128)(2,1)S(1)} %collective-permute-done.3.refs_4_), channel_id=1, source_target_pairs={{16,24},{8,0},{17,25},{9,1},{18,26},{10,2},{19,27},{11,3},{20,28},... | collective-permute-start | bytes 786440 | tf_op jit(solution)/shard_map/ppermute | solution.py:181
  59.7 1.2 %compare_convert_fusion.refs_1_ = f32[1,512]{1,0:T(1,128)} fusion(s32[1,128]{1,0:T(1,128)S(1)} %get-tuple-element.10, s32[1,128]{1,0:T(1,128)S(1)} %get-tuple-element.11, s32[1,128]{1,0:T(1,128)S(1)} %get-tuple-element.12, s32[1,128]{1,0:T(1,128)S(1)} %get-tuple-element.13, s32[]{:T(128)} %bitcast.10), kind=kLoop, calls=%fused_computation.23 | loop fusion | flops 2560 | bytes 4100 | tf_op jit(solution)/shard_map/convert_element_type | solution.py:163
  60.9 2.2 %convolution_convert_fusion.2.refs_0_ = bf16[128,512]{1,0:T(8,128)(2,1)} fusion(bf16[1024,512]{1,0:T(8,128)(2,1)} %param.15, f32[1024]{0:T(1024)S(1)} %copy-done.5, f32[1024]{0:T(1024)S(1)} %copy-done.6, f32[128]{0:T(128)S(1)} %add_sqrt_fusion, f32[128]{0:T(128)S(1)} %broadcast_multiply_fusion, bf16[128,512]{1,0:T(8,128)(2,1)S(1)} %get-tuple-element.5, ...), kind=kOutput, calls=%fused_computation.2 | convolution fusion | flops 136249344 | bytes 1451009 | tf_op jit(solution)/shard_map/dot_general | solution.py:278
  63.1 0.0 collective-permute-done.6
  63.1 0.0 collective-permute-done.4
  63.1 3.5 %collective-permute-done.5 = bf16[128,1024]{1,0:T(8,128)(2,1)S(1)} collective-permute-done((bf16[128,1024]{1,0:T(8,128)(2,1)S(1)}, bf16[128,1024]{1,0:T(8,128)(2,1)S(1)}, u32[]{:S(2)}, u32[]{:S(2)}) %collective-permute-start.5) | collective-permute-done | bytes 262176 | tf_op jit(solution)/shard_map/ppermute | solution.py:181
  66.6 0.8 %broadcast_select_fusion = (bf16[128,1024]{1,0:T(8,128)(2,1)}, bf16[128,1024]{1,0:T(8,128)(2,1)}) fusion(bf16[128,1024]{1,0:T(8,128)(2,1)S(1)} %collective-permute-done.6, bf16[128,1024]{1,0:T(8,128)(2,1)S(1)} %collective-permute-done.5, pred[]{:T(512)S(6)} %le.3, bf16[128,1024]{1,0:T(8,128)(2,1)S(1)} %collective-permute-done.4, pred[]{:T(512)S(6)} %ge.3), kind=kLoop, calls=%fused_computation.17 | loop fusion | flops 262144 | bytes 1310722 | tf_op jit(solution)/shard_map/jit(_where)/select_n | solution.py:186
  67.5 0.0 copy-done.2
  67.5 0.0 copy-done.4
  67.5 4.2 %shard_map.105 = bf16[128,512]{1,0:T(8,128)(2,1)} custom-call(bf16[128,512]{1,0:T(8,128)(2,1)} %convolution_convert_fusion.2.refs_0_, f32[1,512]{1,0:T(1,128)} %compare_convert_fusion.refs_1_, f32[128,1]{1,0:T(8,128)} %fusion.6.refs_2_, bf16[128,1024]{1,0:T(8,128)(2,1)} %copy-done.2, bf16[128,1024]{1,0:T(8,128)(2,1)} %copy-done.4, ...), custom_call_target="tpu_custom_call" | custom-call | flops 268435456 | bytes 1310720 | tf_op jit(solution)/shard_map/pallas_call | solution.py:165
  (10 shorter events, 0.1 us)
Async XLA Ops:
  0.6 43.7 %copy-start = (bf16[1024,512]{1,0:T(8,128)(2,1)S(1)}, bf16[1024,512]{1,0:T(8,128)(2,1)}, u32[]{:S(2)}) copy-start(bf16[1024,512]{1,0:T(8,128)(2,1)} %param.16) | copy-start | bytes 3145732
  1.5 42.9 %copy-start.5 = (f32[1024]{0:T(1024)S(1)}, f32[1024]{0:T(1024)}, u32[]{:S(2)}) copy-start(f32[1024]{0:T(1024)} %param.14) | copy-start | bytes 12292
  1.5 42.9 %copy-start.6 = (f32[1024]{0:T(1024)S(1)}, f32[1024]{0:T(1024)}, u32[]{:S(2)}) copy-start(f32[1024]{0:T(1024)} %param.13) | copy-start | bytes 12292
  2.6 13.7 %copy-start.1 = (bf16[2,128,512]{2,1,0:T(8,128)(2,1)}, bf16[2,128,512]{2,1,0:T(8,128)(2,1)S(1)}, u32[]{:S(2)}) copy-start(bf16[2,128,512]{2,1,0:T(8,128)(2,1)S(1)} %broadcast_select_fusion.2.res_ref) | copy-start | bytes 786436
  2.6 7.7 %collective-permute-start = (bf16[2,64,512]{2,1,0:T(8,128)(2,1)S(1)}, bf16[2,64,512]{2,1,0:T(8,128)(2,1)S(1)}, u32[]{:S(2)}, u32[]{:S(2)}) collective-permute-start(bf16[2,64,512]{2,1,0:T(8,128)(2,1)S(1)} %get-tuple-element.8), channel_id=1, source_target_pairs={{0,8},{8,16},{16,24},{1,9},{9,17},{17,25},{2,10},{10,18},{18,26},{... | collective-permute-start | bytes 393224 | tf_op jit(solution)/shard_map/ppermute | solution.py:20
  7.5 6.9 %collective-permute-start.1 = (bf16[2,64,512]{2,1,0:T(8,128)(2,1)S(1)}, bf16[2,64,512]{2,1,0:T(8,128)(2,1)S(1)}, u32[]{:S(2)}, u32[]{:S(2)}) collective-permute-start(bf16[2,64,512]{2,1,0:T(8,128)(2,1)S(1)} %get-tuple-element.9), channel_id=1, source_target_pairs={{8,0},{16,8},{24,16},{9,1},{17,9},{25,17},{10,2},{18,10},{26,18},{... | collective-permute-start | bytes 393224 | tf_op jit(solution)/shard_map/ppermute | solution.py:21
  15.2 29.6 %copy-start.3 = (bf16[1024,512]{1,0:T(8,128)(2,1)S(1)}, bf16[1024,512]{1,0:T(8,128)(2,1)}, u32[]{:S(2)}) copy-start(bf16[1024,512]{1,0:T(8,128)(2,1)} %param.17) | copy-start | bytes 3145732
  16.2 31.6 %copy-start.7 = (s32[2]{0:T(128)S(1)}, s32[2]{0:T(128)}, u32[]{:S(2)}) copy-start(s32[2]{0:T(128)} %param.10) | copy-start | bytes 28
  38.9 5.0 %collective-permute-start.2 = (bf16[1,128,512]{2,1,0:T(8,128)(2,1)S(1)}, bf16[1,128,512]{2,1,0:T(8,128)(2,1)S(1)}, u32[]{:S(2)}, u32[]{:S(2)}) collective-permute-start(bf16[1,128,512]{2,1,0:T(8,128)(2,1)S(1)} %get-tuple-element.4), channel_id=1, source_target_pairs={{0,4},{4,0},{1,5},{5,1},{2,6},{6,2},{3,7},{7,3},{8,12},{12,8},{9,1... | collective-permute-start | bytes 393224 | tf_op jit(solution)/shard_map/ppermute | solution.py:123
  45.1 22.3 %copy-start.2 = (bf16[128,1024]{1,0:T(8,128)(2,1)}, bf16[128,1024]{1,0:T(8,128)(2,1)S(1)}, u32[]{:S(2)}) copy-start(bf16[128,1024]{1,0:T(8,128)(2,1)S(1)} %pad_maximum_fusion.3.refs_3_) | copy-start | bytes 786436
  45.1 13.2 %collective-permute-start.3 = (bf16[128,1024]{1,0:T(8,128)(2,1)S(1)}, bf16[128,1024]{1,0:T(8,128)(2,1)S(1)}, u32[]{:S(2)}, u32[]{:S(2)}) collective-permute-start(bf16[128,1024]{1,0:T(8,128)(2,1)S(1)} %pad_maximum_fusion.3.refs_3_), channel_id=1, source_target_pairs={{0,16},{8,24},{16,0},{24,8},{1,17},{9,25},{17,1},{25,9},{2,18},{10... | collective-permute-start | bytes 786440 | tf_op jit(solution)/shard_map/ppermute | solution.py:180
  49.7 13.5 %collective-permute-start.6 = (bf16[128,1024]{1,0:T(8,128)(2,1)S(1)}, bf16[128,1024]{1,0:T(8,128)(2,1)S(1)}, u32[]{:S(2)}, u32[]{:S(2)}) collective-permute-start(bf16[128,1024]{1,0:T(8,128)(2,1)S(1)} %pad_maximum_fusion.3.refs_3_), channel_id=1, source_target_pairs={{8,0},{16,8},{24,16},{9,1},{17,9},{25,17},{10,2},{18,10},{26,18},{... | collective-permute-start | bytes 786440 | tf_op jit(solution)/shard_map/ppermute | solution.py:179
  51.0 12.2 %collective-permute-start.4 = (bf16[128,1024]{1,0:T(8,128)(2,1)S(1)}, bf16[128,1024]{1,0:T(8,128)(2,1)S(1)}, u32[]{:S(2)}, u32[]{:S(2)}) collective-permute-start(bf16[128,1024]{1,0:T(8,128)(2,1)S(1)} %pad_maximum_fusion.3.refs_3_), channel_id=1, source_target_pairs={{0,8},{8,16},{16,24},{1,9},{9,17},{17,25},{2,10},{10,18},{18,26},{... | collective-permute-start | bytes 786440 | tf_op jit(solution)/shard_map/ppermute | solution.py:178
  58.4 9.1 %copy-start.4 = (bf16[128,1024]{1,0:T(8,128)(2,1)}, bf16[128,1024]{1,0:T(8,128)(2,1)S(1)}, u32[]{:S(2)}) copy-start(bf16[128,1024]{1,0:T(8,128)(2,1)S(1)} %collective-permute-done.3.refs_4_) | copy-start | bytes 786436
  58.4 8.3 %collective-permute-start.5 = (bf16[128,1024]{1,0:T(8,128)(2,1)S(1)}, bf16[128,1024]{1,0:T(8,128)(2,1)S(1)}, u32[]{:S(2)}, u32[]{:S(2)}) collective-permute-start(bf16[128,1024]{1,0:T(8,128)(2,1)S(1)} %collective-permute-done.3.refs_4_), channel_id=1, source_target_pairs={{16,24},{8,0},{17,25},{9,1},{18,26},{10,2},{19,27},{11,3},{20,28},... | collective-permute-start | bytes 786440 | tf_op jit(solution)/shard_map/ppermute | solution.py:181
